TPU v7x, 128 devices: a whole 4x4x4 slice. The times are simulated.
128 devices in a mesh: px: 8 (over y, core), py: 16 (over z, x).
Axes of the slice: x: 4, y: 4, z: 4, core: 2. Of those that a mesh axis runs over, the one named last changes fastest.
Arguments:
- kappa: bfloat16 [301056, 128], P(('px', 'py')), may hold values from -6 to 6
- send_list: int32 [128, 128, 192], P(('px', 'py')), may hold values from 0 to 2351, as said below
- dest_slot: int32 [128, 128, 192], P(('px', 'py')), may hold values from 0 to 2047, as said below
- send_count: int32 [128, 128], P(('px', 'py')), may hold values from 0 to 192, as said below
Outputs:
- flexion: float32 [4, 4096, 8192], P(None, 'px', 'py')
Inputs may be any that keep to these rules, and one draw needn't show every extreme that they name: For k < send_count[a, d], send_list[a, d, k] is a row of source a's own 2352 tiles; later entries are 0. Over all sources a and k < send_count[a, d], dest_slot[a, d, k] names every slot of patch d exactly once; later entries are 0. send_count[a, d] is nonzero only where d's patch row equals a's px index or is one less; it is a multiple of 4, and reaches 192 in every draw. Summed over the sources a whose px index is one more than d's patch row, it is exactly 512.
All inputs are finite; a program needn't handle non-finite values.
Results may differ from a plain program's by a relative error of at most 0.0065.
Values may be sent and summed in bfloat16 or wider, within the bound.
No kernel may reach another device: no remote copies, remote signals or barrier semaphores. Data moves between devices by JAX's collectives and lax.ppermute only.
A program may use at most 64 MiB of HBM per device.

v0:
```python
import math

import jax
import jax.numpy as jnp
from jax import lax
from jax.sharding import PartitionSpec as P

PATCH_ROWS = 512
PATCH_COLS = 512


def shifted(shard, axis, by):
    size = lax.axis_size(axis)
    pairs = [(i, i + by) for i in range(size) if 0 <= i + by < size]
    return lax.ppermute(shard, axis, pairs)


def padded(block, sides, width):
    for axis, dim in sides:
        count = lax.axis_size(axis)
        forward = [(i, i + 1) for i in range(count - 1)]
        backward = [(target, source) for source, target in forward]
        low = lax.ppermute(
            lax.slice_in_dim(block, block.shape[dim] - width, None, axis=dim), axis, forward
        )
        high = lax.ppermute(lax.slice_in_dim(block, 0, width, axis=dim), axis, backward)
        block = jnp.concatenate([low, block, high], axis=dim)
    return block


def dft_tables(length):
    positions = jnp.arange(length, dtype=jnp.int32)
    phases = positions[:, None] * positions[None, :] % length
    angles = phases.astype(jnp.float32) * (2.0 * math.pi / length)
    return (jnp.cos(angles), jnp.sin(angles))


def wavenumbers(length):
    positions = jnp.arange(length, dtype=jnp.int32)
    signed = positions - length * (positions >= (length + 1) // 2).astype(jnp.int32)
    return signed.astype(jnp.float32) * (2.0 / length)


def flexion_fields(pixels):
    row_count = pixels.shape[0]
    col_count = pixels.shape[1]
    cos_cols, sin_cols = dft_tables(col_count)
    cos_rows, sin_rows = dft_tables(row_count)
    forward_cols = jnp.concatenate([cos_cols, sin_cols], axis=1).astype(jnp.bfloat16)
    halves = jnp.dot(pixels, forward_cols, preferred_element_type=jnp.float32)
    stacked = jnp.concatenate([halves[:, :col_count], halves[:, col_count:]], axis=0).astype(
        jnp.bfloat16
    )
    forward_rows = jnp.concatenate(
        [
            jnp.concatenate([cos_rows, -sin_rows], axis=1),
            jnp.concatenate([-sin_rows, -cos_rows], axis=1),
        ],
        axis=0,
    ).astype(jnp.bfloat16)
    spectrum = jnp.dot(forward_rows, stacked, preferred_element_type=jnp.float32)
    real_part = spectrum[:row_count]
    imag_part = spectrum[row_count:]
    across = wavenumbers(col_count)[None, :]
    down = wavenumbers(row_count)[:, None]
    scale = 1.0 / (row_count * col_count)
    power = across * across + down * down
    safe_power = jnp.where(power > 0, power, 1.0)
    cube_real = across * across * across - 3.0 * across * down * down
    cube_imag = 3.0 * across * across * down - down * down * down
    one_real = (-down * real_part - across * imag_part) * scale
    one_imag = (across * real_part - down * imag_part) * scale
    kernel_real = -cube_imag / safe_power
    kernel_imag = cube_real / safe_power
    three_real = (kernel_real * real_part - kernel_imag * imag_part) * scale
    three_imag = (kernel_real * imag_part + kernel_imag * real_part) * scale
    spectra = jnp.concatenate(
        [
            jnp.concatenate([one_real, three_real], axis=1),
            jnp.concatenate([one_imag, three_imag], axis=1),
        ],
        axis=0,
    ).astype(jnp.bfloat16)
    inverse_rows = jnp.concatenate(
        [
            jnp.concatenate([cos_rows, -sin_rows], axis=1),
            jnp.concatenate([sin_rows, cos_rows], axis=1),
        ],
        axis=0,
    ).astype(jnp.bfloat16)
    columns_done = jnp.dot(inverse_rows, spectra, preferred_element_type=jnp.float32).astype(
        jnp.bfloat16
    )
    arranged = jnp.concatenate(
        [
            jnp.concatenate(
                [columns_done[:row_count, :col_count], columns_done[row_count:, :col_count]], axis=1
            ),
            jnp.concatenate(
                [columns_done[:row_count, col_count:], columns_done[row_count:, col_count:]], axis=1
            ),
        ],
        axis=0,
    )
    inverse_cols = jnp.concatenate(
        [
            jnp.concatenate([cos_cols, sin_cols], axis=1),
            jnp.concatenate([-sin_cols, cos_cols], axis=1),
        ],
        axis=0,
    ).astype(jnp.bfloat16)
    result = jnp.dot(arranged, inverse_cols, preferred_element_type=jnp.float32)
    return jnp.stack(
        [
            result[:row_count, :col_count],
            result[:row_count, col_count:],
            result[row_count:, :col_count],
            result[row_count:, col_count:],
        ]
    ).astype(jnp.bfloat16)


def blend_edges(extended, has_top, has_bottom, has_left, has_right, width):
    values = extended.astype(jnp.float32)
    row_count = values.shape[1] - 2 * width
    col_count = values.shape[2] - 2 * width
    ramp = (jnp.arange(width, dtype=jnp.float32) + 0.5) / width
    top_weight = jnp.where(has_top, ramp, 1.0)[None, :, None]
    bottom_weight = jnp.where(has_bottom, ramp[::-1], 1.0)[None, :, None]
    middle = values[:, width : width + row_count, :]
    top_band = top_weight * middle[:, :width] + (1.0 - top_weight) * values[:, :width]
    bottom_band = (
        bottom_weight * middle[:, row_count - width :]
        + (1.0 - bottom_weight) * values[:, row_count + width :]
    )
    middle = jnp.concatenate([top_band, middle[:, width : row_count - width], bottom_band], axis=1)
    left_weight = jnp.where(has_left, ramp, 1.0)[None, None, :]
    right_weight = jnp.where(has_right, ramp[::-1], 1.0)[None, None, :]
    inner = middle[:, :, width : width + col_count]
    left_band = left_weight * inner[:, :, :width] + (1.0 - left_weight) * middle[:, :, :width]
    right_band = (
        right_weight * inner[:, :, col_count - width :]
        + (1.0 - right_weight) * middle[:, :, col_count + width :]
    )
    return jnp.concatenate([left_band, inner[:, :, width : col_count - width], right_band], axis=2)


def on_device(kappa, send_list, dest_slot, send_count):
    tile_width = kappa.shape[1]
    rows_axis = lax.axis_size("px")
    cols_axis = lax.axis_size("py")
    band_index = lax.axis_index("px")
    column_index = lax.axis_index("py")
    tile_lists = send_list[0].reshape(rows_axis, cols_axis, -1)
    slot_lists = dest_slot[0].reshape(rows_axis, cols_axis, -1)
    pair_counts = send_count[0].reshape(rows_axis, cols_axis)
    slot_depth = tile_lists.shape[2]
    upper_band = jnp.maximum(band_index - 1, 0)
    picked_lists = jnp.stack([tile_lists[band_index], tile_lists[upper_band]], axis=1)
    picked_slots = jnp.stack([slot_lists[band_index], slot_lists[upper_band]], axis=1)
    upper_counts = jnp.where(band_index > 0, pair_counts[upper_band], 0)
    picked_counts = jnp.stack([pair_counts[band_index], upper_counts], axis=1)
    live_mask = jnp.arange(slot_depth, dtype=jnp.int32)[None, None, :] < picked_counts[:, :, None]
    slot_codes = jnp.where(live_mask, picked_slots + 1, 0)
    whole_band, band_lists, band_codes = (
        lax.all_gather(kappa, "py", axis=0, tiled=True),
        lax.all_gather(picked_lists, "py", axis=0, tiled=True),
        lax.all_gather(slot_codes, "py", axis=0, tiled=True),
    )
    own_lists = band_lists.reshape(cols_axis, cols_axis, 2, slot_depth)[:, column_index]
    arrived_codes = band_codes.reshape(cols_axis, cols_axis, 2, slot_depth)[:, column_index]
    offsets = (jnp.arange(cols_axis, dtype=jnp.int32) * kappa.shape[0])[:, None, None]
    tile_values = whole_band[own_lists + offsets]
    raised_values, raised_codes = shifted((tile_values[:, 1], arrived_codes[:, 1]), "px", -1)
    all_values = jnp.concatenate(
        [tile_values[:, 0].reshape(-1, tile_width), raised_values.reshape(-1, tile_width)], axis=0
    )
    all_codes = jnp.concatenate([arrived_codes[:, 0].reshape(-1), raised_codes.reshape(-1)], axis=0)
    slot_total = PATCH_ROWS * PATCH_COLS // tile_width
    target = jnp.where(all_codes > 0, all_codes - 1, slot_total)
    patch_tiles = (
        jnp.zeros((slot_total, tile_width), kappa.dtype).at[target].set(all_values, mode="drop")
    )
    fields = flexion_fields(patch_tiles.reshape(PATCH_ROWS, PATCH_COLS))
    extended = padded(fields, (("px", 1), ("py", 2)), tile_width)
    return blend_edges(
        extended,
        band_index > 0,
        band_index < rows_axis - 1,
        column_index > 0,
        column_index < cols_axis - 1,
        tile_width,
    )


def solution(mesh):
    placed = (
        P(("px", "py"), None),
        P(("px", "py"), None, None),
        P(("px", "py"), None, None),
        P(("px", "py"), None),
    )
    return jax.shard_map(
        on_device, mesh=mesh, in_specs=placed, out_specs=P(None, "px", "py"), check_vma=False
    )
```

profile of v0, /device:TPU:40, one launch (start us, length us, event | category | flops | bytes accessed | tf_op | source)
XLA Modules:
  0.0 210.4 jit_solution(5844957314642020017)
XLA Ops:
  6.5 0.7 all-gather.2.cloned.1.call-update
  7.3 0.5 broadcast.420
  7.8 1.3 reduce.3
  9.2 1.0 copy.5
  10.2 1.0 copy.6
  11.3 25.3 %all_gather.9 = s32[256,2,192]{2,0,1:T(8,128)S(1)} all-gather(s32[16,2,192]{2,0,1:T(8,128)S(1)} %fusion.57), channel_id=1, replica_groups=mesh['px'=8,'py'=16] {'py'}, dimensions={0}, use_global_device_ids=true | all-gather | bytes 417792 | tf_op jit(solution)/shard_map/all_gather | solution.py:168
  36.7 1.9 collective-permute-start
  38.7 23.4 %all_gather.11 = s32[256,2,192]{2,0,1:T(8,128)S(1)} all-gather(s32[16,2,192]{2,0,1:T(8,128)S(1)} %pad_add_fusion), channel_id=1, replica_groups=mesh['px'=8,'py'=16] {'py'}, dimensions={0}, use_global_device_ids=true | all-gather | bytes 417792 | tf_op jit(solution)/shard_map/all_gather | solution.py:167
  62.3 0.1 reshape.198
  62.4 4.0 %fusion.54 = bf16[512,512]{1,0:T(8,128)(2,1)S(1)} fusion(), kind=kLoop, calls=%fused_computation.93 | loop fusion | flops 4194304 | bytes 524288 | tf_op jit(solution)/shard_map/neg | solution.py:86
  66.4 4.3 %fusion.50 = (bf16[512,512]{1,0:T(8,128)(2,1)S(1)}, bf16[512,512]{1,0:T(8,128)(2,1)S(1)}) fusion(), kind=kLoop, calls=%fused_computation.89 | loop fusion | flops 4194304 | bytes 1048576 | tf_op jit(solution)/shard_map/sin | solution.py:35
  70.7 5.0 %negate_convert_fusion = (bf16[512,512]{1,0:T(8,128)(2,1)}, bf16[512,512]{1,0:T(8,128)(2,1)}) fusion(), kind=kLoop, calls=%fused_computation.70 | loop fusion | flops 4718592 | bytes 1048576 | tf_op jit(solution)/shard_map/convert.29
  75.7 5.0 %fusion.52 = (bf16[512,512]{1,0:T(8,128)(2,1)}, bf16[512,512]{1,0:T(8,128)(2,1)}) fusion(), kind=kLoop, calls=%fused_computation.91 | loop fusion | flops 4194304 | bytes 1048576 | tf_op jit(solution)/shard_map/convert.33
  80.7 1.2 fusion.2
  82.1 8.6 %all-gather.2.cloned.1.call-done = bf16[37632,128]{1,0:T(8,128)(2,1)} async-done(((bf16[2352,128]{1,0:T(8,128)(2,1)}), bf16[37632,128]{1,0:T(8,128)(2,1)}) %all-gather.2.cloned.1.call-update) | async-done | bytes 9633808 | tf_op jit(solution)/shard_map/all_gather | solution.py:166
  90.7 21.4 %gather_fusion = bf16[6144,128]{1,0:T(8,128)(2,1)S(1)} fusion(bf16[37632,128]{1,0:T(8,128)(2,1)} %all-gather.2.cloned.1.call-done, s32[6144]{0:T(1024)S(1)} %broadcast_clamp_fusion), kind=kCustom, calls=%fused_computation | custom fusion | bytes 3170304 | tf_op jit(solution)/shard_map/gather | solution.py:173
  112.2 0.1 fusion.71
  112.3 2.1 collective-permute-start.1
  114.4 9.4 %collective-permute-done.1 = bf16[16,192,128]{2,1,0:T(8,128)(2,1)S(1)} collective-permute-done((bf16[16,192,128]{2,1,0:T(8,128)(2,1)S(1)}, bf16[16,192,128]{2,1,0:T(8,128)(2,1)S(1)}, u32[]{:S(2)}, u32[]{:S(2)}) %collective-permute-start.1) | collective-permute-done | bytes 786464 | tf_op jit(solution)/shard_map/ppermute | solution.py:15
  123.8 21.4 %scatter_custom_fusion = bf16[2048,128]{1,0:T(8,128)(2,1)S(1)} fusion(s32[6144]{0:T(1024)S(1)} %bitcast.53, bf16[3072,128]{1,0:T(8,128)(2,1)S(1)} %bitcast.47, bf16[]{:T(256)} %constant.88, bf16[3072,128]{1,0:T(8,128)(2,1)S(1)} %bitcast.46, bf16[]{:T(256)} %constant.24.clone.1), kind=kCustom, calls=%fused_computation.44 | custom fusion | flops 3145728 | bytes 2097156 | tf_op jit(solution)/shard_map/scatter | solution.py:182
  145.2 0.3 reshape.195
  145.6 0.7 convolution_convert_fusion
  146.4 0.4 copy-done
  146.8 0.1 copy-done.1
  146.9 0.2 copy-done.4
  147.1 1.3 fusion.1
  148.4 1.4 multiply_convert_fusion.3
  149.8 2.4 %fusion.29 = bf16[1024,1024]{0,1:T(8,128)(2,1)S(1)} fusion(bf16[512,512]{0,1:T(8,128)(2,1)S(1)} %get-tuple-element.19, bf16[512,512]{0,1:T(8,128)(2,1)S(1)} %get-tuple-element.18, bf16[512,512]{0,1:T(8,128)(2,1)S(1)} %get-tuple-element.20, bf16[512,512]{0,1:T(8,128)(2,1)S(1)} %get-tuple-element.17, bf16[512,1024]{1,0:T(8,128)(2,1)S(1)} %copy-done, ...), kind=kOutput, calls=%fused_computation.37 | convolution fusion | flops 2163212288 | bytes 6291456 | tf_op jit(solution)/shard_map/dot_general | solution.py:91
  152.1 0.2 fusion.70
  152.3 2.4 %fusion.24 = bf16[1024,1024]{1,0:T(8,128)(2,1)S(1)} fusion(bf16[512,512]{1,0:T(8,128)(2,1)S(1)} %copy-done.2, bf16[512,512]{1,0:T(8,128)(2,1)S(1)} %copy-done.1, bf16[512,1024]{1,0:T(8,128)(2,1)S(1)} %get-tuple-element.36, bf16[512,512]{0,1:T(8,128)(2,1)S(1)} %get-tuple-element.28, bf16[512,512]{0,1:T(8,128)(2,1)S(1)} %get-tuple-element.29, ...), kind=kOutput, calls=%fused_computation.36 | convolution fusion | flops 2163212288 | bytes 6291456 | tf_op jit(solution)/shard_map/dot_general | solution.py:112
  154.8 0.2 slice_bitcast_fusion.4
  155.0 3.6 %collective-permute-start.2 = (bf16[4,128,512]{2,1,0:T(8,128)(2,1)S(1)}, bf16[4,128,512]{2,1,0:T(8,128)(2,1)S(1)}, u32[]{:S(2)}, u32[]{:S(2)}) collective-permute-start(bf16[4,128,512]{2,1,0:T(8,128)(2,1)S(1)} %get-tuple-element.21), channel_id=1, source_target_pairs={{0,16},{16,32},{32,48},{48,64},{64,80},{80,96},{96,112},{1,17},{17... | collective-permute-start | bytes 1572872 | tf_op jit(solution)/shard_map/ppermute | solution.py:23
  158.7 2.1 %collective-permute-start.3 = (bf16[4,128,512]{2,1,0:T(8,128)(2,1)S(1)}, bf16[4,128,512]{2,1,0:T(8,128)(2,1)S(1)}, u32[]{:S(2)}, u32[]{:S(2)}) collective-permute-start(bf16[4,128,512]{2,1,0:T(8,128)(2,1)S(1)} %get-tuple-element.22), channel_id=1, source_target_pairs={{16,0},{32,16},{48,32},{64,48},{80,64},{96,80},{112,96},{17,1},{33... | collective-permute-start | bytes 1572872 | tf_op jit(solution)/shard_map/ppermute | solution.py:26
  160.8 4.9 %collective-permute-done.2 = bf16[4,128,512]{2,1,0:T(8,128)(2,1)S(1)} collective-permute-done((bf16[4,128,512]{2,1,0:T(8,128)(2,1)S(1)}, bf16[4,128,512]{2,1,0:T(8,128)(2,1)S(1)}, u32[]{:S(2)}, u32[]{:S(2)}) %collective-permute-start.2) | collective-permute-done | bytes 524320 | tf_op jit(solution)/shard_map/ppermute | solution.py:23
  165.7 1.8 collective-permute-done.3
  167.5 1.5 pad_maximum_fusion.20
  168.9 2.1 collective-permute-start.4
  171.0 5.9 %collective-permute-start.5 = (bf16[4,768,128]{2,1,0:T(8,128)(2,1)}, bf16[4,768,128]{2,1,0:T(8,128)(2,1)}, u32[]{:S(2)}, u32[]{:S(2)}) collective-permute-start(bf16[4,768,128]{2,1,0:T(8,128)(2,1)} %get-tuple-element.14), channel_id=1, source_target_pairs={{1,0},{2,1},{3,2},{4,3},{5,4},{6,5},{7,6},{8,7},{9,8},{10,9},{11,1... | collective-permute-start | bytes 2359304 | tf_op jit(solution)/shard_map/ppermute | solution.py:26
  176.9 0.1 reverse.4
  177.0 15.9 %collective-permute-done.4 = bf16[4,768,128]{2,1,0:T(8,128)(2,1)} collective-permute-done((bf16[4,768,128]{2,1,0:T(8,128)(2,1)}, bf16[4,768,128]{2,1,0:T(8,128)(2,1)}, u32[]{:S(2)}, u32[]{:S(2)}) %collective-permute-start.4) | collective-permute-done | bytes 786464 | tf_op jit(solution)/shard_map/ppermute | solution.py:23
  193.0 1.8 collective-permute-done.5
  194.7 4.6 %maximum_convert_fusion = f32[4,768,768]{2,1,0:T(8,128)S(1)} fusion(bf16[4,768,128]{2,1,0:T(8,128)(2,1)} %collective-permute-done.5, bf16[4,128,512]{2,1,0:T(8,128)(2,1)S(1)} %collective-permute-done.3, bf16[1,512,512]{2,1,0:T(8,128)(2,1)S(1)} %get-tuple-element.24, bf16[1,512,512]{2,1,0:T(8,128)(2,1)S(1)} %get-tuple-element.25, ...), kind=kLoop, calls=%fused_computation.3 | loop fusion | flops 37748736 | bytes 14155776 | tf_op jit(solution)/shard_map/convert_element_type | solution.py:124
  199.3 0.2 slice.154
  199.6 0.5 fusion.33
  200.1 0.6 pad_maximum_fusion
  200.7 0.1 slice.157
  200.8 0.2 fusion.42
  201.1 2.5 %pad_maximum_fusion.1 = f32[4,512,512]{2,1,0:T(8,128)} fusion(f32[4,512,128]{2,1,0:T(8,128)S(1)} %get-tuple-element.12, f32[4,512,256]{2,1,0:T(8,128)S(1)} %slice.157, f32[4,512,128]{2,1,0:T(8,128)S(1)} %get-tuple-element.11), kind=kLoop, calls=%fused_computation.4 | loop fusion | flops 2097152 | bytes 8388608 | tf_op jit(solution)/shard_map/concatenate | solution.py:145
  (37 shorter events, 0.8 us)
Async XLA Ops:
  6.5 84.2 %all-gather.2.cloned.1.call-start = ((), (), s32[]{:S(2)}) async-start(), calls=%async_computation | async-start | bytes 10235904 | tf_op jit(solution)/shard_map/all_gather | solution.py:166
  36.7 45.3 %collective-permute-start = (s32[16,192]{1,0:T(8,128)S(1)}, s32[16,192]{1,0:T(8,128)S(1)}, u32[]{:S(2)}, u32[]{:S(2)}) collective-permute-start(s32[16,192]{1,0:T(8,128)S(1)} %get-tuple-element.41), channel_id=1, source_target_pairs={{16,0},{32,16},{48,32},{64,48},{80,64},{96,80},{112,96},{17,1},{33... | collective-permute-start | bytes 36872 | tf_op jit(solution)/shard_map/ppermute | solution.py:15
  112.3 11.6 %collective-permute-start.1 = (bf16[16,192,128]{2,1,0:T(8,128)(2,1)S(1)}, bf16[16,192,128]{2,1,0:T(8,128)(2,1)S(1)}, u32[]{:S(2)}, u32[]{:S(2)}) collective-permute-start(bf16[16,192,128]{2,1,0:T(8,128)(2,1)S(1)} %get-tuple-element.32), channel_id=1, source_target_pairs={{16,0},{32,16},{48,32},{64,48},{80,64},{96,80},{112,96},{17,1},{33... | collective-permute-start | bytes 2359304 | tf_op jit(solution)/shard_map/ppermute | solution.py:15
  145.5 1.2 copy-start
  145.5 1.3 copy-start.1
  145.6 1.5 copy-start.4
  148.4 1.4 copy-start.2
  148.4 1.4 copy-start.3
  155.0 10.7 %collective-permute-start.2 = (bf16[4,128,512]{2,1,0:T(8,128)(2,1)S(1)}, bf16[4,128,512]{2,1,0:T(8,128)(2,1)S(1)}, u32[]{:S(2)}, u32[]{:S(2)}) collective-permute-start(bf16[4,128,512]{2,1,0:T(8,128)(2,1)S(1)} %get-tuple-element.21), channel_id=1, source_target_pairs={{0,16},{16,32},{32,48},{48,64},{64,80},{80,96},{96,112},{1,17},{17... | collective-permute-start | bytes 1572872 | tf_op jit(solution)/shard_map/ppermute | solution.py:23
  158.7 8.8 %collective-permute-start.3 = (bf16[4,128,512]{2,1,0:T(8,128)(2,1)S(1)}, bf16[4,128,512]{2,1,0:T(8,128)(2,1)S(1)}, u32[]{:S(2)}, u32[]{:S(2)}) collective-permute-start(bf16[4,128,512]{2,1,0:T(8,128)(2,1)S(1)} %get-tuple-element.22), channel_id=1, source_target_pairs={{16,0},{32,16},{48,32},{64,48},{80,64},{96,80},{112,96},{17,1},{33... | collective-permute-start | bytes 1572872 | tf_op jit(solution)/shard_map/ppermute | solution.py:26
  168.9 24.0 %collective-permute-start.4 = (bf16[4,768,128]{2,1,0:T(8,128)(2,1)}, bf16[4,768,128]{2,1,0:T(8,128)(2,1)}, u32[]{:S(2)}, u32[]{:S(2)}) collective-permute-start(bf16[4,768,128]{2,1,0:T(8,128)(2,1)} %get-tuple-element.13), channel_id=1, source_target_pairs={{0,1},{1,2},{2,3},{3,4},{4,5},{5,6},{6,7},{7,8},{8,9},{9,10},{10,1... | collective-permute-start | bytes 2359304 | tf_op jit(solution)/shard_map/ppermute | solution.py:23
  171.0 23.7 %collective-permute-start.5 = (bf16[4,768,128]{2,1,0:T(8,128)(2,1)}, bf16[4,768,128]{2,1,0:T(8,128)(2,1)}, u32[]{:S(2)}, u32[]{:S(2)}) collective-permute-start(bf16[4,768,128]{2,1,0:T(8,128)(2,1)} %get-tuple-element.14), channel_id=1, source_target_pairs={{1,0},{2,1},{3,2},{4,3},{5,4},{6,5},{7,6},{8,7},{9,8},{10,9},{11,1... | collective-permute-start | bytes 2359304 | tf_op jit(solution)/shard_map/ppermute | solution.py:26
Sparse Core Ops, SparseCore 0:
  9.5 81.1 all-gather.1
where the time goes:
time: 214 us; the launch traced here: 210 us
  other arithmetic  53.8 us (25%)
  blocking collectives  48.7 us (23%)
  waiting for transfers between devices  43.2 us (20%)
  local copies, waits for them, and re-layouts  26.4 us (12%)
  starting transfers between devices  17.7 us (8%)
  between operations  13.8 us (6%)
  matrix products  6.84 us (3%)
    all_gather x1, blocking collectives, on_device(): lax.all_gather(slot_codes, 'py', axis=0, tiled=True)  25.3 us
    all_gather x1, blocking collectives, on_device(): lax.all_gather(picked_lists, 'py', axis=0, tiled=True)  23.4 us
    gather x1, local copies, waits for them, and re-layouts, on_device(): tile_values = whole_band[own_lists + offsets]  21.4 us
    scatter x1, other arithmetic, on_device(): jnp.zeros((slot_total, tile_width), kappa.dtype).at[target]  21.4 us
    ppermute x2, waiting for transfers between devices, padded(): lax.ppermute(lax.slice_in_dim(block, block.shape[dim] - width, None, axis...  20.8 us
    another operation x4, other arithmetic  12.6 us
    ppermute x2, waiting for transfers between devices, shifted(): return lax.ppermute(shard, axis, pairs)  9.44 us
    all_gather x1, waiting for transfers between devices, on_device(): lax.all_gather(kappa, 'py', axis=0, tiled=True)  8.64 us
  transfers between devices with their start and end apart: 7, of which 6 were waited for; matrix products, arithmetic and copies ran while one was open for 11% of the time, Pallas kernels for 0%

commit v1 on v0

v1 whole, which is shorter than its diff:
```python
import math

import jax
import ml_dtypes
import numpy as np
import jax.numpy as jnp
from jax import lax
from jax.sharding import PartitionSpec as P

PATCH_ROWS = 512
PATCH_COLS = 512


def shifted(shard, axis, by):
    size = lax.axis_size(axis)
    pairs = [(i, i + by) for i in range(size) if 0 <= i + by < size]
    return lax.ppermute(shard, axis, pairs)


def padded(block, sides, width):
    for axis, dim in sides:
        count = lax.axis_size(axis)
        forward = [(i, i + 1) for i in range(count - 1)]
        backward = [(target, source) for source, target in forward]
        low = lax.ppermute(
            lax.slice_in_dim(block, block.shape[dim] - width, None, axis=dim), axis, forward
        )
        high = lax.ppermute(lax.slice_in_dim(block, 0, width, axis=dim), axis, backward)
        block = jnp.concatenate([low, block, high], axis=dim)
    return block


def dft_tables(length):
    positions = np.arange(length, dtype=np.int64)
    phases = positions[:, None] * positions[None, :] % length
    angles = phases.astype(np.float32) * np.float32(2.0 * math.pi / length)
    return (np.cos(angles).astype(np.float32), np.sin(angles).astype(np.float32))


def table(values):
    return jnp.asarray(values.astype(ml_dtypes.bfloat16))


def wavenumbers(length):
    positions = jnp.arange(length, dtype=jnp.int32)
    signed = positions - length * (positions >= (length + 1) // 2).astype(jnp.int32)
    return signed.astype(jnp.float32) * (2.0 / length)


def dot32(a, b):
    return jnp.dot(a, b, preferred_element_type=jnp.float32)


def flexion_fields(pixels):
    row_count = pixels.shape[0]
    col_count = pixels.shape[1]
    assert row_count == col_count
    cos_np, sin_np = dft_tables(row_count)
    cosine, sine = table(cos_np), table(sin_np)
    n = row_count
    halves = jnp.concatenate([dot32(pixels, cosine), dot32(pixels, sine)], axis=1).astype(
        jnp.bfloat16
    )
    by_cos = dot32(cosine, halves)
    by_sin = dot32(sine, halves)
    real_part = by_cos[:, :n] - by_sin[:, n:]
    imag_part = -(by_sin[:, :n] + by_cos[:, n:])
    across = wavenumbers(col_count)[None, :]
    down = wavenumbers(row_count)[:, None]
    scale = 1.0 / (row_count * col_count)
    power = across * across + down * down
    safe_power = jnp.where(power > 0, power, 1.0)
    cube_real = across * across * across - 3.0 * across * down * down
    cube_imag = 3.0 * across * across * down - down * down * down
    one_real = (-down * real_part - across * imag_part) * scale
    one_imag = (across * real_part - down * imag_part) * scale
    kernel_real = -cube_imag / safe_power
    kernel_imag = cube_real / safe_power
    three_real = (kernel_real * real_part - kernel_imag * imag_part) * scale
    three_imag = (kernel_real * imag_part + kernel_imag * real_part) * scale
    spectra = jnp.concatenate([one_real, three_real, one_imag, three_imag], axis=1).astype(
        jnp.bfloat16
    )
    by_cos = dot32(cosine, spectra)
    by_sin = dot32(sine, spectra)
    columns_done = jnp.concatenate(
        [
            by_cos[:, : 2 * n] - by_sin[:, 2 * n :],
            by_sin[:, : 2 * n] + by_cos[:, 2 * n :],
        ],
        axis=1,
    ).astype(jnp.bfloat16)
    arranged = jnp.concatenate(
        [columns_done[:, k * n : (k + 1) * n] for k in range(4)], axis=0
    )
    by_cos = dot32(arranged, cosine)
    by_sin = dot32(arranged, sine)
    return jnp.stack(
        [
            by_cos[:n] - by_sin[2 * n : 3 * n],
            by_sin[:n] + by_cos[2 * n : 3 * n],
            by_cos[n : 2 * n] - by_sin[3 * n :],
            by_sin[n : 2 * n] + by_cos[3 * n :],
        ]
    ).astype(jnp.bfloat16)


def blend_edges(extended, has_top, has_bottom, has_left, has_right, width):
    values = extended.astype(jnp.float32)
    row_count = values.shape[1] - 2 * width
    col_count = values.shape[2] - 2 * width
    ramp = (jnp.arange(width, dtype=jnp.float32) + 0.5) / width
    top_weight = jnp.where(has_top, ramp, 1.0)[None, :, None]
    bottom_weight = jnp.where(has_bottom, ramp[::-1], 1.0)[None, :, None]
    middle = values[:, width : width + row_count, :]
    top_band = top_weight * middle[:, :width] + (1.0 - top_weight) * values[:, :width]
    bottom_band = (
        bottom_weight * middle[:, row_count - width :]
        + (1.0 - bottom_weight) * values[:, row_count + width :]
    )
    middle = jnp.concatenate([top_band, middle[:, width : row_count - width], bottom_band], axis=1)
    left_weight = jnp.where(has_left, ramp, 1.0)[None, None, :]
    right_weight = jnp.where(has_right, ramp[::-1], 1.0)[None, None, :]
    inner = middle[:, :, width : width + col_count]
    left_band = left_weight * inner[:, :, :width] + (1.0 - left_weight) * middle[:, :, :width]
    right_band = (
        right_weight * inner[:, :, col_count - width :]
        + (1.0 - right_weight) * middle[:, :, col_count + width :]
    )
    return jnp.concatenate([left_band, inner[:, :, width : col_count - width], right_band], axis=2)


def one_hot_rows(codes, count, values):
    picks = codes[None, :] == jnp.arange(1, count + 1, dtype=jnp.int32)[:, None]
    return jnp.dot(
        picks.astype(values.dtype), values, preferred_element_type=jnp.float32
    ).astype(values.dtype)


def on_device(kappa, send_list, dest_slot, send_count):
    tile_width = kappa.shape[1]
    rows_axis = lax.axis_size("px")
    cols_axis = lax.axis_size("py")
    band_index = lax.axis_index("px")
    column_index = lax.axis_index("py")
    tile_lists = send_list[0].reshape(rows_axis, cols_axis, -1)
    slot_lists = dest_slot[0].reshape(rows_axis, cols_axis, -1)
    pair_counts = send_count[0].reshape(rows_axis, cols_axis)
    slot_depth = tile_lists.shape[2]
    upper_band = jnp.maximum(band_index - 1, 0)
    picked_lists = jnp.stack([tile_lists[band_index], tile_lists[upper_band]], axis=1)
    picked_slots = jnp.stack([slot_lists[band_index], slot_lists[upper_band]], axis=1)
    upper_counts = jnp.where(band_index > 0, pair_counts[upper_band], 0)
    picked_counts = jnp.stack([pair_counts[band_index], upper_counts], axis=1)
    live_mask = jnp.arange(slot_depth, dtype=jnp.int32)[None, None, :] < picked_counts[:, :, None]
    slot_codes = jnp.where(live_mask, picked_slots + 1, 0)
    sent_picks = picked_lists.reshape(-1)[:, None] == jnp.arange(kappa.shape[0], dtype=jnp.int32)
    sent_values = jnp.dot(
        sent_picks.astype(kappa.dtype), kappa, preferred_element_type=jnp.float32
    ).astype(kappa.dtype)
    sent_values = sent_values.reshape(cols_axis, 2, slot_depth, tile_width)
    arrived = lax.all_to_all(sent_values, "py", 0, 0, tiled=True)
    arrived_codes = lax.all_to_all(slot_codes, "py", 0, 0, tiled=True)
    rise_total = PATCH_ROWS * PATCH_COLS // tile_width // 4
    rise_codes = arrived_codes[:, 1].reshape(-1)
    rise_live = rise_codes > 0
    rise_place = jnp.where(rise_live, jnp.cumsum(rise_live.astype(jnp.int32)), 0)
    packed_values = one_hot_rows(rise_place, rise_total, arrived[:, 1].reshape(-1, tile_width))
    packed_picks = rise_place[None, :] == jnp.arange(1, rise_total + 1, dtype=jnp.int32)[:, None]
    packed_codes = jnp.sum(jnp.where(packed_picks, rise_codes[None, :], 0), axis=1)
    raised_values, raised_codes = shifted((packed_values, packed_codes), "px", -1)
    all_values = jnp.concatenate(
        [arrived[:, 0].reshape(-1, tile_width), raised_values], axis=0
    )
    all_codes = jnp.concatenate([arrived_codes[:, 0].reshape(-1), raised_codes], axis=0)
    slot_total = PATCH_ROWS * PATCH_COLS // tile_width
    patch_tiles = one_hot_rows(all_codes, slot_total, all_values)
    fields = flexion_fields(patch_tiles.reshape(PATCH_ROWS, PATCH_COLS))
    extended = padded(fields, (("px", 1), ("py", 2)), tile_width)
    return blend_edges(
        extended,
        band_index > 0,
        band_index < rows_axis - 1,
        column_index > 0,
        column_index < cols_axis - 1,
        tile_width,
    )


def solution(mesh):
    placed = (
        P(("px", "py"), None),
        P(("px", "py"), None, None),
        P(("px", "py"), None, None),
        P(("px", "py"), None),
    )
    return jax.shard_map(
        on_device, mesh=mesh, in_specs=placed, out_specs=P(None, "px", "py"), check_vma=False
    )
```

time: 214 us -> 132 us (0.62)
  the two profiles are of different devices: /device:TPU:40 before, /device:TPU:15 now
where the time goes in v1:
time: 132 us; the launch traced here: 131 us
  waiting for transfers between devices  47 us (36%)
  starting transfers between devices  32.6 us (25%)
  matrix products  29.9 us (23%)
  other arithmetic  16.4 us (12%)
  local copies, waits for them, and re-layouts  4.83 us (4%)
    ppermute x2, waiting for transfers between devices, padded(): lax.ppermute(lax.slice_in_dim(block, block.shape[dim] - width, None, axis...  18.4 us
    dot_general x1, matrix products, on_device(): jnp.dot(sent_picks.astype(kappa.dtype), kappa, preferred_element_type=jnp...  16.8 us
    all_to_all x1, waiting for transfers between devices, on_device(): arrived = lax.all_to_all(sent_values, 'py', 0, 0, tiled=True)  14.4 us
    ppermute x2, waiting for transfers between devices, padded(): lax.ppermute(lax.slice_in_dim(block, 0, width, axis=dim), axis, backward)  10.6 us
    dot_general x8, matrix products, dot32(): return jnp.dot(a, b, preferred_element_type=jnp.float32)  7.79 us
    all_to_all x1, starting transfers between devices, on_device(): arrived_codes = lax.all_to_all(slot_codes, 'py', 0, 0, tiled=True)  7.7 us
    ppermute x2, starting transfers between devices, shifted(): return lax.ppermute(shard, axis, pairs)  7.35 us
    all_to_all x1, starting transfers between devices, on_device(): arrived = lax.all_to_all(sent_values, 'py', 0, 0, tiled=True)  6.66 us
  transfers between devices with their start and end apart: 8, of which 6 were waited for; matrix products, arithmetic and copies ran while one was open for 16% of the time, Pallas kernels for 0%

profile of v1, /device:TPU:15, one launch (start us, length us, event | category | flops | bytes accessed | tf_op | source)
XLA Modules:
  0.0 131.1 jit_solution(6569262728445752392)
XLA Ops:
  0.0 0.5 broadcast.334
  0.5 1.3 %reduce.11 = s32[128]{0:T(128)S(1)} reduce(s32[1,128]{1,0:T(1,128)} %param.9, s32[]{:T(128)} %broadcast.334), dimensions={0}, to_apply=%param.9.reduce_sub_computation.3 | reduce | bytes 1028 | tf_op args[3]
  1.9 1.0 copy.12
  3.0 0.6 copy.13
  3.7 7.7 %all-to-all-start = ((s32[16,2,192]{2,1,0:T(2,128)}), s32[16,2,192]{2,1,0:T(2,128)S(1)}, u32[]{:S(2)}, u32[]{:S(2)}) async-start(s32[16,2,192]{2,1,0:T(2,128)} %copy.13), calls=%async_computation | async-start | bytes 65536 | tf_op jit(solution)/shard_map/all_to_all | solution.py:163
  11.4 1.0 copy.14
  12.6 16.8 %fusion.8 = bf16[6144,128]{1,0:T(8,128)(2,1)} fusion(bf16[2352,128]{1,0:T(8,128)(2,1)S(1)} %copy-done, s32[6144]{0:T(1024)S(1)} %eq.26), kind=kOutput, calls=%fused_computation.10 | convolution fusion | flops 3714613248 | bytes 2199552 | tf_op jit(solution)/shard_map/dot_general | solution.py:158
  29.4 6.7 %all-to-all-start.1 = ((bf16[16,2,192,128]{3,2,1,0:T(8,128)(2,1)}), bf16[16,2,192,128]{3,2,1,0:T(8,128)(2,1)S(1)}, u32[]{:S(2)}, u32[]{:S(2)}) async-start(bf16[16,2,192,128]{3,2,1,0:T(8,128)(2,1)} %bitcast.7), calls=%async_computation.1 | async-start | bytes 3145728 | tf_op jit(solution)/shard_map/all_to_all | solution.py:162
  36.1 0.1 slice_reduce_fusion
  36.3 0.3 reduce-window.9
  36.8 0.1 slice_reduce_fusion.1
  37.0 0.8 fusion.9
  37.8 3.7 %collective-permute-start = (s32[512]{0:T(512)S(1)}, s32[512]{0:T(512)S(1)}, u32[]{:S(2)}, u32[]{:S(2)}) collective-permute-start(s32[512]{0:T(512)S(1)} %fusion.9), channel_id=1, source_target_pairs={{16,0},{32,16},{48,32},{64,48},{80,64},{96,80},{112,96},{17,1},{33... | collective-permute-start | bytes 6152 | tf_op jit(solution)/shard_map/ppermute | solution.py:17
  41.5 14.4 %all-to-all-done.1 = bf16[16,2,192,128]{3,2,1,0:T(8,128)(2,1)S(1)} async-done(((bf16[16,2,192,128]{3,2,1,0:T(8,128)(2,1)}), bf16[16,2,192,128]{3,2,1,0:T(8,128)(2,1)S(1)}, u32[]{:S(2)}, u32[]{:S(2)}) %all-to-all-start.1) | async-done | bytes 1572896 | tf_op jit(solution)/shard_map/all_to_all | solution.py:162
  55.9 0.1 fusion.62
  56.0 1.0 fusion.19
  57.1 3.6 %collective-permute-start.1 = (bf16[512,128]{1,0:T(8,128)(2,1)S(1)}, bf16[512,128]{1,0:T(8,128)(2,1)S(1)}, u32[]{:S(2)}, u32[]{:S(2)}) collective-permute-start(bf16[512,128]{1,0:T(8,128)(2,1)S(1)} %fusion.19), channel_id=1, source_target_pairs={{16,0},{32,16},{48,32},{64,48},{80,64},{96,80},{112,96},{17,1},{33... | collective-permute-start | bytes 393224 | tf_op jit(solution)/shard_map/ppermute | solution.py:17
  60.8 3.5 %collective-permute-done.1 = bf16[512,128]{1,0:T(8,128)(2,1)S(1)} collective-permute-done((bf16[512,128]{1,0:T(8,128)(2,1)S(1)}, bf16[512,128]{1,0:T(8,128)(2,1)S(1)}, u32[]{:S(2)}, u32[]{:S(2)}) %collective-permute-start.1) | collective-permute-done | bytes 131104 | tf_op jit(solution)/shard_map/ppermute | solution.py:17
  64.4 4.3 %fusion.12 = bf16[2048,128]{1,0:T(8,128)(2,1)S(1)} fusion(s32[3584]{0:T(1024)S(1)} %pad_add_fusion.1, s32[2048]{0:T(1024)S(1)} %iota_add_fusion, bf16[512,128]{1,0:T(8,128)(2,1)S(1)} %collective-permute-done.1, bf16[3072,128]{1,0:T(8,128)(2,1)S(1)} %bitcast.35), kind=kOutput, calls=%fused_computation.18 | convolution fusion | flops 1888485376 | bytes 1464320 | tf_op jit(solution)/shard_map/dot_general | solution.py:135
  68.6 0.3 reshape.138
  69.0 0.5 convolution_convert_fusion
  69.5 0.5 convolution_convert_fusion.1
  70.0 0.7 fusion.33
  70.7 0.7 fusion.34
  71.5 0.3 multiply_convert_fusion.3
  71.8 1.0 multiply_convert_fusion.2
  72.8 1.3 fusion.42
  74.0 1.3 fusion.41
  75.3 1.2 fusion.16
  76.7 1.3 fusion.40
  77.9 1.5 %fusion.39 = f32[2048,512]{1,0:T(8,128)S(1)} fusion(bf16[512,512]{1,0:T(8,128)(2,1)S(1)} %copy-done.2, bf16[512,512]{1,0:T(8,128)(2,1)S(1)} %get-tuple-element.37, bf16[512,512]{1,0:T(8,128)(2,1)S(1)} %get-tuple-element.36, bf16[512,512]{1,0:T(8,128)(2,1)S(1)} %get-tuple-element.35, bf16[512,512]{1,0:T(8,128)(2,1)S(1)} %get-tuple-element.34), kind=kOutput, calls=%fused_computation.77 | convolution fusion | flops 1082130432 | bytes 6815744 | tf_op jit(solution)/shard_map/dot_general | solution.py:51
  79.5 1.2 fusion.35
  80.8 1.9 %collective-permute-start.2 = (bf16[4,128,512]{2,1,0:T(8,128)(2,1)S(1)}, bf16[4,128,512]{2,1,0:T(8,128)(2,1)S(1)}, u32[]{:S(2)}, u32[]{:S(2)}) collective-permute-start(bf16[4,128,512]{2,1,0:T(8,128)(2,1)S(1)} %get-tuple-element.30), channel_id=1, source_target_pairs={{0,16},{16,32},{32,48},{48,64},{64,80},{80,96},{96,112},{1,17},{17... | collective-permute-start | bytes 1572872 | tf_op jit(solution)/shard_map/ppermute | solution.py:25
  82.7 2.4 %collective-permute-start.3 = (bf16[4,128,512]{2,1,0:T(8,128)(2,1)S(1)}, bf16[4,128,512]{2,1,0:T(8,128)(2,1)S(1)}, u32[]{:S(2)}, u32[]{:S(2)}) collective-permute-start(bf16[4,128,512]{2,1,0:T(8,128)(2,1)S(1)} %get-tuple-element.31), channel_id=1, source_target_pairs={{16,0},{32,16},{48,32},{64,48},{80,64},{96,80},{112,96},{17,1},{33... | collective-permute-start | bytes 1572872 | tf_op jit(solution)/shard_map/ppermute | solution.py:28
  85.1 3.7 %collective-permute-done.2 = bf16[4,128,512]{2,1,0:T(8,128)(2,1)S(1)} collective-permute-done((bf16[4,128,512]{2,1,0:T(8,128)(2,1)S(1)}, bf16[4,128,512]{2,1,0:T(8,128)(2,1)S(1)}, u32[]{:S(2)}, u32[]{:S(2)}) %collective-permute-start.2) | collective-permute-done | bytes 524320 | tf_op jit(solution)/shard_map/ppermute | solution.py:25
  88.8 4.4 %collective-permute-done.3 = bf16[4,128,512]{2,1,0:T(8,128)(2,1)S(1)} collective-permute-done((bf16[4,128,512]{2,1,0:T(8,128)(2,1)S(1)}, bf16[4,128,512]{2,1,0:T(8,128)(2,1)S(1)}, u32[]{:S(2)}, u32[]{:S(2)}) %collective-permute-start.3) | collective-permute-done | bytes 524320 | tf_op jit(solution)/shard_map/ppermute | solution.py:28
  93.2 1.5 %pad_maximum_fusion.10 = (bf16[4,768,128]{2,1,0:T(8,128)(2,1)}, bf16[4,768,128]{2,1,0:T(8,128)(2,1)}) fusion(bf16[4,128,512]{2,1,0:T(8,128)(2,1)S(1)} %collective-permute-done.3, bf16[4,128,512]{2,1,0:T(8,128)(2,1)S(1)} %collective-permute-done.2, bf16[1,512,512]{2,1,0:T(8,128)(2,1)S(1)} %get-tuple-element.18, ...), kind=kLoop, calls=%fused_computation.66 | loop fusion | flops 9437184 | bytes 4718592 | tf_op jit(solution)/shard_map/slice | solution.py:26
  94.7 4.6 %collective-permute-start.4 = (bf16[4,768,128]{2,1,0:T(8,128)(2,1)}, bf16[4,768,128]{2,1,0:T(8,128)(2,1)}, u32[]{:S(2)}, u32[]{:S(2)}) collective-permute-start(bf16[4,768,128]{2,1,0:T(8,128)(2,1)} %get-tuple-element.25), channel_id=1, source_target_pairs={{0,1},{1,2},{2,3},{3,4},{4,5},{5,6},{6,7},{7,8},{8,9},{9,10},{10,1... | collective-permute-start | bytes 2359304 | tf_op jit(solution)/shard_map/ppermute | solution.py:25
  99.3 1.9 %collective-permute-start.5 = (bf16[4,768,128]{2,1,0:T(8,128)(2,1)}, bf16[4,768,128]{2,1,0:T(8,128)(2,1)}, u32[]{:S(2)}, u32[]{:S(2)}) collective-permute-start(bf16[4,768,128]{2,1,0:T(8,128)(2,1)} %get-tuple-element.26), channel_id=1, source_target_pairs={{1,0},{2,1},{3,2},{4,3},{5,4},{6,5},{7,6},{8,7},{9,8},{10,9},{11,1... | collective-permute-start | bytes 2359304 | tf_op jit(solution)/shard_map/ppermute | solution.py:28
  101.4 14.7 %collective-permute-done.4 = bf16[4,768,128]{2,1,0:T(8,128)(2,1)} collective-permute-done((bf16[4,768,128]{2,1,0:T(8,128)(2,1)}, bf16[4,768,128]{2,1,0:T(8,128)(2,1)}, u32[]{:S(2)}, u32[]{:S(2)}) %collective-permute-start.4) | collective-permute-done | bytes 786464 | tf_op jit(solution)/shard_map/ppermute | solution.py:25
  116.1 6.2 %collective-permute-done.5 = bf16[4,768,128]{2,1,0:T(8,128)(2,1)} collective-permute-done((bf16[4,768,128]{2,1,0:T(8,128)(2,1)}, bf16[4,768,128]{2,1,0:T(8,128)(2,1)}, u32[]{:S(2)}, u32[]{:S(2)}) %collective-permute-start.5) | collective-permute-done | bytes 786464 | tf_op jit(solution)/shard_map/ppermute | solution.py:28
  122.3 4.6 %maximum_convert_fusion = f32[4,768,768]{2,1,0:T(8,128)S(1)} fusion(bf16[4,768,128]{2,1,0:T(8,128)(2,1)} %collective-permute-done.5, bf16[4,128,512]{2,1,0:T(8,128)(2,1)S(1)} %collective-permute-done.3, bf16[1,512,512]{2,1,0:T(8,128)(2,1)S(1)} %get-tuple-element.18, bf16[1,512,512]{2,1,0:T(8,128)(2,1)S(1)} %get-tuple-element.19, ...), kind=kLoop, calls=%fused_computation.13 | loop fusion | flops 37748736 | bytes 14155776 | tf_op jit(solution)/shard_map/convert_element_type | solution.py:109
  126.9 0.2 slice.201
  127.1 0.5 fusion.18
  127.7 0.6 pad_maximum_fusion
  128.3 0.1 slice.204
  128.4 0.2 fusion.23
  128.7 2.5 %pad_maximum_fusion.1 = f32[4,512,512]{2,1,0:T(8,128)} fusion(f32[4,512,128]{2,1,0:T(8,128)S(1)} %get-tuple-element.24, f32[4,512,256]{2,1,0:T(8,128)S(1)} %slice.204, f32[4,512,128]{2,1,0:T(8,128)S(1)} %get-tuple-element.23), kind=kLoop, calls=%fused_computation.14 | loop fusion | flops 2097152 | bytes 8388608 | tf_op jit(solution)/shard_map/concatenate | solution.py:130
  (40 shorter events, 1.2 us)
Async XLA Ops:
  0.0 12.6 %copy-start = (bf16[2352,128]{1,0:T(8,128)(2,1)S(1)}, bf16[2352,128]{1,0:T(8,128)(2,1)}, u32[]{:S(2)}) copy-start(bf16[2352,128]{1,0:T(8,128)(2,1)} %param.6) | copy-start | bytes 1806340
  3.7 25.8 %all-to-all-start = ((s32[16,2,192]{2,1,0:T(2,128)}), s32[16,2,192]{2,1,0:T(2,128)S(1)}, u32[]{:S(2)}, u32[]{:S(2)}) async-start(s32[16,2,192]{2,1,0:T(2,128)} %copy.13), calls=%async_computation | async-start | bytes 65536 | tf_op jit(solution)/shard_map/all_to_all | solution.py:163
  29.4 26.5 %all-to-all-start.1 = ((bf16[16,2,192,128]{3,2,1,0:T(8,128)(2,1)}), bf16[16,2,192,128]{3,2,1,0:T(8,128)(2,1)S(1)}, u32[]{:S(2)}, u32[]{:S(2)}) async-start(bf16[16,2,192,128]{3,2,1,0:T(8,128)(2,1)} %bitcast.7), calls=%async_computation.1 | async-start | bytes 3145728 | tf_op jit(solution)/shard_map/all_to_all | solution.py:162
  37.8 23.0 %collective-permute-start = (s32[512]{0:T(512)S(1)}, s32[512]{0:T(512)S(1)}, u32[]{:S(2)}, u32[]{:S(2)}) collective-permute-start(s32[512]{0:T(512)S(1)} %fusion.9), channel_id=1, source_target_pairs={{16,0},{32,16},{48,32},{64,48},{80,64},{96,80},{112,96},{17,1},{33... | collective-permute-start | bytes 6152 | tf_op jit(solution)/shard_map/ppermute | solution.py:17
  57.1 7.3 %collective-permute-start.1 = (bf16[512,128]{1,0:T(8,128)(2,1)S(1)}, bf16[512,128]{1,0:T(8,128)(2,1)S(1)}, u32[]{:S(2)}, u32[]{:S(2)}) collective-permute-start(bf16[512,128]{1,0:T(8,128)(2,1)S(1)} %fusion.19), channel_id=1, source_target_pairs={{16,0},{32,16},{48,32},{64,48},{80,64},{96,80},{112,96},{17,1},{33... | collective-permute-start | bytes 393224 | tf_op jit(solution)/shard_map/ppermute | solution.py:17
  64.4 4.6 %copy-start.2 = (bf16[512,512]{1,0:T(8,128)(2,1)S(1)}, bf16[512,512]{1,0:T(8,128)(2,1)}, u32[]{:S(2)}) copy-start(bf16[512,512]{1,0:T(8,128)(2,1)} %constant.58.clone) | copy-start | bytes 1572868
  64.4 5.1 %copy-start.3 = (bf16[512,512]{1,0:T(8,128)(2,1)S(1)}, bf16[512,512]{1,0:T(8,128)(2,1)}, u32[]{:S(2)}) copy-start(bf16[512,512]{1,0:T(8,128)(2,1)} %constant.57.clone) | copy-start | bytes 1572868
  80.8 8.0 %collective-permute-start.2 = (bf16[4,128,512]{2,1,0:T(8,128)(2,1)S(1)}, bf16[4,128,512]{2,1,0:T(8,128)(2,1)S(1)}, u32[]{:S(2)}, u32[]{:S(2)}) collective-permute-start(bf16[4,128,512]{2,1,0:T(8,128)(2,1)S(1)} %get-tuple-element.30), channel_id=1, source_target_pairs={{0,16},{16,32},{32,48},{48,64},{64,80},{80,96},{96,112},{1,17},{17... | collective-permute-start | bytes 1572872 | tf_op jit(solution)/shard_map/ppermute | solution.py:25
  82.7 10.5 %collective-permute-start.3 = (bf16[4,128,512]{2,1,0:T(8,128)(2,1)S(1)}, bf16[4,128,512]{2,1,0:T(8,128)(2,1)S(1)}, u32[]{:S(2)}, u32[]{:S(2)}) collective-permute-start(bf16[4,128,512]{2,1,0:T(8,128)(2,1)S(1)} %get-tuple-element.31), channel_id=1, source_target_pairs={{16,0},{32,16},{48,32},{64,48},{80,64},{96,80},{112,96},{17,1},{33... | collective-permute-start | bytes 1572872 | tf_op jit(solution)/shard_map/ppermute | solution.py:28
  94.7 21.4 %collective-permute-start.4 = (bf16[4,768,128]{2,1,0:T(8,128)(2,1)}, bf16[4,768,128]{2,1,0:T(8,128)(2,1)}, u32[]{:S(2)}, u32[]{:S(2)}) collective-permute-start(bf16[4,768,128]{2,1,0:T(8,128)(2,1)} %get-tuple-element.25), channel_id=1, source_target_pairs={{0,1},{1,2},{2,3},{3,4},{4,5},{5,6},{6,7},{7,8},{8,9},{9,10},{10,1... | collective-permute-start | bytes 2359304 | tf_op jit(solution)/shard_map/ppermute | solution.py:25
  99.3 23.0 %collective-permute-start.5 = (bf16[4,768,128]{2,1,0:T(8,128)(2,1)}, bf16[4,768,128]{2,1,0:T(8,128)(2,1)}, u32[]{:S(2)}, u32[]{:S(2)}) collective-permute-start(bf16[4,768,128]{2,1,0:T(8,128)(2,1)} %get-tuple-element.26), channel_id=1, source_target_pairs={{1,0},{2,1},{3,2},{4,3},{5,4},{6,5},{7,6},{8,7},{9,8},{10,9},{11,1... | collective-permute-start | bytes 2359304 | tf_op jit(solution)/shard_map/ppermute | solution.py:28
  128.6 2.5 %copy-start.1 = (bf16[2352,128]{1,0:T(8,128)(2,1)S(1)}, bf16[2352,128]{1,0:T(8,128)(2,1)}, u32[]{:S(2)}) copy-start(bf16[2352,128]{1,0:T(8,128)(2,1)} %param.6) | copy-start | bytes 1806340

commit v2 on v1

--- a/solution.py
+++ b/solution.py
@@ -132,9 +132,59 @@
 
 def one_hot_rows(codes, count, values):
     picks = codes[None, :] == jnp.arange(1, count + 1, dtype=jnp.int32)[:, None]
-    return jnp.dot(
-        picks.astype(values.dtype), values, preferred_element_type=jnp.float32
-    ).astype(values.dtype)
+    return jnp.dot(picks.astype(values.dtype), values, preferred_element_type=jnp.float32)
+
+
+def gathered_rows(table_rows, picks):
+    chosen = picks.reshape(-1)[:, None] == jnp.arange(table_rows.shape[0], dtype=jnp.int32)
+    values = jnp.dot(chosen.astype(table_rows.dtype), table_rows, preferred_element_type=jnp.float32)
+    return values.astype(table_rows.dtype).reshape(picks.shape + table_rows.shape[1:])
+
+
+CODE_SPLIT = 64
+CODE_ROWS = 16
+
+
+def with_codes(values, codes):
+    depth, width = values.shape[1], values.shape[2]
+    halves = jnp.concatenate([codes // CODE_SPLIT, codes % CODE_SPLIT], axis=1)
+    code_rows = halves.reshape(values.shape[0], -1, width).astype(values.dtype)
+    pad = jnp.zeros((values.shape[0], CODE_ROWS - code_rows.shape[1], width), values.dtype)
+    return jnp.concatenate([values, code_rows, pad], axis=1)
+
+
+def split_codes(payload, depth):
+    width = payload.shape[2]
+    used = 2 * depth // width
+    halves = payload[:, depth : depth + used].reshape(payload.shape[0], 2 * depth)
+    halves = halves.astype(jnp.int32)
+    codes = halves[:, :depth] * CODE_SPLIT + halves[:, depth:]
+    return payload[:, :depth].reshape(-1, width), codes.reshape(-1)
+
+
+def sent_block(kappa, lists, slots, counts):
+    depth = lists.shape[1]
+    live = jnp.arange(depth, dtype=jnp.int32)[None, :] < counts[:, None]
+    codes = jnp.where(live, slots + 1, 0)
+    return with_codes(gathered_rows(kappa, lists), codes)
+
+
+def diagonal(block, row_by, col_by):
+    rows, cols = lax.axis_size("px"), lax.axis_size("py")
+    pairs = [
+        (i * cols + j, (i + row_by) * cols + j + col_by)
+        for i in range(rows)
+        for j in range(cols)
+        if 0 <= i + row_by < rows and 0 <= j + col_by < cols
+    ]
+    return lax.ppermute(block, ("px", "py"), pairs)
+
+
+def row_blend(own, above, below, top_weight, bottom_weight, width):
+    count = own.shape[1]
+    top = top_weight * own[:, :width] + (1.0 - top_weight) * above
+    bottom = bottom_weight * own[:, count - width :] + (1.0 - bottom_weight) * below
+    return jnp.concatenate([top, own[:, width : count - width], bottom], axis=1)
 
 
 def on_device(kappa, send_list, dest_slot, send_count):
@@ -148,42 +198,56 @@
     pair_counts = send_count[0].reshape(rows_axis, cols_axis)
     slot_depth = tile_lists.shape[2]
     upper_band = jnp.maximum(band_index - 1, 0)
-    picked_lists = jnp.stack([tile_lists[band_index], tile_lists[upper_band]], axis=1)
-    picked_slots = jnp.stack([slot_lists[band_index], slot_lists[upper_band]], axis=1)
     upper_counts = jnp.where(band_index > 0, pair_counts[upper_band], 0)
-    picked_counts = jnp.stack([pair_counts[band_index], upper_counts], axis=1)
-    live_mask = jnp.arange(slot_depth, dtype=jnp.int32)[None, None, :] < picked_counts[:, :, None]
-    slot_codes = jnp.where(live_mask, picked_slots + 1, 0)
-    sent_picks = picked_lists.reshape(-1)[:, None] == jnp.arange(kappa.shape[0], dtype=jnp.int32)
-    sent_values = jnp.dot(
-        sent_picks.astype(kappa.dtype), kappa, preferred_element_type=jnp.float32
-    ).astype(kappa.dtype)
-    sent_values = sent_values.reshape(cols_axis, 2, slot_depth, tile_width)
-    arrived = lax.all_to_all(sent_values, "py", 0, 0, tiled=True)
-    arrived_codes = lax.all_to_all(slot_codes, "py", 0, 0, tiled=True)
+    same_sent = sent_block(
+        kappa, tile_lists[band_index], slot_lists[band_index], pair_counts[band_index]
+    )
+    same_arrived = lax.all_to_all(same_sent, "py", 0, 0, tiled=True)
+    rise_sent = sent_block(kappa, tile_lists[upper_band], slot_lists[upper_band], upper_counts)
+    rise_arrived = lax.all_to_all(rise_sent, "py", 0, 0, tiled=True)
+    same_values, same_codes = split_codes(same_arrived, slot_depth)
+    rise_values, rise_codes = split_codes(rise_arrived, slot_depth)
     rise_total = PATCH_ROWS * PATCH_COLS // tile_width // 4
-    rise_codes = arrived_codes[:, 1].reshape(-1)
     rise_live = rise_codes > 0
     rise_place = jnp.where(rise_live, jnp.cumsum(rise_live.astype(jnp.int32)), 0)
-    packed_values = one_hot_rows(rise_place, rise_total, arrived[:, 1].reshape(-1, tile_width))
+    packed_values = one_hot_rows(rise_place, rise_total, rise_values).astype(kappa.dtype)
     packed_picks = rise_place[None, :] == jnp.arange(1, rise_total + 1, dtype=jnp.int32)[:, None]
     packed_codes = jnp.sum(jnp.where(packed_picks, rise_codes[None, :], 0), axis=1)
     raised_values, raised_codes = shifted((packed_values, packed_codes), "px", -1)
-    all_values = jnp.concatenate(
-        [arrived[:, 0].reshape(-1, tile_width), raised_values], axis=0
-    )
-    all_codes = jnp.concatenate([arrived_codes[:, 0].reshape(-1), raised_codes], axis=0)
     slot_total = PATCH_ROWS * PATCH_COLS // tile_width
-    patch_tiles = one_hot_rows(all_codes, slot_total, all_values)
+    patch_tiles = (
+        one_hot_rows(same_codes, slot_total, same_values)
+        + one_hot_rows(raised_codes, slot_total, raised_values)
+    ).astype(kappa.dtype)
     fields = flexion_fields(patch_tiles.reshape(PATCH_ROWS, PATCH_COLS))
-    extended = padded(fields, (("px", 1), ("py", 2)), tile_width)
-    return blend_edges(
-        extended,
-        band_index > 0,
-        band_index < rows_axis - 1,
-        column_index > 0,
-        column_index < cols_axis - 1,
-        tile_width,
+    width = tile_width
+    last = PATCH_ROWS - width
+    above = shifted(fields[:, last:], "px", 1)
+    below = shifted(fields[:, :width], "px", -1)
+    left = shifted(fields[:, :, last:], "py", 1)
+    right = shifted(fields[:, :, :width], "py", -1)
+    above_left = diagonal(fields[:, last:, last:], 1, 1)
+    above_right = diagonal(fields[:, last:, :width], 1, -1)
+    below_left = diagonal(fields[:, :width, last:], -1, 1)
+    below_right = diagonal(fields[:, :width, :width], -1, -1)
+    ramp = (jnp.arange(width, dtype=jnp.float32) + 0.5) / width
+    top_weight = jnp.where(band_index > 0, ramp, 1.0)[None, :, None]
+    bottom_weight = jnp.where(band_index < rows_axis - 1, ramp[::-1], 1.0)[None, :, None]
+    left_weight = jnp.where(column_index > 0, ramp, 1.0)[None, None, :]
+    right_weight = jnp.where(column_index < cols_axis - 1, ramp[::-1], 1.0)[None, None, :]
+    f32 = lambda x: x.astype(jnp.float32)
+    inner = row_blend(f32(fields), f32(above), f32(below), top_weight, bottom_weight, width)
+    left_strip = row_blend(
+        f32(left), f32(above_left), f32(below_left), top_weight, bottom_weight, width
+    )
+    right_strip = row_blend(
+        f32(right), f32(above_right), f32(below_right), top_weight, bottom_weight, width
+    )
+    col_count = inner.shape[2]
+    left_band = left_weight * inner[:, :, :width] + (1.0 - left_weight) * left_strip
+    right_band = right_weight * inner[:, :, col_count - width :] + (1.0 - right_weight) * right_strip
+    return jnp.concatenate(
+        [left_band, inner[:, :, width : col_count - width], right_band], axis=2
     )
 
 

time: 132 us -> 123 us (0.932)
  the two profiles are of different devices: /device:TPU:15 before, /device:TPU:40 now
where the time goes in v2:
time: 123 us
  starting transfers between devices  43.1 us (35%)
  waiting for transfers between devices  34 us (28%)
  matrix products  24.5 us (20%)
  other arithmetic  12.6 us (10%)
  local copies, waits for them, and re-layouts  7.84 us (6%)
    ppermute x6, starting transfers between devices, shifted(): return lax.ppermute(shard, axis, pairs)  16.4 us
    all_to_all x1, waiting for transfers between devices, on_device(): same_arrived = lax.all_to_all(same_sent, 'py', 0, 0, tiled=True)  12.4 us
    ppermute x4, starting transfers between devices, diagonal(): return lax.ppermute(block, ('px', 'py'), pairs)  12.4 us
    dot_general x2, matrix products, gathered_rows(): jnp.dot(chosen.astype(table_rows.dtype), table_rows, preferred_element_ty...  11.2 us
    all_to_all x1, waiting for transfers between devices, on_device(): rise_arrived = lax.all_to_all(rise_sent, 'py', 0, 0, tiled=True)  11.2 us
    all_to_all x1, starting transfers between devices, on_device(): same_arrived = lax.all_to_all(same_sent, 'py', 0, 0, tiled=True)  7.89 us
    dot_general x8, matrix products, dot32(): return jnp.dot(a, b, preferred_element_type=jnp.float32)  7.52 us
    all_to_all x1, starting transfers between devices, on_device(): rise_arrived = lax.all_to_all(rise_sent, 'py', 0, 0, tiled=True)  6.34 us
  transfers between devices with their start and end apart: 12, of which 4 were waited for; matrix products, arithmetic and copies ran while one was open for 5% of the time, Pallas kernels for 0%

profile of v2, /device:TPU:40, one launch (start us, length us, event | category | flops | bytes accessed | tf_op | source)
XLA Modules:
  0.0 122.6 jit_solution(1765865060192984218)
XLA Ops:
  0.0 1.0 copy.19
  1.1 0.5 broadcast.383
  1.6 1.3 %reduce.5 = s32[128]{0:T(128)S(1)} reduce(s32[1,128]{1,0:T(1,128)} %param.9, s32[]{:T(128)} %broadcast.383), dimensions={0}, to_apply=%param.9.reduce_sub_computation.3 | reduce | bytes 1028 | tf_op args[3]
  3.2 1.0 copy.18
  4.4 5.6 %fusion.13 = bf16[3072,128]{1,0:T(8,128)(2,1)S(1)} fusion(bf16[2352,128]{1,0:T(8,128)(2,1)S(1)} %copy-done, s32[3072]{0:T(1024)S(1)} %eq.89), kind=kOutput, calls=%fused_computation.18 | convolution fusion | flops 1857306624 | bytes 1400832 | tf_op jit(solution)/shard_map/dot_general | solution.py:140
  10.0 5.6 %fusion.14 = bf16[3072,128]{1,0:T(8,128)(2,1)S(1)} fusion(bf16[2352,128]{1,0:T(8,128)(2,1)S(1)} %copy-done, s32[3072]{0:T(1024)S(1)} %eq.39), kind=kOutput, calls=%fused_computation.19 | convolution fusion | flops 1857306624 | bytes 1400832 | tf_op jit(solution)/shard_map/dot_general | solution.py:140
  15.7 1.6 %maximum_maximum_fusion.1 = (bf16[16,208,128]{2,1,0:T(8,128)(2,1)}, bf16[16,208,128]{2,1,0:T(8,128)(2,1)}) fusion(bf16[16,3,128]{2,1,0:T(4,128)(2,1)S(1)} %convert_element_type.130, bf16[16,192,128]{2,1,0:T(8,128)(2,1)S(1)} %bitcast.65, bf16[208]{0:T(256)(128)(2,1)S(1)} %pad.33.clone, bf16[16,3,128]{2,1,0:T(4,128)(2,1)S(1)} %convert_element_type.126, ...), kind=kLoop, calls=%fused_computation.66 | loop fusion | flops 4685824 | bytes 3301792 | tf_op jit(solution)/shard_map/concatenate | solution.py:153
  17.3 7.9 %all-to-all-start = ((bf16[16,208,128]{2,1,0:T(8,128)(2,1)}), bf16[16,208,128]{2,1,0:T(8,128)(2,1)S(1)}, u32[]{:S(2)}, u32[]{:S(2)}) async-start(bf16[16,208,128]{2,1,0:T(8,128)(2,1)} %get-tuple-element.60), calls=%async_computation | async-start | bytes 1703936 | tf_op jit(solution)/shard_map/all_to_all | solution.py:205
  25.2 12.4 %all-to-all-done = bf16[16,208,128]{2,1,0:T(8,128)(2,1)S(1)} async-done(((bf16[16,208,128]{2,1,0:T(8,128)(2,1)}), bf16[16,208,128]{2,1,0:T(8,128)(2,1)S(1)}, u32[]{:S(2)}, u32[]{:S(2)}) %all-to-all-start) | async-done | bytes 852000 | tf_op jit(solution)/shard_map/all_to_all | solution.py:205
  37.6 6.3 %all-to-all-start.1 = ((bf16[16,208,128]{2,1,0:T(8,128)(2,1)}), bf16[16,208,128]{2,1,0:T(8,128)(2,1)S(1)}, u32[]{:S(2)}, u32[]{:S(2)}) async-start(bf16[16,208,128]{2,1,0:T(8,128)(2,1)} %get-tuple-element.59), calls=%async_computation.1 | async-start | bytes 1703936 | tf_op jit(solution)/shard_map/all_to_all | solution.py:207
  44.3 11.2 %all-to-all-done.1 = bf16[16,208,128]{2,1,0:T(8,128)(2,1)S(1)} async-done(((bf16[16,208,128]{2,1,0:T(8,128)(2,1)}), bf16[16,208,128]{2,1,0:T(8,128)(2,1)S(1)}, u32[]{:S(2)}, u32[]{:S(2)}) %all-to-all-start.1) | async-done | bytes 852000 | tf_op jit(solution)/shard_map/all_to_all | solution.py:207
  55.6 0.3 reduce-window.9
  56.3 0.8 fusion.10
  57.1 1.0 fusion.27
  58.2 1.9 %collective-permute-start.1 = (bf16[512,128]{1,0:T(8,128)(2,1)S(1)}, bf16[512,128]{1,0:T(8,128)(2,1)S(1)}, u32[]{:S(2)}, u32[]{:S(2)}) collective-permute-start(bf16[512,128]{1,0:T(8,128)(2,1)S(1)} %fusion.27), channel_id=1, source_target_pairs={{16,0},{32,16},{48,32},{64,48},{80,64},{96,80},{112,96},{17,1},{33... | collective-permute-start | bytes 393224 | tf_op jit(solution)/shard_map/ppermute | solution.py:17
  60.1 2.6 %collective-permute-start = (s32[512]{0:T(512)S(1)}, s32[512]{0:T(512)S(1)}, u32[]{:S(2)}, u32[]{:S(2)}) collective-permute-start(s32[512]{0:T(512)S(1)} %fusion.10), channel_id=1, source_target_pairs={{16,0},{32,16},{48,32},{64,48},{80,64},{96,80},{112,96},{17,1},{33... | collective-permute-start | bytes 6152 | tf_op jit(solution)/shard_map/ppermute | solution.py:17
  62.8 3.7 %fusion.2 = f32[2048,128]{1,0:T(8,128)S(1)} fusion(bf16[3072,128]{1,0:T(8,128)(2,1)S(1)} %bitcast.64, s32[3072]{0:T(1024)S(1)} %eq.43, s32[2048]{0:T(1024)S(1)} %iota_add_fusion), kind=kOutput, calls=%fused_computation.4 | convolution fusion | flops 1616904192 | bytes 1855488 | tf_op jit(solution)/shard_map/dot_general | solution.py:135
  66.6 1.1 fusion.20
  67.7 0.3 reshape.165
  68.0 0.5 convolution_convert_fusion
  68.5 0.5 convolution_convert_fusion.1
  69.0 0.7 fusion.41
  69.7 0.7 fusion.40
  70.5 0.3 multiply_convert_fusion.3
  70.8 1.0 multiply_convert_fusion.2
  71.8 1.3 %fusion.48 = f32[512,2048]{1,0:T(8,128)S(1)} fusion(bf16[512,512]{1,0:T(8,128)(2,1)S(1)} %copy-done.4, bf16[512,512]{1,0:T(8,128)(2,1)S(1)} %get-tuple-element.25, bf16[512,512]{1,0:T(8,128)(2,1)S(1)} %get-tuple-element.26, bf16[512,512]{1,0:T(8,128)(2,1)S(1)} %get-tuple-element.24, bf16[512,512]{1,0:T(8,128)(2,1)S(1)} %get-tuple-element.9), kind=kOutput, calls=%fused_computation.75 | convolution fusion | flops 1082130432 | bytes 6815744 | tf_op jit(solution)/shard_map/dot_general | solution.py:51
  73.0 1.3 %fusion.49 = f32[512,2048]{1,0:T(8,128)S(1)} fusion(bf16[512,512]{1,0:T(8,128)(2,1)S(1)} %copy-done.3, bf16[512,512]{1,0:T(8,128)(2,1)S(1)} %get-tuple-element.25, bf16[512,512]{1,0:T(8,128)(2,1)S(1)} %get-tuple-element.26, bf16[512,512]{1,0:T(8,128)(2,1)S(1)} %get-tuple-element.24, bf16[512,512]{1,0:T(8,128)(2,1)S(1)} %get-tuple-element.9), kind=kOutput, calls=%fused_computation.76 | convolution fusion | flops 1082130432 | bytes 6815744 | tf_op jit(solution)/shard_map/dot_general | solution.py:51
  74.3 1.2 fusion.24
  75.7 1.3 %fusion.46 = f32[2048,512]{1,0:T(8,128)S(1)} fusion(bf16[512,512]{1,0:T(8,128)(2,1)S(1)} %copy-done.4, bf16[512,512]{1,0:T(8,128)(2,1)S(1)} %get-tuple-element.44, bf16[512,512]{1,0:T(8,128)(2,1)S(1)} %get-tuple-element.43, bf16[512,512]{1,0:T(8,128)(2,1)S(1)} %get-tuple-element.42, bf16[512,512]{1,0:T(8,128)(2,1)S(1)} %get-tuple-element.41), kind=kOutput, calls=%fused_computation.73 | convolution fusion | flops 1082130432 | bytes 6815744 | tf_op jit(solution)/shard_map/dot_general | solution.py:51
  76.9 1.3 %fusion.47 = f32[2048,512]{1,0:T(8,128)S(1)} fusion(bf16[512,512]{1,0:T(8,128)(2,1)S(1)} %copy-done.3, bf16[512,512]{1,0:T(8,128)(2,1)S(1)} %get-tuple-element.44, bf16[512,512]{1,0:T(8,128)(2,1)S(1)} %get-tuple-element.43, bf16[512,512]{1,0:T(8,128)(2,1)S(1)} %get-tuple-element.42, bf16[512,512]{1,0:T(8,128)(2,1)S(1)} %get-tuple-element.41), kind=kOutput, calls=%fused_computation.74 | convolution fusion | flops 1082130432 | bytes 6815744 | tf_op jit(solution)/shard_map/dot_general | solution.py:51
  78.2 1.2 %fusion.42 = (bf16[1,512,512]{2,1,0:T(8,128)(2,1)S(1)}, bf16[1,512,512]{2,1,0:T(8,128)(2,1)S(1)}, bf16[1,512,512]{2,1,0:T(8,128)(2,1)S(1)}, bf16[1,512,512]{2,1,0:T(8,128)(2,1)S(1)}) fusion(f32[2048,512]{1,0:T(8,128)S(1)} %fusion.46, f32[2048,512]{1,0:T(8,128)S(1)} %fusion.47), kind=kLoop, calls=%fused_computation.69 | loop fusion | flops 2097152 | bytes 10485760 | tf_op jit(solution)/shard_map/stack | solution.py:98
  79.5 0.4 pad_maximum_fusion.4
  80.0 1.9 %collective-permute-start.2 = (bf16[4,128,512]{2,1,0:T(8,128)(2,1)S(1)}, bf16[4,128,512]{2,1,0:T(8,128)(2,1)S(1)}, u32[]{:S(2)}, u32[]{:S(2)}) collective-permute-start(bf16[4,128,512]{2,1,0:T(8,128)(2,1)S(1)} %get-tuple-element.33), channel_id=1, source_target_pairs={{0,16},{16,32},{32,48},{48,64},{64,80},{80,96},{96,112},{1,17},{17... | collective-permute-start | bytes 1572872 | tf_op jit(solution)/shard_map/ppermute | solution.py:17
  81.9 3.6 %collective-permute-start.3 = (bf16[4,128,512]{2,1,0:T(8,128)(2,1)S(1)}, bf16[4,128,512]{2,1,0:T(8,128)(2,1)S(1)}, u32[]{:S(2)}, u32[]{:S(2)}) collective-permute-start(bf16[4,128,512]{2,1,0:T(8,128)(2,1)S(1)} %get-tuple-element.34), channel_id=1, source_target_pairs={{16,0},{32,16},{48,32},{64,48},{80,64},{96,80},{112,96},{17,1},{33... | collective-permute-start | bytes 1572872 | tf_op jit(solution)/shard_map/ppermute | solution.py:17
  86.0 4.4 %collective-permute-start.7 = (bf16[4,512,128]{2,1,0:T(8,128)(2,1)S(1)}, bf16[4,512,128]{2,1,0:T(8,128)(2,1)S(1)}, u32[]{:S(2)}, u32[]{:S(2)}) collective-permute-start(bf16[4,512,128]{2,1,0:T(8,128)(2,1)S(1)} %get-tuple-element.32), channel_id=1, source_target_pairs={{1,0},{2,1},{3,2},{4,3},{5,4},{6,5},{7,6},{8,7},{9,8},{10,9},{11,1... | collective-permute-start | bytes 1572872 | tf_op jit(solution)/shard_map/ppermute | solution.py:17
  90.4 1.9 %collective-permute-start.4 = (bf16[4,512,128]{2,1,0:T(8,128)(2,1)S(1)}, bf16[4,512,128]{2,1,0:T(8,128)(2,1)S(1)}, u32[]{:S(2)}, u32[]{:S(2)}) collective-permute-start(bf16[4,512,128]{2,1,0:T(8,128)(2,1)S(1)} %get-tuple-element.31), channel_id=1, source_target_pairs={{0,1},{1,2},{2,3},{3,4},{4,5},{5,6},{6,7},{7,8},{8,9},{9,10},{10,1... | collective-permute-start | bytes 1572872 | tf_op jit(solution)/shard_map/ppermute | solution.py:17
  92.5 5.0 %collective-permute-start.8 = (bf16[4,128,128]{2,1,0:T(8,128)(2,1)S(1)}, bf16[4,128,128]{2,1,0:T(8,128)(2,1)S(1)}, u32[]{:S(2)}, u32[]{:S(2)}) collective-permute-start(bf16[4,128,128]{2,1,0:T(8,128)(2,1)S(1)} %get-tuple-element.28), channel_id=1, source_target_pairs={{1,16},{2,17},{3,18},{4,19},{5,20},{6,21},{7,22},{8,23},{9,24},{10... | collective-permute-start | bytes 393224 | tf_op jit(solution)/shard_map/ppermute | solution.py:180
  97.5 2.3 %collective-permute-start.9 = (bf16[4,128,128]{2,1,0:T(8,128)(2,1)S(1)}, bf16[4,128,128]{2,1,0:T(8,128)(2,1)S(1)}, u32[]{:S(2)}, u32[]{:S(2)}) collective-permute-start(bf16[4,128,128]{2,1,0:T(8,128)(2,1)S(1)} %get-tuple-element.30), channel_id=1, source_target_pairs={{17,0},{18,1},{19,2},{20,3},{21,4},{22,5},{23,6},{24,7},{25,8},{26... | collective-permute-start | bytes 393224 | tf_op jit(solution)/shard_map/ppermute | solution.py:180
  99.8 3.2 %collective-permute-start.6 = (bf16[4,128,128]{2,1,0:T(8,128)(2,1)S(1)}, bf16[4,128,128]{2,1,0:T(8,128)(2,1)S(1)}, u32[]{:S(2)}, u32[]{:S(2)}) collective-permute-start(bf16[4,128,128]{2,1,0:T(8,128)(2,1)S(1)} %get-tuple-element.29), channel_id=1, source_target_pairs={{16,1},{17,2},{18,3},{19,4},{20,5},{21,6},{22,7},{23,8},{24,9},{25... | collective-permute-start | bytes 393224 | tf_op jit(solution)/shard_map/ppermute | solution.py:180
  103.0 0.3 fusion.33
  103.3 5.6 %collective-permute-done.4 = bf16[4,512,128]{2,1,0:T(8,128)(2,1)S(1)} collective-permute-done((bf16[4,512,128]{2,1,0:T(8,128)(2,1)S(1)}, bf16[4,512,128]{2,1,0:T(8,128)(2,1)S(1)}, u32[]{:S(2)}, u32[]{:S(2)}) %collective-permute-start.4) | collective-permute-done | bytes 524320 | tf_op jit(solution)/shard_map/ppermute | solution.py:17
  109.0 1.9 %collective-permute-start.5 = (bf16[4,128,128]{2,1,0:T(8,128)(2,1)S(1)}, bf16[4,128,128]{2,1,0:T(8,128)(2,1)S(1)}, u32[]{:S(2)}, u32[]{:S(2)}) collective-permute-start(bf16[4,128,128]{2,1,0:T(8,128)(2,1)S(1)} %get-tuple-element.27), channel_id=1, source_target_pairs={{0,17},{1,18},{2,19},{3,20},{4,21},{5,22},{6,23},{7,24},{8,25},{9,... | collective-permute-start | bytes 393224 | tf_op jit(solution)/shard_map/ppermute | solution.py:180
  110.9 0.4 pad_maximum_fusion
  111.5 1.8 %copy-done.2 = f32[4,512,512]{2,1,0:T(8,128)} copy-done((f32[4,512,512]{2,1,0:T(8,128)}, f32[4,512,512]{2,1,0:T(8,128)S(1)}, u32[]{:S(2)}) %copy-start.2) | copy-done | bytes 4194328
  113.4 4.8 %collective-permute-done.5 = bf16[4,128,128]{2,1,0:T(8,128)(2,1)S(1)} collective-permute-done((bf16[4,128,128]{2,1,0:T(8,128)(2,1)S(1)}, bf16[4,128,128]{2,1,0:T(8,128)(2,1)S(1)}, u32[]{:S(2)}, u32[]{:S(2)}) %collective-permute-start.5) | collective-permute-done | bytes 131104 | tf_op jit(solution)/shard_map/ppermute | solution.py:180
  118.2 0.2 fusion.51
  118.7 1.3 %slice-done = f32[4,512,256]{2,1,0:T(8,128)S(1)} async-done(((f32[4,512,512]{2,1,0:T(8,128)}), f32[4,512,256]{2,1,0:T(8,128)S(1)}, s32[]{:S(2)}) %slice-start) | async-done | bytes 2097176 | tf_op jit(solution)/shard_map/slice | solution.py:250
  120.1 2.5 %pad_maximum_fusion.1 = f32[4,512,512]{2,1,0:T(8,128)} fusion(f32[4,512,128]{2,1,0:T(8,128)S(1)} %get-tuple-element.21, f32[4,512,256]{2,1,0:T(8,128)S(1)} %slice-done, f32[4,512,128]{2,1,0:T(8,128)S(1)} %get-tuple-element.20), kind=kLoop, calls=%fused_computation.15 | loop fusion | flops 2097152 | bytes 8388608 | tf_op jit(solution)/shard_map/concatenate | solution.py:249
  (65 shorter events, 2.8 us)
Async XLA Ops:
  0.0 4.4 %copy-start = (bf16[2352,128]{1,0:T(8,128)(2,1)S(1)}, bf16[2352,128]{1,0:T(8,128)(2,1)}, u32[]{:S(2)}) copy-start(bf16[2352,128]{1,0:T(8,128)(2,1)} %param.6) | copy-start | bytes 1806340
  17.3 20.4 %all-to-all-start = ((bf16[16,208,128]{2,1,0:T(8,128)(2,1)}), bf16[16,208,128]{2,1,0:T(8,128)(2,1)S(1)}, u32[]{:S(2)}, u32[]{:S(2)}) async-start(bf16[16,208,128]{2,1,0:T(8,128)(2,1)} %get-tuple-element.60), calls=%async_computation | async-start | bytes 1703936 | tf_op jit(solution)/shard_map/all_to_all | solution.py:205
  37.6 17.8 %all-to-all-start.1 = ((bf16[16,208,128]{2,1,0:T(8,128)(2,1)}), bf16[16,208,128]{2,1,0:T(8,128)(2,1)S(1)}, u32[]{:S(2)}, u32[]{:S(2)}) async-start(bf16[16,208,128]{2,1,0:T(8,128)(2,1)} %get-tuple-element.59), calls=%async_computation.1 | async-start | bytes 1703936 | tf_op jit(solution)/shard_map/all_to_all | solution.py:207
  58.2 8.4 %collective-permute-start.1 = (bf16[512,128]{1,0:T(8,128)(2,1)S(1)}, bf16[512,128]{1,0:T(8,128)(2,1)S(1)}, u32[]{:S(2)}, u32[]{:S(2)}) collective-permute-start(bf16[512,128]{1,0:T(8,128)(2,1)S(1)} %fusion.27), channel_id=1, source_target_pairs={{16,0},{32,16},{48,32},{64,48},{80,64},{96,80},{112,96},{17,1},{33... | collective-permute-start | bytes 393224 | tf_op jit(solution)/shard_map/ppermute | solution.py:17
  60.1 6.5 %collective-permute-start = (s32[512]{0:T(512)S(1)}, s32[512]{0:T(512)S(1)}, u32[]{:S(2)}, u32[]{:S(2)}) collective-permute-start(s32[512]{0:T(512)S(1)} %fusion.10), channel_id=1, source_target_pairs={{16,0},{32,16},{48,32},{64,48},{80,64},{96,80},{112,96},{17,1},{33... | collective-permute-start | bytes 6152 | tf_op jit(solution)/shard_map/ppermute | solution.py:17
  62.8 5.2 %copy-start.4 = (bf16[512,512]{1,0:T(8,128)(2,1)S(1)}, bf16[512,512]{1,0:T(8,128)(2,1)}, u32[]{:S(2)}) copy-start(bf16[512,512]{1,0:T(8,128)(2,1)} %constant.98.clone) | copy-start | bytes 1572868
  66.5 1.9 %copy-start.3 = (bf16[512,512]{1,0:T(8,128)(2,1)S(1)}, bf16[512,512]{1,0:T(8,128)(2,1)}, u32[]{:S(2)}) copy-start(bf16[512,512]{1,0:T(8,128)(2,1)} %constant.97.clone) | copy-start | bytes 1572868
  80.0 17.5 %collective-permute-start.2 = (bf16[4,128,512]{2,1,0:T(8,128)(2,1)S(1)}, bf16[4,128,512]{2,1,0:T(8,128)(2,1)S(1)}, u32[]{:S(2)}, u32[]{:S(2)}) collective-permute-start(bf16[4,128,512]{2,1,0:T(8,128)(2,1)S(1)} %get-tuple-element.33), channel_id=1, source_target_pairs={{0,16},{16,32},{32,48},{48,64},{64,80},{80,96},{96,112},{1,17},{17... | collective-permute-start | bytes 1572872 | tf_op jit(solution)/shard_map/ppermute | solution.py:17
  81.9 17.9 %collective-permute-start.3 = (bf16[4,128,512]{2,1,0:T(8,128)(2,1)S(1)}, bf16[4,128,512]{2,1,0:T(8,128)(2,1)S(1)}, u32[]{:S(2)}, u32[]{:S(2)}) collective-permute-start(bf16[4,128,512]{2,1,0:T(8,128)(2,1)S(1)} %get-tuple-element.34), channel_id=1, source_target_pairs={{16,0},{32,16},{48,32},{64,48},{80,64},{96,80},{112,96},{17,1},{33... | collective-permute-start | bytes 1572872 | tf_op jit(solution)/shard_map/ppermute | solution.py:17
  86.0 25.5 %collective-permute-start.7 = (bf16[4,512,128]{2,1,0:T(8,128)(2,1)S(1)}, bf16[4,512,128]{2,1,0:T(8,128)(2,1)S(1)}, u32[]{:S(2)}, u32[]{:S(2)}) collective-permute-start(bf16[4,512,128]{2,1,0:T(8,128)(2,1)S(1)} %get-tuple-element.32), channel_id=1, source_target_pairs={{1,0},{2,1},{3,2},{4,3},{5,4},{6,5},{7,6},{8,7},{9,8},{10,9},{11,1... | collective-permute-start | bytes 1572872 | tf_op jit(solution)/shard_map/ppermute | solution.py:17
  90.4 18.6 %collective-permute-start.4 = (bf16[4,512,128]{2,1,0:T(8,128)(2,1)S(1)}, bf16[4,512,128]{2,1,0:T(8,128)(2,1)S(1)}, u32[]{:S(2)}, u32[]{:S(2)}) collective-permute-start(bf16[4,512,128]{2,1,0:T(8,128)(2,1)S(1)} %get-tuple-element.31), channel_id=1, source_target_pairs={{0,1},{1,2},{2,3},{3,4},{4,5},{5,6},{6,7},{7,8},{8,9},{9,10},{10,1... | collective-permute-start | bytes 1572872 | tf_op jit(solution)/shard_map/ppermute | solution.py:17
  92.5 20.9 %collective-permute-start.8 = (bf16[4,128,128]{2,1,0:T(8,128)(2,1)S(1)}, bf16[4,128,128]{2,1,0:T(8,128)(2,1)S(1)}, u32[]{:S(2)}, u32[]{:S(2)}) collective-permute-start(bf16[4,128,128]{2,1,0:T(8,128)(2,1)S(1)} %get-tuple-element.28), channel_id=1, source_target_pairs={{1,16},{2,17},{3,18},{4,19},{5,20},{6,21},{7,22},{8,23},{9,24},{10... | collective-permute-start | bytes 393224 | tf_op jit(solution)/shard_map/ppermute | solution.py:180
  97.5 15.9 %collective-permute-start.9 = (bf16[4,128,128]{2,1,0:T(8,128)(2,1)S(1)}, bf16[4,128,128]{2,1,0:T(8,128)(2,1)S(1)}, u32[]{:S(2)}, u32[]{:S(2)}) collective-permute-start(bf16[4,128,128]{2,1,0:T(8,128)(2,1)S(1)} %get-tuple-element.30), channel_id=1, source_target_pairs={{17,0},{18,1},{19,2},{20,3},{21,4},{22,5},{23,6},{24,7},{25,8},{26... | collective-permute-start | bytes 393224 | tf_op jit(solution)/shard_map/ppermute | solution.py:180
  99.8 13.6 %collective-permute-start.6 = (bf16[4,128,128]{2,1,0:T(8,128)(2,1)S(1)}, bf16[4,128,128]{2,1,0:T(8,128)(2,1)S(1)}, u32[]{:S(2)}, u32[]{:S(2)}) collective-permute-start(bf16[4,128,128]{2,1,0:T(8,128)(2,1)S(1)} %get-tuple-element.29), channel_id=1, source_target_pairs={{16,1},{17,2},{18,3},{19,4},{20,5},{21,6},{22,7},{23,8},{24,9},{25... | collective-permute-start | bytes 393224 | tf_op jit(solution)/shard_map/ppermute | solution.py:180
  109.0 9.3 %collective-permute-start.5 = (bf16[4,128,128]{2,1,0:T(8,128)(2,1)S(1)}, bf16[4,128,128]{2,1,0:T(8,128)(2,1)S(1)}, u32[]{:S(2)}, u32[]{:S(2)}) collective-permute-start(bf16[4,128,128]{2,1,0:T(8,128)(2,1)S(1)} %get-tuple-element.27), channel_id=1, source_target_pairs={{0,17},{1,18},{2,19},{3,20},{4,21},{5,22},{6,23},{7,24},{8,25},{9,... | collective-permute-start | bytes 393224 | tf_op jit(solution)/shard_map/ppermute | solution.py:180
  111.3 2.0 %copy-start.2 = (f32[4,512,512]{2,1,0:T(8,128)}, f32[4,512,512]{2,1,0:T(8,128)S(1)}, u32[]{:S(2)}) copy-start(f32[4,512,512]{2,1,0:T(8,128)S(1)} %pad_maximum_fusion) | copy-start | bytes 12582916
  118.5 1.6 %slice-start = ((f32[4,512,512]{2,1,0:T(8,128)}), f32[4,512,256]{2,1,0:T(8,128)S(1)}, s32[]{:S(2)}) async-start(f32[4,512,512]{2,1,0:T(8,128)} %copy-done.2), calls=%async_computation.2 | async-start | bytes 4194304 | tf_op jit(solution)/shard_map/slice | solution.py:250
  118.7 3.9 %copy-start.1 = (bf16[2352,128]{1,0:T(8,128)(2,1)S(1)}, bf16[2352,128]{1,0:T(8,128)(2,1)}, u32[]{:S(2)}) copy-start(bf16[2352,128]{1,0:T(8,128)(2,1)} %param.6) | copy-start | bytes 1806340

commit v3 on v2

--- a/solution.py
+++ b/solution.py
@@ -202,18 +202,18 @@
     same_sent = sent_block(
         kappa, tile_lists[band_index], slot_lists[band_index], pair_counts[band_index]
     )
-    same_arrived = lax.all_to_all(same_sent, "py", 0, 0, tiled=True)
     rise_sent = sent_block(kappa, tile_lists[upper_band], slot_lists[upper_band], upper_counts)
-    rise_arrived = lax.all_to_all(rise_sent, "py", 0, 0, tiled=True)
-    same_values, same_codes = split_codes(same_arrived, slot_depth)
-    rise_values, rise_codes = split_codes(rise_arrived, slot_depth)
+    arrived = lax.all_to_all(jnp.stack([same_sent, rise_sent], axis=1), "py", 0, 0, tiled=True)
+    same_values, same_codes = split_codes(arrived[:, 0], slot_depth)
+    rise_values, rise_codes = split_codes(arrived[:, 1], slot_depth)
     rise_total = PATCH_ROWS * PATCH_COLS // tile_width // 4
     rise_live = rise_codes > 0
     rise_place = jnp.where(rise_live, jnp.cumsum(rise_live.astype(jnp.int32)), 0)
     packed_values = one_hot_rows(rise_place, rise_total, rise_values).astype(kappa.dtype)
     packed_picks = rise_place[None, :] == jnp.arange(1, rise_total + 1, dtype=jnp.int32)[:, None]
     packed_codes = jnp.sum(jnp.where(packed_picks, rise_codes[None, :], 0), axis=1)
-    raised_values, raised_codes = shifted((packed_values, packed_codes), "px", -1)
+    packed = with_codes(packed_values.reshape(1, rise_total, tile_width), packed_codes[None])
+    raised_values, raised_codes = split_codes(shifted(packed, "px", -1), rise_total)
     slot_total = PATCH_ROWS * PATCH_COLS // tile_width
     patch_tiles = (
         one_hot_rows(same_codes, slot_total, same_values)

time: 123 us -> 113 us (0.919)
  starting transfers between devices: 43.1 us -> 32.1 us
    all_to_all x2 -> x1, starting transfers between devices: 14.2 us -> 7.9 us  [on_device(): lax.all_to_all(jnp.stack([same_sent, rise_sent], axis=1), 'py', 0, 0, til...]
    ppermute x6 -> x5, starting transfers between devices: 16.4 us -> 13.5 us  [shifted(): return lax.ppermute(shard, axis, pairs)]
    another operation x6 -> x8, other arithmetic: 2.92 us -> 4.65 us
    ppermute x4, starting transfers between devices: 12.4 us -> 10.7 us  [diagonal(): return lax.ppermute(block, ('px', 'py'), pairs)]
    concatenate x1, other arithmetic: 1.59 us -> 0.14 us  [with_codes(): return jnp.concatenate([values, code_rows, pad], axis=1)]
    all_to_all x2 -> x1, waiting for transfers between devices: 23.6 us -> 24 us  [on_device(): lax.all_to_all(jnp.stack([same_sent, rise_sent], axis=1), 'py', 0, 0, til...]
    ppermute x6 -> x5, waiting for transfers between devices: 5.62 us -> 5.26 us  [shifted(): return lax.ppermute(shard, axis, pairs)]
  transfers between devices with their start and end apart: 12 -> 10, of which waited for: 4 -> 3; matrix products, arithmetic and copies ran while one was open for 5% -> 5% of each run, Pallas kernels for 0% -> 0%
where the time goes in v3:
time: 113 us; the launch traced here: 112 us
  waiting for transfers between devices  33.9 us (30%)
  starting transfers between devices  32.1 us (28%)
  matrix products  24.5 us (22%)
  other arithmetic  12.9 us (11%)
  local copies, waits for them, and re-layouts  8.26 us (7%)
    all_to_all x1, waiting for transfers between devices, on_device(): lax.all_to_all(jnp.stack([same_sent, rise_sent], axis=1), 'py', 0, 0, til...  24 us
    ppermute x5, starting transfers between devices, shifted(): return lax.ppermute(shard, axis, pairs)  13.5 us
    dot_general x2, matrix products, gathered_rows(): jnp.dot(chosen.astype(table_rows.dtype), table_rows, preferred_element_ty...  11.2 us
    ppermute x4, starting transfers between devices, diagonal(): return lax.ppermute(block, ('px', 'py'), pairs)  10.7 us
    all_to_all x1, starting transfers between devices, on_device(): lax.all_to_all(jnp.stack([same_sent, rise_sent], axis=1), 'py', 0, 0, til...  7.9 us
    dot_general x8, matrix products, dot32(): return jnp.dot(a, b, preferred_element_type=jnp.float32)  7.53 us
    dot_general x3, matrix products, one_hot_rows(): jnp.dot(picks.astype(values.dtype), values, preferred_element_type=jnp.fl...  5.82 us
    ppermute x5, waiting for transfers between devices, shifted(): return lax.ppermute(shard, axis, pairs)  5.26 us
  transfers between devices with their start and end apart: 10, of which 3 were waited for; matrix products, arithmetic and copies ran while one was open for 5% of the time, Pallas kernels for 0%

profile of v3, /device:TPU:40, one launch (start us, length us, event | category | flops | bytes accessed | tf_op | source)
XLA Modules:
  0.0 112.1 jit_solution(11706316259554802143)
XLA Ops:
  0.0 1.0 copy.21
  1.1 0.5 broadcast.526
  1.6 1.3 %reduce.5 = s32[128]{0:T(128)S(1)} reduce(s32[1,128]{1,0:T(1,128)} %param.9, s32[]{:T(128)} %broadcast.526), dimensions={0}, to_apply=%param.9.reduce_sub_computation.3 | reduce | bytes 1028 | tf_op args[3]
  3.2 1.0 copy.20
  4.4 5.6 %fusion.14 = bf16[3072,128]{1,0:T(8,128)(2,1)S(1)} fusion(bf16[2352,128]{1,0:T(8,128)(2,1)S(1)} %copy-done, s32[3072]{0:T(1024)S(1)} %eq.43), kind=kOutput, calls=%fused_computation.19 | convolution fusion | flops 1857306624 | bytes 1400832 | tf_op jit(solution)/shard_map/dot_general | solution.py:140
  10.0 5.6 %fusion.13 = bf16[3072,128]{1,0:T(8,128)(2,1)S(1)} fusion(bf16[2352,128]{1,0:T(8,128)(2,1)S(1)} %copy-done, s32[3072]{0:T(1024)S(1)} %eq.89), kind=kOutput, calls=%fused_computation.18 | convolution fusion | flops 1857306624 | bytes 1400832 | tf_op jit(solution)/shard_map/dot_general | solution.py:140
  15.7 0.4 maximum_bitcast_fusion
  16.1 1.3 %pad_maximum_fusion.5 = bf16[16,2,208,128]{3,2,1,0:T(8,128)(2,1)} fusion(bf16[16,1,208,128]{3,2,1,0:T(8,128)(2,1)S(1)} %get-tuple-element.64, bf16[16,1,208,128]{3,2,1,0:T(8,128)(2,1)S(1)} %get-tuple-element.63), kind=kLoop, calls=%fused_computation.34 | loop fusion | flops 851968 | bytes 3407872 | tf_op jit(solution)/shard_map/stack | solution.py:206
  17.4 7.9 %all-to-all-start = ((bf16[16,2,208,128]{3,2,1,0:T(8,128)(2,1)}), bf16[16,2,208,128]{3,2,1,0:T(8,128)(2,1)S(1)}, u32[]{:S(2)}, u32[]{:S(2)}) async-start(bf16[16,2,208,128]{3,2,1,0:T(8,128)(2,1)} %pad_maximum_fusion.5), calls=%async_computation | async-start | bytes 3407872 | tf_op jit(solution)/shard_map/all_to_all | solution.py:206
  25.6 24.0 %all-to-all-done = bf16[16,2,208,128]{3,2,1,0:T(8,128)(2,1)S(1)} async-done(((bf16[16,2,208,128]{3,2,1,0:T(8,128)(2,1)}), bf16[16,2,208,128]{3,2,1,0:T(8,128)(2,1)S(1)}, u32[]{:S(2)}, u32[]{:S(2)}) %all-to-all-start) | async-done | bytes 1703968 | tf_op jit(solution)/shard_map/all_to_all | solution.py:206
  50.2 0.3 reduce-window.9
  50.8 0.8 fusion.10
  51.6 1.0 fusion.30
  52.8 2.1 %collective-permute-start = (bf16[1,528,128]{2,1,0:T(8,128)(2,1)S(1)}, bf16[1,528,128]{2,1,0:T(8,128)(2,1)S(1)}, u32[]{:S(2)}, u32[]{:S(2)}) collective-permute-start(bf16[1,528,128]{2,1,0:T(8,128)(2,1)S(1)} %maximum_maximum_fusion), channel_id=1, source_target_pairs={{16,0},{32,16},{48,32},{64,48},{80,64},{96,80},{112,96},{17,1},{33... | collective-permute-start | bytes 405512 | tf_op jit(solution)/shard_map/ppermute | solution.py:17
  54.9 3.7 %fusion.2 = f32[2048,128]{1,0:T(8,128)S(1)} fusion(bf16[3072,128]{1,0:T(8,128)(2,1)S(1)} %bitcast.105, s32[3072]{0:T(1024)S(1)} %eq.93, s32[2048]{0:T(1024)S(1)} %iota_add_fusion), kind=kOutput, calls=%fused_computation.4 | convolution fusion | flops 1616904192 | bytes 1855488 | tf_op jit(solution)/shard_map/dot_general | solution.py:135
  58.7 1.1 fusion.20
  59.8 0.3 reshape.276
  60.1 0.5 convolution_convert_fusion
  60.6 0.5 convolution_convert_fusion.1
  61.1 0.7 fusion.44
  61.8 0.7 fusion.43
  62.6 0.3 multiply_convert_fusion.3
  62.9 1.0 multiply_convert_fusion.2
  63.9 1.3 %fusion.51 = f32[512,2048]{1,0:T(8,128)S(1)} fusion(bf16[512,512]{1,0:T(8,128)(2,1)S(1)} %copy-done.4, bf16[512,512]{1,0:T(8,128)(2,1)S(1)} %get-tuple-element.25, bf16[512,512]{1,0:T(8,128)(2,1)S(1)} %get-tuple-element.26, bf16[512,512]{1,0:T(8,128)(2,1)S(1)} %get-tuple-element.24, bf16[512,512]{1,0:T(8,128)(2,1)S(1)} %get-tuple-element.9), kind=kOutput, calls=%fused_computation.79 | convolution fusion | flops 1082130432 | bytes 6815744 | tf_op jit(solution)/shard_map/dot_general | solution.py:51
  65.1 1.3 %fusion.52 = f32[512,2048]{1,0:T(8,128)S(1)} fusion(bf16[512,512]{1,0:T(8,128)(2,1)S(1)} %copy-done.3, bf16[512,512]{1,0:T(8,128)(2,1)S(1)} %get-tuple-element.25, bf16[512,512]{1,0:T(8,128)(2,1)S(1)} %get-tuple-element.26, bf16[512,512]{1,0:T(8,128)(2,1)S(1)} %get-tuple-element.24, bf16[512,512]{1,0:T(8,128)(2,1)S(1)} %get-tuple-element.9), kind=kOutput, calls=%fused_computation.80 | convolution fusion | flops 1082130432 | bytes 6815744 | tf_op jit(solution)/shard_map/dot_general | solution.py:51
  66.4 1.2 %fusion.24 = (bf16[512,1024]{1,0:T(8,128)(2,1)S(1)}, bf16[512,1024]{1,0:T(8,128)(2,1)S(1)}) fusion(f32[512,2048]{1,0:T(8,128)S(1)} %fusion.51, f32[512,2048]{1,0:T(8,128)S(1)} %fusion.52), kind=kLoop, calls=%fused_computation.28 | loop fusion | flops 2097152 | bytes 10485760 | tf_op jit(solution)/shard_map/convert.12
  67.8 1.3 %fusion.49 = f32[2048,512]{1,0:T(8,128)S(1)} fusion(bf16[512,512]{1,0:T(8,128)(2,1)S(1)} %copy-done.4, bf16[512,512]{1,0:T(8,128)(2,1)S(1)} %get-tuple-element.46, bf16[512,512]{1,0:T(8,128)(2,1)S(1)} %get-tuple-element.45, bf16[512,512]{1,0:T(8,128)(2,1)S(1)} %get-tuple-element.44, bf16[512,512]{1,0:T(8,128)(2,1)S(1)} %get-tuple-element.43), kind=kOutput, calls=%fused_computation.77 | convolution fusion | flops 1082130432 | bytes 6815744 | tf_op jit(solution)/shard_map/dot_general | solution.py:51
  69.1 1.3 %fusion.50 = f32[2048,512]{1,0:T(8,128)S(1)} fusion(bf16[512,512]{1,0:T(8,128)(2,1)S(1)} %copy-done.3, bf16[512,512]{1,0:T(8,128)(2,1)S(1)} %get-tuple-element.46, bf16[512,512]{1,0:T(8,128)(2,1)S(1)} %get-tuple-element.45, bf16[512,512]{1,0:T(8,128)(2,1)S(1)} %get-tuple-element.44, bf16[512,512]{1,0:T(8,128)(2,1)S(1)} %get-tuple-element.43), kind=kOutput, calls=%fused_computation.78 | convolution fusion | flops 1082130432 | bytes 6815744 | tf_op jit(solution)/shard_map/dot_general | solution.py:51
  70.3 1.2 %fusion.45 = (bf16[1,512,512]{2,1,0:T(8,128)(2,1)S(1)}, bf16[1,512,512]{2,1,0:T(8,128)(2,1)S(1)}, bf16[1,512,512]{2,1,0:T(8,128)(2,1)S(1)}, bf16[1,512,512]{2,1,0:T(8,128)(2,1)S(1)}) fusion(f32[2048,512]{1,0:T(8,128)S(1)} %fusion.49, f32[2048,512]{1,0:T(8,128)S(1)} %fusion.50), kind=kLoop, calls=%fused_computation.73 | loop fusion | flops 2097152 | bytes 10485760 | tf_op jit(solution)/shard_map/stack | solution.py:98
  71.6 0.4 pad_maximum_fusion.4
  72.1 2.4 %collective-permute-start.1 = (bf16[4,128,512]{2,1,0:T(8,128)(2,1)S(1)}, bf16[4,128,512]{2,1,0:T(8,128)(2,1)S(1)}, u32[]{:S(2)}, u32[]{:S(2)}) collective-permute-start(bf16[4,128,512]{2,1,0:T(8,128)(2,1)S(1)} %get-tuple-element.33), channel_id=1, source_target_pairs={{0,16},{16,32},{32,48},{48,64},{64,80},{80,96},{96,112},{1,17},{17... | collective-permute-start | bytes 1572872 | tf_op jit(solution)/shard_map/ppermute | solution.py:17
  74.5 3.2 %collective-permute-start.2 = (bf16[4,128,512]{2,1,0:T(8,128)(2,1)S(1)}, bf16[4,128,512]{2,1,0:T(8,128)(2,1)S(1)}, u32[]{:S(2)}, u32[]{:S(2)}) collective-permute-start(bf16[4,128,512]{2,1,0:T(8,128)(2,1)S(1)} %get-tuple-element.34), channel_id=1, source_target_pairs={{16,0},{32,16},{48,32},{64,48},{80,64},{96,80},{112,96},{17,1},{33... | collective-permute-start | bytes 1572872 | tf_op jit(solution)/shard_map/ppermute | solution.py:17
  77.9 0.2 fusion.87
  78.1 2.0 %collective-permute-start.6 = (bf16[4,512,128]{2,1,0:T(8,128)(2,1)S(1)}, bf16[4,512,128]{2,1,0:T(8,128)(2,1)S(1)}, u32[]{:S(2)}, u32[]{:S(2)}) collective-permute-start(bf16[4,512,128]{2,1,0:T(8,128)(2,1)S(1)} %get-tuple-element.32), channel_id=1, source_target_pairs={{1,0},{2,1},{3,2},{4,3},{5,4},{6,5},{7,6},{8,7},{9,8},{10,9},{11,1... | collective-permute-start | bytes 1572872 | tf_op jit(solution)/shard_map/ppermute | solution.py:17
  80.1 3.8 %collective-permute-start.3 = (bf16[4,512,128]{2,1,0:T(8,128)(2,1)S(1)}, bf16[4,512,128]{2,1,0:T(8,128)(2,1)S(1)}, u32[]{:S(2)}, u32[]{:S(2)}) collective-permute-start(bf16[4,512,128]{2,1,0:T(8,128)(2,1)S(1)} %get-tuple-element.31), channel_id=1, source_target_pairs={{0,1},{1,2},{2,3},{3,4},{4,5},{5,6},{6,7},{7,8},{8,9},{9,10},{10,1... | collective-permute-start | bytes 1572872 | tf_op jit(solution)/shard_map/ppermute | solution.py:17
  84.1 3.3 %collective-permute-start.7 = (bf16[4,128,128]{2,1,0:T(8,128)(2,1)S(1)}, bf16[4,128,128]{2,1,0:T(8,128)(2,1)S(1)}, u32[]{:S(2)}, u32[]{:S(2)}) collective-permute-start(bf16[4,128,128]{2,1,0:T(8,128)(2,1)S(1)} %get-tuple-element.28), channel_id=1, source_target_pairs={{1,16},{2,17},{3,18},{4,19},{5,20},{6,21},{7,22},{8,23},{9,24},{10... | collective-permute-start | bytes 393224 | tf_op jit(solution)/shard_map/ppermute | solution.py:180
  87.4 2.6 %collective-permute-start.8 = (bf16[4,128,128]{2,1,0:T(8,128)(2,1)S(1)}, bf16[4,128,128]{2,1,0:T(8,128)(2,1)S(1)}, u32[]{:S(2)}, u32[]{:S(2)}) collective-permute-start(bf16[4,128,128]{2,1,0:T(8,128)(2,1)S(1)} %get-tuple-element.30), channel_id=1, source_target_pairs={{17,0},{18,1},{19,2},{20,3},{21,4},{22,5},{23,6},{24,7},{25,8},{26... | collective-permute-start | bytes 393224 | tf_op jit(solution)/shard_map/ppermute | solution.py:180
  90.1 2.8 %collective-permute-start.5 = (bf16[4,128,128]{2,1,0:T(8,128)(2,1)S(1)}, bf16[4,128,128]{2,1,0:T(8,128)(2,1)S(1)}, u32[]{:S(2)}, u32[]{:S(2)}) collective-permute-start(bf16[4,128,128]{2,1,0:T(8,128)(2,1)S(1)} %get-tuple-element.29), channel_id=1, source_target_pairs={{16,1},{17,2},{18,3},{19,4},{20,5},{21,6},{22,7},{23,8},{24,9},{25... | collective-permute-start | bytes 393224 | tf_op jit(solution)/shard_map/ppermute | solution.py:180
  92.9 0.3 fusion.36
  93.3 5.3 %collective-permute-done.3 = bf16[4,512,128]{2,1,0:T(8,128)(2,1)S(1)} collective-permute-done((bf16[4,512,128]{2,1,0:T(8,128)(2,1)S(1)}, bf16[4,512,128]{2,1,0:T(8,128)(2,1)S(1)}, u32[]{:S(2)}, u32[]{:S(2)}) %collective-permute-start.3) | collective-permute-done | bytes 524320 | tf_op jit(solution)/shard_map/ppermute | solution.py:17
  98.5 1.9 %collective-permute-start.4 = (bf16[4,128,128]{2,1,0:T(8,128)(2,1)S(1)}, bf16[4,128,128]{2,1,0:T(8,128)(2,1)S(1)}, u32[]{:S(2)}, u32[]{:S(2)}) collective-permute-start(bf16[4,128,128]{2,1,0:T(8,128)(2,1)S(1)} %get-tuple-element.27), channel_id=1, source_target_pairs={{0,17},{1,18},{2,19},{3,20},{4,21},{5,22},{6,23},{7,24},{8,25},{9,... | collective-permute-start | bytes 393224 | tf_op jit(solution)/shard_map/ppermute | solution.py:180
  100.4 0.4 pad_maximum_fusion
  100.9 2.0 %copy-done.2 = f32[4,512,512]{2,1,0:T(8,128)} copy-done((f32[4,512,512]{2,1,0:T(8,128)}, f32[4,512,512]{2,1,0:T(8,128)S(1)}, u32[]{:S(2)}) %copy-start.2) | copy-done | bytes 4194328
  103.2 4.6 %collective-permute-done.4 = bf16[4,128,128]{2,1,0:T(8,128)(2,1)S(1)} collective-permute-done((bf16[4,128,128]{2,1,0:T(8,128)(2,1)S(1)}, bf16[4,128,128]{2,1,0:T(8,128)(2,1)S(1)}, u32[]{:S(2)}, u32[]{:S(2)}) %collective-permute-start.4) | collective-permute-done | bytes 131104 | tf_op jit(solution)/shard_map/ppermute | solution.py:180
  107.8 0.2 fusion.54
  108.0 0.2 fusion.34
  108.3 1.3 %slice-done = f32[4,512,256]{2,1,0:T(8,128)S(1)} async-done(((f32[4,512,512]{2,1,0:T(8,128)}), f32[4,512,256]{2,1,0:T(8,128)S(1)}, s32[]{:S(2)}) %slice-start) | async-done | bytes 2097176 | tf_op jit(solution)/shard_map/slice | solution.py:250
  109.6 2.5 %pad_maximum_fusion.1 = f32[4,512,512]{2,1,0:T(8,128)} fusion(f32[4,512,128]{2,1,0:T(8,128)S(1)} %get-tuple-element.21, f32[4,512,256]{2,1,0:T(8,128)S(1)} %slice-done, f32[4,512,128]{2,1,0:T(8,128)S(1)} %get-tuple-element.20), kind=kLoop, calls=%fused_computation.15 | loop fusion | flops 2097152 | bytes 8388608 | tf_op jit(solution)/shard_map/concatenate | solution.py:249
  (69 shorter events, 2.7 us)
Async XLA Ops:
  0.0 4.4 %copy-start = (bf16[2352,128]{1,0:T(8,128)(2,1)S(1)}, bf16[2352,128]{1,0:T(8,128)(2,1)}, u32[]{:S(2)}) copy-start(bf16[2352,128]{1,0:T(8,128)(2,1)} %param.6) | copy-start | bytes 1806340
  17.4 32.1 %all-to-all-start = ((bf16[16,2,208,128]{3,2,1,0:T(8,128)(2,1)}), bf16[16,2,208,128]{3,2,1,0:T(8,128)(2,1)S(1)}, u32[]{:S(2)}, u32[]{:S(2)}) async-start(bf16[16,2,208,128]{3,2,1,0:T(8,128)(2,1)} %pad_maximum_fusion.5), calls=%async_computation | async-start | bytes 3407872 | tf_op jit(solution)/shard_map/all_to_all | solution.py:206
  52.8 5.8 %collective-permute-start = (bf16[1,528,128]{2,1,0:T(8,128)(2,1)S(1)}, bf16[1,528,128]{2,1,0:T(8,128)(2,1)S(1)}, u32[]{:S(2)}, u32[]{:S(2)}) collective-permute-start(bf16[1,528,128]{2,1,0:T(8,128)(2,1)S(1)} %maximum_maximum_fusion), channel_id=1, source_target_pairs={{16,0},{32,16},{48,32},{64,48},{80,64},{96,80},{112,96},{17,1},{33... | collective-permute-start | bytes 405512 | tf_op jit(solution)/shard_map/ppermute | solution.py:17
  58.6 1.5 %copy-start.4 = (bf16[512,512]{1,0:T(8,128)(2,1)S(1)}, bf16[512,512]{1,0:T(8,128)(2,1)}, u32[]{:S(2)}) copy-start(bf16[512,512]{1,0:T(8,128)(2,1)} %constant.117.clone) | copy-start | bytes 1572868
  58.7 1.9 %copy-start.3 = (bf16[512,512]{1,0:T(8,128)(2,1)S(1)}, bf16[512,512]{1,0:T(8,128)(2,1)}, u32[]{:S(2)}) copy-start(bf16[512,512]{1,0:T(8,128)(2,1)} %constant.116.clone) | copy-start | bytes 1572868
  72.1 15.3 %collective-permute-start.1 = (bf16[4,128,512]{2,1,0:T(8,128)(2,1)S(1)}, bf16[4,128,512]{2,1,0:T(8,128)(2,1)S(1)}, u32[]{:S(2)}, u32[]{:S(2)}) collective-permute-start(bf16[4,128,512]{2,1,0:T(8,128)(2,1)S(1)} %get-tuple-element.33), channel_id=1, source_target_pairs={{0,16},{16,32},{32,48},{48,64},{64,80},{80,96},{96,112},{1,17},{17... | collective-permute-start | bytes 1572872 | tf_op jit(solution)/shard_map/ppermute | solution.py:17
  74.5 15.5 %collective-permute-start.2 = (bf16[4,128,512]{2,1,0:T(8,128)(2,1)S(1)}, bf16[4,128,512]{2,1,0:T(8,128)(2,1)S(1)}, u32[]{:S(2)}, u32[]{:S(2)}) collective-permute-start(bf16[4,128,512]{2,1,0:T(8,128)(2,1)S(1)} %get-tuple-element.34), channel_id=1, source_target_pairs={{16,0},{32,16},{48,32},{64,48},{80,64},{96,80},{112,96},{17,1},{33... | collective-permute-start | bytes 1572872 | tf_op jit(solution)/shard_map/ppermute | solution.py:17
  78.1 24.9 %collective-permute-start.6 = (bf16[4,512,128]{2,1,0:T(8,128)(2,1)S(1)}, bf16[4,512,128]{2,1,0:T(8,128)(2,1)S(1)}, u32[]{:S(2)}, u32[]{:S(2)}) collective-permute-start(bf16[4,512,128]{2,1,0:T(8,128)(2,1)S(1)} %get-tuple-element.32), channel_id=1, source_target_pairs={{1,0},{2,1},{3,2},{4,3},{5,4},{6,5},{7,6},{8,7},{9,8},{10,9},{11,1... | collective-permute-start | bytes 1572872 | tf_op jit(solution)/shard_map/ppermute | solution.py:17
  80.1 18.4 %collective-permute-start.3 = (bf16[4,512,128]{2,1,0:T(8,128)(2,1)S(1)}, bf16[4,512,128]{2,1,0:T(8,128)(2,1)S(1)}, u32[]{:S(2)}, u32[]{:S(2)}) collective-permute-start(bf16[4,512,128]{2,1,0:T(8,128)(2,1)S(1)} %get-tuple-element.31), channel_id=1, source_target_pairs={{0,1},{1,2},{2,3},{3,4},{4,5},{5,6},{6,7},{7,8},{8,9},{9,10},{10,1... | collective-permute-start | bytes 1572872 | tf_op jit(solution)/shard_map/ppermute | solution.py:17
  84.1 19.0 %collective-permute-start.7 = (bf16[4,128,128]{2,1,0:T(8,128)(2,1)S(1)}, bf16[4,128,128]{2,1,0:T(8,128)(2,1)S(1)}, u32[]{:S(2)}, u32[]{:S(2)}) collective-permute-start(bf16[4,128,128]{2,1,0:T(8,128)(2,1)S(1)} %get-tuple-element.28), channel_id=1, source_target_pairs={{1,16},{2,17},{3,18},{4,19},{5,20},{6,21},{7,22},{8,23},{9,24},{10... | collective-permute-start | bytes 393224 | tf_op jit(solution)/shard_map/ppermute | solution.py:180
  87.4 15.7 %collective-permute-start.8 = (bf16[4,128,128]{2,1,0:T(8,128)(2,1)S(1)}, bf16[4,128,128]{2,1,0:T(8,128)(2,1)S(1)}, u32[]{:S(2)}, u32[]{:S(2)}) collective-permute-start(bf16[4,128,128]{2,1,0:T(8,128)(2,1)S(1)} %get-tuple-element.30), channel_id=1, source_target_pairs={{17,0},{18,1},{19,2},{20,3},{21,4},{22,5},{23,6},{24,7},{25,8},{26... | collective-permute-start | bytes 393224 | tf_op jit(solution)/shard_map/ppermute | solution.py:180
  90.1 13.1 %collective-permute-start.5 = (bf16[4,128,128]{2,1,0:T(8,128)(2,1)S(1)}, bf16[4,128,128]{2,1,0:T(8,128)(2,1)S(1)}, u32[]{:S(2)}, u32[]{:S(2)}) collective-permute-start(bf16[4,128,128]{2,1,0:T(8,128)(2,1)S(1)} %get-tuple-element.29), channel_id=1, source_target_pairs={{16,1},{17,2},{18,3},{19,4},{20,5},{21,6},{22,7},{23,8},{24,9},{25... | collective-permute-start | bytes 393224 | tf_op jit(solution)/shard_map/ppermute | solution.py:180
  98.5 9.3 %collective-permute-start.4 = (bf16[4,128,128]{2,1,0:T(8,128)(2,1)S(1)}, bf16[4,128,128]{2,1,0:T(8,128)(2,1)S(1)}, u32[]{:S(2)}, u32[]{:S(2)}) collective-permute-start(bf16[4,128,128]{2,1,0:T(8,128)(2,1)S(1)} %get-tuple-element.27), channel_id=1, source_target_pairs={{0,17},{1,18},{2,19},{3,20},{4,21},{5,22},{6,23},{7,24},{8,25},{9,... | collective-permute-start | bytes 393224 | tf_op jit(solution)/shard_map/ppermute | solution.py:180
  100.9 2.0 %copy-start.2 = (f32[4,512,512]{2,1,0:T(8,128)}, f32[4,512,512]{2,1,0:T(8,128)S(1)}, u32[]{:S(2)}) copy-start(f32[4,512,512]{2,1,0:T(8,128)S(1)} %pad_maximum_fusion) | copy-start | bytes 12582916
  108.0 1.6 %slice-start = ((f32[4,512,512]{2,1,0:T(8,128)}), f32[4,512,256]{2,1,0:T(8,128)S(1)}, s32[]{:S(2)}) async-start(f32[4,512,512]{2,1,0:T(8,128)} %copy-done.2), calls=%async_computation.1 | async-start | bytes 4194304 | tf_op jit(solution)/shard_map/slice | solution.py:250
  109.6 2.5 %copy-start.1 = (bf16[2352,128]{1,0:T(8,128)(2,1)S(1)}, bf16[2352,128]{1,0:T(8,128)(2,1)}, u32[]{:S(2)}) copy-start(bf16[2352,128]{1,0:T(8,128)(2,1)} %param.6) | copy-start | bytes 1806340

commit v4 on v3

--- a/solution.py
+++ b/solution.py
@@ -1,8 +1,6 @@
 import math
 
 import jax
-import ml_dtypes
-import numpy as np
 import jax.numpy as jnp
 from jax import lax
 from jax.sharding import PartitionSpec as P
@@ -31,14 +29,10 @@
 
 
 def dft_tables(length):
-    positions = np.arange(length, dtype=np.int64)
+    positions = jnp.arange(length, dtype=jnp.int32)
     phases = positions[:, None] * positions[None, :] % length
-    angles = phases.astype(np.float32) * np.float32(2.0 * math.pi / length)
-    return (np.cos(angles).astype(np.float32), np.sin(angles).astype(np.float32))
-
-
-def table(values):
-    return jnp.asarray(values.astype(ml_dtypes.bfloat16))
+    angles = phases.astype(jnp.float32) * (2.0 * math.pi / length)
+    return (jnp.cos(angles), jnp.sin(angles))
 
 
 def wavenumbers(length):
@@ -55,16 +49,14 @@
     row_count = pixels.shape[0]
     col_count = pixels.shape[1]
     assert row_count == col_count
-    cos_np, sin_np = dft_tables(row_count)
-    cosine, sine = table(cos_np), table(sin_np)
     n = row_count
-    halves = jnp.concatenate([dot32(pixels, cosine), dot32(pixels, sine)], axis=1).astype(
-        jnp.bfloat16
-    )
-    by_cos = dot32(cosine, halves)
-    by_sin = dot32(sine, halves)
-    real_part = by_cos[:, :n] - by_sin[:, n:]
-    imag_part = -(by_sin[:, :n] + by_cos[:, n:])
+    cosine, sine = dft_tables(n)
+    side_by_side = jnp.concatenate([cosine, sine], axis=1).astype(jnp.bfloat16)
+    stacked = jnp.concatenate([cosine, sine], axis=0).astype(jnp.bfloat16)
+    halves = dot32(pixels, side_by_side).astype(jnp.bfloat16)
+    products = dot32(stacked, halves)
+    real_part = products[:n, :n] - products[n:, n:]
+    imag_part = -(products[n:, :n] + products[:n, n:])
     across = wavenumbers(col_count)[None, :]
     down = wavenumbers(row_count)[:, None]
     scale = 1.0 / (row_count * col_count)
@@ -81,20 +73,19 @@
     spectra = jnp.concatenate([one_real, three_real, one_imag, three_imag], axis=1).astype(
         jnp.bfloat16
     )
-    by_cos = dot32(cosine, spectra)
-    by_sin = dot32(sine, spectra)
+    products = dot32(stacked, spectra)
     columns_done = jnp.concatenate(
         [
-            by_cos[:, : 2 * n] - by_sin[:, 2 * n :],
-            by_sin[:, : 2 * n] + by_cos[:, 2 * n :],
+            products[:n, : 2 * n] - products[n:, 2 * n :],
+            products[n:, : 2 * n] + products[:n, 2 * n :],
         ],
         axis=1,
     ).astype(jnp.bfloat16)
     arranged = jnp.concatenate(
         [columns_done[:, k * n : (k + 1) * n] for k in range(4)], axis=0
     )
-    by_cos = dot32(arranged, cosine)
-    by_sin = dot32(arranged, sine)
+    products = dot32(arranged, side_by_side)
+    by_cos, by_sin = products[:, :n], products[:, n:]
     return jnp.stack(
         [
             by_cos[:n] - by_sin[2 * n : 3 * n],

time: 113 us -> 115 us (1.018)
  other arithmetic: 12.9 us -> 18.7 us
  waiting for transfers between devices: 33.9 us -> 29.5 us
    another operation x6 -> x7, other arithmetic: 2.92 us -> 9.13 us
    all_to_all x1, waiting for transfers between devices: 24 us -> 19.6 us  [on_device(): lax.all_to_all(jnp.stack([same_sent, rise_sent], axis=1), 'py', 0, 0, til...]
    dot_general x8 -> x3, matrix products: 7.53 us -> 8.54 us  [dot32(): return jnp.dot(a, b, preferred_element_type=jnp.float32)]
    unnamed x15 -> x11, local copies, waits for them, and re-layouts: 4.58 us -> 4.57 us
  transfers between devices with their start and end apart: 10 -> 10, of which waited for: 3 -> 3; matrix products, arithmetic and copies ran while one was open for 5% -> 9% of each run, Pallas kernels for 0% -> 0%
where the time goes in v4:
time: 115 us
  starting transfers between devices  32.1 us (28%)
  waiting for transfers between devices  29.5 us (26%)
  matrix products  25.5 us (22%)
  other arithmetic  18.7 us (16%)
  local copies, waits for them, and re-layouts  8.23 us (7%)
    all_to_all x1, waiting for transfers between devices, on_device(): lax.all_to_all(jnp.stack([same_sent, rise_sent], axis=1), 'py', 0, 0, til...  19.6 us
    ppermute x5, starting transfers between devices, shifted(): return lax.ppermute(shard, axis, pairs)  13.5 us
    dot_general x2, matrix products, gathered_rows(): jnp.dot(chosen.astype(table_rows.dtype), table_rows, preferred_element_ty...  11.2 us
    ppermute x4, starting transfers between devices, diagonal(): return lax.ppermute(block, ('px', 'py'), pairs)  10.7 us
    another operation x7, other arithmetic  9.13 us
    dot_general x3, matrix products, dot32(): return jnp.dot(a, b, preferred_element_type=jnp.float32)  8.54 us
    all_to_all x1, starting transfers between devices, on_device(): lax.all_to_all(jnp.stack([same_sent, rise_sent], axis=1), 'py', 0, 0, til...  7.9 us
    dot_general x3, matrix products, one_hot_rows(): jnp.dot(picks.astype(values.dtype), values, preferred_element_type=jnp.fl...  5.83 us
  transfers between devices with their start and end apart: 10, of which 3 were waited for; matrix products, arithmetic and copies ran while one was open for 9% of the time, Pallas kernels for 0%

profile of v4, /device:TPU:40, one launch (start us, length us, event | category | flops | bytes accessed | tf_op | source)
XLA Modules:
  0.0 114.5 jit_solution(8883659343457115747)
XLA Ops:
  0.0 1.0 copy.19
  1.1 0.5 broadcast.538
  1.6 1.3 %reduce.5 = s32[128]{0:T(128)S(1)} reduce(s32[1,128]{1,0:T(1,128)} %param.7, s32[]{:T(128)} %broadcast.538), dimensions={0}, to_apply=%param.7.reduce_sub_computation.3 | reduce | bytes 1028 | tf_op args[3]
  3.2 1.0 copy.18
  4.4 5.6 %fusion.14 = bf16[3072,128]{1,0:T(8,128)(2,1)S(1)} fusion(bf16[2352,128]{1,0:T(8,128)(2,1)S(1)} %copy-done, s32[3072]{0:T(1024)S(1)} %eq.44), kind=kOutput, calls=%fused_computation.19 | convolution fusion | flops 1857306624 | bytes 1400832 | tf_op jit(solution)/shard_map/dot_general | solution.py:131
  10.0 5.6 %fusion.13 = bf16[3072,128]{1,0:T(8,128)(2,1)S(1)} fusion(bf16[2352,128]{1,0:T(8,128)(2,1)S(1)} %copy-done, s32[3072]{0:T(1024)S(1)} %eq.91), kind=kOutput, calls=%fused_computation.18 | convolution fusion | flops 1857306624 | bytes 1400832 | tf_op jit(solution)/shard_map/dot_general | solution.py:131
  15.7 0.4 maximum_bitcast_fusion
  16.1 1.3 %pad_maximum_fusion.3 = bf16[16,2,208,128]{3,2,1,0:T(8,128)(2,1)} fusion(bf16[16,1,208,128]{3,2,1,0:T(8,128)(2,1)S(1)} %get-tuple-element.64, bf16[16,1,208,128]{3,2,1,0:T(8,128)(2,1)S(1)} %get-tuple-element.63), kind=kLoop, calls=%fused_computation.48 | loop fusion | flops 851968 | bytes 3407872 | tf_op jit(solution)/shard_map/stack | solution.py:197
  17.4 7.9 %all-to-all-start = ((bf16[16,2,208,128]{3,2,1,0:T(8,128)(2,1)}), bf16[16,2,208,128]{3,2,1,0:T(8,128)(2,1)S(1)}, u32[]{:S(2)}, u32[]{:S(2)}) async-start(bf16[16,2,208,128]{3,2,1,0:T(8,128)(2,1)} %pad_maximum_fusion.3), calls=%async_computation | async-start | bytes 3407872 | tf_op jit(solution)/shard_map/all_to_all | solution.py:197
  25.5 4.3 %sine_convert_fusion = (bf16[512,512]{1,0:T(8,128)(2,1)S(1)}, bf16[512,512]{1,0:T(8,128)(2,1)S(1)}) fusion(), kind=kLoop, calls=%fused_computation.88 | loop fusion | flops 4194304 | bytes 1048576 | tf_op jit(solution)/shard_map/convert.29
  29.9 19.6 %all-to-all-done = bf16[16,2,208,128]{3,2,1,0:T(8,128)(2,1)S(1)} async-done(((bf16[16,2,208,128]{3,2,1,0:T(8,128)(2,1)}), bf16[16,2,208,128]{3,2,1,0:T(8,128)(2,1)S(1)}, u32[]{:S(2)}, u32[]{:S(2)}) %all-to-all-start) | async-done | bytes 1703968 | tf_op jit(solution)/shard_map/all_to_all | solution.py:197
  50.2 0.3 reduce-window.9
  50.6 0.1 slice_reduce_fusion
  50.8 0.8 fusion.10
  51.6 1.0 fusion.47
  52.7 0.1 maximum_maximum_fusion
  52.8 2.1 %collective-permute-start = (bf16[1,528,128]{2,1,0:T(8,128)(2,1)S(1)}, bf16[1,528,128]{2,1,0:T(8,128)(2,1)S(1)}, u32[]{:S(2)}, u32[]{:S(2)}) collective-permute-start(bf16[1,528,128]{2,1,0:T(8,128)(2,1)S(1)} %maximum_maximum_fusion), channel_id=1, source_target_pairs={{16,0},{32,16},{48,32},{64,48},{80,64},{96,80},{112,96},{17,1},{33... | collective-permute-start | bytes 405512 | tf_op jit(solution)/shard_map/ppermute | solution.py:15
  54.9 3.7 %fusion.2 = f32[2048,128]{1,0:T(8,128)S(1)} fusion(bf16[3072,128]{1,0:T(8,128)(2,1)S(1)} %bitcast.96, s32[3072]{0:T(1024)S(1)} %eq.95, s32[2048]{0:T(1024)S(1)} %iota_add_fusion), kind=kOutput, calls=%fused_computation.4 | convolution fusion | flops 1616904192 | bytes 1855488 | tf_op jit(solution)/shard_map/dot_general | solution.py:126
  58.7 1.1 fusion.20
  59.8 0.3 reshape.276
  60.1 3.8 %fusion.43 = f32[1024,1024]{0,1:T(8,128)} fusion(bf16[512,512]{1,0:T(8,128)(2,1)S(1)} %reshape.276, bf16[512,512]{1,0:T(8,128)(2,1)S(1)} %get-tuple-element.75, bf16[512,512]{1,0:T(8,128)(2,1)S(1)} %get-tuple-element.76), kind=kOutput, calls=%fused_computation.53 | convolution fusion | flops 1615331328 | bytes 5767168 | tf_op jit(solution)/shard_map/dot_general | solution.py:45
  63.9 2.5 %multiply_convert_fusion.3 = (bf16[512,512]{0,1:T(8,128)(2,1)S(1)}, f32[512,512]{0,1:T(8,128)S(1)}, f32[512,512]{0,1:T(8,128)S(1)}) fusion(f32[512]{0:T(512)S(1)} %get-tuple-element.66, f32[512]{0:T(512)S(1)} %get-tuple-element.70, f32[1024,1024]{0,1:T(8,128)} %fusion.43), kind=kLoop, calls=%fused_computation.87 | loop fusion | flops 2097152 | bytes 6819840 | tf_op jit(solution)/shard_map/convert.14
  66.4 1.1 multiply_convert_fusion.2
  67.5 2.4 %fusion.25 = f32[1024,2048]{1,0:T(8,128)S(1)} fusion(bf16[512,512]{0,1:T(8,128)(2,1)S(1)} %get-tuple-element.25, bf16[512,512]{0,1:T(8,128)(2,1)S(1)} %get-tuple-element.26, bf16[512,512]{0,1:T(8,128)(2,1)S(1)} %get-tuple-element.24, bf16[512,512]{0,1:T(8,128)(2,1)S(1)} %get-tuple-element.9, bf16[512,512]{1,0:T(8,128)(2,1)S(1)} %get-tuple-element.75, ...), kind=kOutput, calls=%fused_computation.29 | convolution fusion | flops 2157969408 | bytes 11534336 | tf_op jit(solution)/shard_map/dot_general | solution.py:45
  69.9 0.8 fusion.24
  70.8 2.3 %fusion.33 = f32[2048,1024]{1,0:T(8,128)S(1)} fusion(bf16[512,512]{1,0:T(8,128)(2,1)S(1)} %get-tuple-element.46, bf16[512,512]{1,0:T(8,128)(2,1)S(1)} %get-tuple-element.45, bf16[512,512]{1,0:T(8,128)(2,1)S(1)} %get-tuple-element.44, bf16[512,512]{1,0:T(8,128)(2,1)S(1)} %get-tuple-element.43, bf16[512,512]{1,0:T(8,128)(2,1)S(1)} %get-tuple-element.75, ...), kind=kOutput, calls=%fused_computation.37 | convolution fusion | flops 2157969408 | bytes 11534336 | tf_op jit(solution)/shard_map/dot_general | solution.py:45
  73.2 0.8 fusion.66
  74.0 0.4 pad_maximum_fusion.2
  74.5 2.4 %collective-permute-start.1 = (bf16[4,128,512]{2,1,0:T(8,128)(2,1)S(1)}, bf16[4,128,512]{2,1,0:T(8,128)(2,1)S(1)}, u32[]{:S(2)}, u32[]{:S(2)}) collective-permute-start(bf16[4,128,512]{2,1,0:T(8,128)(2,1)S(1)} %get-tuple-element.33), channel_id=1, source_target_pairs={{0,16},{16,32},{32,48},{48,64},{64,80},{80,96},{96,112},{1,17},{17... | collective-permute-start | bytes 1572872 | tf_op jit(solution)/shard_map/ppermute | solution.py:15
  76.9 3.2 %collective-permute-start.2 = (bf16[4,128,512]{2,1,0:T(8,128)(2,1)S(1)}, bf16[4,128,512]{2,1,0:T(8,128)(2,1)S(1)}, u32[]{:S(2)}, u32[]{:S(2)}) collective-permute-start(bf16[4,128,512]{2,1,0:T(8,128)(2,1)S(1)} %get-tuple-element.34), channel_id=1, source_target_pairs={{16,0},{32,16},{48,32},{64,48},{80,64},{96,80},{112,96},{17,1},{33... | collective-permute-start | bytes 1572872 | tf_op jit(solution)/shard_map/ppermute | solution.py:15
  80.1 0.2 slice.277
  80.3 0.2 fusion.102
  80.5 2.0 %collective-permute-start.6 = (bf16[4,512,128]{2,1,0:T(8,128)(2,1)S(1)}, bf16[4,512,128]{2,1,0:T(8,128)(2,1)S(1)}, u32[]{:S(2)}, u32[]{:S(2)}) collective-permute-start(bf16[4,512,128]{2,1,0:T(8,128)(2,1)S(1)} %get-tuple-element.32), channel_id=1, source_target_pairs={{1,0},{2,1},{3,2},{4,3},{5,4},{6,5},{7,6},{8,7},{9,8},{10,9},{11,1... | collective-permute-start | bytes 1572872 | tf_op jit(solution)/shard_map/ppermute | solution.py:15
  82.5 3.8 %collective-permute-start.3 = (bf16[4,512,128]{2,1,0:T(8,128)(2,1)S(1)}, bf16[4,512,128]{2,1,0:T(8,128)(2,1)S(1)}, u32[]{:S(2)}, u32[]{:S(2)}) collective-permute-start(bf16[4,512,128]{2,1,0:T(8,128)(2,1)S(1)} %get-tuple-element.31), channel_id=1, source_target_pairs={{0,1},{1,2},{2,3},{3,4},{4,5},{5,6},{6,7},{7,8},{8,9},{9,10},{10,1... | collective-permute-start | bytes 1572872 | tf_op jit(solution)/shard_map/ppermute | solution.py:15
  86.4 0.1 fusion.101
  86.5 3.3 %collective-permute-start.7 = (bf16[4,128,128]{2,1,0:T(8,128)(2,1)S(1)}, bf16[4,128,128]{2,1,0:T(8,128)(2,1)S(1)}, u32[]{:S(2)}, u32[]{:S(2)}) collective-permute-start(bf16[4,128,128]{2,1,0:T(8,128)(2,1)S(1)} %get-tuple-element.28), channel_id=1, source_target_pairs={{1,16},{2,17},{3,18},{4,19},{5,20},{6,21},{7,22},{8,23},{9,24},{10... | collective-permute-start | bytes 393224 | tf_op jit(solution)/shard_map/ppermute | solution.py:171
  89.8 2.6 %collective-permute-start.8 = (bf16[4,128,128]{2,1,0:T(8,128)(2,1)S(1)}, bf16[4,128,128]{2,1,0:T(8,128)(2,1)S(1)}, u32[]{:S(2)}, u32[]{:S(2)}) collective-permute-start(bf16[4,128,128]{2,1,0:T(8,128)(2,1)S(1)} %get-tuple-element.30), channel_id=1, source_target_pairs={{17,0},{18,1},{19,2},{20,3},{21,4},{22,5},{23,6},{24,7},{25,8},{26... | collective-permute-start | bytes 393224 | tf_op jit(solution)/shard_map/ppermute | solution.py:171
  92.5 2.8 %collective-permute-start.5 = (bf16[4,128,128]{2,1,0:T(8,128)(2,1)S(1)}, bf16[4,128,128]{2,1,0:T(8,128)(2,1)S(1)}, u32[]{:S(2)}, u32[]{:S(2)}) collective-permute-start(bf16[4,128,128]{2,1,0:T(8,128)(2,1)S(1)} %get-tuple-element.29), channel_id=1, source_target_pairs={{16,1},{17,2},{18,3},{19,4},{20,5},{21,6},{22,7},{23,8},{24,9},{25... | collective-permute-start | bytes 393224 | tf_op jit(solution)/shard_map/ppermute | solution.py:171
  95.3 0.3 fusion.56
  95.7 5.2 %collective-permute-done.3 = bf16[4,512,128]{2,1,0:T(8,128)(2,1)S(1)} collective-permute-done((bf16[4,512,128]{2,1,0:T(8,128)(2,1)S(1)}, bf16[4,512,128]{2,1,0:T(8,128)(2,1)S(1)}, u32[]{:S(2)}, u32[]{:S(2)}) %collective-permute-start.3) | collective-permute-done | bytes 524320 | tf_op jit(solution)/shard_map/ppermute | solution.py:15
  100.9 1.9 %collective-permute-start.4 = (bf16[4,128,128]{2,1,0:T(8,128)(2,1)S(1)}, bf16[4,128,128]{2,1,0:T(8,128)(2,1)S(1)}, u32[]{:S(2)}, u32[]{:S(2)}) collective-permute-start(bf16[4,128,128]{2,1,0:T(8,128)(2,1)S(1)} %get-tuple-element.27), channel_id=1, source_target_pairs={{0,17},{1,18},{2,19},{3,20},{4,21},{5,22},{6,23},{7,24},{8,25},{9,... | collective-permute-start | bytes 393224 | tf_op jit(solution)/shard_map/ppermute | solution.py:171
  102.8 0.4 pad_maximum_fusion
  103.3 2.0 %copy-done.2 = f32[4,512,512]{2,1,0:T(8,128)} copy-done((f32[4,512,512]{2,1,0:T(8,128)}, f32[4,512,512]{2,1,0:T(8,128)S(1)}, u32[]{:S(2)}) %copy-start.2) | copy-done | bytes 4194328
  105.6 4.6 %collective-permute-done.4 = bf16[4,128,128]{2,1,0:T(8,128)(2,1)S(1)} collective-permute-done((bf16[4,128,128]{2,1,0:T(8,128)(2,1)S(1)}, bf16[4,128,128]{2,1,0:T(8,128)(2,1)S(1)}, u32[]{:S(2)}, u32[]{:S(2)}) %collective-permute-start.4) | collective-permute-done | bytes 131104 | tf_op jit(solution)/shard_map/ppermute | solution.py:171
  110.2 0.2 fusion.71
  110.4 0.2 fusion.54
  110.7 1.3 %slice-done = f32[4,512,256]{2,1,0:T(8,128)S(1)} async-done(((f32[4,512,512]{2,1,0:T(8,128)}), f32[4,512,256]{2,1,0:T(8,128)S(1)}, s32[]{:S(2)}) %slice-start) | async-done | bytes 2097176 | tf_op jit(solution)/shard_map/slice | solution.py:241
  112.0 2.5 %pad_maximum_fusion.1 = f32[4,512,512]{2,1,0:T(8,128)} fusion(f32[4,512,128]{2,1,0:T(8,128)S(1)} %get-tuple-element.21, f32[4,512,256]{2,1,0:T(8,128)S(1)} %slice-done, f32[4,512,128]{2,1,0:T(8,128)S(1)} %get-tuple-element.20), kind=kLoop, calls=%fused_computation.15 | loop fusion | flops 2097152 | bytes 8388608 | tf_op jit(solution)/shard_map/concatenate | solution.py:240
  (61 shorter events, 2.2 us)
Async XLA Ops:
  0.0 4.4 %copy-start = (bf16[2352,128]{1,0:T(8,128)(2,1)S(1)}, bf16[2352,128]{1,0:T(8,128)(2,1)}, u32[]{:S(2)}) copy-start(bf16[2352,128]{1,0:T(8,128)(2,1)} %param.4) | copy-start | bytes 1806340
  17.4 32.1 %all-to-all-start = ((bf16[16,2,208,128]{3,2,1,0:T(8,128)(2,1)}), bf16[16,2,208,128]{3,2,1,0:T(8,128)(2,1)S(1)}, u32[]{:S(2)}, u32[]{:S(2)}) async-start(bf16[16,2,208,128]{3,2,1,0:T(8,128)(2,1)} %pad_maximum_fusion.3), calls=%async_computation | async-start | bytes 3407872 | tf_op jit(solution)/shard_map/all_to_all | solution.py:197
  52.8 5.8 %collective-permute-start = (bf16[1,528,128]{2,1,0:T(8,128)(2,1)S(1)}, bf16[1,528,128]{2,1,0:T(8,128)(2,1)S(1)}, u32[]{:S(2)}, u32[]{:S(2)}) collective-permute-start(bf16[1,528,128]{2,1,0:T(8,128)(2,1)S(1)} %maximum_maximum_fusion), channel_id=1, source_target_pairs={{16,0},{32,16},{48,32},{64,48},{80,64},{96,80},{112,96},{17,1},{33... | collective-permute-start | bytes 405512 | tf_op jit(solution)/shard_map/ppermute | solution.py:15
  74.5 15.3 %collective-permute-start.1 = (bf16[4,128,512]{2,1,0:T(8,128)(2,1)S(1)}, bf16[4,128,512]{2,1,0:T(8,128)(2,1)S(1)}, u32[]{:S(2)}, u32[]{:S(2)}) collective-permute-start(bf16[4,128,512]{2,1,0:T(8,128)(2,1)S(1)} %get-tuple-element.33), channel_id=1, source_target_pairs={{0,16},{16,32},{32,48},{48,64},{64,80},{80,96},{96,112},{1,17},{17... | collective-permute-start | bytes 1572872 | tf_op jit(solution)/shard_map/ppermute | solution.py:15
  76.9 15.5 %collective-permute-start.2 = (bf16[4,128,512]{2,1,0:T(8,128)(2,1)S(1)}, bf16[4,128,512]{2,1,0:T(8,128)(2,1)S(1)}, u32[]{:S(2)}, u32[]{:S(2)}) collective-permute-start(bf16[4,128,512]{2,1,0:T(8,128)(2,1)S(1)} %get-tuple-element.34), channel_id=1, source_target_pairs={{16,0},{32,16},{48,32},{64,48},{80,64},{96,80},{112,96},{17,1},{33... | collective-permute-start | bytes 1572872 | tf_op jit(solution)/shard_map/ppermute | solution.py:15
  80.5 24.9 %collective-permute-start.6 = (bf16[4,512,128]{2,1,0:T(8,128)(2,1)S(1)}, bf16[4,512,128]{2,1,0:T(8,128)(2,1)S(1)}, u32[]{:S(2)}, u32[]{:S(2)}) collective-permute-start(bf16[4,512,128]{2,1,0:T(8,128)(2,1)S(1)} %get-tuple-element.32), channel_id=1, source_target_pairs={{1,0},{2,1},{3,2},{4,3},{5,4},{6,5},{7,6},{8,7},{9,8},{10,9},{11,1... | collective-permute-start | bytes 1572872 | tf_op jit(solution)/shard_map/ppermute | solution.py:15
  82.5 18.4 %collective-permute-start.3 = (bf16[4,512,128]{2,1,0:T(8,128)(2,1)S(1)}, bf16[4,512,128]{2,1,0:T(8,128)(2,1)S(1)}, u32[]{:S(2)}, u32[]{:S(2)}) collective-permute-start(bf16[4,512,128]{2,1,0:T(8,128)(2,1)S(1)} %get-tuple-element.31), channel_id=1, source_target_pairs={{0,1},{1,2},{2,3},{3,4},{4,5},{5,6},{6,7},{7,8},{8,9},{9,10},{10,1... | collective-permute-start | bytes 1572872 | tf_op jit(solution)/shard_map/ppermute | solution.py:15
  86.5 19.0 %collective-permute-start.7 = (bf16[4,128,128]{2,1,0:T(8,128)(2,1)S(1)}, bf16[4,128,128]{2,1,0:T(8,128)(2,1)S(1)}, u32[]{:S(2)}, u32[]{:S(2)}) collective-permute-start(bf16[4,128,128]{2,1,0:T(8,128)(2,1)S(1)} %get-tuple-element.28), channel_id=1, source_target_pairs={{1,16},{2,17},{3,18},{4,19},{5,20},{6,21},{7,22},{8,23},{9,24},{10... | collective-permute-start | bytes 393224 | tf_op jit(solution)/shard_map/ppermute | solution.py:171
  89.8 15.7 %collective-permute-start.8 = (bf16[4,128,128]{2,1,0:T(8,128)(2,1)S(1)}, bf16[4,128,128]{2,1,0:T(8,128)(2,1)S(1)}, u32[]{:S(2)}, u32[]{:S(2)}) collective-permute-start(bf16[4,128,128]{2,1,0:T(8,128)(2,1)S(1)} %get-tuple-element.30), channel_id=1, source_target_pairs={{17,0},{18,1},{19,2},{20,3},{21,4},{22,5},{23,6},{24,7},{25,8},{26... | collective-permute-start | bytes 393224 | tf_op jit(solution)/shard_map/ppermute | solution.py:171
  92.5 13.1 %collective-permute-start.5 = (bf16[4,128,128]{2,1,0:T(8,128)(2,1)S(1)}, bf16[4,128,128]{2,1,0:T(8,128)(2,1)S(1)}, u32[]{:S(2)}, u32[]{:S(2)}) collective-permute-start(bf16[4,128,128]{2,1,0:T(8,128)(2,1)S(1)} %get-tuple-element.29), channel_id=1, source_target_pairs={{16,1},{17,2},{18,3},{19,4},{20,5},{21,6},{22,7},{23,8},{24,9},{25... | collective-permute-start | bytes 393224 | tf_op jit(solution)/shard_map/ppermute | solution.py:171
  100.9 9.3 %collective-permute-start.4 = (bf16[4,128,128]{2,1,0:T(8,128)(2,1)S(1)}, bf16[4,128,128]{2,1,0:T(8,128)(2,1)S(1)}, u32[]{:S(2)}, u32[]{:S(2)}) collective-permute-start(bf16[4,128,128]{2,1,0:T(8,128)(2,1)S(1)} %get-tuple-element.27), channel_id=1, source_target_pairs={{0,17},{1,18},{2,19},{3,20},{4,21},{5,22},{6,23},{7,24},{8,25},{9,... | collective-permute-start | bytes 393224 | tf_op jit(solution)/shard_map/ppermute | solution.py:171
  103.3 2.0 %copy-start.2 = (f32[4,512,512]{2,1,0:T(8,128)}, f32[4,512,512]{2,1,0:T(8,128)S(1)}, u32[]{:S(2)}) copy-start(f32[4,512,512]{2,1,0:T(8,128)S(1)} %pad_maximum_fusion) | copy-start | bytes 12582916
  110.4 1.6 %slice-start = ((f32[4,512,512]{2,1,0:T(8,128)}), f32[4,512,256]{2,1,0:T(8,128)S(1)}, s32[]{:S(2)}) async-start(f32[4,512,512]{2,1,0:T(8,128)} %copy-done.2), calls=%async_computation.1 | async-start | bytes 4194304 | tf_op jit(solution)/shard_map/slice | solution.py:241
  112.0 2.5 %copy-start.1 = (bf16[2352,128]{1,0:T(8,128)(2,1)S(1)}, bf16[2352,128]{1,0:T(8,128)(2,1)}, u32[]{:S(2)}) copy-start(bf16[2352,128]{1,0:T(8,128)(2,1)} %param.4) | copy-start | bytes 1806340

commit v5 on v3

--- a/solution.py
+++ b/solution.py
@@ -167,17 +167,6 @@
     live = jnp.arange(depth, dtype=jnp.int32)[None, :] < counts[:, None]
     codes = jnp.where(live, slots + 1, 0)
     return with_codes(gathered_rows(kappa, lists), codes)
-
-
-def diagonal(block, row_by, col_by):
-    rows, cols = lax.axis_size("px"), lax.axis_size("py")
-    pairs = [
-        (i * cols + j, (i + row_by) * cols + j + col_by)
-        for i in range(rows)
-        for j in range(cols)
-        if 0 <= i + row_by < rows and 0 <= j + col_by < cols
-    ]
-    return lax.ppermute(block, ("px", "py"), pairs)
 
 
 def row_blend(own, above, below, top_weight, bottom_weight, width):
@@ -226,10 +215,14 @@
     below = shifted(fields[:, :width], "px", -1)
     left = shifted(fields[:, :, last:], "py", 1)
     right = shifted(fields[:, :, :width], "py", -1)
-    above_left = diagonal(fields[:, last:, last:], 1, 1)
-    above_right = diagonal(fields[:, last:, :width], 1, -1)
-    below_left = diagonal(fields[:, :width, last:], -1, 1)
-    below_right = diagonal(fields[:, :width, :width], -1, -1)
+    corners_left = shifted(
+        jnp.concatenate([above[:, :, last:], below[:, :, last:]], axis=1), "py", 1
+    )
+    corners_right = shifted(
+        jnp.concatenate([above[:, :, :width], below[:, :, :width]], axis=1), "py", -1
+    )
+    above_left, below_left = corners_left[:, :width], corners_left[:, width:]
+    above_right, below_right = corners_right[:, :width], corners_right[:, width:]
     ramp = (jnp.arange(width, dtype=jnp.float32) + 0.5) / width
     top_weight = jnp.where(band_index > 0, ramp, 1.0)[None, :, None]
     bottom_weight = jnp.where(band_index < rows_axis - 1, ramp[::-1], 1.0)[None, :, None]

time: 113 us -> 113 us (level)
  the two profiles are of different devices: /device:TPU:40 before, /device:TPU:14 now
where the time goes in v5:
time: 113 us; the launch traced here: 112 us
  starting transfers between devices  31.7 us (28%)
  waiting for transfers between devices  29.5 us (26%)
  matrix products  24.5 us (22%)
  other arithmetic  14.9 us (13%)
  local copies, waits for them, and re-layouts  10.9 us (10%)
    ppermute x7, starting transfers between devices, shifted(): return lax.ppermute(shard, axis, pairs)  23.5 us
    all_to_all x1, waiting for transfers between devices, on_device(): lax.all_to_all(jnp.stack([same_sent, rise_sent], axis=1), 'py', 0, 0, til...  21.4 us
    dot_general x2, matrix products, gathered_rows(): jnp.dot(chosen.astype(table_rows.dtype), table_rows, preferred_element_ty...  11.2 us
    all_to_all x1, starting transfers between devices, on_device(): lax.all_to_all(jnp.stack([same_sent, rise_sent], axis=1), 'py', 0, 0, til...  8.26 us
    ppermute x7, waiting for transfers between devices, shifted(): return lax.ppermute(shard, axis, pairs)  8.05 us
    dot_general x8, matrix products, dot32(): return jnp.dot(a, b, preferred_element_type=jnp.float32)  7.54 us
    dot_general x3, matrix products, one_hot_rows(): jnp.dot(picks.astype(values.dtype), values, preferred_element_type=jnp.fl...  5.82 us
    unnamed x17, local copies, waits for them, and re-layouts  4.53 us
  transfers between devices with their start and end apart: 8, of which 3 were waited for; matrix products, arithmetic and copies ran while one was open for 6% of the time, Pallas kernels for 0%

profile of v5, /device:TPU:14, one launch (start us, length us, event | category | flops | bytes accessed | tf_op | source)
XLA Modules:
  0.0 112.1 jit_solution(9061943992248456206)
XLA Ops:
  0.0 0.5 broadcast.526
  0.5 1.3 %reduce.5 = s32[128]{0:T(128)S(1)} reduce(s32[1,128]{1,0:T(1,128)} %param.9, s32[]{:T(128)} %broadcast.526), dimensions={0}, to_apply=%param.9.reduce_sub_computation.3 | reduce | bytes 1028 | tf_op args[3]
  1.9 1.0 copy.20
  3.1 1.0 copy.21
  4.3 5.6 %fusion.13 = bf16[3072,128]{1,0:T(8,128)(2,1)S(1)} fusion(bf16[2352,128]{1,0:T(8,128)(2,1)S(1)} %copy-done, s32[3072]{0:T(1024)S(1)} %eq.89), kind=kOutput, calls=%fused_computation.18 | convolution fusion | flops 1857306624 | bytes 1400832 | tf_op jit(solution)/shard_map/dot_general | solution.py:140
  9.9 5.6 %fusion.14 = bf16[3072,128]{1,0:T(8,128)(2,1)S(1)} fusion(bf16[2352,128]{1,0:T(8,128)(2,1)S(1)} %copy-done, s32[3072]{0:T(1024)S(1)} %eq.43), kind=kOutput, calls=%fused_computation.19 | convolution fusion | flops 1857306624 | bytes 1400832 | tf_op jit(solution)/shard_map/dot_general | solution.py:140
  15.6 0.4 maximum_bitcast_fusion
  16.0 1.3 %pad_maximum_fusion.5 = bf16[16,2,208,128]{3,2,1,0:T(8,128)(2,1)} fusion(bf16[16,1,208,128]{3,2,1,0:T(8,128)(2,1)S(1)} %get-tuple-element.64, bf16[16,1,208,128]{3,2,1,0:T(8,128)(2,1)S(1)} %get-tuple-element.63), kind=kLoop, calls=%fused_computation.34 | loop fusion | flops 851968 | bytes 3407872 | tf_op jit(solution)/shard_map/stack | solution.py:195
  17.4 8.3 %all-to-all-start = ((bf16[16,2,208,128]{3,2,1,0:T(8,128)(2,1)}), bf16[16,2,208,128]{3,2,1,0:T(8,128)(2,1)S(1)}, u32[]{:S(2)}, u32[]{:S(2)}) async-start(bf16[16,2,208,128]{3,2,1,0:T(8,128)(2,1)} %pad_maximum_fusion.5), calls=%async_computation | async-start | bytes 3407872 | tf_op jit(solution)/shard_map/all_to_all | solution.py:195
  25.9 21.4 %all-to-all-done = bf16[16,2,208,128]{3,2,1,0:T(8,128)(2,1)S(1)} async-done(((bf16[16,2,208,128]{3,2,1,0:T(8,128)(2,1)}), bf16[16,2,208,128]{3,2,1,0:T(8,128)(2,1)S(1)}, u32[]{:S(2)}, u32[]{:S(2)}) %all-to-all-start) | async-done | bytes 1703968 | tf_op jit(solution)/shard_map/all_to_all | solution.py:195
  47.8 0.3 reduce-window.9
  48.4 0.8 fusion.10
  49.2 1.0 fusion.30
  50.6 2.1 %collective-permute-start = (bf16[1,528,128]{2,1,0:T(8,128)(2,1)S(1)}, bf16[1,528,128]{2,1,0:T(8,128)(2,1)S(1)}, u32[]{:S(2)}, u32[]{:S(2)}) collective-permute-start(bf16[1,528,128]{2,1,0:T(8,128)(2,1)S(1)} %maximum_maximum_fusion), channel_id=1, source_target_pairs={{16,0},{32,16},{48,32},{64,48},{80,64},{96,80},{112,96},{17,1},{33... | collective-permute-start | bytes 405512 | tf_op jit(solution)/shard_map/ppermute | solution.py:17
  52.7 3.7 %fusion.2 = f32[2048,128]{1,0:T(8,128)S(1)} fusion(bf16[3072,128]{1,0:T(8,128)(2,1)S(1)} %bitcast.105, s32[3072]{0:T(1024)S(1)} %eq.93, s32[2048]{0:T(1024)S(1)} %iota_add_fusion), kind=kOutput, calls=%fused_computation.4 | convolution fusion | flops 1616904192 | bytes 1855488 | tf_op jit(solution)/shard_map/dot_general | solution.py:135
  56.4 1.1 fusion.20
  57.5 0.3 reshape.276
  57.9 0.5 convolution_convert_fusion
  58.4 0.5 convolution_convert_fusion.1
  58.9 0.7 fusion.43
  59.6 0.7 fusion.44
  60.4 0.3 multiply_convert_fusion.3
  60.7 0.9 multiply_convert_fusion.2
  61.6 1.3 %fusion.51 = f32[512,2048]{1,0:T(8,128)S(1)} fusion(bf16[512,512]{1,0:T(8,128)(2,1)S(1)} %copy-done.5, bf16[512,512]{1,0:T(8,128)(2,1)S(1)} %get-tuple-element.25, bf16[512,512]{1,0:T(8,128)(2,1)S(1)} %get-tuple-element.26, bf16[512,512]{1,0:T(8,128)(2,1)S(1)} %get-tuple-element.24, bf16[512,512]{1,0:T(8,128)(2,1)S(1)} %get-tuple-element.9), kind=kOutput, calls=%fused_computation.79 | convolution fusion | flops 1082130432 | bytes 6815744 | tf_op jit(solution)/shard_map/dot_general | solution.py:51
  62.9 1.3 %fusion.52 = f32[512,2048]{1,0:T(8,128)S(1)} fusion(bf16[512,512]{1,0:T(8,128)(2,1)S(1)} %copy-done.4, bf16[512,512]{1,0:T(8,128)(2,1)S(1)} %get-tuple-element.25, bf16[512,512]{1,0:T(8,128)(2,1)S(1)} %get-tuple-element.26, bf16[512,512]{1,0:T(8,128)(2,1)S(1)} %get-tuple-element.24, bf16[512,512]{1,0:T(8,128)(2,1)S(1)} %get-tuple-element.9), kind=kOutput, calls=%fused_computation.80 | convolution fusion | flops 1082130432 | bytes 6815744 | tf_op jit(solution)/shard_map/dot_general | solution.py:51
  64.1 1.2 %fusion.24 = (bf16[512,1024]{1,0:T(8,128)(2,1)S(1)}, bf16[512,1024]{1,0:T(8,128)(2,1)S(1)}) fusion(f32[512,2048]{1,0:T(8,128)S(1)} %fusion.51, f32[512,2048]{1,0:T(8,128)S(1)} %fusion.52), kind=kLoop, calls=%fused_computation.28 | loop fusion | flops 2097152 | bytes 10485760 | tf_op jit(solution)/shard_map/convert.12
  65.5 1.3 %fusion.49 = f32[2048,512]{1,0:T(8,128)S(1)} fusion(bf16[512,512]{1,0:T(8,128)(2,1)S(1)} %copy-done.5, bf16[512,512]{1,0:T(8,128)(2,1)S(1)} %get-tuple-element.42, bf16[512,512]{1,0:T(8,128)(2,1)S(1)} %get-tuple-element.41, bf16[512,512]{1,0:T(8,128)(2,1)S(1)} %get-tuple-element.40, bf16[512,512]{1,0:T(8,128)(2,1)S(1)} %get-tuple-element.39), kind=kOutput, calls=%fused_computation.77 | convolution fusion | flops 1082130432 | bytes 6815744 | tf_op jit(solution)/shard_map/dot_general | solution.py:51
  66.8 1.3 %fusion.50 = f32[2048,512]{1,0:T(8,128)S(1)} fusion(bf16[512,512]{1,0:T(8,128)(2,1)S(1)} %copy-done.4, bf16[512,512]{1,0:T(8,128)(2,1)S(1)} %get-tuple-element.42, bf16[512,512]{1,0:T(8,128)(2,1)S(1)} %get-tuple-element.41, bf16[512,512]{1,0:T(8,128)(2,1)S(1)} %get-tuple-element.40, bf16[512,512]{1,0:T(8,128)(2,1)S(1)} %get-tuple-element.39), kind=kOutput, calls=%fused_computation.78 | convolution fusion | flops 1082130432 | bytes 6815744 | tf_op jit(solution)/shard_map/dot_general | solution.py:51
  68.1 1.2 %fusion.45 = (bf16[1,512,512]{2,1,0:T(8,128)(2,1)S(1)}, bf16[1,512,512]{2,1,0:T(8,128)(2,1)S(1)}, bf16[1,512,512]{2,1,0:T(8,128)(2,1)S(1)}, bf16[1,512,512]{2,1,0:T(8,128)(2,1)S(1)}) fusion(f32[2048,512]{1,0:T(8,128)S(1)} %fusion.49, f32[2048,512]{1,0:T(8,128)S(1)} %fusion.50), kind=kLoop, calls=%fused_computation.73 | loop fusion | flops 2097152 | bytes 10485760 | tf_op jit(solution)/shard_map/stack | solution.py:98
  69.3 2.5 %pad_maximum_fusion.4 = (bf16[4,512,512]{2,1,0:T(8,128)(2,1)S(1)}, f32[4,512,512]{2,1,0:T(8,128)}) fusion(bf16[1,512,512]{2,1,0:T(8,128)(2,1)S(1)} %get-tuple-element.15, bf16[1,512,512]{2,1,0:T(8,128)(2,1)S(1)} %get-tuple-element.16, bf16[1,512,512]{2,1,0:T(8,128)(2,1)S(1)} %get-tuple-element.17, bf16[1,512,512]{2,1,0:T(8,128)(2,1)S(1)} %get-tuple-element.14), kind=kLoop, calls=%fused_computation.31 | loop fusion | flops 4194304 | bytes 8388608 | tf_op jit(solution)/shard_map/stack | solution.py:98
  71.8 1.1 fusion.87
  72.9 2.4 %collective-permute-start.1 = (bf16[4,128,512]{2,1,0:T(8,128)(2,1)}, bf16[4,128,512]{2,1,0:T(8,128)(2,1)S(1)}, u32[]{:S(2)}, u32[]{:S(2)}) collective-permute-start(bf16[4,128,512]{2,1,0:T(8,128)(2,1)} %get-tuple-element.29), channel_id=1, source_target_pairs={{0,16},{16,32},{32,48},{48,64},{64,80},{80,96},{96,112},{1,17},{17... | collective-permute-start | bytes 1572872 | tf_op jit(solution)/shard_map/ppermute | solution.py:17
  75.3 3.2 %collective-permute-start.2 = (bf16[4,128,512]{2,1,0:T(8,128)(2,1)}, bf16[4,128,512]{2,1,0:T(8,128)(2,1)S(1)}, u32[]{:S(2)}, u32[]{:S(2)}) collective-permute-start(bf16[4,128,512]{2,1,0:T(8,128)(2,1)} %get-tuple-element.30), channel_id=1, source_target_pairs={{16,0},{32,16},{48,32},{64,48},{80,64},{96,80},{112,96},{17,1},{33... | collective-permute-start | bytes 1572872 | tf_op jit(solution)/shard_map/ppermute | solution.py:17
  78.5 0.2 fusion.86
  78.7 6.0 %collective-permute-start.3 = (bf16[4,512,128]{2,1,0:T(8,128)(2,1)S(1)}, bf16[4,512,128]{2,1,0:T(8,128)(2,1)S(1)}, u32[]{:S(2)}, u32[]{:S(2)}) collective-permute-start(bf16[4,512,128]{2,1,0:T(8,128)(2,1)S(1)} %get-tuple-element.27), channel_id=1, source_target_pairs={{0,1},{1,2},{2,3},{3,4},{4,5},{5,6},{6,7},{7,8},{8,9},{9,10},{10,1... | collective-permute-start | bytes 1572872 | tf_op jit(solution)/shard_map/ppermute | solution.py:17
  84.6 1.9 %collective-permute-start.5 = (bf16[4,512,128]{2,1,0:T(8,128)(2,1)S(1)}, bf16[4,512,128]{2,1,0:T(8,128)(2,1)S(1)}, u32[]{:S(2)}, u32[]{:S(2)}) collective-permute-start(bf16[4,512,128]{2,1,0:T(8,128)(2,1)S(1)} %get-tuple-element.28), channel_id=1, source_target_pairs={{1,0},{2,1},{3,2},{4,3},{5,4},{6,5},{7,6},{8,7},{9,8},{10,9},{11,1... | collective-permute-start | bytes 1572872 | tf_op jit(solution)/shard_map/ppermute | solution.py:17
  86.6 1.9 %slice.283 = f32[4,256,512]{2,1,0:T(8,128)S(1)} slice(f32[4,512,512]{2,1,0:T(8,128)} %get-tuple-element.32), slice={[0:4], [128:384], [0:512]} | slice | bytes 4194304 | tf_op jit(solution)/shard_map/slice | solution.py:176
  88.7 1.9 %collective-permute-start.6 = (bf16[4,256,128]{2,1,0:T(8,128)(2,1)S(1)}, bf16[4,256,128]{2,1,0:T(8,128)(2,1)S(1)}, u32[]{:S(2)}, u32[]{:S(2)}) collective-permute-start(bf16[4,256,128]{2,1,0:T(8,128)(2,1)S(1)} %pad_maximum_fusion.14), channel_id=1, source_target_pairs={{1,0},{2,1},{3,2},{4,3},{5,4},{6,5},{7,6},{8,7},{9,8},{10,9},{11,1... | collective-permute-start | bytes 786440 | tf_op jit(solution)/shard_map/ppermute | solution.py:17
  90.6 6.0 %collective-permute-start.4 = (bf16[4,256,128]{2,1,0:T(8,128)(2,1)S(1)}, bf16[4,256,128]{2,1,0:T(8,128)(2,1)S(1)}, u32[]{:S(2)}, u32[]{:S(2)}) collective-permute-start(bf16[4,256,128]{2,1,0:T(8,128)(2,1)S(1)} %pad_maximum_fusion.13), channel_id=1, source_target_pairs={{0,1},{1,2},{2,3},{3,4},{4,5},{5,6},{6,7},{7,8},{8,9},{9,10},{10,1... | collective-permute-start | bytes 786440 | tf_op jit(solution)/shard_map/ppermute | solution.py:17
  96.7 0.4 fusion.36
  97.0 0.4 pad_maximum_fusion
  97.5 2.0 %copy-done.3 = f32[4,512,512]{2,1,0:T(8,128)} copy-done((f32[4,512,512]{2,1,0:T(8,128)}, f32[4,512,512]{2,1,0:T(8,128)S(1)}, u32[]{:S(2)}) %copy-start.3) | copy-done | bytes 4194328
  99.6 3.9 %collective-permute-done.5 = bf16[4,512,128]{2,1,0:T(8,128)(2,1)S(1)} collective-permute-done((bf16[4,512,128]{2,1,0:T(8,128)(2,1)S(1)}, bf16[4,512,128]{2,1,0:T(8,128)(2,1)S(1)}, u32[]{:S(2)}, u32[]{:S(2)}) %collective-permute-start.5) | collective-permute-done | bytes 524320 | tf_op jit(solution)/shard_map/ppermute | solution.py:17
  103.6 4.2 %collective-permute-done.6 = bf16[4,256,128]{2,1,0:T(8,128)(2,1)S(1)} collective-permute-done((bf16[4,256,128]{2,1,0:T(8,128)(2,1)S(1)}, bf16[4,256,128]{2,1,0:T(8,128)(2,1)S(1)}, u32[]{:S(2)}, u32[]{:S(2)}) %collective-permute-start.6) | collective-permute-done | bytes 262176 | tf_op jit(solution)/shard_map/ppermute | solution.py:17
  107.8 0.2 fusion.54
  108.0 0.3 fusion.34
  108.3 1.3 %slice-done = f32[4,512,256]{2,1,0:T(8,128)S(1)} async-done(((f32[4,512,512]{2,1,0:T(8,128)}), f32[4,512,256]{2,1,0:T(8,128)S(1)}, s32[]{:S(2)}) %slice-start) | async-done | bytes 2097176 | tf_op jit(solution)/shard_map/slice | solution.py:243
  109.6 2.5 %pad_maximum_fusion.1 = f32[4,512,512]{2,1,0:T(8,128)} fusion(f32[4,512,128]{2,1,0:T(8,128)S(1)} %get-tuple-element.21, f32[4,512,256]{2,1,0:T(8,128)S(1)} %slice-done, f32[4,512,128]{2,1,0:T(8,128)S(1)} %get-tuple-element.20), kind=kLoop, calls=%fused_computation.15 | loop fusion | flops 2097152 | bytes 8388608 | tf_op jit(solution)/shard_map/concatenate | solution.py:242
  (70 shorter events, 2.5 us)
Async XLA Ops:
  0.0 4.3 %copy-start = (bf16[2352,128]{1,0:T(8,128)(2,1)S(1)}, bf16[2352,128]{1,0:T(8,128)(2,1)}, u32[]{:S(2)}) copy-start(bf16[2352,128]{1,0:T(8,128)(2,1)} %param.6) | copy-start | bytes 1806340
  17.4 29.9 %all-to-all-start = ((bf16[16,2,208,128]{3,2,1,0:T(8,128)(2,1)}), bf16[16,2,208,128]{3,2,1,0:T(8,128)(2,1)S(1)}, u32[]{:S(2)}, u32[]{:S(2)}) async-start(bf16[16,2,208,128]{3,2,1,0:T(8,128)(2,1)} %pad_maximum_fusion.5), calls=%async_computation | async-start | bytes 3407872 | tf_op jit(solution)/shard_map/all_to_all | solution.py:195
  50.6 5.8 %collective-permute-start = (bf16[1,528,128]{2,1,0:T(8,128)(2,1)S(1)}, bf16[1,528,128]{2,1,0:T(8,128)(2,1)S(1)}, u32[]{:S(2)}, u32[]{:S(2)}) collective-permute-start(bf16[1,528,128]{2,1,0:T(8,128)(2,1)S(1)} %maximum_maximum_fusion), channel_id=1, source_target_pairs={{16,0},{32,16},{48,32},{64,48},{80,64},{96,80},{112,96},{17,1},{33... | collective-permute-start | bytes 405512 | tf_op jit(solution)/shard_map/ppermute | solution.py:17
  56.4 1.5 %copy-start.5 = (bf16[512,512]{1,0:T(8,128)(2,1)S(1)}, bf16[512,512]{1,0:T(8,128)(2,1)}, u32[]{:S(2)}) copy-start(bf16[512,512]{1,0:T(8,128)(2,1)} %constant.117.clone) | copy-start | bytes 1572868
  56.4 1.9 %copy-start.4 = (bf16[512,512]{1,0:T(8,128)(2,1)S(1)}, bf16[512,512]{1,0:T(8,128)(2,1)}, u32[]{:S(2)}) copy-start(bf16[512,512]{1,0:T(8,128)(2,1)} %constant.116.clone) | copy-start | bytes 1572868
  72.9 15.7 %collective-permute-start.1 = (bf16[4,128,512]{2,1,0:T(8,128)(2,1)}, bf16[4,128,512]{2,1,0:T(8,128)(2,1)S(1)}, u32[]{:S(2)}, u32[]{:S(2)}) collective-permute-start(bf16[4,128,512]{2,1,0:T(8,128)(2,1)} %get-tuple-element.29), channel_id=1, source_target_pairs={{0,16},{16,32},{32,48},{48,64},{64,80},{80,96},{96,112},{1,17},{17... | collective-permute-start | bytes 1572872 | tf_op jit(solution)/shard_map/ppermute | solution.py:17
  75.3 13.3 %collective-permute-start.2 = (bf16[4,128,512]{2,1,0:T(8,128)(2,1)}, bf16[4,128,512]{2,1,0:T(8,128)(2,1)S(1)}, u32[]{:S(2)}, u32[]{:S(2)}) collective-permute-start(bf16[4,128,512]{2,1,0:T(8,128)(2,1)} %get-tuple-element.30), channel_id=1, source_target_pairs={{16,0},{32,16},{48,32},{64,48},{80,64},{96,80},{112,96},{17,1},{33... | collective-permute-start | bytes 1572872 | tf_op jit(solution)/shard_map/ppermute | solution.py:17
  78.7 20.8 %collective-permute-start.3 = (bf16[4,512,128]{2,1,0:T(8,128)(2,1)S(1)}, bf16[4,512,128]{2,1,0:T(8,128)(2,1)S(1)}, u32[]{:S(2)}, u32[]{:S(2)}) collective-permute-start(bf16[4,512,128]{2,1,0:T(8,128)(2,1)S(1)} %get-tuple-element.27), channel_id=1, source_target_pairs={{0,1},{1,2},{2,3},{3,4},{4,5},{5,6},{6,7},{7,8},{8,9},{9,10},{10,1... | collective-permute-start | bytes 1572872 | tf_op jit(solution)/shard_map/ppermute | solution.py:17
  84.6 18.8 %collective-permute-start.5 = (bf16[4,512,128]{2,1,0:T(8,128)(2,1)S(1)}, bf16[4,512,128]{2,1,0:T(8,128)(2,1)S(1)}, u32[]{:S(2)}, u32[]{:S(2)}) collective-permute-start(bf16[4,512,128]{2,1,0:T(8,128)(2,1)S(1)} %get-tuple-element.28), channel_id=1, source_target_pairs={{1,0},{2,1},{3,2},{4,3},{5,4},{6,5},{7,6},{8,7},{9,8},{10,9},{11,1... | collective-permute-start | bytes 1572872 | tf_op jit(solution)/shard_map/ppermute | solution.py:17
  86.6 10.1 %copy-start.2 = (f32[4,512,512]{2,1,0:T(8,128)S(1)}, f32[4,512,512]{2,1,0:T(8,128)}, u32[]{:S(2)}) copy-start(f32[4,512,512]{2,1,0:T(8,128)} %get-tuple-element.32) | copy-start | bytes 12582916
  88.7 19.1 %collective-permute-start.6 = (bf16[4,256,128]{2,1,0:T(8,128)(2,1)S(1)}, bf16[4,256,128]{2,1,0:T(8,128)(2,1)S(1)}, u32[]{:S(2)}, u32[]{:S(2)}) collective-permute-start(bf16[4,256,128]{2,1,0:T(8,128)(2,1)S(1)} %pad_maximum_fusion.14), channel_id=1, source_target_pairs={{1,0},{2,1},{3,2},{4,3},{5,4},{6,5},{7,6},{8,7},{9,8},{10,9},{11,1... | collective-permute-start | bytes 786440 | tf_op jit(solution)/shard_map/ppermute | solution.py:17
  90.6 17.2 %collective-permute-start.4 = (bf16[4,256,128]{2,1,0:T(8,128)(2,1)S(1)}, bf16[4,256,128]{2,1,0:T(8,128)(2,1)S(1)}, u32[]{:S(2)}, u32[]{:S(2)}) collective-permute-start(bf16[4,256,128]{2,1,0:T(8,128)(2,1)S(1)} %pad_maximum_fusion.13), channel_id=1, source_target_pairs={{0,1},{1,2},{2,3},{3,4},{4,5},{5,6},{6,7},{7,8},{8,9},{9,10},{10,1... | collective-permute-start | bytes 786440 | tf_op jit(solution)/shard_map/ppermute | solution.py:17
  97.5 2.0 %copy-start.3 = (f32[4,512,512]{2,1,0:T(8,128)}, f32[4,512,512]{2,1,0:T(8,128)S(1)}, u32[]{:S(2)}) copy-start(f32[4,512,512]{2,1,0:T(8,128)S(1)} %pad_maximum_fusion) | copy-start | bytes 12582916
  108.0 1.6 %slice-start = ((f32[4,512,512]{2,1,0:T(8,128)}), f32[4,512,256]{2,1,0:T(8,128)S(1)}, s32[]{:S(2)}) async-start(f32[4,512,512]{2,1,0:T(8,128)} %copy-done.3), calls=%async_computation.1 | async-start | bytes 4194304 | tf_op jit(solution)/shard_map/slice | solution.py:243
  109.6 2.5 %copy-start.1 = (bf16[2352,128]{1,0:T(8,128)(2,1)S(1)}, bf16[2352,128]{1,0:T(8,128)(2,1)}, u32[]{:S(2)}) copy-start(bf16[2352,128]{1,0:T(8,128)(2,1)} %param.6) | copy-start | bytes 1806340

commit v6 on v5

--- a/solution.py
+++ b/solution.py
@@ -211,18 +211,18 @@
     fields = flexion_fields(patch_tiles.reshape(PATCH_ROWS, PATCH_COLS))
     width = tile_width
     last = PATCH_ROWS - width
+    left = shifted(fields[:, :, last:], "py", 1)
+    right = shifted(fields[:, :, :width], "py", -1)
     above = shifted(fields[:, last:], "px", 1)
     below = shifted(fields[:, :width], "px", -1)
-    left = shifted(fields[:, :, last:], "py", 1)
-    right = shifted(fields[:, :, :width], "py", -1)
-    corners_left = shifted(
-        jnp.concatenate([above[:, :, last:], below[:, :, last:]], axis=1), "py", 1
-    )
-    corners_right = shifted(
-        jnp.concatenate([above[:, :, :width], below[:, :, :width]], axis=1), "py", -1
-    )
-    above_left, below_left = corners_left[:, :width], corners_left[:, width:]
-    above_right, below_right = corners_right[:, :width], corners_right[:, width:]
+    corners_above = shifted(
+        jnp.concatenate([left[:, last:], right[:, last:]], axis=2), "px", 1
+    )
+    corners_below = shifted(
+        jnp.concatenate([left[:, :width], right[:, :width]], axis=2), "px", -1
+    )
+    above_left, above_right = corners_above[:, :, :width], corners_above[:, :, width:]
+    below_left, below_right = corners_below[:, :, :width], corners_below[:, :, width:]
     ramp = (jnp.arange(width, dtype=jnp.float32) + 0.5) / width
     top_weight = jnp.where(band_index > 0, ramp, 1.0)[None, :, None]
     bottom_weight = jnp.where(band_index < rows_axis - 1, ramp[::-1], 1.0)[None, :, None]

time: 113 us -> 112 us (level)
  the two profiles are of different devices: /device:TPU:14 before, /device:TPU:11 now
where the time goes in v6:
time: 112 us; the launch traced here: 111 us
  starting transfers between devices  30.3 us (27%)
  waiting for transfers between devices  30.2 us (27%)
  matrix products  24.5 us (22%)
  other arithmetic  14.9 us (13%)
  local copies, waits for them, and re-layouts  10.7 us (10%)
    ppermute x7, starting transfers between devices, shifted(): return lax.ppermute(shard, axis, pairs)  22.6 us
    all_to_all x1, waiting for transfers between devices, on_device(): lax.all_to_all(jnp.stack([same_sent, rise_sent], axis=1), 'py', 0, 0, til...  21.7 us
    dot_general x2, matrix products, gathered_rows(): jnp.dot(chosen.astype(table_rows.dtype), table_rows, preferred_element_ty...  11.2 us
    ppermute x7, waiting for transfers between devices, shifted(): return lax.ppermute(shard, axis, pairs)  8.49 us
    all_to_all x1, starting transfers between devices, on_device(): lax.all_to_all(jnp.stack([same_sent, rise_sent], axis=1), 'py', 0, 0, til...  7.76 us
    dot_general x8, matrix products, dot32(): return jnp.dot(a, b, preferred_element_type=jnp.float32)  7.5 us
    dot_general x3, matrix products, one_hot_rows(): jnp.dot(picks.astype(values.dtype), values, preferred_element_type=jnp.fl...  5.82 us
    unnamed x17, local copies, waits for them, and re-layouts  4.59 us
  transfers between devices with their start and end apart: 8, of which 4 were waited for; matrix products, arithmetic and copies ran while one was open for 6% of the time, Pallas kernels for 0%

profile of v6, /device:TPU:11, one launch (start us, length us, event | category | flops | bytes accessed | tf_op | source)
XLA Modules:
  0.0 111.2 jit_solution(15520265250313751205)
XLA Ops:
  0.0 1.0 copy.21
  1.1 0.5 broadcast.526
  1.6 1.3 %reduce.5 = s32[128]{0:T(128)S(1)} reduce(s32[1,128]{1,0:T(1,128)} %param.9, s32[]{:T(128)} %broadcast.526), dimensions={0}, to_apply=%param.9.reduce_sub_computation.3 | reduce | bytes 1028 | tf_op args[3]
  3.2 1.0 copy.20
  4.4 5.6 %fusion.14 = bf16[3072,128]{1,0:T(8,128)(2,1)S(1)} fusion(bf16[2352,128]{1,0:T(8,128)(2,1)S(1)} %copy-done, s32[3072]{0:T(1024)S(1)} %eq.43), kind=kOutput, calls=%fused_computation.19 | convolution fusion | flops 1857306624 | bytes 1400832 | tf_op jit(solution)/shard_map/dot_general | solution.py:140
  10.0 5.6 %fusion.13 = bf16[3072,128]{1,0:T(8,128)(2,1)S(1)} fusion(bf16[2352,128]{1,0:T(8,128)(2,1)S(1)} %copy-done, s32[3072]{0:T(1024)S(1)} %eq.89), kind=kOutput, calls=%fused_computation.18 | convolution fusion | flops 1857306624 | bytes 1400832 | tf_op jit(solution)/shard_map/dot_general | solution.py:140
  15.7 0.4 maximum_bitcast_fusion
  16.1 1.3 %pad_maximum_fusion.5 = bf16[16,2,208,128]{3,2,1,0:T(8,128)(2,1)} fusion(bf16[16,1,208,128]{3,2,1,0:T(8,128)(2,1)S(1)} %get-tuple-element.64, bf16[16,1,208,128]{3,2,1,0:T(8,128)(2,1)S(1)} %get-tuple-element.63), kind=kLoop, calls=%fused_computation.34 | loop fusion | flops 851968 | bytes 3407872 | tf_op jit(solution)/shard_map/stack | solution.py:195
  17.4 7.8 %all-to-all-start = ((bf16[16,2,208,128]{3,2,1,0:T(8,128)(2,1)}), bf16[16,2,208,128]{3,2,1,0:T(8,128)(2,1)S(1)}, u32[]{:S(2)}, u32[]{:S(2)}) async-start(bf16[16,2,208,128]{3,2,1,0:T(8,128)(2,1)} %pad_maximum_fusion.5), calls=%async_computation | async-start | bytes 3407872 | tf_op jit(solution)/shard_map/all_to_all | solution.py:195
  25.4 21.7 %all-to-all-done = bf16[16,2,208,128]{3,2,1,0:T(8,128)(2,1)S(1)} async-done(((bf16[16,2,208,128]{3,2,1,0:T(8,128)(2,1)}), bf16[16,2,208,128]{3,2,1,0:T(8,128)(2,1)S(1)}, u32[]{:S(2)}, u32[]{:S(2)}) %all-to-all-start) | async-done | bytes 1703968 | tf_op jit(solution)/shard_map/all_to_all | solution.py:195
  47.8 0.3 reduce-window.9
  48.4 0.8 fusion.10
  49.2 1.0 fusion.30
  50.4 4.3 %collective-permute-start = (bf16[1,528,128]{2,1,0:T(8,128)(2,1)S(1)}, bf16[1,528,128]{2,1,0:T(8,128)(2,1)S(1)}, u32[]{:S(2)}, u32[]{:S(2)}) collective-permute-start(bf16[1,528,128]{2,1,0:T(8,128)(2,1)S(1)} %maximum_maximum_fusion), channel_id=1, source_target_pairs={{16,0},{32,16},{48,32},{64,48},{80,64},{96,80},{112,96},{17,1},{33... | collective-permute-start | bytes 405512 | tf_op jit(solution)/shard_map/ppermute | solution.py:17
  54.7 3.7 %fusion.2 = f32[2048,128]{1,0:T(8,128)S(1)} fusion(bf16[3072,128]{1,0:T(8,128)(2,1)S(1)} %bitcast.105, s32[3072]{0:T(1024)S(1)} %eq.93, s32[2048]{0:T(1024)S(1)} %iota_add_fusion), kind=kOutput, calls=%fused_computation.4 | convolution fusion | flops 1616904192 | bytes 1855488 | tf_op jit(solution)/shard_map/dot_general | solution.py:135
  58.5 1.1 fusion.20
  59.5 0.3 reshape.276
  59.9 0.5 convolution_convert_fusion
  60.4 0.5 convolution_convert_fusion.1
  60.9 0.7 fusion.44
  61.6 0.7 fusion.43
  62.4 0.3 multiply_convert_fusion.3
  62.7 0.9 multiply_convert_fusion.2
  63.6 1.3 %fusion.51 = f32[512,2048]{1,0:T(8,128)S(1)} fusion(bf16[512,512]{1,0:T(8,128)(2,1)S(1)} %copy-done.5, bf16[512,512]{1,0:T(8,128)(2,1)S(1)} %get-tuple-element.25, bf16[512,512]{1,0:T(8,128)(2,1)S(1)} %get-tuple-element.26, bf16[512,512]{1,0:T(8,128)(2,1)S(1)} %get-tuple-element.24, bf16[512,512]{1,0:T(8,128)(2,1)S(1)} %get-tuple-element.9), kind=kOutput, calls=%fused_computation.79 | convolution fusion | flops 1082130432 | bytes 6815744 | tf_op jit(solution)/shard_map/dot_general | solution.py:51
  64.9 1.3 %fusion.52 = f32[512,2048]{1,0:T(8,128)S(1)} fusion(bf16[512,512]{1,0:T(8,128)(2,1)S(1)} %copy-done.4, bf16[512,512]{1,0:T(8,128)(2,1)S(1)} %get-tuple-element.25, bf16[512,512]{1,0:T(8,128)(2,1)S(1)} %get-tuple-element.26, bf16[512,512]{1,0:T(8,128)(2,1)S(1)} %get-tuple-element.24, bf16[512,512]{1,0:T(8,128)(2,1)S(1)} %get-tuple-element.9), kind=kOutput, calls=%fused_computation.80 | convolution fusion | flops 1082130432 | bytes 6815744 | tf_op jit(solution)/shard_map/dot_general | solution.py:51
  66.2 1.2 %fusion.24 = (bf16[512,1024]{1,0:T(8,128)(2,1)S(1)}, bf16[512,1024]{1,0:T(8,128)(2,1)S(1)}) fusion(f32[512,2048]{1,0:T(8,128)S(1)} %fusion.51, f32[512,2048]{1,0:T(8,128)S(1)} %fusion.52), kind=kLoop, calls=%fused_computation.28 | loop fusion | flops 2097152 | bytes 10485760 | tf_op jit(solution)/shard_map/convert.12
  67.5 1.3 %fusion.49 = f32[2048,512]{1,0:T(8,128)S(1)} fusion(bf16[512,512]{1,0:T(8,128)(2,1)S(1)} %copy-done.5, bf16[512,512]{1,0:T(8,128)(2,1)S(1)} %get-tuple-element.42, bf16[512,512]{1,0:T(8,128)(2,1)S(1)} %get-tuple-element.41, bf16[512,512]{1,0:T(8,128)(2,1)S(1)} %get-tuple-element.40, bf16[512,512]{1,0:T(8,128)(2,1)S(1)} %get-tuple-element.39), kind=kOutput, calls=%fused_computation.77 | convolution fusion | flops 1082130432 | bytes 6815744 | tf_op jit(solution)/shard_map/dot_general | solution.py:51
  68.8 1.3 %fusion.50 = f32[2048,512]{1,0:T(8,128)S(1)} fusion(bf16[512,512]{1,0:T(8,128)(2,1)S(1)} %copy-done.4, bf16[512,512]{1,0:T(8,128)(2,1)S(1)} %get-tuple-element.42, bf16[512,512]{1,0:T(8,128)(2,1)S(1)} %get-tuple-element.41, bf16[512,512]{1,0:T(8,128)(2,1)S(1)} %get-tuple-element.40, bf16[512,512]{1,0:T(8,128)(2,1)S(1)} %get-tuple-element.39), kind=kOutput, calls=%fused_computation.78 | convolution fusion | flops 1082130432 | bytes 6815744 | tf_op jit(solution)/shard_map/dot_general | solution.py:51
  70.1 1.2 %fusion.45 = (bf16[1,512,512]{2,1,0:T(8,128)(2,1)S(1)}, bf16[1,512,512]{2,1,0:T(8,128)(2,1)S(1)}, bf16[1,512,512]{2,1,0:T(8,128)(2,1)S(1)}, bf16[1,512,512]{2,1,0:T(8,128)(2,1)S(1)}) fusion(f32[2048,512]{1,0:T(8,128)S(1)} %fusion.49, f32[2048,512]{1,0:T(8,128)S(1)} %fusion.50), kind=kLoop, calls=%fused_computation.73 | loop fusion | flops 2097152 | bytes 10485760 | tf_op jit(solution)/shard_map/stack | solution.py:98
  71.3 2.5 %pad_maximum_fusion.4 = (bf16[4,512,512]{2,1,0:T(8,128)(2,1)S(1)}, f32[4,512,512]{2,1,0:T(8,128)}) fusion(bf16[1,512,512]{2,1,0:T(8,128)(2,1)S(1)} %get-tuple-element.15, bf16[1,512,512]{2,1,0:T(8,128)(2,1)S(1)} %get-tuple-element.16, bf16[1,512,512]{2,1,0:T(8,128)(2,1)S(1)} %get-tuple-element.17, bf16[1,512,512]{2,1,0:T(8,128)(2,1)S(1)} %get-tuple-element.14), kind=kLoop, calls=%fused_computation.31 | loop fusion | flops 4194304 | bytes 8388608 | tf_op jit(solution)/shard_map/stack | solution.py:98
  73.7 1.0 fusion.86
  74.8 4.9 %collective-permute-start.4 = (bf16[4,512,128]{2,1,0:T(8,128)(2,1)}, bf16[4,512,128]{2,1,0:T(8,128)(2,1)S(1)}, u32[]{:S(2)}, u32[]{:S(2)}) collective-permute-start(bf16[4,512,128]{2,1,0:T(8,128)(2,1)} %get-tuple-element.28), channel_id=1, source_target_pairs={{1,0},{2,1},{3,2},{4,3},{5,4},{6,5},{7,6},{8,7},{9,8},{10,9},{11,1... | collective-permute-start | bytes 1572872 | tf_op jit(solution)/shard_map/ppermute | solution.py:17
  79.7 1.9 %collective-permute-start.3 = (bf16[4,512,128]{2,1,0:T(8,128)(2,1)S(1)}, bf16[4,512,128]{2,1,0:T(8,128)(2,1)S(1)}, u32[]{:S(2)}, u32[]{:S(2)}) collective-permute-start(bf16[4,512,128]{2,1,0:T(8,128)(2,1)S(1)} %get-tuple-element.27), channel_id=1, source_target_pairs={{0,1},{1,2},{2,3},{3,4},{4,5},{5,6},{6,7},{7,8},{8,9},{9,10},{10,1... | collective-permute-start | bytes 1572872 | tf_op jit(solution)/shard_map/ppermute | solution.py:17
  81.8 3.4 %collective-permute-start.1 = (bf16[4,128,512]{2,1,0:T(8,128)(2,1)S(1)}, bf16[4,128,512]{2,1,0:T(8,128)(2,1)S(1)}, u32[]{:S(2)}, u32[]{:S(2)}) collective-permute-start(bf16[4,128,512]{2,1,0:T(8,128)(2,1)S(1)} %get-tuple-element.29), channel_id=1, source_target_pairs={{0,16},{16,32},{32,48},{48,64},{64,80},{80,96},{96,112},{1,17},{17... | collective-permute-start | bytes 1572872 | tf_op jit(solution)/shard_map/ppermute | solution.py:17
  85.2 1.9 %collective-permute-start.2 = (bf16[4,128,512]{2,1,0:T(8,128)(2,1)S(1)}, bf16[4,128,512]{2,1,0:T(8,128)(2,1)S(1)}, u32[]{:S(2)}, u32[]{:S(2)}) collective-permute-start(bf16[4,128,512]{2,1,0:T(8,128)(2,1)S(1)} %get-tuple-element.30), channel_id=1, source_target_pairs={{16,0},{32,16},{48,32},{64,48},{80,64},{96,80},{112,96},{17,1},{33... | collective-permute-start | bytes 1572872 | tf_op jit(solution)/shard_map/ppermute | solution.py:17
  87.1 1.9 %slice.283 = f32[4,256,512]{2,1,0:T(8,128)S(1)} slice(f32[4,512,512]{2,1,0:T(8,128)} %get-tuple-element.32), slice={[0:4], [128:384], [0:512]} | slice | bytes 4194304 | tf_op jit(solution)/shard_map/slice | solution.py:176
  89.0 2.3 %collective-permute-done.4 = bf16[4,512,128]{2,1,0:T(8,128)(2,1)S(1)} collective-permute-done((bf16[4,512,128]{2,1,0:T(8,128)(2,1)}, bf16[4,512,128]{2,1,0:T(8,128)(2,1)S(1)}, u32[]{:S(2)}, u32[]{:S(2)}) %collective-permute-start.4) | collective-permute-done | bytes 524320 | tf_op jit(solution)/shard_map/ppermute | solution.py:17
  91.4 3.5 %collective-permute-done.3 = bf16[4,512,128]{2,1,0:T(8,128)(2,1)S(1)} collective-permute-done((bf16[4,512,128]{2,1,0:T(8,128)(2,1)S(1)}, bf16[4,512,128]{2,1,0:T(8,128)(2,1)S(1)}, u32[]{:S(2)}, u32[]{:S(2)}) %collective-permute-start.3) | collective-permute-done | bytes 524320 | tf_op jit(solution)/shard_map/ppermute | solution.py:17
  94.9 4.2 %collective-permute-start.5 = (bf16[4,128,256]{2,1,0:T(8,128)(2,1)S(1)}, bf16[4,128,256]{2,1,0:T(8,128)(2,1)S(1)}, u32[]{:S(2)}, u32[]{:S(2)}) collective-permute-start(bf16[4,128,256]{2,1,0:T(8,128)(2,1)S(1)} %pad_maximum_fusion.13), channel_id=1, source_target_pairs={{0,16},{16,32},{32,48},{48,64},{64,80},{80,96},{96,112},{1,17},{17... | collective-permute-start | bytes 786440 | tf_op jit(solution)/shard_map/ppermute | solution.py:17
  99.2 1.9 %collective-permute-start.6 = (bf16[4,128,256]{2,1,0:T(8,128)(2,1)S(1)}, bf16[4,128,256]{2,1,0:T(8,128)(2,1)S(1)}, u32[]{:S(2)}, u32[]{:S(2)}) collective-permute-start(bf16[4,128,256]{2,1,0:T(8,128)(2,1)S(1)} %pad_maximum_fusion.14), channel_id=1, source_target_pairs={{16,0},{32,16},{48,32},{64,48},{80,64},{96,80},{112,96},{17,1},{33... | collective-permute-start | bytes 786440 | tf_op jit(solution)/shard_map/ppermute | solution.py:17
  101.1 0.3 fusion.36
  101.5 0.4 pad_maximum_fusion
  102.0 2.0 %copy-done.3 = f32[4,512,512]{2,1,0:T(8,128)} copy-done((f32[4,512,512]{2,1,0:T(8,128)}, f32[4,512,512]{2,1,0:T(8,128)S(1)}, u32[]{:S(2)}) %copy-start.3) | copy-done | bytes 4194328
  104.2 2.7 %collective-permute-done.6 = bf16[4,128,256]{2,1,0:T(8,128)(2,1)S(1)} collective-permute-done((bf16[4,128,256]{2,1,0:T(8,128)(2,1)S(1)}, bf16[4,128,256]{2,1,0:T(8,128)(2,1)S(1)}, u32[]{:S(2)}, u32[]{:S(2)}) %collective-permute-start.6) | collective-permute-done | bytes 262176 | tf_op jit(solution)/shard_map/ppermute | solution.py:17
  106.9 0.2 fusion.54
  107.1 0.3 fusion.34
  107.4 1.3 %slice-done = f32[4,512,256]{2,1,0:T(8,128)S(1)} async-done(((f32[4,512,512]{2,1,0:T(8,128)}), f32[4,512,256]{2,1,0:T(8,128)S(1)}, s32[]{:S(2)}) %slice-start) | async-done | bytes 2097176 | tf_op jit(solution)/shard_map/slice | solution.py:243
  108.7 2.5 %pad_maximum_fusion.1 = f32[4,512,512]{2,1,0:T(8,128)} fusion(f32[4,512,128]{2,1,0:T(8,128)S(1)} %get-tuple-element.21, f32[4,512,256]{2,1,0:T(8,128)S(1)} %slice-done, f32[4,512,128]{2,1,0:T(8,128)S(1)} %get-tuple-element.20), kind=kLoop, calls=%fused_computation.15 | loop fusion | flops 2097152 | bytes 8388608 | tf_op jit(solution)/shard_map/concatenate | solution.py:242
  (70 shorter events, 2.5 us)
Async XLA Ops:
  0.0 4.4 %copy-start = (bf16[2352,128]{1,0:T(8,128)(2,1)S(1)}, bf16[2352,128]{1,0:T(8,128)(2,1)}, u32[]{:S(2)}) copy-start(bf16[2352,128]{1,0:T(8,128)(2,1)} %param.6) | copy-start | bytes 1806340
  17.4 29.7 %all-to-all-start = ((bf16[16,2,208,128]{3,2,1,0:T(8,128)(2,1)}), bf16[16,2,208,128]{3,2,1,0:T(8,128)(2,1)S(1)}, u32[]{:S(2)}, u32[]{:S(2)}) async-start(bf16[16,2,208,128]{3,2,1,0:T(8,128)(2,1)} %pad_maximum_fusion.5), calls=%async_computation | async-start | bytes 3407872 | tf_op jit(solution)/shard_map/all_to_all | solution.py:195
  50.4 8.1 %collective-permute-start = (bf16[1,528,128]{2,1,0:T(8,128)(2,1)S(1)}, bf16[1,528,128]{2,1,0:T(8,128)(2,1)S(1)}, u32[]{:S(2)}, u32[]{:S(2)}) collective-permute-start(bf16[1,528,128]{2,1,0:T(8,128)(2,1)S(1)} %maximum_maximum_fusion), channel_id=1, source_target_pairs={{16,0},{32,16},{48,32},{64,48},{80,64},{96,80},{112,96},{17,1},{33... | collective-permute-start | bytes 405512 | tf_op jit(solution)/shard_map/ppermute | solution.py:17
  58.4 1.5 %copy-start.5 = (bf16[512,512]{1,0:T(8,128)(2,1)S(1)}, bf16[512,512]{1,0:T(8,128)(2,1)}, u32[]{:S(2)}) copy-start(bf16[512,512]{1,0:T(8,128)(2,1)} %constant.117.clone) | copy-start | bytes 1572868
  58.4 1.9 %copy-start.4 = (bf16[512,512]{1,0:T(8,128)(2,1)S(1)}, bf16[512,512]{1,0:T(8,128)(2,1)}, u32[]{:S(2)}) copy-start(bf16[512,512]{1,0:T(8,128)(2,1)} %constant.116.clone) | copy-start | bytes 1572868
  74.8 16.6 %collective-permute-start.4 = (bf16[4,512,128]{2,1,0:T(8,128)(2,1)}, bf16[4,512,128]{2,1,0:T(8,128)(2,1)S(1)}, u32[]{:S(2)}, u32[]{:S(2)}) collective-permute-start(bf16[4,512,128]{2,1,0:T(8,128)(2,1)} %get-tuple-element.28), channel_id=1, source_target_pairs={{1,0},{2,1},{3,2},{4,3},{5,4},{6,5},{7,6},{8,7},{9,8},{10,9},{11,1... | collective-permute-start | bytes 1572872 | tf_op jit(solution)/shard_map/ppermute | solution.py:17
  79.7 15.1 %collective-permute-start.3 = (bf16[4,512,128]{2,1,0:T(8,128)(2,1)S(1)}, bf16[4,512,128]{2,1,0:T(8,128)(2,1)S(1)}, u32[]{:S(2)}, u32[]{:S(2)}) collective-permute-start(bf16[4,512,128]{2,1,0:T(8,128)(2,1)S(1)} %get-tuple-element.27), channel_id=1, source_target_pairs={{0,1},{1,2},{2,3},{3,4},{4,5},{5,6},{6,7},{7,8},{8,9},{9,10},{10,1... | collective-permute-start | bytes 1572872 | tf_op jit(solution)/shard_map/ppermute | solution.py:17
  81.8 19.3 %collective-permute-start.1 = (bf16[4,128,512]{2,1,0:T(8,128)(2,1)S(1)}, bf16[4,128,512]{2,1,0:T(8,128)(2,1)S(1)}, u32[]{:S(2)}, u32[]{:S(2)}) collective-permute-start(bf16[4,128,512]{2,1,0:T(8,128)(2,1)S(1)} %get-tuple-element.29), channel_id=1, source_target_pairs={{0,16},{16,32},{32,48},{48,64},{64,80},{80,96},{96,112},{1,17},{17... | collective-permute-start | bytes 1572872 | tf_op jit(solution)/shard_map/ppermute | solution.py:17
  85.2 16.0 %collective-permute-start.2 = (bf16[4,128,512]{2,1,0:T(8,128)(2,1)S(1)}, bf16[4,128,512]{2,1,0:T(8,128)(2,1)S(1)}, u32[]{:S(2)}, u32[]{:S(2)}) collective-permute-start(bf16[4,128,512]{2,1,0:T(8,128)(2,1)S(1)} %get-tuple-element.30), channel_id=1, source_target_pairs={{16,0},{32,16},{48,32},{64,48},{80,64},{96,80},{112,96},{17,1},{33... | collective-permute-start | bytes 1572872 | tf_op jit(solution)/shard_map/ppermute | solution.py:17
  87.1 14.0 %copy-start.2 = (f32[4,512,512]{2,1,0:T(8,128)S(1)}, f32[4,512,512]{2,1,0:T(8,128)}, u32[]{:S(2)}) copy-start(f32[4,512,512]{2,1,0:T(8,128)} %get-tuple-element.32) | copy-start | bytes 12582916
  94.9 9.3 %collective-permute-start.5 = (bf16[4,128,256]{2,1,0:T(8,128)(2,1)S(1)}, bf16[4,128,256]{2,1,0:T(8,128)(2,1)S(1)}, u32[]{:S(2)}, u32[]{:S(2)}) collective-permute-start(bf16[4,128,256]{2,1,0:T(8,128)(2,1)S(1)} %pad_maximum_fusion.13), channel_id=1, source_target_pairs={{0,16},{16,32},{32,48},{48,64},{64,80},{80,96},{96,112},{1,17},{17... | collective-permute-start | bytes 786440 | tf_op jit(solution)/shard_map/ppermute | solution.py:17
  99.2 7.7 %collective-permute-start.6 = (bf16[4,128,256]{2,1,0:T(8,128)(2,1)S(1)}, bf16[4,128,256]{2,1,0:T(8,128)(2,1)S(1)}, u32[]{:S(2)}, u32[]{:S(2)}) collective-permute-start(bf16[4,128,256]{2,1,0:T(8,128)(2,1)S(1)} %pad_maximum_fusion.14), channel_id=1, source_target_pairs={{16,0},{32,16},{48,32},{64,48},{80,64},{96,80},{112,96},{17,1},{33... | collective-permute-start | bytes 786440 | tf_op jit(solution)/shard_map/ppermute | solution.py:17
  101.9 2.0 %copy-start.3 = (f32[4,512,512]{2,1,0:T(8,128)}, f32[4,512,512]{2,1,0:T(8,128)S(1)}, u32[]{:S(2)}) copy-start(f32[4,512,512]{2,1,0:T(8,128)S(1)} %pad_maximum_fusion) | copy-start | bytes 12582916
  107.1 1.6 %slice-start = ((f32[4,512,512]{2,1,0:T(8,128)}), f32[4,512,256]{2,1,0:T(8,128)S(1)}, s32[]{:S(2)}) async-start(f32[4,512,512]{2,1,0:T(8,128)} %copy-done.3), calls=%async_computation.1 | async-start | bytes 4194304 | tf_op jit(solution)/shard_map/slice | solution.py:243
  108.7 2.5 %copy-start.1 = (bf16[2352,128]{1,0:T(8,128)(2,1)S(1)}, bf16[2352,128]{1,0:T(8,128)(2,1)}, u32[]{:S(2)}) copy-start(bf16[2352,128]{1,0:T(8,128)(2,1)} %param.6) | copy-start | bytes 1806340

commit v7 on v6

--- a/solution.py
+++ b/solution.py
@@ -5,6 +5,7 @@
 import numpy as np
 import jax.numpy as jnp
 from jax import lax
+from jax.experimental import pallas as pl
 from jax.sharding import PartitionSpec as P
 
 PATCH_ROWS = 512
@@ -228,20 +229,73 @@
     bottom_weight = jnp.where(band_index < rows_axis - 1, ramp[::-1], 1.0)[None, :, None]
     left_weight = jnp.where(column_index > 0, ramp, 1.0)[None, None, :]
     right_weight = jnp.where(column_index < cols_axis - 1, ramp[::-1], 1.0)[None, None, :]
-    f32 = lambda x: x.astype(jnp.float32)
-    inner = row_blend(f32(fields), f32(above), f32(below), top_weight, bottom_weight, width)
-    left_strip = row_blend(
-        f32(left), f32(above_left), f32(below_left), top_weight, bottom_weight, width
-    )
-    right_strip = row_blend(
-        f32(right), f32(above_right), f32(below_right), top_weight, bottom_weight, width
-    )
-    col_count = inner.shape[2]
-    left_band = left_weight * inner[:, :, :width] + (1.0 - left_weight) * left_strip
-    right_band = right_weight * inner[:, :, col_count - width :] + (1.0 - right_weight) * right_strip
-    return jnp.concatenate(
-        [left_band, inner[:, :, width : col_count - width], right_band], axis=2
-    )
+    weights = (
+        top_weight[0, :, :],
+        bottom_weight[0, :, :],
+        left_weight[0, :, :],
+        right_weight[0, :, :],
+    )
+    return blended(fields, above, below, left, right, corners_above, corners_below, weights)
+
+
+def blend_kernel(own_ref, above_ref, below_ref, left_ref, right_ref, ca_ref, cb_ref,
+                 tw_ref, bw_ref, lw_ref, rw_ref, out_ref):
+    width = above_ref.shape[1]
+    count = own_ref.shape[1]
+    last = count - width
+    tw, bw, lw, rw = tw_ref[...], bw_ref[...], lw_ref[...], rw_ref[...]
+    own = own_ref[0].astype(jnp.float32)
+    above = above_ref[0].astype(jnp.float32)
+    below = below_ref[0].astype(jnp.float32)
+    out_ref[0, :width] = tw * own[:width] + (1.0 - tw) * above
+    out_ref[0, width:last] = own[width:last]
+    out_ref[0, last:] = bw * own[last:] + (1.0 - bw) * below
+    for strip_ref, corner, col, weight in (
+        (left_ref, slice(0, width), slice(0, width), lw),
+        (right_ref, slice(width, 2 * width), slice(last, count), rw),
+    ):
+        strip = strip_ref[0].astype(jnp.float32)
+        upper = ca_ref[0, :, corner].astype(jnp.float32)
+        lower = cb_ref[0, :, corner].astype(jnp.float32)
+        strip_rows = jnp.concatenate(
+            [
+                tw * strip[:width] + (1.0 - tw) * upper,
+                strip[width:last],
+                bw * strip[last:] + (1.0 - bw) * lower,
+            ],
+            axis=0,
+        )
+        out_ref[0, :, col] = weight * out_ref[0, :, col] + (1.0 - weight) * strip_rows
+
+
+def blended(fields, above, below, left, right, corners_above, corners_below, weights):
+    planes, count = fields.shape[0], fields.shape[1]
+    width = above.shape[1]
+    per_plane = lambda shape: pl.BlockSpec((1,) + shape, lambda f: (f, 0, 0))
+    whole = lambda shape: pl.BlockSpec(shape, lambda f: (0, 0))
+    return pl.pallas_call(
+        blend_kernel,
+        grid=(planes,),
+        in_specs=[
+            per_plane((count, count)),
+            per_plane((width, count)),
+            per_plane((width, count)),
+            per_plane((count, width)),
+            per_plane((count, width)),
+            per_plane((width, 2 * width)),
+            per_plane((width, 2 * width)),
+            whole((width, 1)),
+            whole((width, 1)),
+            whole((1, width)),
+            whole((1, width)),
+        ],
+        out_specs=per_plane((count, count)),
+        out_shape=jax.ShapeDtypeStruct(fields.shape, jnp.float32),
+        cost_estimate=pl.CostEstimate(
+            flops=12 * planes * count * width, bytes_accessed=planes * count * count * 6,
+            transcendentals=0,
+        ),
+    )(fields, above, below, left, right, corners_above, corners_below, *weights)
 
 
 def solution(mesh):

time: 112 us -> 113 us (level)
  the two profiles are of different devices: /device:TPU:11 before, /device:TPU:14 now
where the time goes in v7:
time: 113 us; the launch traced here: 112 us
  waiting for transfers between devices  34 us (30%)
  starting transfers between devices  28.1 us (25%)
  matrix products  24.5 us (22%)
  other arithmetic  10.6 us (9%)
  local copies, waits for them, and re-layouts  9.04 us (8%)
  Pallas kernels  5.47 us (5%)
    all_to_all x1, waiting for transfers between devices, on_device(): lax.all_to_all(jnp.stack([same_sent, rise_sent], axis=1), 'py', 0, 0, til...  21.5 us
    ppermute x7, starting transfers between devices, shifted(): return lax.ppermute(shard, axis, pairs)  19.8 us
    ppermute x7, waiting for transfers between devices, shifted(): return lax.ppermute(shard, axis, pairs)  12.4 us
    dot_general x2, matrix products, gathered_rows(): jnp.dot(chosen.astype(table_rows.dtype), table_rows, preferred_element_ty...  11.2 us
    all_to_all x1, starting transfers between devices, on_device(): lax.all_to_all(jnp.stack([same_sent, rise_sent], axis=1), 'py', 0, 0, til...  8.26 us
    dot_general x8, matrix products, dot32(): return jnp.dot(a, b, preferred_element_type=jnp.float32)  7.53 us
    dot_general x3, matrix products, one_hot_rows(): jnp.dot(picks.astype(values.dtype), values, preferred_element_type=jnp.fl...  5.8 us
    pallas_call x1, Pallas kernels, blended(): pl.pallas_call(blend_kernel, grid=(planes,), in_specs=[per_plane((count,...  5.47 us
  transfers between devices with their start and end apart: 8, of which 4 were waited for; matrix products, arithmetic and copies ran while one was open for 8% of the time, Pallas kernels for 0%

profile of v7, /device:TPU:14, one launch (start us, length us, event | category | flops | bytes accessed | tf_op | source)
XLA Modules:
  0.0 112.1 jit_solution(16343785282766724752)
XLA Ops:
  0.0 0.5 broadcast.508
  0.5 1.3 %reduce.5 = s32[128]{0:T(128)S(1)} reduce(s32[1,128]{1,0:T(1,128)} %param.9, s32[]{:T(128)} %broadcast.508), dimensions={0}, to_apply=%param.9.reduce_sub_computation.3 | reduce | bytes 1028 | tf_op args[3]
  1.9 1.0 copy.24
  3.2 1.0 copy.23
  4.3 5.6 %fusion.14 = bf16[3072,128]{1,0:T(8,128)(2,1)S(1)} fusion(bf16[2352,128]{1,0:T(8,128)(2,1)S(1)} %copy-done, s32[3072]{0:T(1024)S(1)} %eq.43), kind=kOutput, calls=%fused_computation.17 | convolution fusion | flops 1857306624 | bytes 1400832 | tf_op jit(solution)/shard_map/dot_general | solution.py:141
  9.9 5.6 %fusion.13 = bf16[3072,128]{1,0:T(8,128)(2,1)S(1)} fusion(bf16[2352,128]{1,0:T(8,128)(2,1)S(1)} %copy-done, s32[3072]{0:T(1024)S(1)} %eq.89), kind=kOutput, calls=%fused_computation.16 | convolution fusion | flops 1857306624 | bytes 1400832 | tf_op jit(solution)/shard_map/dot_general | solution.py:141
  15.6 0.4 maximum_bitcast_fusion
  16.0 1.3 %pad_maximum_fusion.3 = bf16[16,2,208,128]{3,2,1,0:T(8,128)(2,1)} fusion(bf16[16,1,208,128]{3,2,1,0:T(8,128)(2,1)S(1)} %get-tuple-element.48, bf16[16,1,208,128]{3,2,1,0:T(8,128)(2,1)S(1)} %get-tuple-element.47), kind=kLoop, calls=%fused_computation.32 | loop fusion | flops 851968 | bytes 3407872 | tf_op jit(solution)/shard_map/stack | solution.py:196
  17.3 8.3 %all-to-all-start = ((bf16[16,2,208,128]{3,2,1,0:T(8,128)(2,1)}), bf16[16,2,208,128]{3,2,1,0:T(8,128)(2,1)S(1)}, u32[]{:S(2)}, u32[]{:S(2)}) async-start(bf16[16,2,208,128]{3,2,1,0:T(8,128)(2,1)} %pad_maximum_fusion.3), calls=%async_computation | async-start | bytes 3407872 | tf_op jit(solution)/shard_map/all_to_all | solution.py:196
  25.7 21.5 %all-to-all-done = bf16[16,2,208,128]{3,2,1,0:T(8,128)(2,1)S(1)} async-done(((bf16[16,2,208,128]{3,2,1,0:T(8,128)(2,1)}), bf16[16,2,208,128]{3,2,1,0:T(8,128)(2,1)S(1)}, u32[]{:S(2)}, u32[]{:S(2)}) %all-to-all-start) | async-done | bytes 1703968 | tf_op jit(solution)/shard_map/all_to_all | solution.py:196
  47.7 0.3 reduce-window.9
  48.4 0.8 fusion.10
  49.2 1.0 fusion.30
  50.4 2.1 %collective-permute-start = (bf16[1,528,128]{2,1,0:T(8,128)(2,1)S(1)}, bf16[1,528,128]{2,1,0:T(8,128)(2,1)S(1)}, u32[]{:S(2)}, u32[]{:S(2)}) collective-permute-start(bf16[1,528,128]{2,1,0:T(8,128)(2,1)S(1)} %maximum_maximum_fusion), channel_id=1, source_target_pairs={{16,0},{32,16},{48,32},{64,48},{80,64},{96,80},{112,96},{17,1},{33... | collective-permute-start | bytes 405512 | tf_op jit(solution)/shard_map/ppermute | solution.py:18
  52.7 3.7 %fusion.2 = f32[2048,128]{1,0:T(8,128)S(1)} fusion(bf16[3072,128]{1,0:T(8,128)(2,1)S(1)} %bitcast.109, s32[3072]{0:T(1024)S(1)} %eq.93, s32[2048]{0:T(1024)S(1)} %iota_add_fusion), kind=kOutput, calls=%fused_computation.4 | convolution fusion | flops 1616904192 | bytes 1855488 | tf_op jit(solution)/shard_map/dot_general | solution.py:136
  56.4 1.1 fusion.20
  57.5 0.3 reshape.276
  57.8 0.5 convolution_convert_fusion
  58.3 0.5 convolution_convert_fusion.1
  58.8 0.7 fusion.39
  59.6 0.7 fusion.40
  60.3 0.3 multiply_convert_fusion.3
  60.6 1.0 multiply_convert_fusion.2
  61.6 1.3 %fusion.48 = f32[512,2048]{1,0:T(8,128)S(1)} fusion(bf16[512,512]{1,0:T(8,128)(2,1)S(1)} %copy-done.3, bf16[512,512]{1,0:T(8,128)(2,1)S(1)} %get-tuple-element.17, bf16[512,512]{1,0:T(8,128)(2,1)S(1)} %get-tuple-element.18, bf16[512,512]{1,0:T(8,128)(2,1)S(1)} %get-tuple-element.16, bf16[512,512]{1,0:T(8,128)(2,1)S(1)} %get-tuple-element.5), kind=kOutput, calls=%fused_computation.68 | convolution fusion | flops 1082130432 | bytes 6815744 | tf_op jit(solution)/shard_map/dot_general | solution.py:52
  62.9 1.3 %fusion.47 = f32[512,2048]{1,0:T(8,128)S(1)} fusion(bf16[512,512]{1,0:T(8,128)(2,1)S(1)} %copy-done.2, bf16[512,512]{1,0:T(8,128)(2,1)S(1)} %get-tuple-element.17, bf16[512,512]{1,0:T(8,128)(2,1)S(1)} %get-tuple-element.18, bf16[512,512]{1,0:T(8,128)(2,1)S(1)} %get-tuple-element.16, bf16[512,512]{1,0:T(8,128)(2,1)S(1)} %get-tuple-element.5), kind=kOutput, calls=%fused_computation.67 | convolution fusion | flops 1082130432 | bytes 6815744 | tf_op jit(solution)/shard_map/dot_general | solution.py:52
  64.1 1.2 %fusion.24 = (bf16[512,1024]{1,0:T(8,128)(2,1)S(1)}, bf16[512,1024]{1,0:T(8,128)(2,1)S(1)}) fusion(f32[512,2048]{1,0:T(8,128)S(1)} %fusion.47, f32[512,2048]{1,0:T(8,128)S(1)} %fusion.48), kind=kLoop, calls=%fused_computation.26 | loop fusion | flops 2097152 | bytes 10485760 | tf_op jit(solution)/shard_map/convert.12
  65.5 1.3 %fusion.46 = f32[2048,512]{1,0:T(8,128)S(1)} fusion(bf16[512,512]{1,0:T(8,128)(2,1)S(1)} %copy-done.3, bf16[512,512]{1,0:T(8,128)(2,1)S(1)} %get-tuple-element.28, bf16[512,512]{1,0:T(8,128)(2,1)S(1)} %get-tuple-element.27, bf16[512,512]{1,0:T(8,128)(2,1)S(1)} %get-tuple-element.26, bf16[512,512]{1,0:T(8,128)(2,1)S(1)} %get-tuple-element.25), kind=kOutput, calls=%fused_computation.66 | convolution fusion | flops 1082130432 | bytes 6815744 | tf_op jit(solution)/shard_map/dot_general | solution.py:52
  66.8 1.3 %fusion.45 = f32[2048,512]{1,0:T(8,128)S(1)} fusion(bf16[512,512]{1,0:T(8,128)(2,1)S(1)} %copy-done.2, bf16[512,512]{1,0:T(8,128)(2,1)S(1)} %get-tuple-element.28, bf16[512,512]{1,0:T(8,128)(2,1)S(1)} %get-tuple-element.27, bf16[512,512]{1,0:T(8,128)(2,1)S(1)} %get-tuple-element.26, bf16[512,512]{1,0:T(8,128)(2,1)S(1)} %get-tuple-element.25), kind=kOutput, calls=%fused_computation.65 | convolution fusion | flops 1082130432 | bytes 6815744 | tf_op jit(solution)/shard_map/dot_general | solution.py:52
  68.1 1.2 %fusion.41 = (bf16[1,512,512]{2,1,0:T(8,128)(2,1)S(1)}, bf16[1,512,512]{2,1,0:T(8,128)(2,1)S(1)}, bf16[1,512,512]{2,1,0:T(8,128)(2,1)S(1)}, bf16[1,512,512]{2,1,0:T(8,128)(2,1)S(1)}) fusion(f32[2048,512]{1,0:T(8,128)S(1)} %fusion.45, f32[2048,512]{1,0:T(8,128)S(1)} %fusion.46), kind=kLoop, calls=%fused_computation.61 | loop fusion | flops 2097152 | bytes 10485760 | tf_op jit(solution)/shard_map/stack | solution.py:99
  69.3 0.3 pad_maximum_fusion.2.own_ref
  69.6 1.3 %fusion.79 = (bf16[4,512,128]{2,1,0:T(8,128)(2,1)}, bf16[4,512,128]{2,1,0:T(8,128)(2,1)}) fusion(bf16[4,512,512]{2,1,0:T(8,128)(2,1)S(1)} %pad_maximum_fusion.2.own_ref), kind=kLoop, calls=%fused_computation.158 | loop fusion | bytes 2097152 | tf_op jit(solution)/shard_map/slice | solution.py:216
  70.9 5.9 %collective-permute-start.3 = (bf16[4,512,128]{2,1,0:T(8,128)(2,1)}, bf16[4,512,128]{2,1,0:T(8,128)(2,1)S(1)}, u32[]{:S(2)}, u32[]{:S(2)}) collective-permute-start(bf16[4,512,128]{2,1,0:T(8,128)(2,1)} %get-tuple-element.20), channel_id=1, source_target_pairs={{0,1},{1,2},{2,3},{3,4},{4,5},{5,6},{6,7},{7,8},{8,9},{9,10},{10,1... | collective-permute-start | bytes 1572872 | tf_op jit(solution)/shard_map/ppermute | solution.py:18
  76.9 1.9 %collective-permute-start.4 = (bf16[4,512,128]{2,1,0:T(8,128)(2,1)}, bf16[4,512,128]{2,1,0:T(8,128)(2,1)}, u32[]{:S(2)}, u32[]{:S(2)}) collective-permute-start(bf16[4,512,128]{2,1,0:T(8,128)(2,1)} %get-tuple-element.19), channel_id=1, source_target_pairs={{1,0},{2,1},{3,2},{4,3},{5,4},{6,5},{7,6},{8,7},{9,8},{10,9},{11,1... | collective-permute-start | bytes 1572872 | tf_op jit(solution)/shard_map/ppermute | solution.py:18
  78.9 1.1 fusion.80
  80.0 2.1 %collective-permute-start.1 = (bf16[4,128,512]{2,1,0:T(8,128)(2,1)}, bf16[4,128,512]{2,1,0:T(8,128)(2,1)S(1)}, u32[]{:S(2)}, u32[]{:S(2)}) collective-permute-start(bf16[4,128,512]{2,1,0:T(8,128)(2,1)} %get-tuple-element.22), channel_id=1, source_target_pairs={{0,16},{16,32},{32,48},{48,64},{64,80},{80,96},{96,112},{1,17},{17... | collective-permute-start | bytes 1572872 | tf_op jit(solution)/shard_map/ppermute | solution.py:18
  82.1 3.4 %collective-permute-start.2 = (bf16[4,128,512]{2,1,0:T(8,128)(2,1)}, bf16[4,128,512]{2,1,0:T(8,128)(2,1)S(1)}, u32[]{:S(2)}, u32[]{:S(2)}) collective-permute-start(bf16[4,128,512]{2,1,0:T(8,128)(2,1)} %get-tuple-element.21), channel_id=1, source_target_pairs={{16,0},{32,16},{48,32},{64,48},{80,64},{96,80},{112,96},{17,1},{33... | collective-permute-start | bytes 1572872 | tf_op jit(solution)/shard_map/ppermute | solution.py:18
  85.5 3.5 %collective-permute-done.3.left_ref = bf16[4,512,128]{2,1,0:T(8,128)(2,1)S(1)} collective-permute-done((bf16[4,512,128]{2,1,0:T(8,128)(2,1)}, bf16[4,512,128]{2,1,0:T(8,128)(2,1)S(1)}, u32[]{:S(2)}, u32[]{:S(2)}) %collective-permute-start.3) | collective-permute-done | bytes 524320 | tf_op jit(solution)/shard_map/ppermute | solution.py:18
  89.0 6.2 %collective-permute-done.4.right_ref = bf16[4,512,128]{2,1,0:T(8,128)(2,1)} collective-permute-done((bf16[4,512,128]{2,1,0:T(8,128)(2,1)}, bf16[4,512,128]{2,1,0:T(8,128)(2,1)}, u32[]{:S(2)}, u32[]{:S(2)}) %collective-permute-start.4) | collective-permute-done | bytes 524320 | tf_op jit(solution)/shard_map/ppermute | solution.py:18
  95.2 1.0 fusion.84
  96.3 2.0 %collective-permute-start.6 = (bf16[4,128,256]{2,1,0:T(8,128)(2,1)S(1)}, bf16[4,128,256]{2,1,0:T(8,128)(2,1)S(1)}, u32[]{:S(2)}, u32[]{:S(2)}) collective-permute-start(bf16[4,128,256]{2,1,0:T(8,128)(2,1)S(1)} %pad_maximum_fusion.12), channel_id=1, source_target_pairs={{16,0},{32,16},{48,32},{64,48},{80,64},{96,80},{112,96},{17,1},{33... | collective-permute-start | bytes 786440 | tf_op jit(solution)/shard_map/ppermute | solution.py:18
  98.3 2.4 %collective-permute-start.5 = (bf16[4,128,256]{2,1,0:T(8,128)(2,1)S(1)}, bf16[4,128,256]{2,1,0:T(8,128)(2,1)S(1)}, u32[]{:S(2)}, u32[]{:S(2)}) collective-permute-start(bf16[4,128,256]{2,1,0:T(8,128)(2,1)S(1)} %pad_maximum_fusion.11), channel_id=1, source_target_pairs={{0,16},{16,32},{32,48},{48,64},{64,80},{80,96},{96,112},{1,17},{17... | collective-permute-start | bytes 786440 | tf_op jit(solution)/shard_map/ppermute | solution.py:18
  100.6 0.6 fusion.70
  101.2 0.7 copy.25.bw_ref
  102.0 0.5 broadcast_select_fusion.1.lw_ref
  102.5 0.6 multiply_select_fusion.tw_ref
  103.2 2.8 %collective-permute-done.5.ca_ref = bf16[4,128,256]{2,1,0:T(8,128)(2,1)S(1)} collective-permute-done((bf16[4,128,256]{2,1,0:T(8,128)(2,1)S(1)}, bf16[4,128,256]{2,1,0:T(8,128)(2,1)S(1)}, u32[]{:S(2)}, u32[]{:S(2)}) %collective-permute-start.5) | collective-permute-done | bytes 262176 | tf_op jit(solution)/shard_map/ppermute | solution.py:18
  106.0 0.7 copy-done.8
  106.7 5.5 %shard_map.64 = f32[4,512,512]{2,1,0:T(8,128)} custom-call(bf16[4,512,512]{2,1,0:T(8,128)(2,1)} %copy-done.1, bf16[4,128,512]{2,1,0:T(8,128)(2,1)} %copy-done.5, bf16[4,128,512]{2,1,0:T(8,128)(2,1)} %copy-done.6, bf16[4,512,128]{2,1,0:T(8,128)(2,1)} %copy-done.4, bf16[4,512,128]{2,1,0:T(8,128)(2,1)} %collective-permute-done.4.right_ref, ...), custom_call_target="tpu_custom_call" | custom-call | flops 3145728 | bytes 6291456 | tf_op jit(solution)/shard_map/pallas_call | solution.py:276
  (66 shorter events, 2.2 us)
Async XLA Ops:
  0.0 4.3 %copy-start = (bf16[2352,128]{1,0:T(8,128)(2,1)S(1)}, bf16[2352,128]{1,0:T(8,128)(2,1)}, u32[]{:S(2)}) copy-start(bf16[2352,128]{1,0:T(8,128)(2,1)} %param.6) | copy-start | bytes 1806340
  17.3 29.9 %all-to-all-start = ((bf16[16,2,208,128]{3,2,1,0:T(8,128)(2,1)}), bf16[16,2,208,128]{3,2,1,0:T(8,128)(2,1)S(1)}, u32[]{:S(2)}, u32[]{:S(2)}) async-start(bf16[16,2,208,128]{3,2,1,0:T(8,128)(2,1)} %pad_maximum_fusion.3), calls=%async_computation | async-start | bytes 3407872 | tf_op jit(solution)/shard_map/all_to_all | solution.py:196
  50.4 6.0 %collective-permute-start = (bf16[1,528,128]{2,1,0:T(8,128)(2,1)S(1)}, bf16[1,528,128]{2,1,0:T(8,128)(2,1)S(1)}, u32[]{:S(2)}, u32[]{:S(2)}) collective-permute-start(bf16[1,528,128]{2,1,0:T(8,128)(2,1)S(1)} %maximum_maximum_fusion), channel_id=1, source_target_pairs={{16,0},{32,16},{48,32},{64,48},{80,64},{96,80},{112,96},{17,1},{33... | collective-permute-start | bytes 405512 | tf_op jit(solution)/shard_map/ppermute | solution.py:18
  56.4 1.5 %copy-start.2 = (bf16[512,512]{1,0:T(8,128)(2,1)S(1)}, bf16[512,512]{1,0:T(8,128)(2,1)}, u32[]{:S(2)}) copy-start(bf16[512,512]{1,0:T(8,128)(2,1)} %constant.115.clone) | copy-start | bytes 1572868
  56.4 1.9 %copy-start.3 = (bf16[512,512]{1,0:T(8,128)(2,1)S(1)}, bf16[512,512]{1,0:T(8,128)(2,1)}, u32[]{:S(2)}) copy-start(bf16[512,512]{1,0:T(8,128)(2,1)} %constant.114.clone) | copy-start | bytes 1572868
  69.6 10.4 %copy-start.1 = (bf16[4,512,512]{2,1,0:T(8,128)(2,1)}, bf16[4,512,512]{2,1,0:T(8,128)(2,1)S(1)}, u32[]{:S(2)}) copy-start(bf16[4,512,512]{2,1,0:T(8,128)(2,1)S(1)} %pad_maximum_fusion.2.own_ref) | copy-start | bytes 6291460
  70.9 18.1 %collective-permute-start.3 = (bf16[4,512,128]{2,1,0:T(8,128)(2,1)}, bf16[4,512,128]{2,1,0:T(8,128)(2,1)S(1)}, u32[]{:S(2)}, u32[]{:S(2)}) collective-permute-start(bf16[4,512,128]{2,1,0:T(8,128)(2,1)} %get-tuple-element.20), channel_id=1, source_target_pairs={{0,1},{1,2},{2,3},{3,4},{4,5},{5,6},{6,7},{7,8},{8,9},{9,10},{10,1... | collective-permute-start | bytes 1572872 | tf_op jit(solution)/shard_map/ppermute | solution.py:18
  76.9 18.4 %collective-permute-start.4 = (bf16[4,512,128]{2,1,0:T(8,128)(2,1)}, bf16[4,512,128]{2,1,0:T(8,128)(2,1)}, u32[]{:S(2)}, u32[]{:S(2)}) collective-permute-start(bf16[4,512,128]{2,1,0:T(8,128)(2,1)} %get-tuple-element.19), channel_id=1, source_target_pairs={{1,0},{2,1},{3,2},{4,3},{5,4},{6,5},{7,6},{8,7},{9,8},{10,9},{11,1... | collective-permute-start | bytes 1572872 | tf_op jit(solution)/shard_map/ppermute | solution.py:18
  80.0 23.1 %collective-permute-start.1 = (bf16[4,128,512]{2,1,0:T(8,128)(2,1)}, bf16[4,128,512]{2,1,0:T(8,128)(2,1)S(1)}, u32[]{:S(2)}, u32[]{:S(2)}) collective-permute-start(bf16[4,128,512]{2,1,0:T(8,128)(2,1)} %get-tuple-element.22), channel_id=1, source_target_pairs={{0,16},{16,32},{32,48},{48,64},{64,80},{80,96},{96,112},{1,17},{17... | collective-permute-start | bytes 1572872 | tf_op jit(solution)/shard_map/ppermute | solution.py:18
  82.1 21.0 %collective-permute-start.2 = (bf16[4,128,512]{2,1,0:T(8,128)(2,1)}, bf16[4,128,512]{2,1,0:T(8,128)(2,1)S(1)}, u32[]{:S(2)}, u32[]{:S(2)}) collective-permute-start(bf16[4,128,512]{2,1,0:T(8,128)(2,1)} %get-tuple-element.21), channel_id=1, source_target_pairs={{16,0},{32,16},{48,32},{64,48},{80,64},{96,80},{112,96},{17,1},{33... | collective-permute-start | bytes 1572872 | tf_op jit(solution)/shard_map/ppermute | solution.py:18
  89.0 17.0 %copy-start.4 = (bf16[4,512,128]{2,1,0:T(8,128)(2,1)}, bf16[4,512,128]{2,1,0:T(8,128)(2,1)S(1)}, u32[]{:S(2)}) copy-start(bf16[4,512,128]{2,1,0:T(8,128)(2,1)S(1)} %collective-permute-done.3.left_ref) | copy-start | bytes 1572868
  96.3 6.9 %collective-permute-start.6 = (bf16[4,128,256]{2,1,0:T(8,128)(2,1)S(1)}, bf16[4,128,256]{2,1,0:T(8,128)(2,1)S(1)}, u32[]{:S(2)}, u32[]{:S(2)}) collective-permute-start(bf16[4,128,256]{2,1,0:T(8,128)(2,1)S(1)} %pad_maximum_fusion.12), channel_id=1, source_target_pairs={{16,0},{32,16},{48,32},{64,48},{80,64},{96,80},{112,96},{17,1},{33... | collective-permute-start | bytes 786440 | tf_op jit(solution)/shard_map/ppermute | solution.py:18
  98.3 7.7 %collective-permute-start.5 = (bf16[4,128,256]{2,1,0:T(8,128)(2,1)S(1)}, bf16[4,128,256]{2,1,0:T(8,128)(2,1)S(1)}, u32[]{:S(2)}, u32[]{:S(2)}) collective-permute-start(bf16[4,128,256]{2,1,0:T(8,128)(2,1)S(1)} %pad_maximum_fusion.11), channel_id=1, source_target_pairs={{0,16},{16,32},{32,48},{48,64},{64,80},{80,96},{96,112},{1,17},{17... | collective-permute-start | bytes 786440 | tf_op jit(solution)/shard_map/ppermute | solution.py:18
  103.1 2.8 %copy-start.5 = (bf16[4,128,512]{2,1,0:T(8,128)(2,1)}, bf16[4,128,512]{2,1,0:T(8,128)(2,1)S(1)}, u32[]{:S(2)}) copy-start(bf16[4,128,512]{2,1,0:T(8,128)(2,1)S(1)} %collective-permute-done.1.above_ref) | copy-start | bytes 1572868
  103.1 2.8 %copy-start.6 = (bf16[4,128,512]{2,1,0:T(8,128)(2,1)}, bf16[4,128,512]{2,1,0:T(8,128)(2,1)S(1)}, u32[]{:S(2)}) copy-start(bf16[4,128,512]{2,1,0:T(8,128)(2,1)S(1)} %collective-permute-done.2.below_ref) | copy-start | bytes 1572868
  103.2 2.8 %copy-start.7 = (bf16[4,128,256]{2,1,0:T(8,128)(2,1)}, bf16[4,128,256]{2,1,0:T(8,128)(2,1)S(1)}, u32[]{:S(2)}) copy-start(bf16[4,128,256]{2,1,0:T(8,128)(2,1)S(1)} %collective-permute-done.6.cb_ref) | copy-start | bytes 786436
  105.9 0.7 copy-start.8

commit v8 on v6

--- a/solution.py
+++ b/solution.py
@@ -5,6 +5,7 @@
 import numpy as np
 import jax.numpy as jnp
 from jax import lax
+from jax.experimental import pallas as pl
 from jax.sharding import PartitionSpec as P
 
 PATCH_ROWS = 512
@@ -228,20 +229,113 @@
     bottom_weight = jnp.where(band_index < rows_axis - 1, ramp[::-1], 1.0)[None, :, None]
     left_weight = jnp.where(column_index > 0, ramp, 1.0)[None, None, :]
     right_weight = jnp.where(column_index < cols_axis - 1, ramp[::-1], 1.0)[None, None, :]
-    f32 = lambda x: x.astype(jnp.float32)
-    inner = row_blend(f32(fields), f32(above), f32(below), top_weight, bottom_weight, width)
-    left_strip = row_blend(
-        f32(left), f32(above_left), f32(below_left), top_weight, bottom_weight, width
-    )
-    right_strip = row_blend(
-        f32(right), f32(above_right), f32(below_right), top_weight, bottom_weight, width
-    )
-    col_count = inner.shape[2]
-    left_band = left_weight * inner[:, :, :width] + (1.0 - left_weight) * left_strip
-    right_band = right_weight * inner[:, :, col_count - width :] + (1.0 - right_weight) * right_strip
-    return jnp.concatenate(
-        [left_band, inner[:, :, width : col_count - width], right_band], axis=2
-    )
+    edges = edge_blend(
+        fields, above, below, left, right, top_weight[0], bottom_weight[0], left_weight[0],
+        right_weight[0],
+    )
+    return corner_blend(
+        edges,
+        fields,
+        jnp.stack([above, below], axis=1),
+        jnp.stack([left, right], axis=1),
+        jnp.stack([corners_above, corners_below], axis=1),
+        jnp.stack([top_weight[0], bottom_weight[0]]),
+        jnp.stack([left_weight[0], right_weight[0]]),
+    )
+
+
+def edge_kernel(own_ref, above_ref, below_ref, left_ref, right_ref, tw_ref, bw_ref, lw_ref,
+                rw_ref, out_ref):
+    row_block = pl.program_id(1)
+    width = left_ref.shape[2]
+    count = own_ref.shape[2]
+    own = own_ref[0].astype(jnp.float32)
+    tw, bw = tw_ref[...], bw_ref[...]
+
+    @pl.when(row_block == 0)
+    def _():
+        out_ref[0] = tw * own + (1.0 - tw) * above_ref[0].astype(jnp.float32)
+
+    @pl.when(row_block == pl.num_programs(1) - 1)
+    def _():
+        out_ref[0] = bw * own + (1.0 - bw) * below_ref[0].astype(jnp.float32)
+
+    @pl.when((row_block > 0) & (row_block < pl.num_programs(1) - 1))
+    def _():
+        out_ref[0] = own
+
+    lw, rw = lw_ref[...], rw_ref[...]
+    out_ref[0, :, :width] = (
+        lw * out_ref[0, :, :width] + (1.0 - lw) * left_ref[0].astype(jnp.float32)
+    )
+    out_ref[0, :, count - width :] = (
+        rw * out_ref[0, :, count - width :] + (1.0 - rw) * right_ref[0].astype(jnp.float32)
+    )
+
+
+def edge_blend(fields, above, below, left, right, tw, bw, lw, rw):
+    planes, count = fields.shape[0], fields.shape[1]
+    width = above.shape[1]
+    blocks = count // width
+    return pl.pallas_call(
+        edge_kernel,
+        grid=(planes, blocks),
+        in_specs=[
+            pl.BlockSpec((1, width, count), lambda f, r: (f, r, 0)),
+            pl.BlockSpec((1, width, count), lambda f, r: (f, 0, 0)),
+            pl.BlockSpec((1, width, count), lambda f, r: (f, 0, 0)),
+            pl.BlockSpec((1, width, width), lambda f, r: (f, r, 0)),
+            pl.BlockSpec((1, width, width), lambda f, r: (f, r, 0)),
+            pl.BlockSpec((width, 1), lambda f, r: (0, 0)),
+            pl.BlockSpec((width, 1), lambda f, r: (0, 0)),
+            pl.BlockSpec((1, width), lambda f, r: (0, 0)),
+            pl.BlockSpec((1, width), lambda f, r: (0, 0)),
+        ],
+        out_specs=pl.BlockSpec((1, width, count), lambda f, r: (f, r, 0)),
+        out_shape=jax.ShapeDtypeStruct(fields.shape, jnp.float32),
+        cost_estimate=pl.CostEstimate(
+            flops=6 * planes * count * count, bytes_accessed=planes * count * count * 7,
+            transcendentals=0,
+        ),
+    )(fields, above, below, left, right, tw, bw, lw, rw)
+
+
+def corner_kernel(edges_ref, own_ref, row_ref, col_ref, corner_ref, rw_ref, cw_ref, out_ref):
+    del edges_ref
+    own = own_ref[0].astype(jnp.float32)
+    row_weight, col_weight = rw_ref[0], cw_ref[0]
+    rows_done = row_weight * own + (1.0 - row_weight) * row_ref[0, 0].astype(jnp.float32)
+    strip_rows = (
+        row_weight * col_ref[0, 0].astype(jnp.float32)
+        + (1.0 - row_weight) * corner_ref[0, 0].astype(jnp.float32)
+    )
+    out_ref[0] = col_weight * rows_done + (1.0 - col_weight) * strip_rows
+
+
+def corner_blend(edges, fields, row_strips, col_strips, corners, row_weights, col_weights):
+    planes, count = fields.shape[0], fields.shape[1]
+    width = row_strips.shape[2]
+    far = count // width - 1
+    return pl.pallas_call(
+        corner_kernel,
+        grid=(planes, 2, 2),
+        in_specs=[
+            pl.BlockSpec(memory_space=pl.ANY),
+            pl.BlockSpec((1, width, width), lambda f, a, c: (f, a * far, c * far)),
+            pl.BlockSpec((1, 1, width, width), lambda f, a, c: (f, a, 0, c * far)),
+            pl.BlockSpec((1, 1, width, width), lambda f, a, c: (f, c, a * far, 0)),
+            pl.BlockSpec((1, 1, width, width), lambda f, a, c: (f, a, 0, c)),
+            pl.BlockSpec((1, width, 1), lambda f, a, c: (a, 0, 0)),
+            pl.BlockSpec((1, 1, width), lambda f, a, c: (c, 0, 0)),
+        ],
+        out_specs=pl.BlockSpec((1, width, width), lambda f, a, c: (f, a * far, c * far)),
+        out_shape=jax.ShapeDtypeStruct(edges.shape, edges.dtype),
+        input_output_aliases={0: 0},
+        cost_estimate=pl.CostEstimate(
+            flops=9 * planes * 4 * width * width, bytes_accessed=planes * 4 * width * width * 12,
+            transcendentals=0,
+        ),
+    )(edges, fields, row_strips, col_strips, corners, row_weights, col_weights)
 
 
 def solution(mesh):

time: 112 us -> 129 us (1.15)
  the two profiles are of different devices: /device:TPU:11 before, /device:TPU:3 now
where the time goes in v8:
time: 129 us; the launch traced here: 127 us
  starting transfers between devices  30 us (23%)
  waiting for transfers between devices  27.6 us (21%)
  matrix products  24.5 us (19%)
  Pallas kernels  21.1 us (16%)
  other arithmetic  13.9 us (11%)
  local copies, waits for them, and re-layouts  9.71 us (8%)
    ppermute x7, starting transfers between devices, shifted(): return lax.ppermute(shard, axis, pairs)  22.3 us
    all_to_all x1, waiting for transfers between devices, on_device(): lax.all_to_all(jnp.stack([same_sent, rise_sent], axis=1), 'py', 0, 0, til...  20.5 us
    pallas_call x1, Pallas kernels, edge_blend(): pl.pallas_call(edge_kernel, grid=(planes, blocks), in_specs=[pl.BlockSpec...  11.3 us
    dot_general x2, matrix products, gathered_rows(): jnp.dot(chosen.astype(table_rows.dtype), table_rows, preferred_element_ty...  11.2 us
    pallas_call x1, Pallas kernels, corner_blend(): pl.pallas_call(corner_kernel, grid=(planes, 2, 2), in_specs=[pl.BlockSpec...  9.75 us
    all_to_all x1, starting transfers between devices, on_device(): lax.all_to_all(jnp.stack([same_sent, rise_sent], axis=1), 'py', 0, 0, til...  7.76 us
    dot_general x8, matrix products, dot32(): return jnp.dot(a, b, preferred_element_type=jnp.float32)  7.53 us
    ppermute x7, waiting for transfers between devices, shifted(): return lax.ppermute(shard, axis, pairs)  7.15 us
  transfers between devices with their start and end apart: 8, of which 3 were waited for; matrix products, arithmetic and copies ran while one was open for 10% of the time, Pallas kernels for 9%

profile of v8, /device:TPU:3, one launch (start us, length us, event | category | flops | bytes accessed | tf_op | source)
XLA Modules:
  0.0 127.4 jit_solution(15377037891263034568)
XLA Ops:
  0.0 0.5 broadcast.564
  0.5 1.3 %reduce.5 = s32[128]{0:T(128)S(1)} reduce(s32[1,128]{1,0:T(1,128)} %param.9, s32[]{:T(128)} %broadcast.564), dimensions={0}, to_apply=%param.9.reduce_sub_computation.3 | reduce | bytes 1028 | tf_op args[3]
  1.9 1.0 copy.37
  3.1 1.0 copy.38
  4.3 5.6 %fusion.13 = bf16[3072,128]{1,0:T(8,128)(2,1)S(1)} fusion(bf16[2352,128]{1,0:T(8,128)(2,1)S(1)} %copy-done, s32[3072]{0:T(1024)S(1)} %eq.89), kind=kOutput, calls=%fused_computation.16 | convolution fusion | flops 1857306624 | bytes 1400832 | tf_op jit(solution)/shard_map/dot_general | solution.py:141
  9.9 5.6 %fusion.14 = bf16[3072,128]{1,0:T(8,128)(2,1)S(1)} fusion(bf16[2352,128]{1,0:T(8,128)(2,1)S(1)} %copy-done, s32[3072]{0:T(1024)S(1)} %eq.43), kind=kOutput, calls=%fused_computation.17 | convolution fusion | flops 1857306624 | bytes 1400832 | tf_op jit(solution)/shard_map/dot_general | solution.py:141
  15.6 0.4 maximum_bitcast_fusion
  16.0 1.3 %pad_maximum_fusion.3 = bf16[16,2,208,128]{3,2,1,0:T(8,128)(2,1)} fusion(bf16[16,1,208,128]{3,2,1,0:T(8,128)(2,1)S(1)} %get-tuple-element.50, bf16[16,1,208,128]{3,2,1,0:T(8,128)(2,1)S(1)} %get-tuple-element.49), kind=kLoop, calls=%fused_computation.32 | loop fusion | flops 851968 | bytes 3407872 | tf_op jit(solution)/shard_map/stack | solution.py:196
  17.4 7.8 %all-to-all-start = ((bf16[16,2,208,128]{3,2,1,0:T(8,128)(2,1)}), bf16[16,2,208,128]{3,2,1,0:T(8,128)(2,1)S(1)}, u32[]{:S(2)}, u32[]{:S(2)}) async-start(bf16[16,2,208,128]{3,2,1,0:T(8,128)(2,1)} %pad_maximum_fusion.3), calls=%async_computation | async-start | bytes 3407872 | tf_op jit(solution)/shard_map/all_to_all | solution.py:196
  25.4 0.6 multiply_select_fusion.1.tw_ref
  26.0 0.5 fusion.78
  26.6 20.5 %all-to-all-done = bf16[16,2,208,128]{3,2,1,0:T(8,128)(2,1)S(1)} async-done(((bf16[16,2,208,128]{3,2,1,0:T(8,128)(2,1)}), bf16[16,2,208,128]{3,2,1,0:T(8,128)(2,1)S(1)}, u32[]{:S(2)}, u32[]{:S(2)}) %all-to-all-start) | async-done | bytes 1703968 | tf_op jit(solution)/shard_map/all_to_all | solution.py:196
  48.2 0.8 fusion.10
  49.0 1.0 fusion.30
  50.3 4.3 %collective-permute-start = (bf16[1,528,128]{2,1,0:T(8,128)(2,1)S(1)}, bf16[1,528,128]{2,1,0:T(8,128)(2,1)S(1)}, u32[]{:S(2)}, u32[]{:S(2)}) collective-permute-start(bf16[1,528,128]{2,1,0:T(8,128)(2,1)S(1)} %maximum_maximum_fusion), channel_id=1, source_target_pairs={{16,0},{32,16},{48,32},{64,48},{80,64},{96,80},{112,96},{17,1},{33... | collective-permute-start | bytes 405512 | tf_op jit(solution)/shard_map/ppermute | solution.py:18
  54.7 3.7 %fusion.2 = f32[2048,128]{1,0:T(8,128)S(1)} fusion(bf16[3072,128]{1,0:T(8,128)(2,1)S(1)} %bitcast.124, s32[3072]{0:T(1024)S(1)} %eq.93, s32[2048]{0:T(1024)S(1)} %iota_add_fusion), kind=kOutput, calls=%fused_computation.4 | convolution fusion | flops 1616904192 | bytes 1855488 | tf_op jit(solution)/shard_map/dot_general | solution.py:136
  58.4 1.1 fusion.20
  59.8 0.5 convolution_convert_fusion
  60.3 0.5 convolution_convert_fusion.1
  60.8 0.7 fusion.39
  61.6 0.7 fusion.40
  62.7 0.9 multiply_convert_fusion.2
  63.6 1.3 fusion.47
  64.9 1.3 fusion.48
  66.1 1.2 fusion.24
  67.5 1.3 %fusion.45 = f32[2048,512]{1,0:T(8,128)S(1)} fusion(bf16[512,512]{1,0:T(8,128)(2,1)S(1)} %copy-done.4, bf16[512,512]{1,0:T(8,128)(2,1)S(1)} %get-tuple-element.28, bf16[512,512]{1,0:T(8,128)(2,1)S(1)} %get-tuple-element.27, bf16[512,512]{1,0:T(8,128)(2,1)S(1)} %get-tuple-element.26, bf16[512,512]{1,0:T(8,128)(2,1)S(1)} %get-tuple-element.25), kind=kOutput, calls=%fused_computation.68 | convolution fusion | flops 1082130432 | bytes 6815744 | tf_op jit(solution)/shard_map/dot_general | solution.py:52
  68.8 1.3 %fusion.46 = f32[2048,512]{1,0:T(8,128)S(1)} fusion(bf16[512,512]{1,0:T(8,128)(2,1)S(1)} %copy-done.3, bf16[512,512]{1,0:T(8,128)(2,1)S(1)} %get-tuple-element.28, bf16[512,512]{1,0:T(8,128)(2,1)S(1)} %get-tuple-element.27, bf16[512,512]{1,0:T(8,128)(2,1)S(1)} %get-tuple-element.26, bf16[512,512]{1,0:T(8,128)(2,1)S(1)} %get-tuple-element.25), kind=kOutput, calls=%fused_computation.69 | convolution fusion | flops 1082130432 | bytes 6815744 | tf_op jit(solution)/shard_map/dot_general | solution.py:52
  70.1 1.2 fusion.41
  71.6 1.4 %fusion.81 = (bf16[4,512,128]{2,1,0:T(8,128)(2,1)}, bf16[4,512,128]{2,1,0:T(8,128)(2,1)}) fusion(bf16[4,512,512]{2,1,0:T(8,128)(2,1)S(1)} %pad_maximum_fusion.2.own_ref), kind=kLoop, calls=%fused_computation.167 | loop fusion | bytes 2097152 | tf_op jit(solution)/shard_map/slice | solution.py:216
  72.9 4.9 %collective-permute-start.4 = (bf16[4,512,128]{2,1,0:T(8,128)(2,1)}, bf16[4,512,128]{2,1,0:T(8,128)(2,1)S(1)}, u32[]{:S(2)}, u32[]{:S(2)}) collective-permute-start(bf16[4,512,128]{2,1,0:T(8,128)(2,1)} %get-tuple-element.19), channel_id=1, source_target_pairs={{1,0},{2,1},{3,2},{4,3},{5,4},{6,5},{7,6},{8,7},{9,8},{10,9},{11,1... | collective-permute-start | bytes 1572872 | tf_op jit(solution)/shard_map/ppermute | solution.py:18
  77.9 0.5 pad_maximum_fusion.19.cw_ref
  78.5 0.7 pad_maximum_fusion.16.rw_ref
  79.2 1.9 %collective-permute-start.3 = (bf16[4,512,128]{2,1,0:T(8,128)(2,1)}, bf16[4,512,128]{2,1,0:T(8,128)(2,1)}, u32[]{:S(2)}, u32[]{:S(2)}) collective-permute-start(bf16[4,512,128]{2,1,0:T(8,128)(2,1)} %get-tuple-element.20), channel_id=1, source_target_pairs={{0,1},{1,2},{2,3},{3,4},{4,5},{5,6},{6,7},{7,8},{8,9},{9,10},{10,1... | collective-permute-start | bytes 1572872 | tf_op jit(solution)/shard_map/ppermute | solution.py:18
  81.1 0.5 broadcast_select_fusion.2.lw_ref
  81.7 0.7 copy.39.bw_ref
  82.5 1.9 %collective-permute-start.2 = (bf16[4,128,512]{2,1,0:T(8,128)(2,1)S(1)}, bf16[4,128,512]{2,1,0:T(8,128)(2,1)S(1)}, u32[]{:S(2)}, u32[]{:S(2)}) collective-permute-start(bf16[4,128,512]{2,1,0:T(8,128)(2,1)S(1)} %get-tuple-element.21), channel_id=1, source_target_pairs={{16,0},{32,16},{48,32},{64,48},{80,64},{96,80},{112,96},{17,1},{33... | collective-permute-start | bytes 1572872 | tf_op jit(solution)/shard_map/ppermute | solution.py:18
  84.4 3.6 %collective-permute-start.1 = (bf16[4,128,512]{2,1,0:T(8,128)(2,1)S(1)}, bf16[4,128,512]{2,1,0:T(8,128)(2,1)S(1)}, u32[]{:S(2)}, u32[]{:S(2)}) collective-permute-start(bf16[4,128,512]{2,1,0:T(8,128)(2,1)S(1)} %get-tuple-element.22), channel_id=1, source_target_pairs={{0,16},{16,32},{32,48},{48,64},{64,80},{80,96},{96,112},{1,17},{17... | collective-permute-start | bytes 1572872 | tf_op jit(solution)/shard_map/ppermute | solution.py:18
  88.1 1.7 %collective-permute-done.4.right_ref = bf16[4,512,128]{2,1,0:T(8,128)(2,1)S(1)} collective-permute-done((bf16[4,512,128]{2,1,0:T(8,128)(2,1)}, bf16[4,512,128]{2,1,0:T(8,128)(2,1)S(1)}, u32[]{:S(2)}, u32[]{:S(2)}) %collective-permute-start.4) | collective-permute-done | bytes 524320 | tf_op jit(solution)/shard_map/ppermute | solution.py:18
  89.8 5.4 %collective-permute-done.3.left_ref = bf16[4,512,128]{2,1,0:T(8,128)(2,1)} collective-permute-done((bf16[4,512,128]{2,1,0:T(8,128)(2,1)}, bf16[4,512,128]{2,1,0:T(8,128)(2,1)}, u32[]{:S(2)}, u32[]{:S(2)}) %collective-permute-start.3) | collective-permute-done | bytes 524320 | tf_op jit(solution)/shard_map/ppermute | solution.py:18
  95.2 1.0 fusion.85
  96.3 2.4 %collective-permute-start.6 = (bf16[4,128,256]{2,1,0:T(8,128)(2,1)S(1)}, bf16[4,128,256]{2,1,0:T(8,128)(2,1)S(1)}, u32[]{:S(2)}, u32[]{:S(2)}) collective-permute-start(bf16[4,128,256]{2,1,0:T(8,128)(2,1)S(1)} %pad_maximum_fusion.15), channel_id=1, source_target_pairs={{16,0},{32,16},{48,32},{64,48},{80,64},{96,80},{112,96},{17,1},{33... | collective-permute-start | bytes 786440 | tf_op jit(solution)/shard_map/ppermute | solution.py:18
  98.7 3.1 %collective-permute-start.5 = (bf16[4,128,256]{2,1,0:T(8,128)(2,1)S(1)}, bf16[4,128,256]{2,1,0:T(8,128)(2,1)S(1)}, u32[]{:S(2)}, u32[]{:S(2)}) collective-permute-start(bf16[4,128,256]{2,1,0:T(8,128)(2,1)S(1)} %pad_maximum_fusion.14), channel_id=1, source_target_pairs={{0,16},{16,32},{32,48},{48,64},{64,80},{80,96},{96,112},{1,17},{17... | collective-permute-start | bytes 786440 | tf_op jit(solution)/shard_map/ppermute | solution.py:18
  101.9 1.1 pad_maximum_fusion.6
  103.0 1.1 copy.43.col_ref
  104.2 1.2 copy.42.row_ref
  105.4 11.3 %shard_map.64.edges_ref = f32[4,512,512]{2,1,0:T(8,128)} custom-call(bf16[4,512,512]{2,1,0:T(8,128)(2,1)} %copy-done.1, bf16[4,128,512]{2,1,0:T(8,128)(2,1)} %copy-done.6, bf16[4,128,512]{2,1,0:T(8,128)(2,1)} %copy-done.5, bf16[4,512,128]{2,1,0:T(8,128)(2,1)} %collective-permute-done.3.left_ref, bf16[4,512,128]{2,1,0:T(8,128)(2,1)} %copy-done.2, ...), custom_call_target="tpu_custom_call" | custom-call | flops 6291456 | bytes 7340032 | tf_op jit(solution)/shard_map/pallas_call | solution.py:280
  116.8 0.9 pad_maximum_fusion.9.corner_ref
  117.6 9.8 %shard_map.65 = f32[4,512,512]{2,1,0:T(8,128)} custom-call(f32[4,512,512]{2,1,0:T(8,128)} %shard_map.64.edges_ref, bf16[4,512,512]{2,1,0:T(8,128)(2,1)} %copy-done.1, bf16[4,2,128,512]{3,2,1,0:T(8,128)(2,1)} %copy.42.row_ref, bf16[4,2,512,128]{3,2,1,0:T(8,128)(2,1)} %copy.43.col_ref, ...), custom_call_target="tpu_custom_call", output_to_operand_aliasing={{}: (0, {})} | custom-call | flops 2359296 | bytes 3145728 | tf_op jit(solution)/shard_map/pallas_call | solution.py:319
  (73 shorter events, 3.7 us)
Async XLA Ops:
  0.0 4.3 %copy-start = (bf16[2352,128]{1,0:T(8,128)(2,1)S(1)}, bf16[2352,128]{1,0:T(8,128)(2,1)}, u32[]{:S(2)}) copy-start(bf16[2352,128]{1,0:T(8,128)(2,1)} %param.6) | copy-start | bytes 1806340
  17.4 29.7 %all-to-all-start = ((bf16[16,2,208,128]{3,2,1,0:T(8,128)(2,1)}), bf16[16,2,208,128]{3,2,1,0:T(8,128)(2,1)S(1)}, u32[]{:S(2)}, u32[]{:S(2)}) async-start(bf16[16,2,208,128]{3,2,1,0:T(8,128)(2,1)} %pad_maximum_fusion.3), calls=%async_computation | async-start | bytes 3407872 | tf_op jit(solution)/shard_map/all_to_all | solution.py:196
  50.3 8.0 %collective-permute-start = (bf16[1,528,128]{2,1,0:T(8,128)(2,1)S(1)}, bf16[1,528,128]{2,1,0:T(8,128)(2,1)S(1)}, u32[]{:S(2)}, u32[]{:S(2)}) collective-permute-start(bf16[1,528,128]{2,1,0:T(8,128)(2,1)S(1)} %maximum_maximum_fusion), channel_id=1, source_target_pairs={{16,0},{32,16},{48,32},{64,48},{80,64},{96,80},{112,96},{17,1},{33... | collective-permute-start | bytes 405512 | tf_op jit(solution)/shard_map/ppermute | solution.py:18
  58.4 1.5 %copy-start.4 = (bf16[512,512]{1,0:T(8,128)(2,1)S(1)}, bf16[512,512]{1,0:T(8,128)(2,1)}, u32[]{:S(2)}) copy-start(bf16[512,512]{1,0:T(8,128)(2,1)} %constant.115.clone) | copy-start | bytes 1572868
  58.4 1.9 %copy-start.3 = (bf16[512,512]{1,0:T(8,128)(2,1)S(1)}, bf16[512,512]{1,0:T(8,128)(2,1)}, u32[]{:S(2)}) copy-start(bf16[512,512]{1,0:T(8,128)(2,1)} %constant.114.clone) | copy-start | bytes 1572868
  71.6 10.9 %copy-start.1 = (bf16[4,512,512]{2,1,0:T(8,128)(2,1)}, bf16[4,512,512]{2,1,0:T(8,128)(2,1)S(1)}, u32[]{:S(2)}) copy-start(bf16[4,512,512]{2,1,0:T(8,128)(2,1)S(1)} %pad_maximum_fusion.2.own_ref) | copy-start | bytes 6291460
  72.9 16.8 %collective-permute-start.4 = (bf16[4,512,128]{2,1,0:T(8,128)(2,1)}, bf16[4,512,128]{2,1,0:T(8,128)(2,1)S(1)}, u32[]{:S(2)}, u32[]{:S(2)}) collective-permute-start(bf16[4,512,128]{2,1,0:T(8,128)(2,1)} %get-tuple-element.19), channel_id=1, source_target_pairs={{1,0},{2,1},{3,2},{4,3},{5,4},{6,5},{7,6},{8,7},{9,8},{10,9},{11,1... | collective-permute-start | bytes 1572872 | tf_op jit(solution)/shard_map/ppermute | solution.py:18
  79.2 16.0 %collective-permute-start.3 = (bf16[4,512,128]{2,1,0:T(8,128)(2,1)}, bf16[4,512,128]{2,1,0:T(8,128)(2,1)}, u32[]{:S(2)}, u32[]{:S(2)}) collective-permute-start(bf16[4,512,128]{2,1,0:T(8,128)(2,1)} %get-tuple-element.20), channel_id=1, source_target_pairs={{0,1},{1,2},{2,3},{3,4},{4,5},{5,6},{6,7},{7,8},{8,9},{9,10},{10,1... | collective-permute-start | bytes 1572872 | tf_op jit(solution)/shard_map/ppermute | solution.py:18
  82.5 21.6 %collective-permute-start.2 = (bf16[4,128,512]{2,1,0:T(8,128)(2,1)S(1)}, bf16[4,128,512]{2,1,0:T(8,128)(2,1)S(1)}, u32[]{:S(2)}, u32[]{:S(2)}) collective-permute-start(bf16[4,128,512]{2,1,0:T(8,128)(2,1)S(1)} %get-tuple-element.21), channel_id=1, source_target_pairs={{16,0},{32,16},{48,32},{64,48},{80,64},{96,80},{112,96},{17,1},{33... | collective-permute-start | bytes 1572872 | tf_op jit(solution)/shard_map/ppermute | solution.py:18
  84.4 19.7 %collective-permute-start.1 = (bf16[4,128,512]{2,1,0:T(8,128)(2,1)S(1)}, bf16[4,128,512]{2,1,0:T(8,128)(2,1)S(1)}, u32[]{:S(2)}, u32[]{:S(2)}) collective-permute-start(bf16[4,128,512]{2,1,0:T(8,128)(2,1)S(1)} %get-tuple-element.22), channel_id=1, source_target_pairs={{0,16},{16,32},{32,48},{48,64},{64,80},{80,96},{96,112},{1,17},{17... | collective-permute-start | bytes 1572872 | tf_op jit(solution)/shard_map/ppermute | solution.py:18
  89.8 13.3 %copy-start.2 = (bf16[4,512,128]{2,1,0:T(8,128)(2,1)}, bf16[4,512,128]{2,1,0:T(8,128)(2,1)S(1)}, u32[]{:S(2)}) copy-start(bf16[4,512,128]{2,1,0:T(8,128)(2,1)S(1)} %collective-permute-done.4.right_ref) | copy-start | bytes 1572868
  96.3 20.5 %collective-permute-start.6 = (bf16[4,128,256]{2,1,0:T(8,128)(2,1)S(1)}, bf16[4,128,256]{2,1,0:T(8,128)(2,1)S(1)}, u32[]{:S(2)}, u32[]{:S(2)}) collective-permute-start(bf16[4,128,256]{2,1,0:T(8,128)(2,1)S(1)} %pad_maximum_fusion.15), channel_id=1, source_target_pairs={{16,0},{32,16},{48,32},{64,48},{80,64},{96,80},{112,96},{17,1},{33... | collective-permute-start | bytes 786440 | tf_op jit(solution)/shard_map/ppermute | solution.py:18
  98.7 18.0 %collective-permute-start.5 = (bf16[4,128,256]{2,1,0:T(8,128)(2,1)S(1)}, bf16[4,128,256]{2,1,0:T(8,128)(2,1)S(1)}, u32[]{:S(2)}, u32[]{:S(2)}) collective-permute-start(bf16[4,128,256]{2,1,0:T(8,128)(2,1)S(1)} %pad_maximum_fusion.14), channel_id=1, source_target_pairs={{0,16},{16,32},{32,48},{48,64},{64,80},{80,96},{96,112},{1,17},{17... | collective-permute-start | bytes 786440 | tf_op jit(solution)/shard_map/ppermute | solution.py:18
  104.1 1.3 %copy-start.5 = (bf16[4,128,512]{2,1,0:T(8,128)(2,1)}, bf16[4,128,512]{2,1,0:T(8,128)(2,1)S(1)}, u32[]{:S(2)}) copy-start(bf16[4,128,512]{2,1,0:T(8,128)(2,1)S(1)} %collective-permute-done.2.below_ref) | copy-start | bytes 1572868
  104.1 1.3 %copy-start.6 = (bf16[4,128,512]{2,1,0:T(8,128)(2,1)}, bf16[4,128,512]{2,1,0:T(8,128)(2,1)S(1)}, u32[]{:S(2)}) copy-start(bf16[4,128,512]{2,1,0:T(8,128)(2,1)S(1)} %collective-permute-done.1.above_ref) | copy-start | bytes 1572868

commit v9 on v6

--- a/solution.py
+++ b/solution.py
@@ -93,9 +93,23 @@
     arranged = jnp.concatenate(
         [columns_done[:, k * n : (k + 1) * n] for k in range(4)], axis=0
     )
+    width = n // 4
+    edge_cols = jnp.concatenate(
+        [cosine[:, :width], cosine[:, n - width :], sine[:, :width], sine[:, n - width :]], axis=1
+    )
+    edge = dot32(arranged, edge_cols)
+    edge_cos, edge_sin = edge[:, : 2 * width], edge[:, 2 * width :]
+    edge_fields = jnp.stack(
+        [
+            edge_cos[:n] - edge_sin[2 * n : 3 * n],
+            edge_sin[:n] + edge_cos[2 * n : 3 * n],
+            edge_cos[n : 2 * n] - edge_sin[3 * n :],
+            edge_sin[n : 2 * n] + edge_cos[3 * n :],
+        ]
+    ).astype(jnp.bfloat16)
     by_cos = dot32(arranged, cosine)
     by_sin = dot32(arranged, sine)
-    return jnp.stack(
+    return edge_fields, jnp.stack(
         [
             by_cos[:n] - by_sin[2 * n : 3 * n],
             by_sin[:n] + by_cos[2 * n : 3 * n],
@@ -208,11 +222,11 @@
         one_hot_rows(same_codes, slot_total, same_values)
         + one_hot_rows(raised_codes, slot_total, raised_values)
     ).astype(kappa.dtype)
-    fields = flexion_fields(patch_tiles.reshape(PATCH_ROWS, PATCH_COLS))
+    edge_fields, fields = flexion_fields(patch_tiles.reshape(PATCH_ROWS, PATCH_COLS))
     width = tile_width
     last = PATCH_ROWS - width
-    left = shifted(fields[:, :, last:], "py", 1)
-    right = shifted(fields[:, :, :width], "py", -1)
+    left = shifted(edge_fields[:, :, width:], "py", 1)
+    right = shifted(edge_fields[:, :, :width], "py", -1)
     above = shifted(fields[:, last:], "px", 1)
     below = shifted(fields[:, :width], "px", -1)
     corners_above = shifted(

time: 112 us -> 109 us (0.973)
  local copies, waits for them, and re-layouts: 10.7 us -> 7.93 us
  other arithmetic: 14.9 us -> 13.4 us
  matrix products: 24.5 us -> 25.8 us
    another operation x2, other arithmetic: 3.68 us -> 1.69 us  [flexion_fields(): jnp.stack([by_cos[:n] - by_sin[2 * n:3 * n], by_sin[:n] + by_cos[2 * n:3...]
    slice x3, local copies, waits for them, and re-layouts: 1.99 us -> 0.24 us  [row_blend(): return jnp.concatenate([top, own[:, width:count - width], bottom], axis=1)]
    dot_general x8 -> x9, matrix products: 7.5 us -> 8.77 us  [dot32(): return jnp.dot(a, b, preferred_element_type=jnp.float32)]
    another operation x6 -> x8, other arithmetic: 2.9 us -> 3.33 us
where the time goes in v9:
time: 109 us; the launch traced here: 108 us
  starting transfers between devices  30.6 us (28%)
  waiting for transfers between devices  30.2 us (28%)
  matrix products  25.8 us (24%)
  other arithmetic  13.4 us (12%)
  local copies, waits for them, and re-layouts  7.93 us (7%)
    ppermute x7, starting transfers between devices, shifted(): return lax.ppermute(shard, axis, pairs)  22.8 us
    all_to_all x1, waiting for transfers between devices, on_device(): lax.all_to_all(jnp.stack([same_sent, rise_sent], axis=1), 'py', 0, 0, til...  21.6 us
    dot_general x2, matrix products, gathered_rows(): jnp.dot(chosen.astype(table_rows.dtype), table_rows, preferred_element_ty...  11.2 us
    dot_general x9, matrix products, dot32(): return jnp.dot(a, b, preferred_element_type=jnp.float32)  8.77 us
    ppermute x7, waiting for transfers between devices, shifted(): return lax.ppermute(shard, axis, pairs)  8.56 us
    all_to_all x1, starting transfers between devices, on_device(): lax.all_to_all(jnp.stack([same_sent, rise_sent], axis=1), 'py', 0, 0, til...  7.76 us
    dot_general x3, matrix products, one_hot_rows(): jnp.dot(picks.astype(values.dtype), values, preferred_element_type=jnp.fl...  5.81 us
    unnamed x17, local copies, waits for them, and re-layouts  4.39 us
  transfers between devices with their start and end apart: 8, of which 4 were waited for; matrix products, arithmetic and copies ran while one was open for 6% of the time, Pallas kernels for 0%

profile of v9, /device:TPU:11, one launch (start us, length us, event | category | flops | bytes accessed | tf_op | source)
XLA Modules:
  0.0 108.4 jit_solution(3169620369591642165)
XLA Ops:
  0.0 1.0 copy.21
  1.1 0.5 broadcast.526
  1.6 1.3 %reduce.5 = s32[128]{0:T(128)S(1)} reduce(s32[1,128]{1,0:T(1,128)} %param.9, s32[]{:T(128)} %broadcast.526), dimensions={0}, to_apply=%param.9.reduce_sub_computation.3 | reduce | bytes 1028 | tf_op args[3]
  3.2 1.0 copy.20
  4.4 5.6 %fusion.14 = bf16[3072,128]{1,0:T(8,128)(2,1)S(1)} fusion(bf16[2352,128]{1,0:T(8,128)(2,1)S(1)} %copy-done, s32[3072]{0:T(1024)S(1)} %eq.43), kind=kOutput, calls=%fused_computation.19 | convolution fusion | flops 1857306624 | bytes 1400832 | tf_op jit(solution)/shard_map/dot_general | solution.py:154
  10.0 5.6 %fusion.13 = bf16[3072,128]{1,0:T(8,128)(2,1)S(1)} fusion(bf16[2352,128]{1,0:T(8,128)(2,1)S(1)} %copy-done, s32[3072]{0:T(1024)S(1)} %eq.89), kind=kOutput, calls=%fused_computation.18 | convolution fusion | flops 1857306624 | bytes 1400832 | tf_op jit(solution)/shard_map/dot_general | solution.py:154
  15.7 0.4 maximum_bitcast_fusion
  16.1 1.3 %pad_maximum_fusion.5 = bf16[16,2,208,128]{3,2,1,0:T(8,128)(2,1)} fusion(bf16[16,1,208,128]{3,2,1,0:T(8,128)(2,1)S(1)} %get-tuple-element.68, bf16[16,1,208,128]{3,2,1,0:T(8,128)(2,1)S(1)} %get-tuple-element.67), kind=kLoop, calls=%fused_computation.34 | loop fusion | flops 851968 | bytes 3407872 | tf_op jit(solution)/shard_map/stack | solution.py:209
  17.4 7.8 %all-to-all-start = ((bf16[16,2,208,128]{3,2,1,0:T(8,128)(2,1)}), bf16[16,2,208,128]{3,2,1,0:T(8,128)(2,1)S(1)}, u32[]{:S(2)}, u32[]{:S(2)}) async-start(bf16[16,2,208,128]{3,2,1,0:T(8,128)(2,1)} %pad_maximum_fusion.5), calls=%async_computation | async-start | bytes 3407872 | tf_op jit(solution)/shard_map/all_to_all | solution.py:209
  25.4 21.6 %all-to-all-done = bf16[16,2,208,128]{3,2,1,0:T(8,128)(2,1)S(1)} async-done(((bf16[16,2,208,128]{3,2,1,0:T(8,128)(2,1)}), bf16[16,2,208,128]{3,2,1,0:T(8,128)(2,1)S(1)}, u32[]{:S(2)}, u32[]{:S(2)}) %all-to-all-start) | async-done | bytes 1703968 | tf_op jit(solution)/shard_map/all_to_all | solution.py:209
  47.8 0.3 reduce-window.9
  48.4 0.8 fusion.10
  49.2 1.0 fusion.30
  50.4 4.3 %collective-permute-start = (bf16[1,528,128]{2,1,0:T(8,128)(2,1)S(1)}, bf16[1,528,128]{2,1,0:T(8,128)(2,1)S(1)}, u32[]{:S(2)}, u32[]{:S(2)}) collective-permute-start(bf16[1,528,128]{2,1,0:T(8,128)(2,1)S(1)} %maximum_maximum_fusion), channel_id=1, source_target_pairs={{16,0},{32,16},{48,32},{64,48},{80,64},{96,80},{112,96},{17,1},{33... | collective-permute-start | bytes 405512 | tf_op jit(solution)/shard_map/ppermute | solution.py:17
  54.7 3.7 %fusion.2 = f32[2048,128]{1,0:T(8,128)S(1)} fusion(bf16[3072,128]{1,0:T(8,128)(2,1)S(1)} %bitcast.114, s32[3072]{0:T(1024)S(1)} %eq.93, s32[2048]{0:T(1024)S(1)} %iota_add_fusion), kind=kOutput, calls=%fused_computation.4 | convolution fusion | flops 1616904192 | bytes 1855488 | tf_op jit(solution)/shard_map/dot_general | solution.py:149
  58.4 1.1 fusion.20
  59.5 0.3 reshape.276
  59.9 0.5 convolution_convert_fusion
  60.4 0.5 convolution_convert_fusion.1
  60.9 0.7 fusion.44
  61.6 0.7 fusion.43
  62.4 0.3 multiply_convert_fusion.3
  62.7 1.0 multiply_convert_fusion.2
  63.6 1.3 %fusion.53 = f32[512,2048]{1,0:T(8,128)S(1)} fusion(bf16[512,512]{1,0:T(8,128)(2,1)S(1)} %copy-done.4, bf16[512,512]{1,0:T(8,128)(2,1)S(1)} %get-tuple-element.29, bf16[512,512]{1,0:T(8,128)(2,1)S(1)} %get-tuple-element.30, bf16[512,512]{1,0:T(8,128)(2,1)S(1)} %get-tuple-element.28, bf16[512,512]{1,0:T(8,128)(2,1)S(1)} %get-tuple-element.9), kind=kOutput, calls=%fused_computation.86 | convolution fusion | flops 1082130432 | bytes 6815744 | tf_op jit(solution)/shard_map/dot_general | solution.py:51
  64.9 1.3 %fusion.54 = f32[512,2048]{1,0:T(8,128)S(1)} fusion(bf16[512,512]{1,0:T(8,128)(2,1)S(1)} %copy-done.3, bf16[512,512]{1,0:T(8,128)(2,1)S(1)} %get-tuple-element.29, bf16[512,512]{1,0:T(8,128)(2,1)S(1)} %get-tuple-element.30, bf16[512,512]{1,0:T(8,128)(2,1)S(1)} %get-tuple-element.28, bf16[512,512]{1,0:T(8,128)(2,1)S(1)} %get-tuple-element.9), kind=kOutput, calls=%fused_computation.87 | convolution fusion | flops 1082130432 | bytes 6815744 | tf_op jit(solution)/shard_map/dot_general | solution.py:51
  66.2 1.2 %fusion.24 = (bf16[512,1024]{1,0:T(8,128)(2,1)S(1)}, bf16[512,1024]{1,0:T(8,128)(2,1)S(1)}) fusion(f32[512,2048]{1,0:T(8,128)S(1)} %fusion.53, f32[512,2048]{1,0:T(8,128)S(1)} %fusion.54), kind=kLoop, calls=%fused_computation.28 | loop fusion | flops 2097152 | bytes 10485760 | tf_op jit(solution)/shard_map/convert.20
  67.5 1.3 %fusion.89 = f32[2048,512]{1,0:T(8,128)S(1)} fusion(bf16[512,512]{1,0:T(8,128)(2,1)S(1)} %copy-done.4, bf16[512,512]{1,0:T(8,128)(2,1)S(1)} %get-tuple-element.46, bf16[512,512]{1,0:T(8,128)(2,1)S(1)} %get-tuple-element.45, bf16[512,512]{1,0:T(8,128)(2,1)S(1)} %get-tuple-element.44, bf16[512,512]{1,0:T(8,128)(2,1)S(1)} %get-tuple-element.43), kind=kOutput, calls=%fused_computation.191 | convolution fusion | flops 1082130432 | bytes 6815744 | tf_op jit(solution)/shard_map/dot_general | solution.py:51
  68.8 1.3 %fusion.90 = f32[2048,512]{1,0:T(8,128)S(1)} fusion(bf16[512,512]{1,0:T(8,128)(2,1)S(1)} %copy-done.3, bf16[512,512]{1,0:T(8,128)(2,1)S(1)} %get-tuple-element.46, bf16[512,512]{1,0:T(8,128)(2,1)S(1)} %get-tuple-element.45, bf16[512,512]{1,0:T(8,128)(2,1)S(1)} %get-tuple-element.44, bf16[512,512]{1,0:T(8,128)(2,1)S(1)} %get-tuple-element.43), kind=kOutput, calls=%fused_computation.192 | convolution fusion | flops 1082130432 | bytes 6815744 | tf_op jit(solution)/shard_map/dot_general | solution.py:51
  70.1 1.2 %fusion.88 = f32[2048,512]{1,0:T(8,128)S(1)} fusion(bf16[512,512]{1,0:T(8,128)(2,1)S(1)} %copy-done.5, bf16[512,512]{1,0:T(8,128)(2,1)S(1)} %get-tuple-element.46, bf16[512,512]{1,0:T(8,128)(2,1)S(1)} %get-tuple-element.45, bf16[512,512]{1,0:T(8,128)(2,1)S(1)} %get-tuple-element.44, bf16[512,512]{1,0:T(8,128)(2,1)S(1)} %get-tuple-element.43), kind=kOutput, calls=%fused_computation.190 | convolution fusion | flops 1082130432 | bytes 6815744 | tf_op jit(solution)/shard_map/dot_general | solution.py:51
  71.4 0.3 fusion.55
  72.0 5.0 %collective-permute-start.4 = (bf16[4,512,128]{2,1,0:T(8,128)(2,1)S(1)}, bf16[4,512,128]{2,1,0:T(8,128)(2,1)S(1)}, u32[]{:S(2)}, u32[]{:S(2)}) collective-permute-start(bf16[4,512,128]{2,1,0:T(8,128)(2,1)S(1)} %get-tuple-element.42), channel_id=1, source_target_pairs={{1,0},{2,1},{3,2},{4,3},{5,4},{6,5},{7,6},{8,7},{9,8},{10,9},{11,1... | collective-permute-start | bytes 1572872 | tf_op jit(solution)/shard_map/ppermute | solution.py:17
  76.9 1.9 %collective-permute-start.3 = (bf16[4,512,128]{2,1,0:T(8,128)(2,1)S(1)}, bf16[4,512,128]{2,1,0:T(8,128)(2,1)S(1)}, u32[]{:S(2)}, u32[]{:S(2)}) collective-permute-start(bf16[4,512,128]{2,1,0:T(8,128)(2,1)S(1)} %get-tuple-element.41), channel_id=1, source_target_pairs={{0,1},{1,2},{2,3},{3,4},{4,5},{5,6},{6,7},{7,8},{8,9},{9,10},{10,1... | collective-permute-start | bytes 1572872 | tf_op jit(solution)/shard_map/ppermute | solution.py:17
  78.9 1.2 %fusion.45 = (bf16[1,512,512]{2,1,0:T(8,128)(2,1)S(1)}, bf16[1,512,512]{2,1,0:T(8,128)(2,1)S(1)}, bf16[1,512,512]{2,1,0:T(8,128)(2,1)S(1)}, bf16[1,512,512]{2,1,0:T(8,128)(2,1)S(1)}) fusion(f32[2048,512]{1,0:T(8,128)S(1)} %fusion.89, f32[2048,512]{1,0:T(8,128)S(1)} %fusion.90), kind=kLoop, calls=%fused_computation.74 | loop fusion | flops 2097152 | bytes 10485760 | tf_op jit(solution)/shard_map/stack | solution.py:112
  80.1 0.4 pad_maximum_fusion.4
  80.7 3.6 %collective-permute-start.1 = (bf16[4,128,512]{2,1,0:T(8,128)(2,1)S(1)}, bf16[4,128,512]{2,1,0:T(8,128)(2,1)S(1)}, u32[]{:S(2)}, u32[]{:S(2)}) collective-permute-start(bf16[4,128,512]{2,1,0:T(8,128)(2,1)S(1)} %get-tuple-element.31), channel_id=1, source_target_pairs={{0,16},{16,32},{32,48},{48,64},{64,80},{80,96},{96,112},{1,17},{17... | collective-permute-start | bytes 1572872 | tf_op jit(solution)/shard_map/ppermute | solution.py:17
  84.3 1.9 %collective-permute-start.2 = (bf16[4,128,512]{2,1,0:T(8,128)(2,1)S(1)}, bf16[4,128,512]{2,1,0:T(8,128)(2,1)S(1)}, u32[]{:S(2)}, u32[]{:S(2)}) collective-permute-start(bf16[4,128,512]{2,1,0:T(8,128)(2,1)S(1)} %get-tuple-element.32), channel_id=1, source_target_pairs={{16,0},{32,16},{48,32},{64,48},{80,64},{96,80},{112,96},{17,1},{33... | collective-permute-start | bytes 1572872 | tf_op jit(solution)/shard_map/ppermute | solution.py:17
  86.4 1.9 %collective-permute-done.4 = bf16[4,512,128]{2,1,0:T(8,128)(2,1)S(1)} collective-permute-done((bf16[4,512,128]{2,1,0:T(8,128)(2,1)S(1)}, bf16[4,512,128]{2,1,0:T(8,128)(2,1)S(1)}, u32[]{:S(2)}, u32[]{:S(2)}) %collective-permute-start.4) | collective-permute-done | bytes 524320 | tf_op jit(solution)/shard_map/ppermute | solution.py:17
  88.3 3.8 %collective-permute-done.3 = bf16[4,512,128]{2,1,0:T(8,128)(2,1)S(1)} collective-permute-done((bf16[4,512,128]{2,1,0:T(8,128)(2,1)S(1)}, bf16[4,512,128]{2,1,0:T(8,128)(2,1)S(1)}, u32[]{:S(2)}, u32[]{:S(2)}) %collective-permute-start.3) | collective-permute-done | bytes 524320 | tf_op jit(solution)/shard_map/ppermute | solution.py:17
  92.1 4.2 %collective-permute-start.5 = (bf16[4,128,256]{2,1,0:T(8,128)(2,1)S(1)}, bf16[4,128,256]{2,1,0:T(8,128)(2,1)S(1)}, u32[]{:S(2)}, u32[]{:S(2)}) collective-permute-start(bf16[4,128,256]{2,1,0:T(8,128)(2,1)S(1)} %pad_maximum_fusion.12), channel_id=1, source_target_pairs={{0,16},{16,32},{32,48},{48,64},{64,80},{80,96},{96,112},{1,17},{17... | collective-permute-start | bytes 786440 | tf_op jit(solution)/shard_map/ppermute | solution.py:17
  96.4 1.9 %collective-permute-start.6 = (bf16[4,128,256]{2,1,0:T(8,128)(2,1)S(1)}, bf16[4,128,256]{2,1,0:T(8,128)(2,1)S(1)}, u32[]{:S(2)}, u32[]{:S(2)}) collective-permute-start(bf16[4,128,256]{2,1,0:T(8,128)(2,1)S(1)} %pad_maximum_fusion.13), channel_id=1, source_target_pairs={{16,0},{32,16},{48,32},{64,48},{80,64},{96,80},{112,96},{17,1},{33... | collective-permute-start | bytes 786440 | tf_op jit(solution)/shard_map/ppermute | solution.py:17
  98.3 0.3 fusion.36
  98.7 0.4 pad_maximum_fusion
  99.3 1.8 %copy-done.2 = f32[4,512,512]{2,1,0:T(8,128)} copy-done((f32[4,512,512]{2,1,0:T(8,128)}, f32[4,512,512]{2,1,0:T(8,128)S(1)}, u32[]{:S(2)}) %copy-start.2) | copy-done | bytes 4194328
  101.2 2.9 %collective-permute-done.6 = bf16[4,128,256]{2,1,0:T(8,128)(2,1)S(1)} collective-permute-done((bf16[4,128,256]{2,1,0:T(8,128)(2,1)S(1)}, bf16[4,128,256]{2,1,0:T(8,128)(2,1)S(1)}, u32[]{:S(2)}, u32[]{:S(2)}) %collective-permute-start.6) | collective-permute-done | bytes 262176 | tf_op jit(solution)/shard_map/ppermute | solution.py:17
  104.1 0.2 fusion.60
  104.3 0.2 fusion.34
  104.6 1.3 %slice-done = f32[4,512,256]{2,1,0:T(8,128)S(1)} async-done(((f32[4,512,512]{2,1,0:T(8,128)}), f32[4,512,256]{2,1,0:T(8,128)S(1)}, s32[]{:S(2)}) %slice-start) | async-done | bytes 2097176 | tf_op jit(solution)/shard_map/slice | solution.py:257
  105.9 2.5 %pad_maximum_fusion.1 = f32[4,512,512]{2,1,0:T(8,128)} fusion(f32[4,512,128]{2,1,0:T(8,128)S(1)} %get-tuple-element.21, f32[4,512,256]{2,1,0:T(8,128)S(1)} %slice-done, f32[4,512,128]{2,1,0:T(8,128)S(1)} %get-tuple-element.20), kind=kLoop, calls=%fused_computation.15 | loop fusion | flops 2097152 | bytes 8388608 | tf_op jit(solution)/shard_map/concatenate | solution.py:256
  (73 shorter events, 3.0 us)
Async XLA Ops:
  0.0 4.4 %copy-start = (bf16[2352,128]{1,0:T(8,128)(2,1)S(1)}, bf16[2352,128]{1,0:T(8,128)(2,1)}, u32[]{:S(2)}) copy-start(bf16[2352,128]{1,0:T(8,128)(2,1)} %param.6) | copy-start | bytes 1806340
  17.4 29.7 %all-to-all-start = ((bf16[16,2,208,128]{3,2,1,0:T(8,128)(2,1)}), bf16[16,2,208,128]{3,2,1,0:T(8,128)(2,1)S(1)}, u32[]{:S(2)}, u32[]{:S(2)}) async-start(bf16[16,2,208,128]{3,2,1,0:T(8,128)(2,1)} %pad_maximum_fusion.5), calls=%async_computation | async-start | bytes 3407872 | tf_op jit(solution)/shard_map/all_to_all | solution.py:209
  50.4 8.1 %collective-permute-start = (bf16[1,528,128]{2,1,0:T(8,128)(2,1)S(1)}, bf16[1,528,128]{2,1,0:T(8,128)(2,1)S(1)}, u32[]{:S(2)}, u32[]{:S(2)}) collective-permute-start(bf16[1,528,128]{2,1,0:T(8,128)(2,1)S(1)} %maximum_maximum_fusion), channel_id=1, source_target_pairs={{16,0},{32,16},{48,32},{64,48},{80,64},{96,80},{112,96},{17,1},{33... | collective-permute-start | bytes 405512 | tf_op jit(solution)/shard_map/ppermute | solution.py:17
  54.7 5.2 %copy-start.4 = (bf16[512,512]{1,0:T(8,128)(2,1)S(1)}, bf16[512,512]{1,0:T(8,128)(2,1)}, u32[]{:S(2)}) copy-start(bf16[512,512]{1,0:T(8,128)(2,1)} %constant.117.clone) | copy-start | bytes 1572868
  58.4 2.0 %copy-start.3 = (bf16[512,512]{1,0:T(8,128)(2,1)S(1)}, bf16[512,512]{1,0:T(8,128)(2,1)}, u32[]{:S(2)}) copy-start(bf16[512,512]{1,0:T(8,128)(2,1)} %constant.116.clone) | copy-start | bytes 1572868
  68.8 1.3 %copy-start.5 = (bf16[512,512]{1,0:T(8,128)(2,1)S(1)}, bf16[512,512]{1,0:T(8,128)(2,1)}, u32[]{:S(2)}) copy-start(bf16[512,512]{1,0:T(8,128)(2,1)} %constant.126) | copy-start | bytes 1572868
  72.0 16.3 %collective-permute-start.4 = (bf16[4,512,128]{2,1,0:T(8,128)(2,1)S(1)}, bf16[4,512,128]{2,1,0:T(8,128)(2,1)S(1)}, u32[]{:S(2)}, u32[]{:S(2)}) collective-permute-start(bf16[4,512,128]{2,1,0:T(8,128)(2,1)S(1)} %get-tuple-element.42), channel_id=1, source_target_pairs={{1,0},{2,1},{3,2},{4,3},{5,4},{6,5},{7,6},{8,7},{9,8},{10,9},{11,1... | collective-permute-start | bytes 1572872 | tf_op jit(solution)/shard_map/ppermute | solution.py:17
  76.9 15.1 %collective-permute-start.3 = (bf16[4,512,128]{2,1,0:T(8,128)(2,1)S(1)}, bf16[4,512,128]{2,1,0:T(8,128)(2,1)S(1)}, u32[]{:S(2)}, u32[]{:S(2)}) collective-permute-start(bf16[4,512,128]{2,1,0:T(8,128)(2,1)S(1)} %get-tuple-element.41), channel_id=1, source_target_pairs={{0,1},{1,2},{2,3},{3,4},{4,5},{5,6},{6,7},{7,8},{8,9},{9,10},{10,1... | collective-permute-start | bytes 1572872 | tf_op jit(solution)/shard_map/ppermute | solution.py:17
  80.7 17.7 %collective-permute-start.1 = (bf16[4,128,512]{2,1,0:T(8,128)(2,1)S(1)}, bf16[4,128,512]{2,1,0:T(8,128)(2,1)S(1)}, u32[]{:S(2)}, u32[]{:S(2)}) collective-permute-start(bf16[4,128,512]{2,1,0:T(8,128)(2,1)S(1)} %get-tuple-element.31), channel_id=1, source_target_pairs={{0,16},{16,32},{32,48},{48,64},{64,80},{80,96},{96,112},{1,17},{17... | collective-permute-start | bytes 1572872 | tf_op jit(solution)/shard_map/ppermute | solution.py:17
  84.3 14.1 %collective-permute-start.2 = (bf16[4,128,512]{2,1,0:T(8,128)(2,1)S(1)}, bf16[4,128,512]{2,1,0:T(8,128)(2,1)S(1)}, u32[]{:S(2)}, u32[]{:S(2)}) collective-permute-start(bf16[4,128,512]{2,1,0:T(8,128)(2,1)S(1)} %get-tuple-element.32), channel_id=1, source_target_pairs={{16,0},{32,16},{48,32},{64,48},{80,64},{96,80},{112,96},{17,1},{33... | collective-permute-start | bytes 1572872 | tf_op jit(solution)/shard_map/ppermute | solution.py:17
  92.1 9.1 %collective-permute-start.5 = (bf16[4,128,256]{2,1,0:T(8,128)(2,1)S(1)}, bf16[4,128,256]{2,1,0:T(8,128)(2,1)S(1)}, u32[]{:S(2)}, u32[]{:S(2)}) collective-permute-start(bf16[4,128,256]{2,1,0:T(8,128)(2,1)S(1)} %pad_maximum_fusion.12), channel_id=1, source_target_pairs={{0,16},{16,32},{32,48},{48,64},{64,80},{80,96},{96,112},{1,17},{17... | collective-permute-start | bytes 786440 | tf_op jit(solution)/shard_map/ppermute | solution.py:17
  96.4 7.7 %collective-permute-start.6 = (bf16[4,128,256]{2,1,0:T(8,128)(2,1)S(1)}, bf16[4,128,256]{2,1,0:T(8,128)(2,1)S(1)}, u32[]{:S(2)}, u32[]{:S(2)}) collective-permute-start(bf16[4,128,256]{2,1,0:T(8,128)(2,1)S(1)} %pad_maximum_fusion.13), channel_id=1, source_target_pairs={{16,0},{32,16},{48,32},{64,48},{80,64},{96,80},{112,96},{17,1},{33... | collective-permute-start | bytes 786440 | tf_op jit(solution)/shard_map/ppermute | solution.py:17
  99.1 2.0 %copy-start.2 = (f32[4,512,512]{2,1,0:T(8,128)}, f32[4,512,512]{2,1,0:T(8,128)S(1)}, u32[]{:S(2)}) copy-start(f32[4,512,512]{2,1,0:T(8,128)S(1)} %pad_maximum_fusion) | copy-start | bytes 12582916
  104.3 1.6 %slice-start = ((f32[4,512,512]{2,1,0:T(8,128)}), f32[4,512,256]{2,1,0:T(8,128)S(1)}, s32[]{:S(2)}) async-start(f32[4,512,512]{2,1,0:T(8,128)} %copy-done.2), calls=%async_computation.1 | async-start | bytes 4194304 | tf_op jit(solution)/shard_map/slice | solution.py:257
  104.6 3.9 %copy-start.1 = (bf16[2352,128]{1,0:T(8,128)(2,1)S(1)}, bf16[2352,128]{1,0:T(8,128)(2,1)}, u32[]{:S(2)}) copy-start(bf16[2352,128]{1,0:T(8,128)(2,1)} %param.6) | copy-start | bytes 1806340

commit v10 on v9

--- a/solution.py
+++ b/solution.py
@@ -196,16 +196,19 @@
     cols_axis = lax.axis_size("py")
     band_index = lax.axis_index("px")
     column_index = lax.axis_index("py")
-    tile_lists = send_list[0].reshape(rows_axis, cols_axis, -1)
-    slot_lists = dest_slot[0].reshape(rows_axis, cols_axis, -1)
-    pair_counts = send_count[0].reshape(rows_axis, cols_axis)
-    slot_depth = tile_lists.shape[2]
+    slot_depth = send_list.shape[2]
     upper_band = jnp.maximum(band_index - 1, 0)
-    upper_counts = jnp.where(band_index > 0, pair_counts[upper_band], 0)
+    band_rows = lambda table, band: lax.dynamic_slice_in_dim(table[0], band * cols_axis, cols_axis)
+    upper_counts = jnp.where(band_index > 0, band_rows(send_count, upper_band), 0)
     same_sent = sent_block(
-        kappa, tile_lists[band_index], slot_lists[band_index], pair_counts[band_index]
-    )
-    rise_sent = sent_block(kappa, tile_lists[upper_band], slot_lists[upper_band], upper_counts)
+        kappa,
+        band_rows(send_list, band_index),
+        band_rows(dest_slot, band_index),
+        band_rows(send_count, band_index),
+    )
+    rise_sent = sent_block(
+        kappa, band_rows(send_list, upper_band), band_rows(dest_slot, upper_band), upper_counts
+    )
     arrived = lax.all_to_all(jnp.stack([same_sent, rise_sent], axis=1), "py", 0, 0, tiled=True)
     same_values, same_codes = split_codes(arrived[:, 0], slot_depth)
     rise_values, rise_codes = split_codes(arrived[:, 1], slot_depth)

time: 109 us -> 107 us (0.982)
  local copies, waits for them, and re-layouts: 7.93 us -> 6.82 us
    unnamed x17 -> x16, local copies, waits for them, and re-layouts: 4.39 us -> 1.98 us
    dynamic_slice x1 -> x3, local copies, waits for them, and re-layouts: 0.01 us -> 1.38 us  [on_device(): lax.dynamic_slice_in_dim(table[0], band * cols_axis, cols_axis)]
    unnamed x1 -> x0, other arithmetic: 1.32 us -> none
    another operation x6 -> x7, other arithmetic: 2.92 us -> 3 us
  transfers between devices with their start and end apart: 8 -> 8, of which waited for: 4 -> 4; matrix products, arithmetic and copies ran while one was open for 6% -> 7% of each run, Pallas kernels for 0% -> 0%
where the time goes in v10:
time: 107 us
  starting transfers between devices  30.6 us (29%)
  waiting for transfers between devices  30.2 us (28%)
  matrix products  25.8 us (24%)
  other arithmetic  13 us (12%)
  local copies, waits for them, and re-layouts  6.82 us (6%)
    ppermute x7, starting transfers between devices, shifted(): return lax.ppermute(shard, axis, pairs)  22.8 us
    all_to_all x1, waiting for transfers between devices, on_device(): lax.all_to_all(jnp.stack([same_sent, rise_sent], axis=1), 'py', 0, 0, til...  21.6 us
    dot_general x2, matrix products, gathered_rows(): jnp.dot(chosen.astype(table_rows.dtype), table_rows, preferred_element_ty...  11.2 us
    dot_general x9, matrix products, dot32(): return jnp.dot(a, b, preferred_element_type=jnp.float32)  8.77 us
    ppermute x7, waiting for transfers between devices, shifted(): return lax.ppermute(shard, axis, pairs)  8.58 us
    all_to_all x1, starting transfers between devices, on_device(): lax.all_to_all(jnp.stack([same_sent, rise_sent], axis=1), 'py', 0, 0, til...  7.76 us
    dot_general x3, matrix products, one_hot_rows(): jnp.dot(picks.astype(values.dtype), values, preferred_element_type=jnp.fl...  5.81 us
    another operation x7, other arithmetic  3 us
  transfers between devices with their start and end apart: 8, of which 4 were waited for; matrix products, arithmetic and copies ran while one was open for 7% of the time, Pallas kernels for 0%

profile of v10, /device:TPU:11, one launch (start us, length us, event | category | flops | bytes accessed | tf_op | source)
XLA Modules:
  0.0 107.0 jit_solution(2994619119478336018)
XLA Ops:
  0.0 1.3 %constant_dynamic-slice_fusion.3 = (s32[1,16,192]{1,2,0:T(8,128)S(1)}, s32[1,16,192]{1,2,0:T(8,128)S(1)}, s32[1,16,192]{1,2,0:T(8,128)S(1)}, s32[1,16,192]{1,2,0:T(8,128)S(1)}) fusion(s32[1,128,192]{1,2,0:T(8,128)} %param.8, s32[]{:T(128)S(6)} %select_n.148, s32[]{:T(128)S(6)} %select_n.152, s32[1,128,192]{1,2,0:T(8,128)} %param.7), kind=kLoop, calls=%fused_computation.165 | loop fusion | bytes 98312 | tf_op jit(solution)/shard_map/dynamic_slice | solution.py:201
  1.3 0.8 fusion.83
  2.9 5.6 %fusion.14 = bf16[3072,128]{1,0:T(8,128)(2,1)S(1)} fusion(bf16[2352,128]{1,0:T(8,128)(2,1)S(1)} %copy-done, s32[3072]{0:T(1024)S(1)} %eq.43), kind=kOutput, calls=%fused_computation.19 | convolution fusion | flops 1857306624 | bytes 1400832 | tf_op jit(solution)/shard_map/dot_general | solution.py:154
  8.5 5.6 %fusion.13 = bf16[3072,128]{1,0:T(8,128)(2,1)S(1)} fusion(bf16[2352,128]{1,0:T(8,128)(2,1)S(1)} %copy-done, s32[3072]{0:T(1024)S(1)} %eq.89), kind=kOutput, calls=%fused_computation.18 | convolution fusion | flops 1857306624 | bytes 1400832 | tf_op jit(solution)/shard_map/dot_general | solution.py:154
  14.2 0.4 maximum_bitcast_fusion
  14.6 1.3 %pad_maximum_fusion.5 = bf16[16,2,208,128]{3,2,1,0:T(8,128)(2,1)} fusion(bf16[16,1,208,128]{3,2,1,0:T(8,128)(2,1)S(1)} %get-tuple-element.66, bf16[16,1,208,128]{3,2,1,0:T(8,128)(2,1)S(1)} %get-tuple-element.65), kind=kLoop, calls=%fused_computation.34 | loop fusion | flops 851968 | bytes 3407872 | tf_op jit(solution)/shard_map/stack | solution.py:212
  15.9 7.8 %all-to-all-start = ((bf16[16,2,208,128]{3,2,1,0:T(8,128)(2,1)}), bf16[16,2,208,128]{3,2,1,0:T(8,128)(2,1)S(1)}, u32[]{:S(2)}, u32[]{:S(2)}) async-start(bf16[16,2,208,128]{3,2,1,0:T(8,128)(2,1)} %pad_maximum_fusion.5), calls=%async_computation | async-start | bytes 3407872 | tf_op jit(solution)/shard_map/all_to_all | solution.py:212
  24.0 21.6 %all-to-all-done = bf16[16,2,208,128]{3,2,1,0:T(8,128)(2,1)S(1)} async-done(((bf16[16,2,208,128]{3,2,1,0:T(8,128)(2,1)}), bf16[16,2,208,128]{3,2,1,0:T(8,128)(2,1)S(1)}, u32[]{:S(2)}, u32[]{:S(2)}) %all-to-all-start) | async-done | bytes 1703968 | tf_op jit(solution)/shard_map/all_to_all | solution.py:212
  46.3 0.3 reduce-window.9
  46.9 0.8 fusion.10
  47.7 1.0 fusion.30
  48.9 4.3 %collective-permute-start = (bf16[1,528,128]{2,1,0:T(8,128)(2,1)S(1)}, bf16[1,528,128]{2,1,0:T(8,128)(2,1)S(1)}, u32[]{:S(2)}, u32[]{:S(2)}) collective-permute-start(bf16[1,528,128]{2,1,0:T(8,128)(2,1)S(1)} %maximum_maximum_fusion), channel_id=1, source_target_pairs={{16,0},{32,16},{48,32},{64,48},{80,64},{96,80},{112,96},{17,1},{33... | collective-permute-start | bytes 405512 | tf_op jit(solution)/shard_map/ppermute | solution.py:17
  53.2 3.7 %fusion.2 = f32[2048,128]{1,0:T(8,128)S(1)} fusion(bf16[3072,128]{1,0:T(8,128)(2,1)S(1)} %bitcast.112, s32[3072]{0:T(1024)S(1)} %eq.93, s32[2048]{0:T(1024)S(1)} %iota_add_fusion), kind=kOutput, calls=%fused_computation.4 | convolution fusion | flops 1616904192 | bytes 1855488 | tf_op jit(solution)/shard_map/dot_general | solution.py:149
  57.0 1.1 %fusion.20 = bf16[2048,128]{1,0:T(8,128)(2,1)S(1)} fusion(f32[2048,128]{1,0:T(8,128)S(1)} %fusion.2, s32[512]{0:T(512)S(1)} %bitcast.121, s32[2048]{0:T(1024)S(1)} %iota_add_fusion, bf16[1,528,128]{2,1,0:T(8,128)(2,1)S(1)} %collective-permute-done), kind=kOutput, calls=%fused_computation.24 | convolution fusion | flops 270008320 | bytes 1714176 | tf_op jit(solution)/shard_map/dot_general | solution.py:149
  58.1 0.3 reshape.285
  58.4 0.5 convolution_convert_fusion
  58.9 0.5 convolution_convert_fusion.1
  59.4 0.7 fusion.44
  60.1 0.7 fusion.43
  60.9 0.3 multiply_convert_fusion.3
  61.2 1.0 multiply_convert_fusion.2
  62.2 1.3 %fusion.53 = f32[512,2048]{1,0:T(8,128)S(1)} fusion(bf16[512,512]{1,0:T(8,128)(2,1)S(1)} %copy-done.4, bf16[512,512]{1,0:T(8,128)(2,1)S(1)} %get-tuple-element.29, bf16[512,512]{1,0:T(8,128)(2,1)S(1)} %get-tuple-element.30, bf16[512,512]{1,0:T(8,128)(2,1)S(1)} %get-tuple-element.28, bf16[512,512]{1,0:T(8,128)(2,1)S(1)} %get-tuple-element.9), kind=kOutput, calls=%fused_computation.86 | convolution fusion | flops 1082130432 | bytes 6815744 | tf_op jit(solution)/shard_map/dot_general | solution.py:51
  63.4 1.3 %fusion.54 = f32[512,2048]{1,0:T(8,128)S(1)} fusion(bf16[512,512]{1,0:T(8,128)(2,1)S(1)} %copy-done.3, bf16[512,512]{1,0:T(8,128)(2,1)S(1)} %get-tuple-element.29, bf16[512,512]{1,0:T(8,128)(2,1)S(1)} %get-tuple-element.30, bf16[512,512]{1,0:T(8,128)(2,1)S(1)} %get-tuple-element.28, bf16[512,512]{1,0:T(8,128)(2,1)S(1)} %get-tuple-element.9), kind=kOutput, calls=%fused_computation.87 | convolution fusion | flops 1082130432 | bytes 6815744 | tf_op jit(solution)/shard_map/dot_general | solution.py:51
  64.7 1.2 %fusion.24 = (bf16[512,1024]{1,0:T(8,128)(2,1)S(1)}, bf16[512,1024]{1,0:T(8,128)(2,1)S(1)}) fusion(f32[512,2048]{1,0:T(8,128)S(1)} %fusion.53, f32[512,2048]{1,0:T(8,128)S(1)} %fusion.54), kind=kLoop, calls=%fused_computation.28 | loop fusion | flops 2097152 | bytes 10485760 | tf_op jit(solution)/shard_map/convert.20
  66.1 1.3 %fusion.89 = f32[2048,512]{1,0:T(8,128)S(1)} fusion(bf16[512,512]{1,0:T(8,128)(2,1)S(1)} %copy-done.4, bf16[512,512]{1,0:T(8,128)(2,1)S(1)} %get-tuple-element.46, bf16[512,512]{1,0:T(8,128)(2,1)S(1)} %get-tuple-element.45, bf16[512,512]{1,0:T(8,128)(2,1)S(1)} %get-tuple-element.44, bf16[512,512]{1,0:T(8,128)(2,1)S(1)} %get-tuple-element.43), kind=kOutput, calls=%fused_computation.193 | convolution fusion | flops 1082130432 | bytes 6815744 | tf_op jit(solution)/shard_map/dot_general | solution.py:51
  67.4 1.3 %fusion.90 = f32[2048,512]{1,0:T(8,128)S(1)} fusion(bf16[512,512]{1,0:T(8,128)(2,1)S(1)} %copy-done.3, bf16[512,512]{1,0:T(8,128)(2,1)S(1)} %get-tuple-element.46, bf16[512,512]{1,0:T(8,128)(2,1)S(1)} %get-tuple-element.45, bf16[512,512]{1,0:T(8,128)(2,1)S(1)} %get-tuple-element.44, bf16[512,512]{1,0:T(8,128)(2,1)S(1)} %get-tuple-element.43), kind=kOutput, calls=%fused_computation.194 | convolution fusion | flops 1082130432 | bytes 6815744 | tf_op jit(solution)/shard_map/dot_general | solution.py:51
  68.6 1.2 %fusion.88 = f32[2048,512]{1,0:T(8,128)S(1)} fusion(bf16[512,512]{1,0:T(8,128)(2,1)S(1)} %copy-done.5, bf16[512,512]{1,0:T(8,128)(2,1)S(1)} %get-tuple-element.46, bf16[512,512]{1,0:T(8,128)(2,1)S(1)} %get-tuple-element.45, bf16[512,512]{1,0:T(8,128)(2,1)S(1)} %get-tuple-element.44, bf16[512,512]{1,0:T(8,128)(2,1)S(1)} %get-tuple-element.43), kind=kOutput, calls=%fused_computation.192 | convolution fusion | flops 1082130432 | bytes 6815744 | tf_op jit(solution)/shard_map/dot_general | solution.py:51
  69.9 0.3 fusion.55
  70.3 0.2 fusion.94
  70.5 5.0 %collective-permute-start.4 = (bf16[4,512,128]{2,1,0:T(8,128)(2,1)S(1)}, bf16[4,512,128]{2,1,0:T(8,128)(2,1)S(1)}, u32[]{:S(2)}, u32[]{:S(2)}) collective-permute-start(bf16[4,512,128]{2,1,0:T(8,128)(2,1)S(1)} %get-tuple-element.42), channel_id=1, source_target_pairs={{1,0},{2,1},{3,2},{4,3},{5,4},{6,5},{7,6},{8,7},{9,8},{10,9},{11,1... | collective-permute-start | bytes 1572872 | tf_op jit(solution)/shard_map/ppermute | solution.py:17
  75.5 1.9 %collective-permute-start.3 = (bf16[4,512,128]{2,1,0:T(8,128)(2,1)S(1)}, bf16[4,512,128]{2,1,0:T(8,128)(2,1)S(1)}, u32[]{:S(2)}, u32[]{:S(2)}) collective-permute-start(bf16[4,512,128]{2,1,0:T(8,128)(2,1)S(1)} %get-tuple-element.41), channel_id=1, source_target_pairs={{0,1},{1,2},{2,3},{3,4},{4,5},{5,6},{6,7},{7,8},{8,9},{9,10},{10,1... | collective-permute-start | bytes 1572872 | tf_op jit(solution)/shard_map/ppermute | solution.py:17
  77.4 1.2 %fusion.45 = (bf16[1,512,512]{2,1,0:T(8,128)(2,1)S(1)}, bf16[1,512,512]{2,1,0:T(8,128)(2,1)S(1)}, bf16[1,512,512]{2,1,0:T(8,128)(2,1)S(1)}, bf16[1,512,512]{2,1,0:T(8,128)(2,1)S(1)}) fusion(f32[2048,512]{1,0:T(8,128)S(1)} %fusion.89, f32[2048,512]{1,0:T(8,128)S(1)} %fusion.90), kind=kLoop, calls=%fused_computation.74 | loop fusion | flops 2097152 | bytes 10485760 | tf_op jit(solution)/shard_map/stack | solution.py:112
  78.7 0.4 pad_maximum_fusion.4
  79.2 3.6 %collective-permute-start.1 = (bf16[4,128,512]{2,1,0:T(8,128)(2,1)S(1)}, bf16[4,128,512]{2,1,0:T(8,128)(2,1)S(1)}, u32[]{:S(2)}, u32[]{:S(2)}) collective-permute-start(bf16[4,128,512]{2,1,0:T(8,128)(2,1)S(1)} %get-tuple-element.31), channel_id=1, source_target_pairs={{0,16},{16,32},{32,48},{48,64},{64,80},{80,96},{96,112},{1,17},{17... | collective-permute-start | bytes 1572872 | tf_op jit(solution)/shard_map/ppermute | solution.py:17
  82.8 1.9 %collective-permute-start.2 = (bf16[4,128,512]{2,1,0:T(8,128)(2,1)S(1)}, bf16[4,128,512]{2,1,0:T(8,128)(2,1)S(1)}, u32[]{:S(2)}, u32[]{:S(2)}) collective-permute-start(bf16[4,128,512]{2,1,0:T(8,128)(2,1)S(1)} %get-tuple-element.32), channel_id=1, source_target_pairs={{16,0},{32,16},{48,32},{64,48},{80,64},{96,80},{112,96},{17,1},{33... | collective-permute-start | bytes 1572872 | tf_op jit(solution)/shard_map/ppermute | solution.py:17
  84.7 0.2 slice.341
  84.9 1.9 %collective-permute-done.4 = bf16[4,512,128]{2,1,0:T(8,128)(2,1)S(1)} collective-permute-done((bf16[4,512,128]{2,1,0:T(8,128)(2,1)S(1)}, bf16[4,512,128]{2,1,0:T(8,128)(2,1)S(1)}, u32[]{:S(2)}, u32[]{:S(2)}) %collective-permute-start.4) | collective-permute-done | bytes 524320 | tf_op jit(solution)/shard_map/ppermute | solution.py:17
  86.8 3.8 %collective-permute-done.3 = bf16[4,512,128]{2,1,0:T(8,128)(2,1)S(1)} collective-permute-done((bf16[4,512,128]{2,1,0:T(8,128)(2,1)S(1)}, bf16[4,512,128]{2,1,0:T(8,128)(2,1)S(1)}, u32[]{:S(2)}, u32[]{:S(2)}) %collective-permute-start.3) | collective-permute-done | bytes 524320 | tf_op jit(solution)/shard_map/ppermute | solution.py:17
  90.7 4.2 %collective-permute-start.5 = (bf16[4,128,256]{2,1,0:T(8,128)(2,1)S(1)}, bf16[4,128,256]{2,1,0:T(8,128)(2,1)S(1)}, u32[]{:S(2)}, u32[]{:S(2)}) collective-permute-start(bf16[4,128,256]{2,1,0:T(8,128)(2,1)S(1)} %pad_maximum_fusion.12), channel_id=1, source_target_pairs={{0,16},{16,32},{32,48},{48,64},{64,80},{80,96},{96,112},{1,17},{17... | collective-permute-start | bytes 786440 | tf_op jit(solution)/shard_map/ppermute | solution.py:17
  94.9 1.9 %collective-permute-start.6 = (bf16[4,128,256]{2,1,0:T(8,128)(2,1)S(1)}, bf16[4,128,256]{2,1,0:T(8,128)(2,1)S(1)}, u32[]{:S(2)}, u32[]{:S(2)}) collective-permute-start(bf16[4,128,256]{2,1,0:T(8,128)(2,1)S(1)} %pad_maximum_fusion.13), channel_id=1, source_target_pairs={{16,0},{32,16},{48,32},{64,48},{80,64},{96,80},{112,96},{17,1},{33... | collective-permute-start | bytes 786440 | tf_op jit(solution)/shard_map/ppermute | solution.py:17
  96.9 0.3 fusion.36
  97.2 0.4 pad_maximum_fusion
  97.9 1.8 %copy-done.2 = f32[4,512,512]{2,1,0:T(8,128)} copy-done((f32[4,512,512]{2,1,0:T(8,128)}, f32[4,512,512]{2,1,0:T(8,128)S(1)}, u32[]{:S(2)}) %copy-start.2) | copy-done | bytes 4194328
  99.7 2.9 %collective-permute-done.6 = bf16[4,128,256]{2,1,0:T(8,128)(2,1)S(1)} collective-permute-done((bf16[4,128,256]{2,1,0:T(8,128)(2,1)S(1)}, bf16[4,128,256]{2,1,0:T(8,128)(2,1)S(1)}, u32[]{:S(2)}, u32[]{:S(2)}) %collective-permute-start.6) | collective-permute-done | bytes 262176 | tf_op jit(solution)/shard_map/ppermute | solution.py:17
  102.6 0.2 fusion.60
  102.9 0.2 fusion.34
  103.1 1.3 %slice-done = f32[4,512,256]{2,1,0:T(8,128)S(1)} async-done(((f32[4,512,512]{2,1,0:T(8,128)}), f32[4,512,256]{2,1,0:T(8,128)S(1)}, s32[]{:S(2)}) %slice-start) | async-done | bytes 2097176 | tf_op jit(solution)/shard_map/slice | solution.py:260
  104.4 2.5 %pad_maximum_fusion.1 = f32[4,512,512]{2,1,0:T(8,128)} fusion(f32[4,512,128]{2,1,0:T(8,128)S(1)} %get-tuple-element.21, f32[4,512,256]{2,1,0:T(8,128)S(1)} %slice-done, f32[4,512,128]{2,1,0:T(8,128)S(1)} %get-tuple-element.20), kind=kLoop, calls=%fused_computation.15 | loop fusion | flops 2097152 | bytes 8388608 | tf_op jit(solution)/shard_map/concatenate | solution.py:259
  (74 shorter events, 3.0 us)
Async XLA Ops:
  0.0 2.9 %copy-start = (bf16[2352,128]{1,0:T(8,128)(2,1)S(1)}, bf16[2352,128]{1,0:T(8,128)(2,1)}, u32[]{:S(2)}) copy-start(bf16[2352,128]{1,0:T(8,128)(2,1)} %param.6) | copy-start | bytes 1806340
  15.9 29.7 %all-to-all-start = ((bf16[16,2,208,128]{3,2,1,0:T(8,128)(2,1)}), bf16[16,2,208,128]{3,2,1,0:T(8,128)(2,1)S(1)}, u32[]{:S(2)}, u32[]{:S(2)}) async-start(bf16[16,2,208,128]{3,2,1,0:T(8,128)(2,1)} %pad_maximum_fusion.5), calls=%async_computation | async-start | bytes 3407872 | tf_op jit(solution)/shard_map/all_to_all | solution.py:212
  48.9 8.1 %collective-permute-start = (bf16[1,528,128]{2,1,0:T(8,128)(2,1)S(1)}, bf16[1,528,128]{2,1,0:T(8,128)(2,1)S(1)}, u32[]{:S(2)}, u32[]{:S(2)}) collective-permute-start(bf16[1,528,128]{2,1,0:T(8,128)(2,1)S(1)} %maximum_maximum_fusion), channel_id=1, source_target_pairs={{16,0},{32,16},{48,32},{64,48},{80,64},{96,80},{112,96},{17,1},{33... | collective-permute-start | bytes 405512 | tf_op jit(solution)/shard_map/ppermute | solution.py:17
  53.2 5.2 %copy-start.4 = (bf16[512,512]{1,0:T(8,128)(2,1)S(1)}, bf16[512,512]{1,0:T(8,128)(2,1)}, u32[]{:S(2)}) copy-start(bf16[512,512]{1,0:T(8,128)(2,1)} %constant.124.clone) | copy-start | bytes 1572868
  56.9 2.0 %copy-start.3 = (bf16[512,512]{1,0:T(8,128)(2,1)S(1)}, bf16[512,512]{1,0:T(8,128)(2,1)}, u32[]{:S(2)}) copy-start(bf16[512,512]{1,0:T(8,128)(2,1)} %constant.123.clone) | copy-start | bytes 1572868
  67.4 1.3 %copy-start.5 = (bf16[512,512]{1,0:T(8,128)(2,1)S(1)}, bf16[512,512]{1,0:T(8,128)(2,1)}, u32[]{:S(2)}) copy-start(bf16[512,512]{1,0:T(8,128)(2,1)} %constant.133) | copy-start | bytes 1572868
  70.5 16.3 %collective-permute-start.4 = (bf16[4,512,128]{2,1,0:T(8,128)(2,1)S(1)}, bf16[4,512,128]{2,1,0:T(8,128)(2,1)S(1)}, u32[]{:S(2)}, u32[]{:S(2)}) collective-permute-start(bf16[4,512,128]{2,1,0:T(8,128)(2,1)S(1)} %get-tuple-element.42), channel_id=1, source_target_pairs={{1,0},{2,1},{3,2},{4,3},{5,4},{6,5},{7,6},{8,7},{9,8},{10,9},{11,1... | collective-permute-start | bytes 1572872 | tf_op jit(solution)/shard_map/ppermute | solution.py:17
  75.5 15.1 %collective-permute-start.3 = (bf16[4,512,128]{2,1,0:T(8,128)(2,1)S(1)}, bf16[4,512,128]{2,1,0:T(8,128)(2,1)S(1)}, u32[]{:S(2)}, u32[]{:S(2)}) collective-permute-start(bf16[4,512,128]{2,1,0:T(8,128)(2,1)S(1)} %get-tuple-element.41), channel_id=1, source_target_pairs={{0,1},{1,2},{2,3},{3,4},{4,5},{5,6},{6,7},{7,8},{8,9},{9,10},{10,1... | collective-permute-start | bytes 1572872 | tf_op jit(solution)/shard_map/ppermute | solution.py:17
  79.2 17.7 %collective-permute-start.1 = (bf16[4,128,512]{2,1,0:T(8,128)(2,1)S(1)}, bf16[4,128,512]{2,1,0:T(8,128)(2,1)S(1)}, u32[]{:S(2)}, u32[]{:S(2)}) collective-permute-start(bf16[4,128,512]{2,1,0:T(8,128)(2,1)S(1)} %get-tuple-element.31), channel_id=1, source_target_pairs={{0,16},{16,32},{32,48},{48,64},{64,80},{80,96},{96,112},{1,17},{17... | collective-permute-start | bytes 1572872 | tf_op jit(solution)/shard_map/ppermute | solution.py:17
  82.8 14.1 %collective-permute-start.2 = (bf16[4,128,512]{2,1,0:T(8,128)(2,1)S(1)}, bf16[4,128,512]{2,1,0:T(8,128)(2,1)S(1)}, u32[]{:S(2)}, u32[]{:S(2)}) collective-permute-start(bf16[4,128,512]{2,1,0:T(8,128)(2,1)S(1)} %get-tuple-element.32), channel_id=1, source_target_pairs={{16,0},{32,16},{48,32},{64,48},{80,64},{96,80},{112,96},{17,1},{33... | collective-permute-start | bytes 1572872 | tf_op jit(solution)/shard_map/ppermute | solution.py:17
  90.7 9.0 %collective-permute-start.5 = (bf16[4,128,256]{2,1,0:T(8,128)(2,1)S(1)}, bf16[4,128,256]{2,1,0:T(8,128)(2,1)S(1)}, u32[]{:S(2)}, u32[]{:S(2)}) collective-permute-start(bf16[4,128,256]{2,1,0:T(8,128)(2,1)S(1)} %pad_maximum_fusion.12), channel_id=1, source_target_pairs={{0,16},{16,32},{32,48},{48,64},{64,80},{80,96},{96,112},{1,17},{17... | collective-permute-start | bytes 786440 | tf_op jit(solution)/shard_map/ppermute | solution.py:17
  94.9 7.7 %collective-permute-start.6 = (bf16[4,128,256]{2,1,0:T(8,128)(2,1)S(1)}, bf16[4,128,256]{2,1,0:T(8,128)(2,1)S(1)}, u32[]{:S(2)}, u32[]{:S(2)}) collective-permute-start(bf16[4,128,256]{2,1,0:T(8,128)(2,1)S(1)} %pad_maximum_fusion.13), channel_id=1, source_target_pairs={{16,0},{32,16},{48,32},{64,48},{80,64},{96,80},{112,96},{17,1},{33... | collective-permute-start | bytes 786440 | tf_op jit(solution)/shard_map/ppermute | solution.py:17
  97.7 2.0 %copy-start.2 = (f32[4,512,512]{2,1,0:T(8,128)}, f32[4,512,512]{2,1,0:T(8,128)S(1)}, u32[]{:S(2)}) copy-start(f32[4,512,512]{2,1,0:T(8,128)S(1)} %pad_maximum_fusion) | copy-start | bytes 12582916
  102.9 1.6 %slice-start = ((f32[4,512,512]{2,1,0:T(8,128)}), f32[4,512,256]{2,1,0:T(8,128)S(1)}, s32[]{:S(2)}) async-start(f32[4,512,512]{2,1,0:T(8,128)} %copy-done.2), calls=%async_computation.1 | async-start | bytes 4194304 | tf_op jit(solution)/shard_map/slice | solution.py:260
  103.1 3.9 %copy-start.1 = (bf16[2352,128]{1,0:T(8,128)(2,1)S(1)}, bf16[2352,128]{1,0:T(8,128)(2,1)}, u32[]{:S(2)}) copy-start(bf16[2352,128]{1,0:T(8,128)(2,1)} %param.6) | copy-start | bytes 1806340

commit v11 on v10

--- a/solution.py
+++ b/solution.py
@@ -246,19 +246,27 @@
     left_weight = jnp.where(column_index > 0, ramp, 1.0)[None, None, :]
     right_weight = jnp.where(column_index < cols_axis - 1, ramp[::-1], 1.0)[None, None, :]
     f32 = lambda x: x.astype(jnp.float32)
-    inner = row_blend(f32(fields), f32(above), f32(below), top_weight, bottom_weight, width)
-    left_strip = row_blend(
-        f32(left), f32(above_left), f32(below_left), top_weight, bottom_weight, width
-    )
-    right_strip = row_blend(
-        f32(right), f32(above_right), f32(below_right), top_weight, bottom_weight, width
-    )
-    col_count = inner.shape[2]
-    left_band = left_weight * inner[:, :, :width] + (1.0 - left_weight) * left_strip
-    right_band = right_weight * inner[:, :, col_count - width :] + (1.0 - right_weight) * right_strip
-    return jnp.concatenate(
-        [left_band, inner[:, :, width : col_count - width], right_band], axis=2
-    )
+    count = fields.shape[1]
+    ones = jnp.ones((count - 2 * width,), jnp.float32)
+    row_weight = jnp.concatenate([top_weight[0, :, 0], ones, bottom_weight[0, :, 0]])[:, None]
+    col_weight = jnp.concatenate([left_weight[0, 0], ones, right_weight[0, 0]])[None, :]
+    zero_rows = jnp.zeros((fields.shape[0], count - 2 * width, 1), jnp.float32)
+    vertical = jnp.concatenate(
+        [f32(above), jnp.broadcast_to(zero_rows, (fields.shape[0], count - 2 * width, count)),
+         f32(below)], axis=1
+    )
+    rows_done = row_weight * f32(fields) + (1.0 - row_weight) * vertical
+    side = lambda strip, upper, lower: row_weight * f32(strip) + (1.0 - row_weight) * jnp.concatenate(
+        [f32(upper), jnp.broadcast_to(zero_rows, (fields.shape[0], count - 2 * width, width)),
+         f32(lower)], axis=1
+    )
+    left_rows = side(left, above_left, below_left)
+    right_rows = side(right, above_right, below_right)
+    horizontal = jnp.concatenate(
+        [left_rows, jnp.broadcast_to(zero_rows[:, :1], (fields.shape[0], count, count - 2 * width)),
+         right_rows], axis=2
+    )
+    return col_weight * rows_done + (1.0 - col_weight) * horizontal
 
 
 def solution(mesh):

time: 107 us -> 105 us (0.981)
  the two profiles are of different devices: /device:TPU:11 before, /device:TPU:40 now
where the time goes in v11:
time: 105 us
  waiting for transfers between devices  37.3 us (36%)
  matrix products  25.8 us (25%)
  starting transfers between devices  24.5 us (23%)
  other arithmetic  13.2 us (13%)
  local copies, waits for them, and re-layouts  3.45 us (3%)
    all_to_all x1, waiting for transfers between devices, on_device(): lax.all_to_all(jnp.stack([same_sent, rise_sent], axis=1), 'py', 0, 0, til...  24 us
    ppermute x7, starting transfers between devices, shifted(): return lax.ppermute(shard, axis, pairs)  16.6 us
    ppermute x7, waiting for transfers between devices, shifted(): return lax.ppermute(shard, axis, pairs)  13.4 us
    dot_general x2, matrix products, gathered_rows(): jnp.dot(chosen.astype(table_rows.dtype), table_rows, preferred_element_ty...  11.2 us
    dot_general x9, matrix products, dot32(): return jnp.dot(a, b, preferred_element_type=jnp.float32)  8.77 us
    all_to_all x1, starting transfers between devices, on_device(): lax.all_to_all(jnp.stack([same_sent, rise_sent], axis=1), 'py', 0, 0, til...  7.89 us
    dot_general x3, matrix products, one_hot_rows(): jnp.dot(picks.astype(values.dtype), values, preferred_element_type=jnp.fl...  5.81 us
    add x1, other arithmetic, on_device(): return col_weight * rows_done + (1.0 - col_weight) * horizontal  3.54 us
  transfers between devices with their start and end apart: 8, of which 5 were waited for; matrix products, arithmetic and copies ran while one was open for 6% of the time, Pallas kernels for 0%

profile of v11, /device:TPU:40, one launch (start us, length us, event | category | flops | bytes accessed | tf_op | source)
XLA Modules:
  0.0 104.8 jit_solution(15168792521929277358)
XLA Ops:
  0.0 1.3 %constant_dynamic-slice_fusion.3 = (s32[1,16,192]{1,2,0:T(8,128)S(1)}, s32[1,16,192]{1,2,0:T(8,128)S(1)}, s32[1,16,192]{1,2,0:T(8,128)S(1)}, s32[1,16,192]{1,2,0:T(8,128)S(1)}) fusion(s32[1,128,192]{1,2,0:T(8,128)} %param.8, s32[]{:T(128)S(6)} %select_n.142, s32[]{:T(128)S(6)} %select_n.146, s32[1,128,192]{1,2,0:T(8,128)} %param.7), kind=kLoop, calls=%fused_computation.162 | loop fusion | bytes 98312 | tf_op jit(solution)/shard_map/dynamic_slice | solution.py:201
  1.3 0.8 fusion.82
  2.9 5.6 %fusion.17 = bf16[3072,128]{1,0:T(8,128)(2,1)S(1)} fusion(bf16[2352,128]{1,0:T(8,128)(2,1)S(1)} %copy-done, s32[3072]{0:T(1024)S(1)} %eq.43), kind=kOutput, calls=%fused_computation.22 | convolution fusion | flops 1857306624 | bytes 1400832 | tf_op jit(solution)/shard_map/dot_general | solution.py:154
  8.5 5.6 %fusion.16 = bf16[3072,128]{1,0:T(8,128)(2,1)S(1)} fusion(bf16[2352,128]{1,0:T(8,128)(2,1)S(1)} %copy-done, s32[3072]{0:T(1024)S(1)} %eq.89), kind=kOutput, calls=%fused_computation.21 | convolution fusion | flops 1857306624 | bytes 1400832 | tf_op jit(solution)/shard_map/dot_general | solution.py:154
  14.2 0.4 maximum_bitcast_fusion
  14.6 1.3 %pad_maximum_fusion.3 = bf16[16,2,208,128]{3,2,1,0:T(8,128)(2,1)} fusion(bf16[16,1,208,128]{3,2,1,0:T(8,128)(2,1)S(1)} %get-tuple-element.62, bf16[16,1,208,128]{3,2,1,0:T(8,128)(2,1)S(1)} %get-tuple-element.61), kind=kLoop, calls=%fused_computation.37 | loop fusion | flops 851968 | bytes 3407872 | tf_op jit(solution)/shard_map/stack | solution.py:212
  15.9 7.9 %all-to-all-start = ((bf16[16,2,208,128]{3,2,1,0:T(8,128)(2,1)}), bf16[16,2,208,128]{3,2,1,0:T(8,128)(2,1)S(1)}, u32[]{:S(2)}, u32[]{:S(2)}) async-start(bf16[16,2,208,128]{3,2,1,0:T(8,128)(2,1)} %pad_maximum_fusion.3), calls=%async_computation | async-start | bytes 3407872 | tf_op jit(solution)/shard_map/all_to_all | solution.py:212
  24.1 24.0 %all-to-all-done = bf16[16,2,208,128]{3,2,1,0:T(8,128)(2,1)S(1)} async-done(((bf16[16,2,208,128]{3,2,1,0:T(8,128)(2,1)}), bf16[16,2,208,128]{3,2,1,0:T(8,128)(2,1)S(1)}, u32[]{:S(2)}, u32[]{:S(2)}) %all-to-all-start) | async-done | bytes 1703968 | tf_op jit(solution)/shard_map/all_to_all | solution.py:212
  48.8 0.3 reduce-window.9
  49.2 0.1 slice_reduce_fusion
  49.4 0.8 fusion.10
  50.1 1.0 fusion.33
  51.2 0.1 maximum_maximum_fusion
  51.3 2.1 %collective-permute-start = (bf16[1,528,128]{2,1,0:T(8,128)(2,1)S(1)}, bf16[1,528,128]{2,1,0:T(8,128)(2,1)S(1)}, u32[]{:S(2)}, u32[]{:S(2)}) collective-permute-start(bf16[1,528,128]{2,1,0:T(8,128)(2,1)S(1)} %maximum_maximum_fusion), channel_id=1, source_target_pairs={{16,0},{32,16},{48,32},{64,48},{80,64},{96,80},{112,96},{17,1},{33... | collective-permute-start | bytes 405512 | tf_op jit(solution)/shard_map/ppermute | solution.py:17
  53.4 3.7 %fusion.2 = f32[2048,128]{1,0:T(8,128)S(1)} fusion(bf16[3072,128]{1,0:T(8,128)(2,1)S(1)} %bitcast.112, s32[3072]{0:T(1024)S(1)} %eq.93, s32[2048]{0:T(1024)S(1)} %iota_add_fusion), kind=kOutput, calls=%fused_computation.4 | convolution fusion | flops 1616904192 | bytes 1855488 | tf_op jit(solution)/shard_map/dot_general | solution.py:149
  57.2 1.1 %fusion.23 = bf16[2048,128]{1,0:T(8,128)(2,1)S(1)} fusion(f32[2048,128]{1,0:T(8,128)S(1)} %fusion.2, s32[512]{0:T(512)S(1)} %bitcast.121, s32[2048]{0:T(1024)S(1)} %iota_add_fusion, bf16[1,528,128]{2,1,0:T(8,128)(2,1)S(1)} %collective-permute-done), kind=kOutput, calls=%fused_computation.27 | convolution fusion | flops 270008320 | bytes 1714176 | tf_op jit(solution)/shard_map/dot_general | solution.py:149
  58.3 0.3 reshape.309
  58.6 0.5 convolution_convert_fusion
  59.1 0.5 convolution_convert_fusion.1
  59.6 0.7 fusion.45
  60.4 0.7 fusion.44
  61.1 0.3 multiply_convert_fusion.3
  61.4 1.0 multiply_convert_fusion.2
  62.4 1.3 %fusion.54 = f32[512,2048]{1,0:T(8,128)S(1)} fusion(bf16[512,512]{1,0:T(8,128)(2,1)S(1)} %copy-done.3, bf16[512,512]{1,0:T(8,128)(2,1)S(1)} %get-tuple-element.21, bf16[512,512]{1,0:T(8,128)(2,1)S(1)} %get-tuple-element.22, bf16[512,512]{1,0:T(8,128)(2,1)S(1)} %get-tuple-element.20, bf16[512,512]{1,0:T(8,128)(2,1)S(1)} %get-tuple-element.5), kind=kOutput, calls=%fused_computation.83 | convolution fusion | flops 1082130432 | bytes 6815744 | tf_op jit(solution)/shard_map/dot_general | solution.py:51
  63.7 1.3 %fusion.55 = f32[512,2048]{1,0:T(8,128)S(1)} fusion(bf16[512,512]{1,0:T(8,128)(2,1)S(1)} %copy-done.2, bf16[512,512]{1,0:T(8,128)(2,1)S(1)} %get-tuple-element.21, bf16[512,512]{1,0:T(8,128)(2,1)S(1)} %get-tuple-element.22, bf16[512,512]{1,0:T(8,128)(2,1)S(1)} %get-tuple-element.20, bf16[512,512]{1,0:T(8,128)(2,1)S(1)} %get-tuple-element.5), kind=kOutput, calls=%fused_computation.84 | convolution fusion | flops 1082130432 | bytes 6815744 | tf_op jit(solution)/shard_map/dot_general | solution.py:51
  64.9 1.2 %fusion.27 = (bf16[512,1024]{1,0:T(8,128)(2,1)S(1)}, bf16[512,1024]{1,0:T(8,128)(2,1)S(1)}) fusion(f32[512,2048]{1,0:T(8,128)S(1)} %fusion.54, f32[512,2048]{1,0:T(8,128)S(1)} %fusion.55), kind=kLoop, calls=%fused_computation.31 | loop fusion | flops 2097152 | bytes 10485760 | tf_op jit(solution)/shard_map/convert.20
  66.3 1.3 %fusion.88 = f32[2048,512]{1,0:T(8,128)S(1)} fusion(bf16[512,512]{1,0:T(8,128)(2,1)S(1)} %copy-done.3, bf16[512,512]{1,0:T(8,128)(2,1)S(1)} %get-tuple-element.32, bf16[512,512]{1,0:T(8,128)(2,1)S(1)} %get-tuple-element.31, bf16[512,512]{1,0:T(8,128)(2,1)S(1)} %get-tuple-element.30, bf16[512,512]{1,0:T(8,128)(2,1)S(1)} %get-tuple-element.29), kind=kOutput, calls=%fused_computation.188 | convolution fusion | flops 1082130432 | bytes 6815744 | tf_op jit(solution)/shard_map/dot_general | solution.py:51
  67.6 1.3 %fusion.89 = f32[2048,512]{1,0:T(8,128)S(1)} fusion(bf16[512,512]{1,0:T(8,128)(2,1)S(1)} %copy-done.2, bf16[512,512]{1,0:T(8,128)(2,1)S(1)} %get-tuple-element.32, bf16[512,512]{1,0:T(8,128)(2,1)S(1)} %get-tuple-element.31, bf16[512,512]{1,0:T(8,128)(2,1)S(1)} %get-tuple-element.30, bf16[512,512]{1,0:T(8,128)(2,1)S(1)} %get-tuple-element.29), kind=kOutput, calls=%fused_computation.189 | convolution fusion | flops 1082130432 | bytes 6815744 | tf_op jit(solution)/shard_map/dot_general | solution.py:51
  68.9 1.2 %fusion.87 = f32[2048,512]{1,0:T(8,128)S(1)} fusion(bf16[512,512]{1,0:T(8,128)(2,1)S(1)} %copy-done.4, bf16[512,512]{1,0:T(8,128)(2,1)S(1)} %get-tuple-element.32, bf16[512,512]{1,0:T(8,128)(2,1)S(1)} %get-tuple-element.31, bf16[512,512]{1,0:T(8,128)(2,1)S(1)} %get-tuple-element.30, bf16[512,512]{1,0:T(8,128)(2,1)S(1)} %get-tuple-element.29), kind=kOutput, calls=%fused_computation.187 | convolution fusion | flops 1082130432 | bytes 6815744 | tf_op jit(solution)/shard_map/dot_general | solution.py:51
  70.1 0.3 fusion.56
  70.4 0.1 pad_maximum_fusion.5
  70.6 0.2 fusion.92
  70.7 2.0 %collective-permute-start.4 = (bf16[4,512,128]{2,1,0:T(8,128)(2,1)S(1)}, bf16[4,512,128]{2,1,0:T(8,128)(2,1)S(1)}, u32[]{:S(2)}, u32[]{:S(2)}) collective-permute-start(bf16[4,512,128]{2,1,0:T(8,128)(2,1)S(1)} %get-tuple-element.28), channel_id=1, source_target_pairs={{1,0},{2,1},{3,2},{4,3},{5,4},{6,5},{7,6},{8,7},{9,8},{10,9},{11,1... | collective-permute-start | bytes 1572872 | tf_op jit(solution)/shard_map/ppermute | solution.py:17
  72.8 3.8 %collective-permute-start.3 = (bf16[4,512,128]{2,1,0:T(8,128)(2,1)S(1)}, bf16[4,512,128]{2,1,0:T(8,128)(2,1)S(1)}, u32[]{:S(2)}, u32[]{:S(2)}) collective-permute-start(bf16[4,512,128]{2,1,0:T(8,128)(2,1)S(1)} %get-tuple-element.27), channel_id=1, source_target_pairs={{0,1},{1,2},{2,3},{3,4},{4,5},{5,6},{6,7},{7,8},{8,9},{9,10},{10,1... | collective-permute-start | bytes 1572872 | tf_op jit(solution)/shard_map/ppermute | solution.py:17
  76.6 1.2 %fusion.46 = (bf16[1,512,512]{2,1,0:T(8,128)(2,1)S(1)}, bf16[1,512,512]{2,1,0:T(8,128)(2,1)S(1)}, bf16[1,512,512]{2,1,0:T(8,128)(2,1)S(1)}, bf16[1,512,512]{2,1,0:T(8,128)(2,1)S(1)}) fusion(f32[2048,512]{1,0:T(8,128)S(1)} %fusion.88, f32[2048,512]{1,0:T(8,128)S(1)} %fusion.89), kind=kLoop, calls=%fused_computation.71 | loop fusion | flops 2097152 | bytes 10485760 | tf_op jit(solution)/shard_map/stack | solution.py:112
  77.9 0.3 pad_maximum_fusion.2
  78.2 1.9 %collective-permute-start.2 = (bf16[4,128,512]{2,1,0:T(8,128)(2,1)S(1)}, bf16[4,128,512]{2,1,0:T(8,128)(2,1)S(1)}, u32[]{:S(2)}, u32[]{:S(2)}) collective-permute-start(bf16[4,128,512]{2,1,0:T(8,128)(2,1)S(1)} %get-tuple-element.24), channel_id=1, source_target_pairs={{16,0},{32,16},{48,32},{64,48},{80,64},{96,80},{112,96},{17,1},{33... | collective-permute-start | bytes 1572872 | tf_op jit(solution)/shard_map/ppermute | solution.py:17
  80.1 2.4 %collective-permute-start.1 = (bf16[4,128,512]{2,1,0:T(8,128)(2,1)S(1)}, bf16[4,128,512]{2,1,0:T(8,128)(2,1)S(1)}, u32[]{:S(2)}, u32[]{:S(2)}) collective-permute-start(bf16[4,128,512]{2,1,0:T(8,128)(2,1)S(1)} %get-tuple-element.23), channel_id=1, source_target_pairs={{0,16},{16,32},{32,48},{48,64},{64,80},{80,96},{96,112},{1,17},{17... | collective-permute-start | bytes 1572872 | tf_op jit(solution)/shard_map/ppermute | solution.py:17
  82.6 4.4 %collective-permute-done.4 = bf16[4,512,128]{2,1,0:T(8,128)(2,1)S(1)} collective-permute-done((bf16[4,512,128]{2,1,0:T(8,128)(2,1)S(1)}, bf16[4,512,128]{2,1,0:T(8,128)(2,1)S(1)}, u32[]{:S(2)}, u32[]{:S(2)}) %collective-permute-start.4) | collective-permute-done | bytes 524320 | tf_op jit(solution)/shard_map/ppermute | solution.py:17
  87.0 4.0 %collective-permute-done.3 = bf16[4,512,128]{2,1,0:T(8,128)(2,1)S(1)} collective-permute-done((bf16[4,512,128]{2,1,0:T(8,128)(2,1)S(1)}, bf16[4,512,128]{2,1,0:T(8,128)(2,1)S(1)}, u32[]{:S(2)}, u32[]{:S(2)}) %collective-permute-start.3) | collective-permute-done | bytes 524320 | tf_op jit(solution)/shard_map/ppermute | solution.py:17
  91.1 1.9 %collective-permute-start.6 = (bf16[4,128,256]{2,1,0:T(8,128)(2,1)S(1)}, bf16[4,128,256]{2,1,0:T(8,128)(2,1)S(1)}, u32[]{:S(2)}, u32[]{:S(2)}) collective-permute-start(bf16[4,128,256]{2,1,0:T(8,128)(2,1)S(1)} %pad_maximum_fusion.11), channel_id=1, source_target_pairs={{16,0},{32,16},{48,32},{64,48},{80,64},{96,80},{112,96},{17,1},{33... | collective-permute-start | bytes 786440 | tf_op jit(solution)/shard_map/ppermute | solution.py:17
  93.1 2.4 %collective-permute-start.5 = (bf16[4,128,256]{2,1,0:T(8,128)(2,1)S(1)}, bf16[4,128,256]{2,1,0:T(8,128)(2,1)S(1)}, u32[]{:S(2)}, u32[]{:S(2)}) collective-permute-start(bf16[4,128,256]{2,1,0:T(8,128)(2,1)S(1)} %pad_maximum_fusion.10), channel_id=1, source_target_pairs={{0,16},{16,32},{32,48},{48,64},{64,80},{80,96},{96,112},{1,17},{17... | collective-permute-start | bytes 786440 | tf_op jit(solution)/shard_map/ppermute | solution.py:17
  95.6 0.1 convert_element_type.165
  95.7 0.1 convert_element_type.164
  95.8 1.1 %collective-permute-done.6 = bf16[4,128,256]{2,1,0:T(8,128)(2,1)S(1)} collective-permute-done((bf16[4,128,256]{2,1,0:T(8,128)(2,1)S(1)}, bf16[4,128,256]{2,1,0:T(8,128)(2,1)S(1)}, u32[]{:S(2)}, u32[]{:S(2)}) %collective-permute-start.6) | collective-permute-done | bytes 262176 | tf_op jit(solution)/shard_map/ppermute | solution.py:17
  96.9 3.8 %collective-permute-done.5 = bf16[4,128,256]{2,1,0:T(8,128)(2,1)S(1)} collective-permute-done((bf16[4,128,256]{2,1,0:T(8,128)(2,1)S(1)}, bf16[4,128,256]{2,1,0:T(8,128)(2,1)S(1)}, u32[]{:S(2)}, u32[]{:S(2)}) %collective-permute-start.5) | collective-permute-done | bytes 262176 | tf_op jit(solution)/shard_map/ppermute | solution.py:17
  100.8 0.4 fusion.41
  101.2 3.5 %fusion.13 = f32[4,512,512]{2,1,0:T(8,128)} fusion(f32[4,128,512]{2,1,0:T(8,128)S(1)} %convert_element_type.165, f32[4,128,512]{2,1,0:T(8,128)S(1)} %convert_element_type.164, f32[4,512,128]{2,1,0:T(8,128)S(1)} %get-tuple-element.50, f32[4,512,128]{2,1,0:T(8,128)S(1)} %get-tuple-element.49, f32[512]{0:T(512)S(1)} %pad.18.clone, ...), kind=kLoop, calls=%fused_computation.17 | loop fusion | flops 14680064 | bytes 10496000 | tf_op jit(solution)/shard_map/add | solution.py:269
  (69 shorter events, 2.4 us)
Async XLA Ops:
  0.0 2.9 %copy-start = (bf16[2352,128]{1,0:T(8,128)(2,1)S(1)}, bf16[2352,128]{1,0:T(8,128)(2,1)}, u32[]{:S(2)}) copy-start(bf16[2352,128]{1,0:T(8,128)(2,1)} %param.6) | copy-start | bytes 1806340
  15.9 32.1 %all-to-all-start = ((bf16[16,2,208,128]{3,2,1,0:T(8,128)(2,1)}), bf16[16,2,208,128]{3,2,1,0:T(8,128)(2,1)S(1)}, u32[]{:S(2)}, u32[]{:S(2)}) async-start(bf16[16,2,208,128]{3,2,1,0:T(8,128)(2,1)} %pad_maximum_fusion.3), calls=%async_computation | async-start | bytes 3407872 | tf_op jit(solution)/shard_map/all_to_all | solution.py:212
  51.3 5.8 %collective-permute-start = (bf16[1,528,128]{2,1,0:T(8,128)(2,1)S(1)}, bf16[1,528,128]{2,1,0:T(8,128)(2,1)S(1)}, u32[]{:S(2)}, u32[]{:S(2)}) collective-permute-start(bf16[1,528,128]{2,1,0:T(8,128)(2,1)S(1)} %maximum_maximum_fusion), channel_id=1, source_target_pairs={{16,0},{32,16},{48,32},{64,48},{80,64},{96,80},{112,96},{17,1},{33... | collective-permute-start | bytes 405512 | tf_op jit(solution)/shard_map/ppermute | solution.py:17
  53.4 5.2 %copy-start.3 = (bf16[512,512]{1,0:T(8,128)(2,1)S(1)}, bf16[512,512]{1,0:T(8,128)(2,1)}, u32[]{:S(2)}) copy-start(bf16[512,512]{1,0:T(8,128)(2,1)} %constant.128.clone) | copy-start | bytes 1572868
  57.2 2.0 %copy-start.2 = (bf16[512,512]{1,0:T(8,128)(2,1)S(1)}, bf16[512,512]{1,0:T(8,128)(2,1)}, u32[]{:S(2)}) copy-start(bf16[512,512]{1,0:T(8,128)(2,1)} %constant.127.clone) | copy-start | bytes 1572868
  67.6 1.3 %copy-start.4 = (bf16[512,512]{1,0:T(8,128)(2,1)S(1)}, bf16[512,512]{1,0:T(8,128)(2,1)}, u32[]{:S(2)}) copy-start(bf16[512,512]{1,0:T(8,128)(2,1)} %constant.137) | copy-start | bytes 1572868
  70.7 16.2 %collective-permute-start.4 = (bf16[4,512,128]{2,1,0:T(8,128)(2,1)S(1)}, bf16[4,512,128]{2,1,0:T(8,128)(2,1)S(1)}, u32[]{:S(2)}, u32[]{:S(2)}) collective-permute-start(bf16[4,512,128]{2,1,0:T(8,128)(2,1)S(1)} %get-tuple-element.28), channel_id=1, source_target_pairs={{1,0},{2,1},{3,2},{4,3},{5,4},{6,5},{7,6},{8,7},{9,8},{10,9},{11,1... | collective-permute-start | bytes 1572872 | tf_op jit(solution)/shard_map/ppermute | solution.py:17
  72.8 18.3 %collective-permute-start.3 = (bf16[4,512,128]{2,1,0:T(8,128)(2,1)S(1)}, bf16[4,512,128]{2,1,0:T(8,128)(2,1)S(1)}, u32[]{:S(2)}, u32[]{:S(2)}) collective-permute-start(bf16[4,512,128]{2,1,0:T(8,128)(2,1)S(1)} %get-tuple-element.27), channel_id=1, source_target_pairs={{0,1},{1,2},{2,3},{3,4},{4,5},{5,6},{6,7},{7,8},{8,9},{9,10},{10,1... | collective-permute-start | bytes 1572872 | tf_op jit(solution)/shard_map/ppermute | solution.py:17
  78.2 17.3 %collective-permute-start.2 = (bf16[4,128,512]{2,1,0:T(8,128)(2,1)S(1)}, bf16[4,128,512]{2,1,0:T(8,128)(2,1)S(1)}, u32[]{:S(2)}, u32[]{:S(2)}) collective-permute-start(bf16[4,128,512]{2,1,0:T(8,128)(2,1)S(1)} %get-tuple-element.24), channel_id=1, source_target_pairs={{16,0},{32,16},{48,32},{64,48},{80,64},{96,80},{112,96},{17,1},{33... | collective-permute-start | bytes 1572872 | tf_op jit(solution)/shard_map/ppermute | solution.py:17
  80.1 15.5 %collective-permute-start.1 = (bf16[4,128,512]{2,1,0:T(8,128)(2,1)S(1)}, bf16[4,128,512]{2,1,0:T(8,128)(2,1)S(1)}, u32[]{:S(2)}, u32[]{:S(2)}) collective-permute-start(bf16[4,128,512]{2,1,0:T(8,128)(2,1)S(1)} %get-tuple-element.23), channel_id=1, source_target_pairs={{0,16},{16,32},{32,48},{48,64},{64,80},{80,96},{96,112},{1,17},{17... | collective-permute-start | bytes 1572872 | tf_op jit(solution)/shard_map/ppermute | solution.py:17
  91.1 5.8 %collective-permute-start.6 = (bf16[4,128,256]{2,1,0:T(8,128)(2,1)S(1)}, bf16[4,128,256]{2,1,0:T(8,128)(2,1)S(1)}, u32[]{:S(2)}, u32[]{:S(2)}) collective-permute-start(bf16[4,128,256]{2,1,0:T(8,128)(2,1)S(1)} %pad_maximum_fusion.11), channel_id=1, source_target_pairs={{16,0},{32,16},{48,32},{64,48},{80,64},{96,80},{112,96},{17,1},{33... | collective-permute-start | bytes 786440 | tf_op jit(solution)/shard_map/ppermute | solution.py:17
  93.1 7.7 %collective-permute-start.5 = (bf16[4,128,256]{2,1,0:T(8,128)(2,1)S(1)}, bf16[4,128,256]{2,1,0:T(8,128)(2,1)S(1)}, u32[]{:S(2)}, u32[]{:S(2)}) collective-permute-start(bf16[4,128,256]{2,1,0:T(8,128)(2,1)S(1)} %pad_maximum_fusion.10), channel_id=1, source_target_pairs={{0,16},{16,32},{32,48},{48,64},{64,80},{80,96},{96,112},{1,17},{17... | collective-permute-start | bytes 786440 | tf_op jit(solution)/shard_map/ppermute | solution.py:17
  101.2 3.6 %copy-start.1 = (bf16[2352,128]{1,0:T(8,128)(2,1)S(1)}, bf16[2352,128]{1,0:T(8,128)(2,1)}, u32[]{:S(2)}) copy-start(bf16[2352,128]{1,0:T(8,128)(2,1)} %param.6) | copy-start | bytes 1806340

commit v12 on v11

--- a/solution.py
+++ b/solution.py
@@ -107,16 +107,21 @@
             edge_sin[n : 2 * n] + edge_cos[3 * n :],
         ]
     ).astype(jnp.bfloat16)
-    by_cos = dot32(arranged, cosine)
-    by_sin = dot32(arranged, sine)
-    return edge_fields, jnp.stack(
+    middle_cols = jnp.concatenate([cosine[:, width : n - width], sine[:, width : n - width]], axis=1)
+    middle = dot32(arranged, middle_cols)
+    mid_cos, mid_sin = middle[:, : n - 2 * width], middle[:, n - 2 * width :]
+    middle_fields = jnp.stack(
         [
-            by_cos[:n] - by_sin[2 * n : 3 * n],
-            by_sin[:n] + by_cos[2 * n : 3 * n],
-            by_cos[n : 2 * n] - by_sin[3 * n :],
-            by_sin[n : 2 * n] + by_cos[3 * n :],
+            mid_cos[:n] - mid_sin[2 * n : 3 * n],
+            mid_sin[:n] + mid_cos[2 * n : 3 * n],
+            mid_cos[n : 2 * n] - mid_sin[3 * n :],
+            mid_sin[n : 2 * n] + mid_cos[3 * n :],
         ]
     ).astype(jnp.bfloat16)
+    fields = jnp.concatenate(
+        [edge_fields[:, :, :width], middle_fields, edge_fields[:, :, width:]], axis=2
+    )
+    return edge_fields, fields
 
 
 def blend_edges(extended, has_top, has_bottom, has_left, has_right, width):

time: 105 us -> 113 us (1.076)
  the two profiles are of different devices: /device:TPU:40 before, /device:TPU:15 now
where the time goes in v12:
time: 113 us
  waiting for transfers between devices  33.7 us (30%)
  starting transfers between devices  31.1 us (28%)
  matrix products  24.6 us (22%)
  other arithmetic  13.2 us (12%)
  local copies, waits for them, and re-layouts  9.63 us (9%)
    ppermute x7, starting transfers between devices, shifted(): return lax.ppermute(shard, axis, pairs)  23.4 us
    all_to_all x1, waiting for transfers between devices, on_device(): lax.all_to_all(jnp.stack([same_sent, rise_sent], axis=1), 'py', 0, 0, til...  20.4 us
    ppermute x7, waiting for transfers between devices, shifted(): return lax.ppermute(shard, axis, pairs)  13.3 us
    dot_general x2, matrix products, gathered_rows(): jnp.dot(chosen.astype(table_rows.dtype), table_rows, preferred_element_ty...  11.2 us
    all_to_all x1, starting transfers between devices, on_device(): lax.all_to_all(jnp.stack([same_sent, rise_sent], axis=1), 'py', 0, 0, til...  7.7 us
    dot_general x8, matrix products, dot32(): return jnp.dot(a, b, preferred_element_type=jnp.float32)  7.63 us
    dot_general x3, matrix products, one_hot_rows(): jnp.dot(picks.astype(values.dtype), values, preferred_element_type=jnp.fl...  5.79 us
    add x1, local copies, waits for them, and re-layouts, on_device(): return col_weight * rows_done + (1.0 - col_weight) * horizontal  5.22 us
  transfers between devices with their start and end apart: 8, of which 5 were waited for; matrix products, arithmetic and copies ran while one was open for 6% of the time, Pallas kernels for 0%

profile of v12, /device:TPU:15, one launch (start us, length us, event | category | flops | bytes accessed | tf_op | source)
XLA Modules:
  0.0 112.7 jit_solution(9060022292925134041)
XLA Ops:
  0.0 1.3 %constant_dynamic-slice_fusion.3 = (s32[1,16,192]{1,2,0:T(8,128)S(1)}, s32[1,16,192]{1,2,0:T(8,128)S(1)}, s32[1,16,192]{1,2,0:T(8,128)S(1)}, s32[1,16,192]{1,2,0:T(8,128)S(1)}) fusion(s32[1,128,192]{1,2,0:T(8,128)} %param.8, s32[]{:T(128)S(6)} %select_n.142, s32[]{:T(128)S(6)} %select_n.146, s32[1,128,192]{1,2,0:T(8,128)} %param.7), kind=kLoop, calls=%fused_computation.164 | loop fusion | bytes 98312 | tf_op jit(solution)/shard_map/dynamic_slice | solution.py:206
  1.3 0.8 fusion.84
  2.9 5.6 %fusion.17 = bf16[3072,128]{1,0:T(8,128)(2,1)S(1)} fusion(bf16[2352,128]{1,0:T(8,128)(2,1)S(1)} %copy-done, s32[3072]{0:T(1024)S(1)} %eq.43), kind=kOutput, calls=%fused_computation.22 | convolution fusion | flops 1857306624 | bytes 1400832 | tf_op jit(solution)/shard_map/dot_general | solution.py:159
  8.5 5.6 %fusion.16 = bf16[3072,128]{1,0:T(8,128)(2,1)S(1)} fusion(bf16[2352,128]{1,0:T(8,128)(2,1)S(1)} %copy-done, s32[3072]{0:T(1024)S(1)} %eq.89), kind=kOutput, calls=%fused_computation.21 | convolution fusion | flops 1857306624 | bytes 1400832 | tf_op jit(solution)/shard_map/dot_general | solution.py:159
  14.2 0.4 maximum_bitcast_fusion
  14.6 1.3 %pad_maximum_fusion.3 = bf16[16,2,208,128]{3,2,1,0:T(8,128)(2,1)} fusion(bf16[16,1,208,128]{3,2,1,0:T(8,128)(2,1)S(1)} %get-tuple-element.62, bf16[16,1,208,128]{3,2,1,0:T(8,128)(2,1)S(1)} %get-tuple-element.61), kind=kLoop, calls=%fused_computation.37 | loop fusion | flops 851968 | bytes 3407872 | tf_op jit(solution)/shard_map/stack | solution.py:217
  15.9 7.7 %all-to-all-start = ((bf16[16,2,208,128]{3,2,1,0:T(8,128)(2,1)}), bf16[16,2,208,128]{3,2,1,0:T(8,128)(2,1)S(1)}, u32[]{:S(2)}, u32[]{:S(2)}) async-start(bf16[16,2,208,128]{3,2,1,0:T(8,128)(2,1)} %pad_maximum_fusion.3), calls=%async_computation | async-start | bytes 3407872 | tf_op jit(solution)/shard_map/all_to_all | solution.py:217
  23.9 20.4 %all-to-all-done = bf16[16,2,208,128]{3,2,1,0:T(8,128)(2,1)S(1)} async-done(((bf16[16,2,208,128]{3,2,1,0:T(8,128)(2,1)}), bf16[16,2,208,128]{3,2,1,0:T(8,128)(2,1)S(1)}, u32[]{:S(2)}, u32[]{:S(2)}) %all-to-all-start) | async-done | bytes 1703968 | tf_op jit(solution)/shard_map/all_to_all | solution.py:217
  44.2 0.1 slice_bitcast_fusion
  44.7 0.3 reduce-window.9
  45.1 0.1 slice_reduce_fusion
  45.4 0.8 fusion.10
  46.2 1.0 fusion.33
  47.2 0.1 maximum_maximum_fusion
  47.4 4.4 %collective-permute-start = (bf16[1,528,128]{2,1,0:T(8,128)(2,1)S(1)}, bf16[1,528,128]{2,1,0:T(8,128)(2,1)S(1)}, u32[]{:S(2)}, u32[]{:S(2)}) collective-permute-start(bf16[1,528,128]{2,1,0:T(8,128)(2,1)S(1)} %maximum_maximum_fusion), channel_id=1, source_target_pairs={{16,0},{32,16},{48,32},{64,48},{80,64},{96,80},{112,96},{17,1},{33... | collective-permute-start | bytes 405512 | tf_op jit(solution)/shard_map/ppermute | solution.py:17
  51.9 3.7 %fusion.2 = f32[2048,128]{1,0:T(8,128)S(1)} fusion(bf16[3072,128]{1,0:T(8,128)(2,1)S(1)} %bitcast.111, s32[3072]{0:T(1024)S(1)} %eq.93, s32[2048]{0:T(1024)S(1)} %iota_add_fusion), kind=kOutput, calls=%fused_computation.4 | convolution fusion | flops 1616904192 | bytes 1855488 | tf_op jit(solution)/shard_map/dot_general | solution.py:154
  55.6 1.1 fusion.23
  56.7 0.3 reshape.309
  57.1 0.5 convolution_convert_fusion
  57.6 0.5 convolution_convert_fusion.1
  58.0 0.7 fusion.40
  58.8 0.7 fusion.41
  59.5 0.3 multiply_convert_fusion.3
  59.9 0.9 multiply_convert_fusion.2
  60.8 1.3 %fusion.53 = f32[512,2048]{1,0:T(8,128)S(1)} fusion(bf16[512,512]{1,0:T(8,128)(2,1)S(1)} %copy-done.3, bf16[512,512]{1,0:T(8,128)(2,1)S(1)} %get-tuple-element.21, bf16[512,512]{1,0:T(8,128)(2,1)S(1)} %get-tuple-element.22, bf16[512,512]{1,0:T(8,128)(2,1)S(1)} %get-tuple-element.20, bf16[512,512]{1,0:T(8,128)(2,1)S(1)} %get-tuple-element.5), kind=kOutput, calls=%fused_computation.82 | convolution fusion | flops 1082130432 | bytes 6815744 | tf_op jit(solution)/shard_map/dot_general | solution.py:51
  62.1 1.3 %fusion.52 = f32[512,2048]{1,0:T(8,128)S(1)} fusion(bf16[512,512]{1,0:T(8,128)(2,1)S(1)} %copy-done.2, bf16[512,512]{1,0:T(8,128)(2,1)S(1)} %get-tuple-element.21, bf16[512,512]{1,0:T(8,128)(2,1)S(1)} %get-tuple-element.22, bf16[512,512]{1,0:T(8,128)(2,1)S(1)} %get-tuple-element.20, bf16[512,512]{1,0:T(8,128)(2,1)S(1)} %get-tuple-element.5), kind=kOutput, calls=%fused_computation.81 | convolution fusion | flops 1082130432 | bytes 6815744 | tf_op jit(solution)/shard_map/dot_general | solution.py:51
  63.3 1.2 %fusion.27 = (bf16[512,1024]{1,0:T(8,128)(2,1)S(1)}, bf16[512,1024]{1,0:T(8,128)(2,1)S(1)}) fusion(f32[512,2048]{1,0:T(8,128)S(1)} %fusion.52, f32[512,2048]{1,0:T(8,128)S(1)} %fusion.53), kind=kLoop, calls=%fused_computation.31 | loop fusion | flops 2097152 | bytes 10485760 | tf_op jit(solution)/shard_map/convert.20
  64.7 0.9 copy-done.5
  65.6 1.3 %fusion.51 = f32[2048,512]{0,1:T(8,128)S(1)} fusion(bf16[512,512]{1,0:T(8,128)(2,1)S(1)} %copy-done.5, bf16[512,512]{1,0:T(8,128)(2,1)S(1)} %get-tuple-element.32, bf16[512,512]{1,0:T(8,128)(2,1)S(1)} %get-tuple-element.31, bf16[512,512]{1,0:T(8,128)(2,1)S(1)} %get-tuple-element.30, bf16[512,512]{1,0:T(8,128)(2,1)S(1)} %get-tuple-element.29), kind=kOutput, calls=%fused_computation.80 | convolution fusion | flops 1082130432 | bytes 6815744 | tf_op jit(solution)/shard_map/dot_general | solution.py:51
  66.9 0.4 fusion.54
  67.3 0.1 pad_maximum_fusion.5
  67.5 5.7 %collective-permute-start.3 = (bf16[4,512,128]{1,2,0:T(8,128)(2,1)S(1)}, bf16[4,512,128]{1,2,0:T(8,128)(2,1)S(1)}, u32[]{:S(2)}, u32[]{:S(2)}) collective-permute-start(bf16[4,512,128]{1,2,0:T(8,128)(2,1)S(1)} %get-tuple-element.28), channel_id=1, source_target_pairs={{0,1},{1,2},{2,3},{3,4},{4,5},{5,6},{6,7},{7,8},{8,9},{9,10},{10,1... | collective-permute-start | bytes 1572872 | tf_op jit(solution)/shard_map/ppermute | solution.py:17
  73.2 1.9 %collective-permute-start.4 = (bf16[4,512,128]{1,2,0:T(8,128)(2,1)S(1)}, bf16[4,512,128]{1,2,0:T(8,128)(2,1)S(1)}, u32[]{:S(2)}, u32[]{:S(2)}) collective-permute-start(bf16[4,512,128]{1,2,0:T(8,128)(2,1)S(1)} %get-tuple-element.27), channel_id=1, source_target_pairs={{1,0},{2,1},{3,2},{4,3},{5,4},{6,5},{7,6},{8,7},{9,8},{10,9},{11,1... | collective-permute-start | bytes 1572872 | tf_op jit(solution)/shard_map/ppermute | solution.py:17
  75.2 1.3 %fusion.50 = f32[2048,512]{0,1:T(8,128)S(1)} fusion(bf16[512,512]{1,0:T(8,128)(2,1)S(1)} %copy-done.4, bf16[512,512]{1,0:T(8,128)(2,1)S(1)} %get-tuple-element.32, bf16[512,512]{1,0:T(8,128)(2,1)S(1)} %get-tuple-element.31, bf16[512,512]{1,0:T(8,128)(2,1)S(1)} %get-tuple-element.30, bf16[512,512]{1,0:T(8,128)(2,1)S(1)} %get-tuple-element.29), kind=kOutput, calls=%fused_computation.79 | convolution fusion | flops 1082130432 | bytes 6815744 | tf_op jit(solution)/shard_map/dot_general | solution.py:51
  76.5 0.4 fusion.58
  76.9 0.2 pad_maximum_fusion.2
  77.1 0.2 fusion.92
  77.3 3.4 %collective-permute-start.1 = (bf16[4,128,512]{1,2,0:T(8,128)(2,1)S(1)}, bf16[4,128,512]{1,2,0:T(8,128)(2,1)S(1)}, u32[]{:S(2)}, u32[]{:S(2)}) collective-permute-start(bf16[4,128,512]{1,2,0:T(8,128)(2,1)S(1)} %get-tuple-element.23), channel_id=1, source_target_pairs={{0,16},{16,32},{32,48},{48,64},{64,80},{80,96},{96,112},{1,17},{17... | collective-permute-start | bytes 1572872 | tf_op jit(solution)/shard_map/ppermute | solution.py:17
  80.7 1.9 %collective-permute-start.2 = (bf16[4,128,512]{1,2,0:T(8,128)(2,1)S(1)}, bf16[4,128,512]{1,2,0:T(8,128)(2,1)S(1)}, u32[]{:S(2)}, u32[]{:S(2)}) collective-permute-start(bf16[4,128,512]{1,2,0:T(8,128)(2,1)S(1)} %get-tuple-element.24), channel_id=1, source_target_pairs={{16,0},{32,16},{48,32},{64,48},{80,64},{96,80},{112,96},{17,1},{33... | collective-permute-start | bytes 1572872 | tf_op jit(solution)/shard_map/ppermute | solution.py:17
  82.6 1.9 %collective-permute-done.3 = bf16[4,512,128]{1,2,0:T(8,128)(2,1)S(1)} collective-permute-done((bf16[4,512,128]{1,2,0:T(8,128)(2,1)S(1)}, bf16[4,512,128]{1,2,0:T(8,128)(2,1)S(1)}, u32[]{:S(2)}, u32[]{:S(2)}) %collective-permute-start.3) | collective-permute-done | bytes 524320 | tf_op jit(solution)/shard_map/ppermute | solution.py:17
  84.6 5.9 %collective-permute-done.4 = bf16[4,512,128]{1,2,0:T(8,128)(2,1)S(1)} collective-permute-done((bf16[4,512,128]{1,2,0:T(8,128)(2,1)S(1)}, bf16[4,512,128]{1,2,0:T(8,128)(2,1)S(1)}, u32[]{:S(2)}, u32[]{:S(2)}) %collective-permute-start.4) | collective-permute-done | bytes 524320 | tf_op jit(solution)/shard_map/ppermute | solution.py:17
  90.5 4.2 %collective-permute-start.5 = (bf16[4,128,256]{1,2,0:T(8,128)(2,1)S(1)}, bf16[4,128,256]{1,2,0:T(8,128)(2,1)S(1)}, u32[]{:S(2)}, u32[]{:S(2)}) collective-permute-start(bf16[4,128,256]{1,2,0:T(8,128)(2,1)S(1)} %pad_maximum_fusion.12), channel_id=1, source_target_pairs={{0,16},{16,32},{32,48},{48,64},{64,80},{80,96},{96,112},{1,17},{17... | collective-permute-start | bytes 786440 | tf_op jit(solution)/shard_map/ppermute | solution.py:17
  94.8 1.9 %collective-permute-start.6 = (bf16[4,128,256]{1,2,0:T(8,128)(2,1)S(1)}, bf16[4,128,256]{1,2,0:T(8,128)(2,1)S(1)}, u32[]{:S(2)}, u32[]{:S(2)}) collective-permute-start(bf16[4,128,256]{1,2,0:T(8,128)(2,1)S(1)} %pad_maximum_fusion.13), channel_id=1, source_target_pairs={{16,0},{32,16},{48,32},{64,48},{80,64},{96,80},{112,96},{17,1},{33... | collective-permute-start | bytes 786440 | tf_op jit(solution)/shard_map/ppermute | solution.py:17
  97.0 1.1 collective-permute-done.5
  98.1 4.4 %collective-permute-done.6 = bf16[4,128,256]{1,2,0:T(8,128)(2,1)S(1)} collective-permute-done((bf16[4,128,256]{1,2,0:T(8,128)(2,1)S(1)}, bf16[4,128,256]{1,2,0:T(8,128)(2,1)S(1)}, u32[]{:S(2)}, u32[]{:S(2)}) %collective-permute-start.6) | collective-permute-done | bytes 262176 | tf_op jit(solution)/shard_map/ppermute | solution.py:17
  102.5 0.3 fusion.37
  102.9 4.6 %fusion.13 = f32[4,512,512]{1,2,0:T(8,128)} fusion(f32[4,128,512]{1,2,0:T(8,128)S(1)} %convert_element_type.165, f32[4,128,512]{1,2,0:T(8,128)S(1)} %convert_element_type.164, f32[4,512,128]{1,2,0:T(8,128)S(1)} %get-tuple-element.50, f32[4,512,128]{1,2,0:T(8,128)S(1)} %get-tuple-element.49, f32[512]{0:T(512)S(1)} %pad.14.clone, ...), kind=kLoop, calls=%fused_computation.17 | loop fusion | flops 23068672 | bytes 10496000 | tf_op jit(solution)/shard_map/add | solution.py:274
  107.5 5.2 %copy.36 = f32[4,512,512]{2,1,0:T(8,128)} copy(f32[4,512,512]{1,2,0:T(8,128)} %fusion.13) | data formatting | bytes 8388608 | tf_op jit(solution)/shard_map/add | solution.py:274
  (71 shorter events, 2.5 us)
Async XLA Ops:
  0.0 2.9 %copy-start = (bf16[2352,128]{1,0:T(8,128)(2,1)S(1)}, bf16[2352,128]{1,0:T(8,128)(2,1)}, u32[]{:S(2)}) copy-start(bf16[2352,128]{1,0:T(8,128)(2,1)} %param.6) | copy-start | bytes 1806340
  15.9 28.3 %all-to-all-start = ((bf16[16,2,208,128]{3,2,1,0:T(8,128)(2,1)}), bf16[16,2,208,128]{3,2,1,0:T(8,128)(2,1)S(1)}, u32[]{:S(2)}, u32[]{:S(2)}) async-start(bf16[16,2,208,128]{3,2,1,0:T(8,128)(2,1)} %pad_maximum_fusion.3), calls=%async_computation | async-start | bytes 3407872 | tf_op jit(solution)/shard_map/all_to_all | solution.py:217
  47.4 8.2 %collective-permute-start = (bf16[1,528,128]{2,1,0:T(8,128)(2,1)S(1)}, bf16[1,528,128]{2,1,0:T(8,128)(2,1)S(1)}, u32[]{:S(2)}, u32[]{:S(2)}) collective-permute-start(bf16[1,528,128]{2,1,0:T(8,128)(2,1)S(1)} %maximum_maximum_fusion), channel_id=1, source_target_pairs={{16,0},{32,16},{48,32},{64,48},{80,64},{96,80},{112,96},{17,1},{33... | collective-permute-start | bytes 405512 | tf_op jit(solution)/shard_map/ppermute | solution.py:17
  51.9 5.1 %copy-start.2 = (bf16[512,512]{1,0:T(8,128)(2,1)S(1)}, bf16[512,512]{1,0:T(8,128)(2,1)}, u32[]{:S(2)}) copy-start(bf16[512,512]{1,0:T(8,128)(2,1)} %constant.128.clone) | copy-start | bytes 1572868
  55.6 2.0 %copy-start.3 = (bf16[512,512]{1,0:T(8,128)(2,1)S(1)}, bf16[512,512]{1,0:T(8,128)(2,1)}, u32[]{:S(2)}) copy-start(bf16[512,512]{1,0:T(8,128)(2,1)} %constant.127.clone) | copy-start | bytes 1572868
  64.5 1.0 copy-start.5
  66.9 8.2 %copy-start.4 = (bf16[512,512]{1,0:T(8,128)(2,1)S(1)}, bf16[512,512]{1,0:T(8,128)(2,1)}, u32[]{:S(2)}) copy-start(bf16[512,512]{1,0:T(8,128)(2,1)} %constant.140) | copy-start | bytes 1572868
  67.5 17.0 %collective-permute-start.3 = (bf16[4,512,128]{1,2,0:T(8,128)(2,1)S(1)}, bf16[4,512,128]{1,2,0:T(8,128)(2,1)S(1)}, u32[]{:S(2)}, u32[]{:S(2)}) collective-permute-start(bf16[4,512,128]{1,2,0:T(8,128)(2,1)S(1)} %get-tuple-element.28), channel_id=1, source_target_pairs={{0,1},{1,2},{2,3},{3,4},{4,5},{5,6},{6,7},{7,8},{8,9},{9,10},{10,1... | collective-permute-start | bytes 1572872 | tf_op jit(solution)/shard_map/ppermute | solution.py:17
  73.2 17.2 %collective-permute-start.4 = (bf16[4,512,128]{1,2,0:T(8,128)(2,1)S(1)}, bf16[4,512,128]{1,2,0:T(8,128)(2,1)S(1)}, u32[]{:S(2)}, u32[]{:S(2)}) collective-permute-start(bf16[4,512,128]{1,2,0:T(8,128)(2,1)S(1)} %get-tuple-element.27), channel_id=1, source_target_pairs={{1,0},{2,1},{3,2},{4,3},{5,4},{6,5},{7,6},{8,7},{9,8},{10,9},{11,1... | collective-permute-start | bytes 1572872 | tf_op jit(solution)/shard_map/ppermute | solution.py:17
  77.3 19.5 %collective-permute-start.1 = (bf16[4,128,512]{1,2,0:T(8,128)(2,1)S(1)}, bf16[4,128,512]{1,2,0:T(8,128)(2,1)S(1)}, u32[]{:S(2)}, u32[]{:S(2)}) collective-permute-start(bf16[4,128,512]{1,2,0:T(8,128)(2,1)S(1)} %get-tuple-element.23), channel_id=1, source_target_pairs={{0,16},{16,32},{32,48},{48,64},{64,80},{80,96},{96,112},{1,17},{17... | collective-permute-start | bytes 1572872 | tf_op jit(solution)/shard_map/ppermute | solution.py:17
  80.7 16.2 %collective-permute-start.2 = (bf16[4,128,512]{1,2,0:T(8,128)(2,1)S(1)}, bf16[4,128,512]{1,2,0:T(8,128)(2,1)S(1)}, u32[]{:S(2)}, u32[]{:S(2)}) collective-permute-start(bf16[4,128,512]{1,2,0:T(8,128)(2,1)S(1)} %get-tuple-element.24), channel_id=1, source_target_pairs={{16,0},{32,16},{48,32},{64,48},{80,64},{96,80},{112,96},{17,1},{33... | collective-permute-start | bytes 1572872 | tf_op jit(solution)/shard_map/ppermute | solution.py:17
  90.5 7.5 %collective-permute-start.5 = (bf16[4,128,256]{1,2,0:T(8,128)(2,1)S(1)}, bf16[4,128,256]{1,2,0:T(8,128)(2,1)S(1)}, u32[]{:S(2)}, u32[]{:S(2)}) collective-permute-start(bf16[4,128,256]{1,2,0:T(8,128)(2,1)S(1)} %pad_maximum_fusion.12), channel_id=1, source_target_pairs={{0,16},{16,32},{32,48},{48,64},{64,80},{80,96},{96,112},{1,17},{17... | collective-permute-start | bytes 786440 | tf_op jit(solution)/shard_map/ppermute | solution.py:17
  94.8 7.7 %collective-permute-start.6 = (bf16[4,128,256]{1,2,0:T(8,128)(2,1)S(1)}, bf16[4,128,256]{1,2,0:T(8,128)(2,1)S(1)}, u32[]{:S(2)}, u32[]{:S(2)}) collective-permute-start(bf16[4,128,256]{1,2,0:T(8,128)(2,1)S(1)} %pad_maximum_fusion.13), channel_id=1, source_target_pairs={{16,0},{32,16},{48,32},{64,48},{80,64},{96,80},{112,96},{17,1},{33... | collective-permute-start | bytes 786440 | tf_op jit(solution)/shard_map/ppermute | solution.py:17
  102.9 9.8 %copy-start.1 = (bf16[2352,128]{1,0:T(8,128)(2,1)S(1)}, bf16[2352,128]{1,0:T(8,128)(2,1)}, u32[]{:S(2)}) copy-start(bf16[2352,128]{1,0:T(8,128)(2,1)} %param.6) | copy-start | bytes 1806340

commit v13 on v11

--- a/solution.py
+++ b/solution.py
@@ -260,13 +260,26 @@
         [f32(upper), jnp.broadcast_to(zero_rows, (fields.shape[0], count - 2 * width, width)),
          f32(lower)], axis=1
     )
-    left_rows = side(left, above_left, below_left)
-    right_rows = side(right, above_right, below_right)
+    no_corner = jnp.zeros_like(f32(above_left))
+    left_rows = side(left, no_corner, no_corner)
+    right_rows = side(right, no_corner, no_corner)
     horizontal = jnp.concatenate(
         [left_rows, jnp.broadcast_to(zero_rows[:, :1], (fields.shape[0], count, count - 2 * width)),
          right_rows], axis=2
     )
-    return col_weight * rows_done + (1.0 - col_weight) * horizontal
+    result = col_weight * rows_done + (1.0 - col_weight) * horizontal
+    last = count - width
+    for rows, row_w, vert, pieces in (
+        (slice(0, width), top_weight[0], above, ((left, above_left), (right, above_right))),
+        (slice(last, count), bottom_weight[0], below, ((left, below_left), (right, below_right))),
+    ):
+        for (strip, corner), cols, col_w in zip(
+            pieces, (slice(0, width), slice(last, count)), (left_weight[0], right_weight[0])
+        ):
+            own_rows = row_w * f32(fields[:, rows, cols]) + (1.0 - row_w) * f32(vert[:, :, cols])
+            strip_rows = row_w * f32(strip[:, rows]) + (1.0 - row_w) * f32(corner)
+            result = result.at[:, rows, cols].set(col_w * own_rows + (1.0 - col_w) * strip_rows)
+    return result
 
 
 def solution(mesh):

time: 105 us -> 114 us (1.086)
  the two profiles are of different devices: /device:TPU:40 before, /device:TPU:15 now
where the time goes in v13:
time: 114 us
  starting transfers between devices  31.6 us (28%)
  waiting for transfers between devices  26.9 us (24%)
  matrix products  25.8 us (23%)
  other arithmetic  18.7 us (16%)
  local copies, waits for them, and re-layouts  10.3 us (9%)
    ppermute x7, starting transfers between devices, shifted(): return lax.ppermute(shard, axis, pairs)  23.8 us
    all_to_all x1, waiting for transfers between devices, on_device(): lax.all_to_all(jnp.stack([same_sent, rise_sent], axis=1), 'py', 0, 0, til...  19 us
    dot_general x2, matrix products, gathered_rows(): jnp.dot(chosen.astype(table_rows.dtype), table_rows, preferred_element_ty...  11.2 us
    dot_general x9, matrix products, dot32(): return jnp.dot(a, b, preferred_element_type=jnp.float32)  8.76 us
    ppermute x7, waiting for transfers between devices, shifted(): return lax.ppermute(shard, axis, pairs)  7.93 us
    all_to_all x1, starting transfers between devices, on_device(): lax.all_to_all(jnp.stack([same_sent, rise_sent], axis=1), 'py', 0, 0, til...  7.71 us
    dot_general x3, matrix products, one_hot_rows(): jnp.dot(picks.astype(values.dtype), values, preferred_element_type=jnp.fl...  5.84 us
    another operation x10, other arithmetic  5.76 us
  transfers between devices with their start and end apart: 8, of which 2 were waited for; matrix products, arithmetic and copies ran while one was open for 14% of the time, Pallas kernels for 0%

profile of v13, /device:TPU:15, one launch (start us, length us, event | category | flops | bytes accessed | tf_op | source)
XLA Modules:
  0.0 113.9 jit_solution(12981687083930798478)
XLA Ops:
  0.0 1.3 %constant_dynamic-slice_fusion.3 = (s32[1,16,192]{1,2,0:T(8,128)S(1)}, s32[1,16,192]{1,2,0:T(8,128)S(1)}, s32[1,16,192]{1,2,0:T(8,128)S(1)}, s32[1,16,192]{1,2,0:T(8,128)S(1)}) fusion(s32[1,128,192]{1,2,0:T(8,128)} %param.16, s32[]{:T(128)S(6)} %select_n.158, s32[]{:T(128)S(6)} %select_n.162, s32[1,128,192]{1,2,0:T(8,128)} %param.15), kind=kLoop, calls=%fused_computation.146 | loop fusion | bytes 98312 | tf_op jit(solution)/shard_map/dynamic_slice | solution.py:201
  1.3 0.8 fusion.82
  2.9 5.6 %fusion.17 = bf16[3072,128]{1,0:T(8,128)(2,1)S(1)} fusion(bf16[2352,128]{1,0:T(8,128)(2,1)S(1)} %copy-done, s32[3072]{0:T(1024)S(1)} %eq.43), kind=kOutput, calls=%fused_computation.22 | convolution fusion | flops 1857306624 | bytes 1400832 | tf_op jit(solution)/shard_map/dot_general | solution.py:154
  8.5 5.6 %fusion.16 = bf16[3072,128]{1,0:T(8,128)(2,1)S(1)} fusion(bf16[2352,128]{1,0:T(8,128)(2,1)S(1)} %copy-done, s32[3072]{0:T(1024)S(1)} %eq.89), kind=kOutput, calls=%fused_computation.21 | convolution fusion | flops 1857306624 | bytes 1400832 | tf_op jit(solution)/shard_map/dot_general | solution.py:154
  14.2 0.4 maximum_bitcast_fusion
  14.6 1.3 %pad_maximum_fusion.3 = bf16[16,2,208,128]{3,2,1,0:T(8,128)(2,1)} fusion(bf16[16,1,208,128]{3,2,1,0:T(8,128)(2,1)S(1)} %get-tuple-element.112, bf16[16,1,208,128]{3,2,1,0:T(8,128)(2,1)S(1)} %get-tuple-element.111), kind=kLoop, calls=%fused_computation.37 | loop fusion | flops 851968 | bytes 3407872 | tf_op jit(solution)/shard_map/stack | solution.py:212
  15.9 7.7 %all-to-all-start = ((bf16[16,2,208,128]{3,2,1,0:T(8,128)(2,1)}), bf16[16,2,208,128]{3,2,1,0:T(8,128)(2,1)S(1)}, u32[]{:S(2)}, u32[]{:S(2)}) async-start(bf16[16,2,208,128]{3,2,1,0:T(8,128)(2,1)} %pad_maximum_fusion.3), calls=%async_computation | async-start | bytes 3407872 | tf_op jit(solution)/shard_map/all_to_all | solution.py:212
  23.9 0.6 fusion.97
  24.5 0.7 and_reduce_fusion
  25.3 19.0 %all-to-all-done = bf16[16,2,208,128]{3,2,1,0:T(8,128)(2,1)S(1)} async-done(((bf16[16,2,208,128]{3,2,1,0:T(8,128)(2,1)}), bf16[16,2,208,128]{3,2,1,0:T(8,128)(2,1)S(1)}, u32[]{:S(2)}, u32[]{:S(2)}) %all-to-all-start) | async-done | bytes 1703968 | tf_op jit(solution)/shard_map/all_to_all | solution.py:212
  45.0 0.3 reduce-window.9
  45.6 0.8 fusion.10
  46.4 1.0 fusion.33
  47.5 4.4 %collective-permute-start = (bf16[1,528,128]{2,1,0:T(8,128)(2,1)S(1)}, bf16[1,528,128]{2,1,0:T(8,128)(2,1)S(1)}, u32[]{:S(2)}, u32[]{:S(2)}) collective-permute-start(bf16[1,528,128]{2,1,0:T(8,128)(2,1)S(1)} %maximum_maximum_fusion), channel_id=1, source_target_pairs={{16,0},{32,16},{48,32},{64,48},{80,64},{96,80},{112,96},{17,1},{33... | collective-permute-start | bytes 405512 | tf_op jit(solution)/shard_map/ppermute | solution.py:17
  51.9 3.7 %fusion.2 = f32[2048,128]{1,0:T(8,128)S(1)} fusion(bf16[3072,128]{1,0:T(8,128)(2,1)S(1)} %bitcast.114, s32[3072]{0:T(1024)S(1)} %eq.93, s32[2048]{0:T(1024)S(1)} %iota_add_fusion), kind=kOutput, calls=%fused_computation.4 | convolution fusion | flops 1616904192 | bytes 1855488 | tf_op jit(solution)/shard_map/dot_general | solution.py:149
  55.7 1.1 fusion.23
  56.8 0.3 reshape.482
  57.1 0.5 convolution_convert_fusion
  57.6 0.5 convolution_convert_fusion.1
  58.1 0.7 fusion.45
  58.9 0.7 fusion.44
  59.6 0.3 multiply_convert_fusion.3
  59.9 0.9 multiply_convert_fusion.2
  60.9 1.3 %fusion.54 = f32[512,2048]{1,0:T(8,128)S(1)} fusion(bf16[512,512]{1,0:T(8,128)(2,1)S(1)} %copy-done.4, bf16[512,512]{1,0:T(8,128)(2,1)S(1)} %get-tuple-element.73, bf16[512,512]{1,0:T(8,128)(2,1)S(1)} %get-tuple-element.74, bf16[512,512]{1,0:T(8,128)(2,1)S(1)} %get-tuple-element.72, bf16[512,512]{1,0:T(8,128)(2,1)S(1)} %get-tuple-element.57), kind=kOutput, calls=%fused_computation.82 | convolution fusion | flops 1082130432 | bytes 6815744 | tf_op jit(solution)/shard_map/dot_general | solution.py:51
  62.1 1.3 %fusion.55 = f32[512,2048]{1,0:T(8,128)S(1)} fusion(bf16[512,512]{1,0:T(8,128)(2,1)S(1)} %copy-done.3, bf16[512,512]{1,0:T(8,128)(2,1)S(1)} %get-tuple-element.73, bf16[512,512]{1,0:T(8,128)(2,1)S(1)} %get-tuple-element.74, bf16[512,512]{1,0:T(8,128)(2,1)S(1)} %get-tuple-element.72, bf16[512,512]{1,0:T(8,128)(2,1)S(1)} %get-tuple-element.57), kind=kOutput, calls=%fused_computation.83 | convolution fusion | flops 1082130432 | bytes 6815744 | tf_op jit(solution)/shard_map/dot_general | solution.py:51
  63.4 1.2 %fusion.27 = (bf16[512,1024]{1,0:T(8,128)(2,1)S(1)}, bf16[512,1024]{1,0:T(8,128)(2,1)S(1)}) fusion(f32[512,2048]{1,0:T(8,128)S(1)} %fusion.54, f32[512,2048]{1,0:T(8,128)S(1)} %fusion.55), kind=kLoop, calls=%fused_computation.31 | loop fusion | flops 2097152 | bytes 10485760 | tf_op jit(solution)/shard_map/convert.20
  64.8 1.3 %fusion.88 = f32[2048,512]{1,0:T(8,128)S(1)} fusion(bf16[512,512]{1,0:T(8,128)(2,1)S(1)} %copy-done.4, bf16[512,512]{1,0:T(8,128)(2,1)S(1)} %get-tuple-element.84, bf16[512,512]{1,0:T(8,128)(2,1)S(1)} %get-tuple-element.83, bf16[512,512]{1,0:T(8,128)(2,1)S(1)} %get-tuple-element.82, bf16[512,512]{1,0:T(8,128)(2,1)S(1)} %get-tuple-element.81), kind=kOutput, calls=%fused_computation.193 | convolution fusion | flops 1082130432 | bytes 6815744 | tf_op jit(solution)/shard_map/dot_general | solution.py:51
  66.1 1.3 %fusion.89 = f32[2048,512]{1,0:T(8,128)S(1)} fusion(bf16[512,512]{1,0:T(8,128)(2,1)S(1)} %copy-done.3, bf16[512,512]{1,0:T(8,128)(2,1)S(1)} %get-tuple-element.84, bf16[512,512]{1,0:T(8,128)(2,1)S(1)} %get-tuple-element.83, bf16[512,512]{1,0:T(8,128)(2,1)S(1)} %get-tuple-element.82, bf16[512,512]{1,0:T(8,128)(2,1)S(1)} %get-tuple-element.81), kind=kOutput, calls=%fused_computation.194 | convolution fusion | flops 1082130432 | bytes 6815744 | tf_op jit(solution)/shard_map/dot_general | solution.py:51
  67.3 1.2 %fusion.87 = f32[2048,512]{1,0:T(8,128)S(1)} fusion(bf16[512,512]{1,0:T(8,128)(2,1)S(1)} %copy-done.8, bf16[512,512]{1,0:T(8,128)(2,1)S(1)} %get-tuple-element.84, bf16[512,512]{1,0:T(8,128)(2,1)S(1)} %get-tuple-element.83, bf16[512,512]{1,0:T(8,128)(2,1)S(1)} %get-tuple-element.82, bf16[512,512]{1,0:T(8,128)(2,1)S(1)} %get-tuple-element.81), kind=kOutput, calls=%fused_computation.192 | convolution fusion | flops 1082130432 | bytes 6815744 | tf_op jit(solution)/shard_map/dot_general | solution.py:51
  68.6 0.3 fusion.56
  69.0 0.2 fusion.92
  69.2 5.7 %collective-permute-start.3 = (bf16[4,512,128]{2,1,0:T(8,128)(2,1)S(1)}, bf16[4,512,128]{2,1,0:T(8,128)(2,1)S(1)}, u32[]{:S(2)}, u32[]{:S(2)}) collective-permute-start(bf16[4,512,128]{2,1,0:T(8,128)(2,1)S(1)} %get-tuple-element.79), channel_id=1, source_target_pairs={{0,1},{1,2},{2,3},{3,4},{4,5},{5,6},{6,7},{7,8},{8,9},{9,10},{10,1... | collective-permute-start | bytes 1572872 | tf_op jit(solution)/shard_map/ppermute | solution.py:17
  74.9 1.9 %collective-permute-start.4 = (bf16[4,512,128]{2,1,0:T(8,128)(2,1)S(1)}, bf16[4,512,128]{2,1,0:T(8,128)(2,1)S(1)}, u32[]{:S(2)}, u32[]{:S(2)}) collective-permute-start(bf16[4,512,128]{2,1,0:T(8,128)(2,1)S(1)} %get-tuple-element.80), channel_id=1, source_target_pairs={{1,0},{2,1},{3,2},{4,3},{5,4},{6,5},{7,6},{8,7},{9,8},{10,9},{11,1... | collective-permute-start | bytes 1572872 | tf_op jit(solution)/shard_map/ppermute | solution.py:17
  76.8 1.2 %fusion.46 = (bf16[1,512,512]{2,1,0:T(8,128)(2,1)S(1)}, bf16[1,512,512]{2,1,0:T(8,128)(2,1)S(1)}, bf16[1,512,512]{2,1,0:T(8,128)(2,1)S(1)}, bf16[1,512,512]{2,1,0:T(8,128)(2,1)S(1)}) fusion(f32[2048,512]{1,0:T(8,128)S(1)} %fusion.88, f32[2048,512]{1,0:T(8,128)S(1)} %fusion.89), kind=kLoop, calls=%fused_computation.70 | loop fusion | flops 2097152 | bytes 10485760 | tf_op jit(solution)/shard_map/stack | solution.py:112
  78.1 0.3 pad_maximum_fusion.2
  78.4 2.2 %collective-permute-start.2 = (bf16[4,128,512]{2,1,0:T(8,128)(2,1)S(1)}, bf16[4,128,512]{2,1,0:T(8,128)(2,1)S(1)}, u32[]{:S(2)}, u32[]{:S(2)}) collective-permute-start(bf16[4,128,512]{2,1,0:T(8,128)(2,1)S(1)} %get-tuple-element.76), channel_id=1, source_target_pairs={{16,0},{32,16},{48,32},{64,48},{80,64},{96,80},{112,96},{17,1},{33... | collective-permute-start | bytes 1572872 | tf_op jit(solution)/shard_map/ppermute | solution.py:17
  80.6 3.6 %collective-permute-start.1 = (bf16[4,128,512]{2,1,0:T(8,128)(2,1)S(1)}, bf16[4,128,512]{2,1,0:T(8,128)(2,1)S(1)}, u32[]{:S(2)}, u32[]{:S(2)}) collective-permute-start(bf16[4,128,512]{2,1,0:T(8,128)(2,1)S(1)} %get-tuple-element.75), channel_id=1, source_target_pairs={{0,16},{16,32},{32,48},{48,64},{64,80},{80,96},{96,112},{1,17},{17... | collective-permute-start | bytes 1572872 | tf_op jit(solution)/shard_map/ppermute | solution.py:17
  84.2 7.9 %collective-permute-done.4 = bf16[4,512,128]{2,1,0:T(8,128)(2,1)S(1)} collective-permute-done((bf16[4,512,128]{2,1,0:T(8,128)(2,1)S(1)}, bf16[4,512,128]{2,1,0:T(8,128)(2,1)S(1)}, u32[]{:S(2)}, u32[]{:S(2)}) %collective-permute-start.4) | collective-permute-done | bytes 524320 | tf_op jit(solution)/shard_map/ppermute | solution.py:17
  92.2 4.2 %collective-permute-start.5 = (bf16[4,128,256]{2,1,0:T(8,128)(2,1)S(1)}, bf16[4,128,256]{2,1,0:T(8,128)(2,1)S(1)}, u32[]{:S(2)}, u32[]{:S(2)}) collective-permute-start(bf16[4,128,256]{2,1,0:T(8,128)(2,1)S(1)} %pad_maximum_fusion.10), channel_id=1, source_target_pairs={{0,16},{16,32},{32,48},{48,64},{64,80},{80,96},{96,112},{1,17},{17... | collective-permute-start | bytes 786440 | tf_op jit(solution)/shard_map/ppermute | solution.py:17
  96.4 0.7 pad_maximum_fusion.11
  97.2 1.9 %collective-permute-start.6 = (bf16[4,128,256]{2,1,0:T(8,128)(2,1)}, bf16[4,128,256]{2,1,0:T(8,128)(2,1)}, u32[]{:S(2)}, u32[]{:S(2)}) collective-permute-start(bf16[4,128,256]{2,1,0:T(8,128)(2,1)} %pad_maximum_fusion.11), channel_id=1, source_target_pairs={{16,0},{32,16},{48,32},{64,48},{80,64},{96,80},{112,96},{17,1},{33... | collective-permute-start | bytes 786440 | tf_op jit(solution)/shard_map/ppermute | solution.py:17
  99.4 0.3 fusion.42
  99.9 1.7 %fusion.13 = f32[4,512,512]{2,1,0:T(8,128)S(1)} fusion(f32[4,128,512]{2,1,0:T(8,128)S(1)} %convert_element_type.201, f32[4,128,512]{2,1,0:T(8,128)S(1)} %convert_element_type.200, f32[4,512,128]{2,1,0:T(8,128)S(1)} %get-tuple-element.90, f32[4,512,128]{2,1,0:T(8,128)S(1)} %get-tuple-element.89, f32[512]{0:T(512)S(1)} %pad.33.clone, ...), kind=kLoop, calls=%fused_computation.17 | loop fusion | flops 14680064 | bytes 10496000 | tf_op jit(solution)/shard_map/add | solution.py:270
  101.9 2.0 %copy-done.2 = f32[4,512,512]{2,1,0:T(8,128)} copy-done((f32[4,512,512]{2,1,0:T(8,128)}, f32[4,512,512]{2,1,0:T(8,128)S(1)}, u32[]{:S(2)}) %copy-start.2) | copy-done | bytes 4194328
  103.9 2.1 %dynamic-slice_select_fusion = f32[4,128,128]{2,1,0:T(8,128)S(1)} fusion(f32[4,512,512]{2,1,0:T(8,128)S(1)} %add_dynamic-update-slice_fusion.2, s32[]{:T(128)} %bitcast.28, s32[]{:T(128)} %bitcast.29, bf16[4,128,256]{2,1,0:T(8,128)(2,1)S(1)} %collective-permute-done.5, bf16[4,128,512]{2,1,0:T(8,128)(2,1)S(1)} %collective-permute-done.1, ...), kind=kLoop, calls=%fused_computation.92 | loop fusion | flops 917504 | bytes 1050633 | tf_op jit(solution)/shard_map/select.5
  106.0 4.1 %scatter.15 = f32[4,512,512]{2,1,0:T(8,128)} dynamic-update-slice(f32[4,512,512]{2,1,0:T(8,128)} %copy-done.2, f32[4,128,128]{2,1,0:T(8,128)S(1)} %dynamic-slice_select_fusion, s32[]{:T(128)} %constant.220.clone.1, s32[]{:T(128)} %bitcast.28, s32[]{:T(128)} %bitcast.29) | dynamic-update-slice | bytes 524292 | tf_op jit(solution)/shard_map/scatter | solution.py:281
  110.1 1.9 %add_dynamic-update-slice_fusion.1 = f32[4,512,512]{2,1,0:T(8,128)} fusion(f32[4,512,512]{2,1,0:T(8,128)} %scatter.15, bf16[4,128,256]{2,1,0:T(8,128)(2,1)} %collective-permute-done.6, bf16[4,128,512]{2,1,0:T(8,128)(2,1)} %copy-done.6, bf16[4,512,512]{2,1,0:T(8,128)(2,1)S(1)} %pad_maximum_fusion.2, f32[128]{0:T(128)S(1)} %get-tuple-element.109, ...), kind=kLoop, calls=%fused_computation.91 | loop fusion | flops 851968 | bytes 788480 | tf_op jit(solution)/shard_map/scatter | solution.py:281
  112.0 1.8 %add_dynamic-update-slice_fusion = f32[4,512,512]{2,1,0:T(8,128)} fusion(f32[4,512,512]{2,1,0:T(8,128)} %add_dynamic-update-slice_fusion.1, bf16[4,128,256]{2,1,0:T(8,128)(2,1)} %collective-permute-done.6, bf16[4,128,512]{2,1,0:T(8,128)(2,1)} %copy-done.6, bf16[4,512,512]{2,1,0:T(8,128)(2,1)S(1)} %pad_maximum_fusion.2, f32[128]{0:T(128)S(1)} %get-tuple-element.109, ...), kind=kLoop, calls=%fused_computation.90 | loop fusion | flops 851968 | bytes 788480 | tf_op jit(solution)/shard_map/scatter | solution.py:281
  (85 shorter events, 3.4 us)
Async XLA Ops:
  0.0 2.9 %copy-start = (bf16[2352,128]{1,0:T(8,128)(2,1)S(1)}, bf16[2352,128]{1,0:T(8,128)(2,1)}, u32[]{:S(2)}) copy-start(bf16[2352,128]{1,0:T(8,128)(2,1)} %param.14) | copy-start | bytes 1806340
  14.6 9.9 %copy-start.7 = (s32[3]{0:T(128)S(1)}, s32[3]{0:T(128)}, u32[]{:S(2)}) copy-start(s32[3]{0:T(128)} %constant.244.clone.1) | copy-start | bytes 40
  15.9 28.3 %all-to-all-start = ((bf16[16,2,208,128]{3,2,1,0:T(8,128)(2,1)}), bf16[16,2,208,128]{3,2,1,0:T(8,128)(2,1)S(1)}, u32[]{:S(2)}, u32[]{:S(2)}) async-start(bf16[16,2,208,128]{3,2,1,0:T(8,128)(2,1)} %pad_maximum_fusion.3), calls=%async_computation | async-start | bytes 3407872 | tf_op jit(solution)/shard_map/all_to_all | solution.py:212
  47.5 8.1 %collective-permute-start = (bf16[1,528,128]{2,1,0:T(8,128)(2,1)S(1)}, bf16[1,528,128]{2,1,0:T(8,128)(2,1)S(1)}, u32[]{:S(2)}, u32[]{:S(2)}) collective-permute-start(bf16[1,528,128]{2,1,0:T(8,128)(2,1)S(1)} %maximum_maximum_fusion), channel_id=1, source_target_pairs={{16,0},{32,16},{48,32},{64,48},{80,64},{96,80},{112,96},{17,1},{33... | collective-permute-start | bytes 405512 | tf_op jit(solution)/shard_map/ppermute | solution.py:17
  51.9 5.2 %copy-start.4 = (bf16[512,512]{1,0:T(8,128)(2,1)S(1)}, bf16[512,512]{1,0:T(8,128)(2,1)}, u32[]{:S(2)}) copy-start(bf16[512,512]{1,0:T(8,128)(2,1)} %constant.247.clone) | copy-start | bytes 1572868
  55.7 2.0 %copy-start.3 = (bf16[512,512]{1,0:T(8,128)(2,1)S(1)}, bf16[512,512]{1,0:T(8,128)(2,1)}, u32[]{:S(2)}) copy-start(bf16[512,512]{1,0:T(8,128)(2,1)} %constant.246.clone) | copy-start | bytes 1572868
  66.0 1.3 %copy-start.8 = (bf16[512,512]{1,0:T(8,128)(2,1)S(1)}, bf16[512,512]{1,0:T(8,128)(2,1)}, u32[]{:S(2)}) copy-start(bf16[512,512]{1,0:T(8,128)(2,1)} %constant.256) | copy-start | bytes 1572868
  69.2 22.9 %collective-permute-start.3 = (bf16[4,512,128]{2,1,0:T(8,128)(2,1)S(1)}, bf16[4,512,128]{2,1,0:T(8,128)(2,1)S(1)}, u32[]{:S(2)}, u32[]{:S(2)}) collective-permute-start(bf16[4,512,128]{2,1,0:T(8,128)(2,1)S(1)} %get-tuple-element.79), channel_id=1, source_target_pairs={{0,1},{1,2},{2,3},{3,4},{4,5},{5,6},{6,7},{7,8},{8,9},{9,10},{10,1... | collective-permute-start | bytes 1572872 | tf_op jit(solution)/shard_map/ppermute | solution.py:17
  74.9 17.2 %collective-permute-start.4 = (bf16[4,512,128]{2,1,0:T(8,128)(2,1)S(1)}, bf16[4,512,128]{2,1,0:T(8,128)(2,1)S(1)}, u32[]{:S(2)}, u32[]{:S(2)}) collective-permute-start(bf16[4,512,128]{2,1,0:T(8,128)(2,1)S(1)} %get-tuple-element.80), channel_id=1, source_target_pairs={{1,0},{2,1},{3,2},{4,3},{5,4},{6,5},{7,6},{8,7},{9,8},{10,9},{11,1... | collective-permute-start | bytes 1572872 | tf_op jit(solution)/shard_map/ppermute | solution.py:17
  78.4 20.7 %collective-permute-start.2 = (bf16[4,128,512]{2,1,0:T(8,128)(2,1)S(1)}, bf16[4,128,512]{2,1,0:T(8,128)(2,1)S(1)}, u32[]{:S(2)}, u32[]{:S(2)}) collective-permute-start(bf16[4,128,512]{2,1,0:T(8,128)(2,1)S(1)} %get-tuple-element.76), channel_id=1, source_target_pairs={{16,0},{32,16},{48,32},{64,48},{80,64},{96,80},{112,96},{17,1},{33... | collective-permute-start | bytes 1572872 | tf_op jit(solution)/shard_map/ppermute | solution.py:17
  80.6 18.6 %collective-permute-start.1 = (bf16[4,128,512]{2,1,0:T(8,128)(2,1)S(1)}, bf16[4,128,512]{2,1,0:T(8,128)(2,1)S(1)}, u32[]{:S(2)}, u32[]{:S(2)}) collective-permute-start(bf16[4,128,512]{2,1,0:T(8,128)(2,1)S(1)} %get-tuple-element.75), channel_id=1, source_target_pairs={{0,16},{16,32},{32,48},{48,64},{64,80},{80,96},{96,112},{1,17},{17... | collective-permute-start | bytes 1572872 | tf_op jit(solution)/shard_map/ppermute | solution.py:17
  92.2 9.5 %copy-start.5 = (bf16[4,512,128]{2,1,0:T(8,128)(2,1)}, bf16[4,512,128]{2,1,0:T(8,128)(2,1)S(1)}, u32[]{:S(2)}) copy-start(bf16[4,512,128]{2,1,0:T(8,128)(2,1)S(1)} %collective-permute-done.3) | copy-start | bytes 1572868
  92.2 9.5 %collective-permute-start.5 = (bf16[4,128,256]{2,1,0:T(8,128)(2,1)S(1)}, bf16[4,128,256]{2,1,0:T(8,128)(2,1)S(1)}, u32[]{:S(2)}, u32[]{:S(2)}) collective-permute-start(bf16[4,128,256]{2,1,0:T(8,128)(2,1)S(1)} %pad_maximum_fusion.10), channel_id=1, source_target_pairs={{0,16},{16,32},{32,48},{48,64},{64,80},{80,96},{96,112},{1,17},{17... | collective-permute-start | bytes 786440 | tf_op jit(solution)/shard_map/ppermute | solution.py:17
  97.2 12.9 %collective-permute-start.6 = (bf16[4,128,256]{2,1,0:T(8,128)(2,1)}, bf16[4,128,256]{2,1,0:T(8,128)(2,1)}, u32[]{:S(2)}, u32[]{:S(2)}) collective-permute-start(bf16[4,128,256]{2,1,0:T(8,128)(2,1)} %pad_maximum_fusion.11), channel_id=1, source_target_pairs={{16,0},{32,16},{48,32},{64,48},{80,64},{96,80},{112,96},{17,1},{33... | collective-permute-start | bytes 786440 | tf_op jit(solution)/shard_map/ppermute | solution.py:17
  99.1 0.8 copy-start.6
  99.9 13.9 %copy-start.1 = (bf16[2352,128]{1,0:T(8,128)(2,1)S(1)}, bf16[2352,128]{1,0:T(8,128)(2,1)}, u32[]{:S(2)}) copy-start(bf16[2352,128]{1,0:T(8,128)(2,1)} %param.14) | copy-start | bytes 1806340
  101.9 2.0 %copy-start.2 = (f32[4,512,512]{2,1,0:T(8,128)}, f32[4,512,512]{2,1,0:T(8,128)S(1)}, u32[]{:S(2)}) copy-start(f32[4,512,512]{2,1,0:T(8,128)S(1)} %add_dynamic-update-slice_fusion.2) | copy-start | bytes 12582916

commit v14 on v11

--- a/solution.py
+++ b/solution.py
@@ -150,9 +150,14 @@
 
 
 def gathered_rows(table_rows, picks):
-    chosen = picks.reshape(-1)[:, None] == jnp.arange(table_rows.shape[0], dtype=jnp.int32)
-    values = jnp.dot(chosen.astype(table_rows.dtype), table_rows, preferred_element_type=jnp.float32)
-    return values.astype(table_rows.dtype).reshape(picks.shape + table_rows.shape[1:])
+    rows, width = table_rows.shape
+    paired = table_rows.reshape(rows // 2, 2 * width)
+    flat = picks.reshape(-1)
+    chosen = (flat // 2)[:, None] == jnp.arange(rows // 2, dtype=jnp.int32)
+    both = jnp.dot(chosen.astype(table_rows.dtype), paired, preferred_element_type=jnp.float32)
+    both = both.astype(table_rows.dtype)
+    values = jnp.where((flat % 2 == 0)[:, None], both[:, :width], both[:, width:])
+    return values.reshape(picks.shape + (width,))
 
 
 CODE_SPLIT = 64

time: 105 us -> 107 us (1.019)
  other arithmetic: 13.2 us -> 16.4 us
  matrix products: 25.8 us -> 23.1 us
  local copies, waits for them, and re-layouts: 3.45 us -> 4.65 us
    select_n x0 -> x4, other arithmetic: none -> 3.18 us  [the longest x2 3.14 us: gathered_rows(): jnp.where((flat % 2 == 0)[:, None], both[:, :width], both[:, width:])]
    dot_general x2, matrix products: 11.2 us -> 8.54 us  [gathered_rows(): jnp.dot(chosen.astype(table_rows.dtype), paired, preferred_element_type=j...]
    reshape x0 -> x3, local copies, waits for them, and re-layouts: none -> 1.44 us  [the longest x1 1.29 us: gathered_rows(): paired = table_rows.reshape(rows // 2, 2 * width)]
where the time goes in v14:
time: 107 us; the launch traced here: 106 us
  waiting for transfers between devices  37.4 us (35%)
  starting transfers between devices  24.3 us (23%)
  matrix products  23.1 us (22%)
  other arithmetic  16.4 us (15%)
  local copies, waits for them, and re-layouts  4.65 us (4%)
    all_to_all x1, waiting for transfers between devices, on_device(): lax.all_to_all(jnp.stack([same_sent, rise_sent], axis=1), 'py', 0, 0, til...  24 us
    ppermute x7, starting transfers between devices, shifted(): return lax.ppermute(shard, axis, pairs)  16.4 us
    ppermute x7, waiting for transfers between devices, shifted(): return lax.ppermute(shard, axis, pairs)  13.5 us
    dot_general x9, matrix products, dot32(): return jnp.dot(a, b, preferred_element_type=jnp.float32)  8.77 us
    dot_general x2, matrix products, gathered_rows(): jnp.dot(chosen.astype(table_rows.dtype), paired, preferred_element_type=j...  8.54 us
    all_to_all x1, starting transfers between devices, on_device(): lax.all_to_all(jnp.stack([same_sent, rise_sent], axis=1), 'py', 0, 0, til...  7.9 us
    dot_general x3, matrix products, one_hot_rows(): jnp.dot(picks.astype(values.dtype), values, preferred_element_type=jnp.fl...  5.8 us
    add x1, other arithmetic, on_device(): return col_weight * rows_done + (1.0 - col_weight) * horizontal  3.54 us
  transfers between devices with their start and end apart: 8, of which 5 were waited for; matrix products, arithmetic and copies ran while one was open for 6% of the time, Pallas kernels for 0%

profile of v14, /device:TPU:40, one launch (start us, length us, event | category | flops | bytes accessed | tf_op | source)
XLA Modules:
  0.0 106.5 jit_solution(6976841108400722906)
XLA Ops:
  0.0 1.2 %constant_dynamic-slice_fusion.3 = (s32[1,16,192]{1,2,0:T(8,128)S(1)}, s32[1,16,192]{1,2,0:T(8,128)S(1)}, s32[1,16,192]{1,2,0:T(8,128)S(1)}, s32[1,16,192]{1,2,0:T(8,128)S(1)}) fusion(s32[1,128,192]{1,2,0:T(8,128)} %param.8, s32[]{:T(128)S(6)} %select_n.183, s32[]{:T(128)S(6)} %select_n.190, s32[1,128,192]{1,2,0:T(8,128)} %param.7), kind=kLoop, calls=%fused_computation.182 | loop fusion | bytes 98312 | tf_op jit(solution)/shard_map/dynamic_slice | solution.py:206
  1.6 0.8 fusion.88
  2.6 1.3 %reshape.410 = bf16[1176,256]{1,0:T(8,128)(2,1)S(1)} reshape(bf16[2352,128]{1,0:T(8,128)(2,1)} %param.6) | data formatting | bytes 1204224 | tf_op jit(solution)/shard_map/reshape | solution.py:154
  4.2 4.3 %fusion.17 = bf16[3072,256]{1,0:T(8,128)(2,1)S(1)} fusion(bf16[1176,256]{1,0:T(8,128)(2,1)S(1)} %reshape.410, s32[3072]{0:T(1024)S(1)} %add_select_fusion.6), kind=kOutput, calls=%fused_computation.22 | convolution fusion | flops 1854087168 | bytes 2187264 | tf_op jit(solution)/shard_map/dot_general | solution.py:157
  8.5 4.3 %fusion.16 = bf16[3072,256]{1,0:T(8,128)(2,1)S(1)} fusion(bf16[1176,256]{1,0:T(8,128)(2,1)S(1)} %reshape.410, s32[3072]{0:T(1024)S(1)} %add_select_fusion.4), kind=kOutput, calls=%fused_computation.21 | convolution fusion | flops 1854087168 | bytes 2187264 | tf_op jit(solution)/shard_map/dot_general | solution.py:157
  12.8 1.6 %slice_select_fusion.1 = bf16[3072,128]{1,0:T(8,128)(2,1)S(1)} fusion(bf16[3072,256]{1,0:T(8,128)(2,1)S(1)} %fusion.17, pred[3072]{0:T(1024)(128)(4,1)S(1)} %fusion.66), kind=kLoop, calls=%fused_computation.70 | loop fusion | flops 393216 | bytes 2362368 | tf_op jit(solution)/shard_map/jit(_where)/select_n | solution.py:159
  14.4 1.6 %slice_select_fusion = bf16[3072,128]{1,0:T(8,128)(2,1)S(1)} fusion(bf16[3072,256]{1,0:T(8,128)(2,1)S(1)} %fusion.16, pred[3072]{0:T(1024)(128)(4,1)S(1)} %fusion.67), kind=kLoop, calls=%fused_computation.69 | loop fusion | flops 393216 | bytes 2362368 | tf_op jit(solution)/shard_map/jit(_where)/select_n | solution.py:159
  16.0 0.4 maximum_bitcast_fusion
  16.4 1.3 %pad_maximum_fusion.3 = bf16[16,2,208,128]{3,2,1,0:T(8,128)(2,1)} fusion(bf16[16,1,208,128]{3,2,1,0:T(8,128)(2,1)S(1)} %get-tuple-element.62, bf16[16,1,208,128]{3,2,1,0:T(8,128)(2,1)S(1)} %get-tuple-element.61), kind=kLoop, calls=%fused_computation.37 | loop fusion | flops 851968 | bytes 3407872 | tf_op jit(solution)/shard_map/stack | solution.py:217
  17.7 7.9 %all-to-all-start = ((bf16[16,2,208,128]{3,2,1,0:T(8,128)(2,1)}), bf16[16,2,208,128]{3,2,1,0:T(8,128)(2,1)S(1)}, u32[]{:S(2)}, u32[]{:S(2)}) async-start(bf16[16,2,208,128]{3,2,1,0:T(8,128)(2,1)} %pad_maximum_fusion.3), calls=%async_computation | async-start | bytes 3407872 | tf_op jit(solution)/shard_map/all_to_all | solution.py:217
  25.9 24.0 %all-to-all-done = bf16[16,2,208,128]{3,2,1,0:T(8,128)(2,1)S(1)} async-done(((bf16[16,2,208,128]{3,2,1,0:T(8,128)(2,1)}), bf16[16,2,208,128]{3,2,1,0:T(8,128)(2,1)S(1)}, u32[]{:S(2)}, u32[]{:S(2)}) %all-to-all-start) | async-done | bytes 1703968 | tf_op jit(solution)/shard_map/all_to_all | solution.py:217
  50.6 0.3 reduce-window.9
  51.2 0.8 fusion.10
  52.0 1.0 fusion.33
  53.0 0.1 maximum_maximum_fusion
  53.1 1.9 %collective-permute-start = (bf16[1,528,128]{2,1,0:T(8,128)(2,1)S(1)}, bf16[1,528,128]{2,1,0:T(8,128)(2,1)S(1)}, u32[]{:S(2)}, u32[]{:S(2)}) collective-permute-start(bf16[1,528,128]{2,1,0:T(8,128)(2,1)S(1)} %maximum_maximum_fusion), channel_id=1, source_target_pairs={{16,0},{32,16},{48,32},{64,48},{80,64},{96,80},{112,96},{17,1},{33... | collective-permute-start | bytes 405512 | tf_op jit(solution)/shard_map/ppermute | solution.py:17
  55.1 3.7 %fusion = f32[2048,128]{1,0:T(8,128)S(1)} fusion(bf16[3072,128]{1,0:T(8,128)(2,1)S(1)} %bitcast.114, s32[3072]{0:T(1024)S(1)} %eq.106, s32[2048]{0:T(1024)S(1)} %iota_add_fusion), kind=kOutput, calls=%fused_computation | convolution fusion | flops 1616904192 | bytes 1855488 | tf_op jit(solution)/shard_map/dot_general | solution.py:149
  58.8 1.1 %fusion.23 = bf16[2048,128]{1,0:T(8,128)(2,1)S(1)} fusion(f32[2048,128]{1,0:T(8,128)S(1)} %fusion, s32[512]{0:T(512)S(1)} %bitcast.121, s32[2048]{0:T(1024)S(1)} %iota_add_fusion, bf16[1,528,128]{2,1,0:T(8,128)(2,1)S(1)} %collective-permute-done), kind=kOutput, calls=%fused_computation.27 | convolution fusion | flops 270008320 | bytes 1714176 | tf_op jit(solution)/shard_map/dot_general | solution.py:149
  59.9 0.3 reshape.420
  60.3 0.5 convolution_convert_fusion
  60.8 0.5 convolution_convert_fusion.1
  61.3 0.7 fusion.45
  62.0 0.7 fusion.44
  62.7 0.3 multiply_convert_fusion.3
  63.1 1.0 multiply_convert_fusion.2
  64.0 1.3 %fusion.54 = f32[512,2048]{1,0:T(8,128)S(1)} fusion(bf16[512,512]{1,0:T(8,128)(2,1)S(1)} %copy-done.1, bf16[512,512]{1,0:T(8,128)(2,1)S(1)} %get-tuple-element.21, bf16[512,512]{1,0:T(8,128)(2,1)S(1)} %get-tuple-element.22, bf16[512,512]{1,0:T(8,128)(2,1)S(1)} %get-tuple-element.20, bf16[512,512]{1,0:T(8,128)(2,1)S(1)} %get-tuple-element.5), kind=kOutput, calls=%fused_computation.85 | convolution fusion | flops 1082130432 | bytes 6815744 | tf_op jit(solution)/shard_map/dot_general | solution.py:51
  65.3 1.3 %fusion.55 = f32[512,2048]{1,0:T(8,128)S(1)} fusion(bf16[512,512]{1,0:T(8,128)(2,1)S(1)} %copy-done, bf16[512,512]{1,0:T(8,128)(2,1)S(1)} %get-tuple-element.21, bf16[512,512]{1,0:T(8,128)(2,1)S(1)} %get-tuple-element.22, bf16[512,512]{1,0:T(8,128)(2,1)S(1)} %get-tuple-element.20, bf16[512,512]{1,0:T(8,128)(2,1)S(1)} %get-tuple-element.5), kind=kOutput, calls=%fused_computation.86 | convolution fusion | flops 1082130432 | bytes 6815744 | tf_op jit(solution)/shard_map/dot_general | solution.py:51
  66.6 1.2 %fusion.27 = (bf16[512,1024]{1,0:T(8,128)(2,1)S(1)}, bf16[512,1024]{1,0:T(8,128)(2,1)S(1)}) fusion(f32[512,2048]{1,0:T(8,128)S(1)} %fusion.54, f32[512,2048]{1,0:T(8,128)S(1)} %fusion.55), kind=kLoop, calls=%fused_computation.31 | loop fusion | flops 2097152 | bytes 10485760 | tf_op jit(solution)/shard_map/convert.20
  67.9 1.3 %fusion.94 = f32[2048,512]{1,0:T(8,128)S(1)} fusion(bf16[512,512]{1,0:T(8,128)(2,1)S(1)} %copy-done.1, bf16[512,512]{1,0:T(8,128)(2,1)S(1)} %get-tuple-element.32, bf16[512,512]{1,0:T(8,128)(2,1)S(1)} %get-tuple-element.31, bf16[512,512]{1,0:T(8,128)(2,1)S(1)} %get-tuple-element.30, bf16[512,512]{1,0:T(8,128)(2,1)S(1)} %get-tuple-element.29), kind=kOutput, calls=%fused_computation.208 | convolution fusion | flops 1082130432 | bytes 6815744 | tf_op jit(solution)/shard_map/dot_general | solution.py:51
  69.2 1.3 %fusion.95 = f32[2048,512]{1,0:T(8,128)S(1)} fusion(bf16[512,512]{1,0:T(8,128)(2,1)S(1)} %copy-done, bf16[512,512]{1,0:T(8,128)(2,1)S(1)} %get-tuple-element.32, bf16[512,512]{1,0:T(8,128)(2,1)S(1)} %get-tuple-element.31, bf16[512,512]{1,0:T(8,128)(2,1)S(1)} %get-tuple-element.30, bf16[512,512]{1,0:T(8,128)(2,1)S(1)} %get-tuple-element.29), kind=kOutput, calls=%fused_computation.209 | convolution fusion | flops 1082130432 | bytes 6815744 | tf_op jit(solution)/shard_map/dot_general | solution.py:51
  70.5 1.2 %fusion.93 = f32[2048,512]{1,0:T(8,128)S(1)} fusion(bf16[512,512]{1,0:T(8,128)(2,1)S(1)} %copy-done.2, bf16[512,512]{1,0:T(8,128)(2,1)S(1)} %get-tuple-element.32, bf16[512,512]{1,0:T(8,128)(2,1)S(1)} %get-tuple-element.31, bf16[512,512]{1,0:T(8,128)(2,1)S(1)} %get-tuple-element.30, bf16[512,512]{1,0:T(8,128)(2,1)S(1)} %get-tuple-element.29), kind=kOutput, calls=%fused_computation.207 | convolution fusion | flops 1082130432 | bytes 6815744 | tf_op jit(solution)/shard_map/dot_general | solution.py:51
  71.8 0.3 fusion.56
  72.0 0.1 pad_maximum_fusion.5
  72.2 0.2 fusion.98
  72.4 2.0 %collective-permute-start.4 = (bf16[4,512,128]{2,1,0:T(8,128)(2,1)S(1)}, bf16[4,512,128]{2,1,0:T(8,128)(2,1)S(1)}, u32[]{:S(2)}, u32[]{:S(2)}) collective-permute-start(bf16[4,512,128]{2,1,0:T(8,128)(2,1)S(1)} %get-tuple-element.28), channel_id=1, source_target_pairs={{1,0},{2,1},{3,2},{4,3},{5,4},{6,5},{7,6},{8,7},{9,8},{10,9},{11,1... | collective-permute-start | bytes 1572872 | tf_op jit(solution)/shard_map/ppermute | solution.py:17
  74.4 3.8 %collective-permute-start.3 = (bf16[4,512,128]{2,1,0:T(8,128)(2,1)S(1)}, bf16[4,512,128]{2,1,0:T(8,128)(2,1)S(1)}, u32[]{:S(2)}, u32[]{:S(2)}) collective-permute-start(bf16[4,512,128]{2,1,0:T(8,128)(2,1)S(1)} %get-tuple-element.27), channel_id=1, source_target_pairs={{0,1},{1,2},{2,3},{3,4},{4,5},{5,6},{6,7},{7,8},{8,9},{9,10},{10,1... | collective-permute-start | bytes 1572872 | tf_op jit(solution)/shard_map/ppermute | solution.py:17
  78.2 1.2 %fusion.46 = (bf16[1,512,512]{2,1,0:T(8,128)(2,1)S(1)}, bf16[1,512,512]{2,1,0:T(8,128)(2,1)S(1)}, bf16[1,512,512]{2,1,0:T(8,128)(2,1)S(1)}, bf16[1,512,512]{2,1,0:T(8,128)(2,1)S(1)}) fusion(f32[2048,512]{1,0:T(8,128)S(1)} %fusion.94, f32[2048,512]{1,0:T(8,128)S(1)} %fusion.95), kind=kLoop, calls=%fused_computation.73 | loop fusion | flops 2097152 | bytes 10485760 | tf_op jit(solution)/shard_map/stack | solution.py:112
  79.5 0.3 pad_maximum_fusion.2
  79.8 2.0 %collective-permute-start.2 = (bf16[4,128,512]{2,1,0:T(8,128)(2,1)S(1)}, bf16[4,128,512]{2,1,0:T(8,128)(2,1)S(1)}, u32[]{:S(2)}, u32[]{:S(2)}) collective-permute-start(bf16[4,128,512]{2,1,0:T(8,128)(2,1)S(1)} %get-tuple-element.24), channel_id=1, source_target_pairs={{16,0},{32,16},{48,32},{64,48},{80,64},{96,80},{112,96},{17,1},{33... | collective-permute-start | bytes 1572872 | tf_op jit(solution)/shard_map/ppermute | solution.py:17
  81.9 2.3 %collective-permute-start.1 = (bf16[4,128,512]{2,1,0:T(8,128)(2,1)S(1)}, bf16[4,128,512]{2,1,0:T(8,128)(2,1)S(1)}, u32[]{:S(2)}, u32[]{:S(2)}) collective-permute-start(bf16[4,128,512]{2,1,0:T(8,128)(2,1)S(1)} %get-tuple-element.23), channel_id=1, source_target_pairs={{0,16},{16,32},{32,48},{48,64},{64,80},{80,96},{96,112},{1,17},{17... | collective-permute-start | bytes 1572872 | tf_op jit(solution)/shard_map/ppermute | solution.py:17
  84.2 4.5 %collective-permute-done.4 = bf16[4,512,128]{2,1,0:T(8,128)(2,1)S(1)} collective-permute-done((bf16[4,512,128]{2,1,0:T(8,128)(2,1)S(1)}, bf16[4,512,128]{2,1,0:T(8,128)(2,1)S(1)}, u32[]{:S(2)}, u32[]{:S(2)}) %collective-permute-start.4) | collective-permute-done | bytes 524320 | tf_op jit(solution)/shard_map/ppermute | solution.py:17
  88.7 4.0 %collective-permute-done.3 = bf16[4,512,128]{2,1,0:T(8,128)(2,1)S(1)} collective-permute-done((bf16[4,512,128]{2,1,0:T(8,128)(2,1)S(1)}, bf16[4,512,128]{2,1,0:T(8,128)(2,1)S(1)}, u32[]{:S(2)}, u32[]{:S(2)}) %collective-permute-start.3) | collective-permute-done | bytes 524320 | tf_op jit(solution)/shard_map/ppermute | solution.py:17
  92.8 1.9 %collective-permute-start.6 = (bf16[4,128,256]{2,1,0:T(8,128)(2,1)S(1)}, bf16[4,128,256]{2,1,0:T(8,128)(2,1)S(1)}, u32[]{:S(2)}, u32[]{:S(2)}) collective-permute-start(bf16[4,128,256]{2,1,0:T(8,128)(2,1)S(1)} %pad_maximum_fusion.11), channel_id=1, source_target_pairs={{16,0},{32,16},{48,32},{64,48},{80,64},{96,80},{112,96},{17,1},{33... | collective-permute-start | bytes 786440 | tf_op jit(solution)/shard_map/ppermute | solution.py:17
  94.8 2.4 %collective-permute-start.5 = (bf16[4,128,256]{2,1,0:T(8,128)(2,1)S(1)}, bf16[4,128,256]{2,1,0:T(8,128)(2,1)S(1)}, u32[]{:S(2)}, u32[]{:S(2)}) collective-permute-start(bf16[4,128,256]{2,1,0:T(8,128)(2,1)S(1)} %pad_maximum_fusion.10), channel_id=1, source_target_pairs={{0,16},{16,32},{32,48},{48,64},{64,80},{80,96},{96,112},{1,17},{17... | collective-permute-start | bytes 786440 | tf_op jit(solution)/shard_map/ppermute | solution.py:17
  97.5 1.1 collective-permute-done.6
  98.7 3.8 %collective-permute-done.5 = bf16[4,128,256]{2,1,0:T(8,128)(2,1)S(1)} collective-permute-done((bf16[4,128,256]{2,1,0:T(8,128)(2,1)S(1)}, bf16[4,128,256]{2,1,0:T(8,128)(2,1)S(1)}, u32[]{:S(2)}, u32[]{:S(2)}) %collective-permute-start.5) | collective-permute-done | bytes 262176 | tf_op jit(solution)/shard_map/ppermute | solution.py:17
  102.5 0.4 fusion.41
  102.9 3.5 %fusion.13 = f32[4,512,512]{2,1,0:T(8,128)} fusion(f32[4,128,512]{2,1,0:T(8,128)S(1)} %convert_element_type.165, f32[4,128,512]{2,1,0:T(8,128)S(1)} %convert_element_type.164, f32[4,512,128]{2,1,0:T(8,128)S(1)} %get-tuple-element.50, f32[4,512,128]{2,1,0:T(8,128)S(1)} %get-tuple-element.49, f32[512]{0:T(512)S(1)} %pad.18.clone, ...), kind=kLoop, calls=%fused_computation.17 | loop fusion | flops 14680064 | bytes 10496000 | tf_op jit(solution)/shard_map/add | solution.py:274
  (72 shorter events, 2.9 us)
Async XLA Ops:
  17.7 32.1 %all-to-all-start = ((bf16[16,2,208,128]{3,2,1,0:T(8,128)(2,1)}), bf16[16,2,208,128]{3,2,1,0:T(8,128)(2,1)S(1)}, u32[]{:S(2)}, u32[]{:S(2)}) async-start(bf16[16,2,208,128]{3,2,1,0:T(8,128)(2,1)} %pad_maximum_fusion.3), calls=%async_computation | async-start | bytes 3407872 | tf_op jit(solution)/shard_map/all_to_all | solution.py:217
  53.1 5.7 %collective-permute-start = (bf16[1,528,128]{2,1,0:T(8,128)(2,1)S(1)}, bf16[1,528,128]{2,1,0:T(8,128)(2,1)S(1)}, u32[]{:S(2)}, u32[]{:S(2)}) collective-permute-start(bf16[1,528,128]{2,1,0:T(8,128)(2,1)S(1)} %maximum_maximum_fusion), channel_id=1, source_target_pairs={{16,0},{32,16},{48,32},{64,48},{80,64},{96,80},{112,96},{17,1},{33... | collective-permute-start | bytes 405512 | tf_op jit(solution)/shard_map/ppermute | solution.py:17
  55.1 5.2 %copy-start.1 = (bf16[512,512]{1,0:T(8,128)(2,1)S(1)}, bf16[512,512]{1,0:T(8,128)(2,1)}, u32[]{:S(2)}) copy-start(bf16[512,512]{1,0:T(8,128)(2,1)} %constant.163.clone) | copy-start | bytes 1572868
  58.8 2.0 %copy-start = (bf16[512,512]{1,0:T(8,128)(2,1)S(1)}, bf16[512,512]{1,0:T(8,128)(2,1)}, u32[]{:S(2)}) copy-start(bf16[512,512]{1,0:T(8,128)(2,1)} %constant.162.clone) | copy-start | bytes 1572868
  69.2 1.3 %copy-start.2 = (bf16[512,512]{1,0:T(8,128)(2,1)S(1)}, bf16[512,512]{1,0:T(8,128)(2,1)}, u32[]{:S(2)}) copy-start(bf16[512,512]{1,0:T(8,128)(2,1)} %constant.172) | copy-start | bytes 1572868
  72.4 16.3 %collective-permute-start.4 = (bf16[4,512,128]{2,1,0:T(8,128)(2,1)S(1)}, bf16[4,512,128]{2,1,0:T(8,128)(2,1)S(1)}, u32[]{:S(2)}, u32[]{:S(2)}) collective-permute-start(bf16[4,512,128]{2,1,0:T(8,128)(2,1)S(1)} %get-tuple-element.28), channel_id=1, source_target_pairs={{1,0},{2,1},{3,2},{4,3},{5,4},{6,5},{7,6},{8,7},{9,8},{10,9},{11,1... | collective-permute-start | bytes 1572872 | tf_op jit(solution)/shard_map/ppermute | solution.py:17
  74.4 18.4 %collective-permute-start.3 = (bf16[4,512,128]{2,1,0:T(8,128)(2,1)S(1)}, bf16[4,512,128]{2,1,0:T(8,128)(2,1)S(1)}, u32[]{:S(2)}, u32[]{:S(2)}) collective-permute-start(bf16[4,512,128]{2,1,0:T(8,128)(2,1)S(1)} %get-tuple-element.27), channel_id=1, source_target_pairs={{0,1},{1,2},{2,3},{3,4},{4,5},{5,6},{6,7},{7,8},{8,9},{9,10},{10,1... | collective-permute-start | bytes 1572872 | tf_op jit(solution)/shard_map/ppermute | solution.py:17
  79.8 17.4 %collective-permute-start.2 = (bf16[4,128,512]{2,1,0:T(8,128)(2,1)S(1)}, bf16[4,128,512]{2,1,0:T(8,128)(2,1)S(1)}, u32[]{:S(2)}, u32[]{:S(2)}) collective-permute-start(bf16[4,128,512]{2,1,0:T(8,128)(2,1)S(1)} %get-tuple-element.24), channel_id=1, source_target_pairs={{16,0},{32,16},{48,32},{64,48},{80,64},{96,80},{112,96},{17,1},{33... | collective-permute-start | bytes 1572872 | tf_op jit(solution)/shard_map/ppermute | solution.py:17
  81.9 15.6 %collective-permute-start.1 = (bf16[4,128,512]{2,1,0:T(8,128)(2,1)S(1)}, bf16[4,128,512]{2,1,0:T(8,128)(2,1)S(1)}, u32[]{:S(2)}, u32[]{:S(2)}) collective-permute-start(bf16[4,128,512]{2,1,0:T(8,128)(2,1)S(1)} %get-tuple-element.23), channel_id=1, source_target_pairs={{0,16},{16,32},{32,48},{48,64},{64,80},{80,96},{96,112},{1,17},{17... | collective-permute-start | bytes 1572872 | tf_op jit(solution)/shard_map/ppermute | solution.py:17
  92.8 5.8 %collective-permute-start.6 = (bf16[4,128,256]{2,1,0:T(8,128)(2,1)S(1)}, bf16[4,128,256]{2,1,0:T(8,128)(2,1)S(1)}, u32[]{:S(2)}, u32[]{:S(2)}) collective-permute-start(bf16[4,128,256]{2,1,0:T(8,128)(2,1)S(1)} %pad_maximum_fusion.11), channel_id=1, source_target_pairs={{16,0},{32,16},{48,32},{64,48},{80,64},{96,80},{112,96},{17,1},{33... | collective-permute-start | bytes 786440 | tf_op jit(solution)/shard_map/ppermute | solution.py:17
  94.8 7.7 %collective-permute-start.5 = (bf16[4,128,256]{2,1,0:T(8,128)(2,1)S(1)}, bf16[4,128,256]{2,1,0:T(8,128)(2,1)S(1)}, u32[]{:S(2)}, u32[]{:S(2)}) collective-permute-start(bf16[4,128,256]{2,1,0:T(8,128)(2,1)S(1)} %pad_maximum_fusion.10), channel_id=1, source_target_pairs={{0,16},{16,32},{32,48},{48,64},{64,80},{80,96},{96,112},{1,17},{17... | collective-permute-start | bytes 786440 | tf_op jit(solution)/shard_map/ppermute | solution.py:17

commit v15 on v11

--- a/solution.py
+++ b/solution.py
@@ -149,6 +149,20 @@
     return jnp.dot(picks.astype(values.dtype), values, preferred_element_type=jnp.float32)
 
 
+def placed_rows(codes, row_count, values):
+    width = values.shape[1]
+    per_row = PATCH_COLS // width
+    slots = codes - 1
+    quarter = slots % per_row
+    spread = jnp.where(
+        quarter[:, None, None] == jnp.arange(per_row, dtype=jnp.int32)[None, :, None],
+        values[:, None, :],
+        jnp.zeros((), values.dtype),
+    ).reshape(values.shape[0], per_row * width)
+    picks = (slots // per_row)[None, :] == jnp.arange(row_count, dtype=jnp.int32)[:, None]
+    return jnp.dot(picks.astype(values.dtype), spread, preferred_element_type=jnp.float32)
+
+
 def gathered_rows(table_rows, picks):
     chosen = picks.reshape(-1)[:, None] == jnp.arange(table_rows.shape[0], dtype=jnp.int32)
     values = jnp.dot(chosen.astype(table_rows.dtype), table_rows, preferred_element_type=jnp.float32)
@@ -221,11 +235,11 @@
     packed = with_codes(packed_values.reshape(1, rise_total, tile_width), packed_codes[None])
     raised_values, raised_codes = split_codes(shifted(packed, "px", -1), rise_total)
     slot_total = PATCH_ROWS * PATCH_COLS // tile_width
-    patch_tiles = (
-        one_hot_rows(same_codes, slot_total, same_values)
-        + one_hot_rows(raised_codes, slot_total, raised_values)
+    pixels = (
+        placed_rows(same_codes, PATCH_ROWS, same_values)
+        + placed_rows(raised_codes, PATCH_ROWS, raised_values)
     ).astype(kappa.dtype)
-    edge_fields, fields = flexion_fields(patch_tiles.reshape(PATCH_ROWS, PATCH_COLS))
+    edge_fields, fields = flexion_fields(pixels)
     width = tile_width
     last = PATCH_ROWS - width
     left = shifted(edge_fields[:, :, width:], "py", 1)

time: 105 us -> 110 us (1.048)
  other arithmetic: 13.2 us -> 20.6 us
  matrix products: 25.8 us -> 23.2 us
    select_n x0 -> x5, other arithmetic: none -> 7.23 us  [the longest x2 7.19 us: placed_rows(): jnp.where(quarter[:, None, None] == jnp.arange(per_row, dtype=jnp.int32)[...]
    dot_general x3 -> x1, matrix products: 5.81 us -> 1.03 us  [one_hot_rows(): jnp.dot(picks.astype(values.dtype), values, preferred_element_type=jnp.fl...]
    dot_general x0 -> x2, matrix products: none -> 2.24 us  [placed_rows(): jnp.dot(picks.astype(values.dtype), spread, preferred_element_type=jnp.fl...]
  transfers between devices with their start and end apart: 8 -> 8, of which waited for: 5 -> 5; matrix products, arithmetic and copies ran while one was open for 6% -> 8% of each run, Pallas kernels for 0% -> 0%
where the time goes in v15:
time: 110 us
  waiting for transfers between devices  37.4 us (34%)
  starting transfers between devices  24.5 us (22%)
  matrix products  23.2 us (21%)
  other arithmetic  20.6 us (19%)
  local copies, waits for them, and re-layouts  3.79 us (3%)
    all_to_all x1, waiting for transfers between devices, on_device(): lax.all_to_all(jnp.stack([same_sent, rise_sent], axis=1), 'py', 0, 0, til...  24 us
    ppermute x7, starting transfers between devices, shifted(): return lax.ppermute(shard, axis, pairs)  16.6 us
    ppermute x7, waiting for transfers between devices, shifted(): return lax.ppermute(shard, axis, pairs)  13.4 us
    dot_general x2, matrix products, gathered_rows(): jnp.dot(chosen.astype(table_rows.dtype), table_rows, preferred_element_ty...  11.2 us
    dot_general x9, matrix products, dot32(): return jnp.dot(a, b, preferred_element_type=jnp.float32)  8.75 us
    all_to_all x1, starting transfers between devices, on_device(): lax.all_to_all(jnp.stack([same_sent, rise_sent], axis=1), 'py', 0, 0, til...  7.89 us
    select_n x2, other arithmetic, placed_rows(): jnp.where(quarter[:, None, None] == jnp.arange(per_row, dtype=jnp.int32)[...  7.19 us
    add x1, other arithmetic, on_device(): return col_weight * rows_done + (1.0 - col_weight) * horizontal  3.54 us
  transfers between devices with their start and end apart: 8, of which 5 were waited for; matrix products, arithmetic and copies ran while one was open for 8% of the time, Pallas kernels for 0%

profile of v15, /device:TPU:40, one launch (start us, length us, event | category | flops | bytes accessed | tf_op | source)
XLA Modules:
  0.0 110.0 jit_solution(16515646956383976605)
XLA Ops:
  0.0 1.3 %constant_dynamic-slice_fusion.3 = (s32[1,16,192]{1,2,0:T(8,128)S(1)}, s32[1,16,192]{1,2,0:T(8,128)S(1)}, s32[1,16,192]{1,2,0:T(8,128)S(1)}, s32[1,16,192]{1,2,0:T(8,128)S(1)}) fusion(s32[1,128,192]{1,2,0:T(8,128)} %param.8, s32[]{:T(128)S(6)} %select_n.193, s32[]{:T(128)S(6)} %select_n.197, s32[1,128,192]{1,2,0:T(8,128)} %param.7), kind=kLoop, calls=%fused_computation.184 | loop fusion | bytes 98312 | tf_op jit(solution)/shard_map/dynamic_slice | solution.py:215
  1.3 0.8 fusion.81
  2.9 5.6 %fusion.12 = bf16[3072,128]{1,0:T(8,128)(2,1)S(1)} fusion(bf16[2352,128]{1,0:T(8,128)(2,1)S(1)} %copy-done, s32[3072]{0:T(1024)S(1)} %eq.123), kind=kOutput, calls=%fused_computation.18 | convolution fusion | flops 1857306624 | bytes 1400832 | tf_op jit(solution)/shard_map/dot_general | solution.py:168
  8.5 5.6 %fusion.11 = bf16[3072,128]{1,0:T(8,128)(2,1)S(1)} fusion(bf16[2352,128]{1,0:T(8,128)(2,1)S(1)} %copy-done, s32[3072]{0:T(1024)S(1)} %eq.127), kind=kOutput, calls=%fused_computation.17 | convolution fusion | flops 1857306624 | bytes 1400832 | tf_op jit(solution)/shard_map/dot_general | solution.py:168
  14.2 0.4 maximum_bitcast_fusion
  14.6 1.3 %pad_maximum_fusion.3 = bf16[16,2,208,128]{3,2,1,0:T(8,128)(2,1)} fusion(bf16[16,1,208,128]{3,2,1,0:T(8,128)(2,1)S(1)} %get-tuple-element.66, bf16[16,1,208,128]{3,2,1,0:T(8,128)(2,1)S(1)} %get-tuple-element.65), kind=kLoop, calls=%fused_computation.33 | loop fusion | flops 851968 | bytes 3407872 | tf_op jit(solution)/shard_map/stack | solution.py:226
  15.9 7.9 %all-to-all-start = ((bf16[16,2,208,128]{3,2,1,0:T(8,128)(2,1)}), bf16[16,2,208,128]{3,2,1,0:T(8,128)(2,1)S(1)}, u32[]{:S(2)}, u32[]{:S(2)}) async-start(bf16[16,2,208,128]{3,2,1,0:T(8,128)(2,1)} %pad_maximum_fusion.3), calls=%async_computation | async-start | bytes 3407872 | tf_op jit(solution)/shard_map/all_to_all | solution.py:226
  24.1 24.0 %all-to-all-done = bf16[16,2,208,128]{3,2,1,0:T(8,128)(2,1)S(1)} async-done(((bf16[16,2,208,128]{3,2,1,0:T(8,128)(2,1)}), bf16[16,2,208,128]{3,2,1,0:T(8,128)(2,1)S(1)}, u32[]{:S(2)}, u32[]{:S(2)}) %all-to-all-start) | async-done | bytes 1703968 | tf_op jit(solution)/shard_map/all_to_all | solution.py:226
  48.6 0.7 copy.32
  49.5 0.3 reduce-window.9
  50.1 0.8 fusion.6
  50.9 1.0 fusion.24
  51.9 0.1 maximum_maximum_fusion
  52.0 2.1 %collective-permute-start = (bf16[1,528,128]{2,1,0:T(8,128)(2,1)S(1)}, bf16[1,528,128]{2,1,0:T(8,128)(2,1)S(1)}, u32[]{:S(2)}, u32[]{:S(2)}) collective-permute-start(bf16[1,528,128]{2,1,0:T(8,128)(2,1)S(1)} %maximum_maximum_fusion), channel_id=1, source_target_pairs={{16,0},{32,16},{48,32},{64,48},{80,64},{96,80},{112,96},{17,1},{33... | collective-permute-start | bytes 405512 | tf_op jit(solution)/shard_map/ppermute | solution.py:17
  54.2 4.6 %broadcast_select_fusion = bf16[3072,4,128]{2,1,0:T(4,128)(2,1)S(1)} fusion(pred[3072,4]{1,0:T(8,128)(4,1)S(1)} %copy.32, bf16[3072,128]{1,0:T(8,128)(2,1)S(1)} %bitcast.120), kind=kLoop, calls=%fused_computation.24 | loop fusion | flops 1572864 | bytes 3944448 | tf_op jit(solution)/shard_map/jit(_where)/select_n | solution.py:157
  58.8 1.8 %fusion.7 = f32[512,512]{1,0:T(8,128)S(1)} fusion(bf16[384,8,4,128]{3,2,1,0:T(4,128)(2,1)S(1)} %bitcast.119, s32[3072]{0:T(1024)S(1)} %get-tuple-element.51), kind=kOutput, calls=%fused_computation.11 | convolution fusion | flops 1612185600 | bytes 4206592 | tf_op jit(solution)/shard_map/dot_general | solution.py:163
  60.7 0.1 iota_compare_fusion.12
  60.8 2.6 %broadcast_select_fusion.1 = bf16[512,4,128]{2,1,0:T(4,128)(2,1)S(1)} fusion(pred[512,4]{1,0:T(8,128)(4,1)S(1)} %iota_compare_fusion.12, bf16[512,128]{1,0:T(8,128)(2,1)S(1)} %slice_bitcast_fusion.2), kind=kLoop, calls=%fused_computation.85 | loop fusion | flops 262144 | bytes 657408 | tf_op jit(solution)/shard_map/jit(_where)/select_n | solution.py:157
  63.4 0.4 fusion.20
  63.9 0.5 convolution_convert_fusion
  64.4 0.5 convolution_convert_fusion.1
  64.9 0.7 fusion.36
  65.6 0.7 fusion.35
  66.4 0.3 multiply_convert_fusion.3
  66.7 1.0 multiply_convert_fusion.2
  67.7 1.3 %fusion.48 = f32[512,2048]{1,0:T(8,128)S(1)} fusion(bf16[512,512]{1,0:T(8,128)(2,1)S(1)} %copy-done.3, bf16[512,512]{1,0:T(8,128)(2,1)S(1)} %get-tuple-element.23, bf16[512,512]{1,0:T(8,128)(2,1)S(1)} %get-tuple-element.24, bf16[512,512]{1,0:T(8,128)(2,1)S(1)} %get-tuple-element.22, bf16[512,512]{1,0:T(8,128)(2,1)S(1)} %get-tuple-element.5), kind=kOutput, calls=%fused_computation.86 | convolution fusion | flops 1082130432 | bytes 6815744 | tf_op jit(solution)/shard_map/dot_general | solution.py:51
  68.9 1.3 %fusion.49 = f32[512,2048]{1,0:T(8,128)S(1)} fusion(bf16[512,512]{1,0:T(8,128)(2,1)S(1)} %copy-done.2, bf16[512,512]{1,0:T(8,128)(2,1)S(1)} %get-tuple-element.23, bf16[512,512]{1,0:T(8,128)(2,1)S(1)} %get-tuple-element.24, bf16[512,512]{1,0:T(8,128)(2,1)S(1)} %get-tuple-element.22, bf16[512,512]{1,0:T(8,128)(2,1)S(1)} %get-tuple-element.5), kind=kOutput, calls=%fused_computation.87 | convolution fusion | flops 1082130432 | bytes 6815744 | tf_op jit(solution)/shard_map/dot_general | solution.py:51
  70.2 1.2 %fusion.19 = (bf16[512,1024]{1,0:T(8,128)(2,1)S(1)}, bf16[512,1024]{1,0:T(8,128)(2,1)S(1)}) fusion(f32[512,2048]{1,0:T(8,128)S(1)} %fusion.48, f32[512,2048]{1,0:T(8,128)S(1)} %fusion.49), kind=kLoop, calls=%fused_computation.29 | loop fusion | flops 2097152 | bytes 10485760 | tf_op jit(solution)/shard_map/convert.20
  71.5 1.3 %fusion.87 = f32[2048,512]{1,0:T(8,128)S(1)} fusion(bf16[512,512]{1,0:T(8,128)(2,1)S(1)} %copy-done.3, bf16[512,512]{1,0:T(8,128)(2,1)S(1)} %get-tuple-element.34, bf16[512,512]{1,0:T(8,128)(2,1)S(1)} %get-tuple-element.33, bf16[512,512]{1,0:T(8,128)(2,1)S(1)} %get-tuple-element.32, bf16[512,512]{1,0:T(8,128)(2,1)S(1)} %get-tuple-element.31), kind=kOutput, calls=%fused_computation.210 | convolution fusion | flops 1082130432 | bytes 6815744 | tf_op jit(solution)/shard_map/dot_general | solution.py:51
  72.8 1.2 %fusion.88 = f32[2048,512]{1,0:T(8,128)S(1)} fusion(bf16[512,512]{1,0:T(8,128)(2,1)S(1)} %copy-done.2, bf16[512,512]{1,0:T(8,128)(2,1)S(1)} %get-tuple-element.34, bf16[512,512]{1,0:T(8,128)(2,1)S(1)} %get-tuple-element.33, bf16[512,512]{1,0:T(8,128)(2,1)S(1)} %get-tuple-element.32, bf16[512,512]{1,0:T(8,128)(2,1)S(1)} %get-tuple-element.31), kind=kOutput, calls=%fused_computation.211 | convolution fusion | flops 1082130432 | bytes 6815744 | tf_op jit(solution)/shard_map/dot_general | solution.py:51
  74.1 1.3 %fusion.86 = f32[2048,512]{1,0:T(8,128)S(1)} fusion(bf16[512,512]{1,0:T(8,128)(2,1)S(1)} %copy-done.4, bf16[512,512]{1,0:T(8,128)(2,1)S(1)} %get-tuple-element.34, bf16[512,512]{1,0:T(8,128)(2,1)S(1)} %get-tuple-element.33, bf16[512,512]{1,0:T(8,128)(2,1)S(1)} %get-tuple-element.32, bf16[512,512]{1,0:T(8,128)(2,1)S(1)} %get-tuple-element.31), kind=kOutput, calls=%fused_computation.209 | convolution fusion | flops 1082130432 | bytes 6815744 | tf_op jit(solution)/shard_map/dot_general | solution.py:51
  75.3 0.3 fusion.50
  75.6 0.1 pad_maximum_fusion.5
  75.8 0.2 fusion.92
  76.0 2.0 %collective-permute-start.4 = (bf16[4,512,128]{2,1,0:T(8,128)(2,1)S(1)}, bf16[4,512,128]{2,1,0:T(8,128)(2,1)S(1)}, u32[]{:S(2)}, u32[]{:S(2)}) collective-permute-start(bf16[4,512,128]{2,1,0:T(8,128)(2,1)S(1)} %get-tuple-element.30), channel_id=1, source_target_pairs={{1,0},{2,1},{3,2},{4,3},{5,4},{6,5},{7,6},{8,7},{9,8},{10,9},{11,1... | collective-permute-start | bytes 1572872 | tf_op jit(solution)/shard_map/ppermute | solution.py:17
  78.0 3.8 %collective-permute-start.3 = (bf16[4,512,128]{2,1,0:T(8,128)(2,1)S(1)}, bf16[4,512,128]{2,1,0:T(8,128)(2,1)S(1)}, u32[]{:S(2)}, u32[]{:S(2)}) collective-permute-start(bf16[4,512,128]{2,1,0:T(8,128)(2,1)S(1)} %get-tuple-element.29), channel_id=1, source_target_pairs={{0,1},{1,2},{2,3},{3,4},{4,5},{5,6},{6,7},{7,8},{8,9},{9,10},{10,1... | collective-permute-start | bytes 1572872 | tf_op jit(solution)/shard_map/ppermute | solution.py:17
  81.8 1.2 %fusion.37 = (bf16[1,512,512]{2,1,0:T(8,128)(2,1)S(1)}, bf16[1,512,512]{2,1,0:T(8,128)(2,1)S(1)}, bf16[1,512,512]{2,1,0:T(8,128)(2,1)S(1)}, bf16[1,512,512]{2,1,0:T(8,128)(2,1)S(1)}) fusion(f32[2048,512]{1,0:T(8,128)S(1)} %fusion.87, f32[2048,512]{1,0:T(8,128)S(1)} %fusion.88), kind=kLoop, calls=%fused_computation.70 | loop fusion | flops 2097152 | bytes 10485760 | tf_op jit(solution)/shard_map/stack | solution.py:112
  83.1 0.3 pad_maximum_fusion.2
  83.4 1.9 %collective-permute-start.2 = (bf16[4,128,512]{2,1,0:T(8,128)(2,1)S(1)}, bf16[4,128,512]{2,1,0:T(8,128)(2,1)S(1)}, u32[]{:S(2)}, u32[]{:S(2)}) collective-permute-start(bf16[4,128,512]{2,1,0:T(8,128)(2,1)S(1)} %get-tuple-element.26), channel_id=1, source_target_pairs={{16,0},{32,16},{48,32},{64,48},{80,64},{96,80},{112,96},{17,1},{33... | collective-permute-start | bytes 1572872 | tf_op jit(solution)/shard_map/ppermute | solution.py:17
  85.4 2.4 %collective-permute-start.1 = (bf16[4,128,512]{2,1,0:T(8,128)(2,1)S(1)}, bf16[4,128,512]{2,1,0:T(8,128)(2,1)S(1)}, u32[]{:S(2)}, u32[]{:S(2)}) collective-permute-start(bf16[4,128,512]{2,1,0:T(8,128)(2,1)S(1)} %get-tuple-element.25), channel_id=1, source_target_pairs={{0,16},{16,32},{32,48},{48,64},{64,80},{80,96},{96,112},{1,17},{17... | collective-permute-start | bytes 1572872 | tf_op jit(solution)/shard_map/ppermute | solution.py:17
  87.8 4.4 %collective-permute-done.4 = bf16[4,512,128]{2,1,0:T(8,128)(2,1)S(1)} collective-permute-done((bf16[4,512,128]{2,1,0:T(8,128)(2,1)S(1)}, bf16[4,512,128]{2,1,0:T(8,128)(2,1)S(1)}, u32[]{:S(2)}, u32[]{:S(2)}) %collective-permute-start.4) | collective-permute-done | bytes 524320 | tf_op jit(solution)/shard_map/ppermute | solution.py:17
  92.2 4.0 %collective-permute-done.3 = bf16[4,512,128]{2,1,0:T(8,128)(2,1)S(1)} collective-permute-done((bf16[4,512,128]{2,1,0:T(8,128)(2,1)S(1)}, bf16[4,512,128]{2,1,0:T(8,128)(2,1)S(1)}, u32[]{:S(2)}, u32[]{:S(2)}) %collective-permute-start.3) | collective-permute-done | bytes 524320 | tf_op jit(solution)/shard_map/ppermute | solution.py:17
  96.3 1.9 %collective-permute-start.6 = (bf16[4,128,256]{2,1,0:T(8,128)(2,1)S(1)}, bf16[4,128,256]{2,1,0:T(8,128)(2,1)S(1)}, u32[]{:S(2)}, u32[]{:S(2)}) collective-permute-start(bf16[4,128,256]{2,1,0:T(8,128)(2,1)S(1)} %pad_maximum_fusion.11), channel_id=1, source_target_pairs={{16,0},{32,16},{48,32},{64,48},{80,64},{96,80},{112,96},{17,1},{33... | collective-permute-start | bytes 786440 | tf_op jit(solution)/shard_map/ppermute | solution.py:17
  98.3 2.4 %collective-permute-start.5 = (bf16[4,128,256]{2,1,0:T(8,128)(2,1)S(1)}, bf16[4,128,256]{2,1,0:T(8,128)(2,1)S(1)}, u32[]{:S(2)}, u32[]{:S(2)}) collective-permute-start(bf16[4,128,256]{2,1,0:T(8,128)(2,1)S(1)} %pad_maximum_fusion.10), channel_id=1, source_target_pairs={{0,16},{16,32},{32,48},{48,64},{64,80},{80,96},{96,112},{1,17},{17... | collective-permute-start | bytes 786440 | tf_op jit(solution)/shard_map/ppermute | solution.py:17
  101.0 1.1 collective-permute-done.6
  102.2 3.8 %collective-permute-done.5 = bf16[4,128,256]{2,1,0:T(8,128)(2,1)S(1)} collective-permute-done((bf16[4,128,256]{2,1,0:T(8,128)(2,1)S(1)}, bf16[4,128,256]{2,1,0:T(8,128)(2,1)S(1)}, u32[]{:S(2)}, u32[]{:S(2)}) %collective-permute-start.5) | collective-permute-done | bytes 262176 | tf_op jit(solution)/shard_map/ppermute | solution.py:17
  106.0 0.4 fusion.32
  106.4 3.5 %fusion.10 = f32[4,512,512]{2,1,0:T(8,128)} fusion(f32[4,128,512]{2,1,0:T(8,128)S(1)} %convert_element_type.165, f32[4,128,512]{2,1,0:T(8,128)S(1)} %convert_element_type.164, f32[4,512,128]{2,1,0:T(8,128)S(1)} %get-tuple-element.54, f32[4,512,128]{2,1,0:T(8,128)S(1)} %get-tuple-element.53, f32[512]{0:T(512)S(1)} %pad.18.clone, ...), kind=kLoop, calls=%fused_computation.15 | loop fusion | flops 14680064 | bytes 10496000 | tf_op jit(solution)/shard_map/add | solution.py:283
  (75 shorter events, 2.9 us)
Async XLA Ops:
  0.0 2.9 %copy-start = (bf16[2352,128]{1,0:T(8,128)(2,1)S(1)}, bf16[2352,128]{1,0:T(8,128)(2,1)}, u32[]{:S(2)}) copy-start(bf16[2352,128]{1,0:T(8,128)(2,1)} %param.6) | copy-start | bytes 1806340
  15.9 32.1 %all-to-all-start = ((bf16[16,2,208,128]{3,2,1,0:T(8,128)(2,1)}), bf16[16,2,208,128]{3,2,1,0:T(8,128)(2,1)S(1)}, u32[]{:S(2)}, u32[]{:S(2)}) async-start(bf16[16,2,208,128]{3,2,1,0:T(8,128)(2,1)} %pad_maximum_fusion.3), calls=%async_computation | async-start | bytes 3407872 | tf_op jit(solution)/shard_map/all_to_all | solution.py:226
  52.0 8.6 %collective-permute-start = (bf16[1,528,128]{2,1,0:T(8,128)(2,1)S(1)}, bf16[1,528,128]{2,1,0:T(8,128)(2,1)S(1)}, u32[]{:S(2)}, u32[]{:S(2)}) collective-permute-start(bf16[1,528,128]{2,1,0:T(8,128)(2,1)S(1)} %maximum_maximum_fusion), channel_id=1, source_target_pairs={{16,0},{32,16},{48,32},{64,48},{80,64},{96,80},{112,96},{17,1},{33... | collective-permute-start | bytes 405512 | tf_op jit(solution)/shard_map/ppermute | solution.py:17
  60.6 3.3 %copy-start.3 = (bf16[512,512]{1,0:T(8,128)(2,1)S(1)}, bf16[512,512]{1,0:T(8,128)(2,1)}, u32[]{:S(2)}) copy-start(bf16[512,512]{1,0:T(8,128)(2,1)} %constant.173.clone) | copy-start | bytes 1572868
  60.6 3.8 %copy-start.2 = (bf16[512,512]{1,0:T(8,128)(2,1)S(1)}, bf16[512,512]{1,0:T(8,128)(2,1)}, u32[]{:S(2)}) copy-start(bf16[512,512]{1,0:T(8,128)(2,1)} %constant.172.clone) | copy-start | bytes 1572868
  72.8 1.3 %copy-start.4 = (bf16[512,512]{1,0:T(8,128)(2,1)S(1)}, bf16[512,512]{1,0:T(8,128)(2,1)}, u32[]{:S(2)}) copy-start(bf16[512,512]{1,0:T(8,128)(2,1)} %constant.182) | copy-start | bytes 1572868
  76.0 16.2 %collective-permute-start.4 = (bf16[4,512,128]{2,1,0:T(8,128)(2,1)S(1)}, bf16[4,512,128]{2,1,0:T(8,128)(2,1)S(1)}, u32[]{:S(2)}, u32[]{:S(2)}) collective-permute-start(bf16[4,512,128]{2,1,0:T(8,128)(2,1)S(1)} %get-tuple-element.30), channel_id=1, source_target_pairs={{1,0},{2,1},{3,2},{4,3},{5,4},{6,5},{7,6},{8,7},{9,8},{10,9},{11,1... | collective-permute-start | bytes 1572872 | tf_op jit(solution)/shard_map/ppermute | solution.py:17
  78.0 18.3 %collective-permute-start.3 = (bf16[4,512,128]{2,1,0:T(8,128)(2,1)S(1)}, bf16[4,512,128]{2,1,0:T(8,128)(2,1)S(1)}, u32[]{:S(2)}, u32[]{:S(2)}) collective-permute-start(bf16[4,512,128]{2,1,0:T(8,128)(2,1)S(1)} %get-tuple-element.29), channel_id=1, source_target_pairs={{0,1},{1,2},{2,3},{3,4},{4,5},{5,6},{6,7},{7,8},{8,9},{9,10},{10,1... | collective-permute-start | bytes 1572872 | tf_op jit(solution)/shard_map/ppermute | solution.py:17
  83.4 17.3 %collective-permute-start.2 = (bf16[4,128,512]{2,1,0:T(8,128)(2,1)S(1)}, bf16[4,128,512]{2,1,0:T(8,128)(2,1)S(1)}, u32[]{:S(2)}, u32[]{:S(2)}) collective-permute-start(bf16[4,128,512]{2,1,0:T(8,128)(2,1)S(1)} %get-tuple-element.26), channel_id=1, source_target_pairs={{16,0},{32,16},{48,32},{64,48},{80,64},{96,80},{112,96},{17,1},{33... | collective-permute-start | bytes 1572872 | tf_op jit(solution)/shard_map/ppermute | solution.py:17
  85.4 15.5 %collective-permute-start.1 = (bf16[4,128,512]{2,1,0:T(8,128)(2,1)S(1)}, bf16[4,128,512]{2,1,0:T(8,128)(2,1)S(1)}, u32[]{:S(2)}, u32[]{:S(2)}) collective-permute-start(bf16[4,128,512]{2,1,0:T(8,128)(2,1)S(1)} %get-tuple-element.25), channel_id=1, source_target_pairs={{0,16},{16,32},{32,48},{48,64},{64,80},{80,96},{96,112},{1,17},{17... | collective-permute-start | bytes 1572872 | tf_op jit(solution)/shard_map/ppermute | solution.py:17
  96.3 5.8 %collective-permute-start.6 = (bf16[4,128,256]{2,1,0:T(8,128)(2,1)S(1)}, bf16[4,128,256]{2,1,0:T(8,128)(2,1)S(1)}, u32[]{:S(2)}, u32[]{:S(2)}) collective-permute-start(bf16[4,128,256]{2,1,0:T(8,128)(2,1)S(1)} %pad_maximum_fusion.11), channel_id=1, source_target_pairs={{16,0},{32,16},{48,32},{64,48},{80,64},{96,80},{112,96},{17,1},{33... | collective-permute-start | bytes 786440 | tf_op jit(solution)/shard_map/ppermute | solution.py:17
  98.3 7.7 %collective-permute-start.5 = (bf16[4,128,256]{2,1,0:T(8,128)(2,1)S(1)}, bf16[4,128,256]{2,1,0:T(8,128)(2,1)S(1)}, u32[]{:S(2)}, u32[]{:S(2)}) collective-permute-start(bf16[4,128,256]{2,1,0:T(8,128)(2,1)S(1)} %pad_maximum_fusion.10), channel_id=1, source_target_pairs={{0,16},{16,32},{32,48},{48,64},{64,80},{80,96},{96,112},{1,17},{17... | collective-permute-start | bytes 786440 | tf_op jit(solution)/shard_map/ppermute | solution.py:17
  106.4 3.6 %copy-start.1 = (bf16[2352,128]{1,0:T(8,128)(2,1)S(1)}, bf16[2352,128]{1,0:T(8,128)(2,1)}, u32[]{:S(2)}) copy-start(bf16[2352,128]{1,0:T(8,128)(2,1)} %param.6) | copy-start | bytes 1806340

commit v16 on v11

--- a/solution.py
+++ b/solution.py
@@ -150,7 +150,11 @@
 
 
 def gathered_rows(table_rows, picks):
-    chosen = picks.reshape(-1)[:, None] == jnp.arange(table_rows.shape[0], dtype=jnp.int32)
+    flat = picks.reshape(-1)
+    rows = jnp.arange(table_rows.shape[0], dtype=jnp.int32)
+    split = lambda x: ((x // CODE_SPLIT).astype(jnp.bfloat16), (x % CODE_SPLIT).astype(jnp.bfloat16))
+    (pick_hi, pick_lo), (row_hi, row_lo) = split(flat), split(rows)
+    chosen = (pick_hi[:, None] == row_hi[None, :]) & (pick_lo[:, None] == row_lo[None, :])
     values = jnp.dot(chosen.astype(table_rows.dtype), table_rows, preferred_element_type=jnp.float32)
     return values.astype(table_rows.dtype).reshape(picks.shape + table_rows.shape[1:])
 

time: 105 us -> 108 us (1.029)
  matrix products: 25.8 us -> 28.6 us
    dot_general x2, matrix products: 11.2 us -> 13.8 us  [gathered_rows(): jnp.dot(chosen.astype(table_rows.dtype), table_rows, preferred_element_ty...]
where the time goes in v16:
time: 108 us
  waiting for transfers between devices  37.4 us (35%)
  matrix products  28.6 us (26%)
  starting transfers between devices  24.3 us (22%)
  other arithmetic  13.3 us (12%)
  local copies, waits for them, and re-layouts  3.44 us (3%)
    all_to_all x1, waiting for transfers between devices, on_device(): lax.all_to_all(jnp.stack([same_sent, rise_sent], axis=1), 'py', 0, 0, til...  24 us
    ppermute x7, starting transfers between devices, shifted(): return lax.ppermute(shard, axis, pairs)  16.4 us
    dot_general x2, matrix products, gathered_rows(): jnp.dot(chosen.astype(table_rows.dtype), table_rows, preferred_element_ty...  13.8 us
    ppermute x7, waiting for transfers between devices, shifted(): return lax.ppermute(shard, axis, pairs)  13.4 us
    dot_general x9, matrix products, dot32(): return jnp.dot(a, b, preferred_element_type=jnp.float32)  8.77 us
    all_to_all x1, starting transfers between devices, on_device(): lax.all_to_all(jnp.stack([same_sent, rise_sent], axis=1), 'py', 0, 0, til...  7.89 us
    dot_general x3, matrix products, one_hot_rows(): jnp.dot(picks.astype(values.dtype), values, preferred_element_type=jnp.fl...  6 us
    add x1, other arithmetic, on_device(): return col_weight * rows_done + (1.0 - col_weight) * horizontal  3.54 us
  transfers between devices with their start and end apart: 8, of which 5 were waited for; matrix products, arithmetic and copies ran while one was open for 6% of the time, Pallas kernels for 0%

profile of v16, /device:TPU:40, one launch (start us, length us, event | category | flops | bytes accessed | tf_op | source)
XLA Modules:
  0.0 107.5 jit_solution(14302869094282542585)
XLA Ops:
  0.0 1.3 %constant_dynamic-slice_fusion.3 = (s32[1,16,192]{1,2,0:T(8,128)S(1)}, s32[1,16,192]{1,2,0:T(8,128)S(1)}, s32[1,16,192]{1,2,0:T(8,128)S(1)}, s32[1,16,192]{1,2,0:T(8,128)S(1)}) fusion(s32[1,128,192]{1,2,0:T(8,128)} %param.8, s32[]{:T(128)S(6)} %select_n.202, s32[]{:T(128)S(6)} %select_n.210, s32[1,128,192]{1,2,0:T(8,128)} %param.7), kind=kLoop, calls=%fused_computation.201 | loop fusion | bytes 98312 | tf_op jit(solution)/shard_map/dynamic_slice | solution.py:205
  1.3 0.8 fusion.105
  3.1 6.9 %fusion.23 = bf16[3072,128]{1,0:T(8,128)(2,1)S(1)} fusion(bf16[2352,128]{1,0:T(8,128)(2,1)S(1)} %copy-done, bf16[2352]{0:T(1024)(128)(2,1)S(1)} %get-tuple-element.78, bf16[2352]{0:T(1024)(128)(2,1)S(1)} %get-tuple-element.77, bf16[3072]{0:T(1024)(128)(2,1)S(1)} %get-tuple-element.50, bf16[3072]{0:T(1024)(128)(2,1)S(1)} %get-tuple-element.49), kind=kOutput, calls=%fused_computation.28 | convolution fusion | flops 1900658688 | bytes 1410240 | tf_op jit(solution)/shard_map/dot_general | solution.py:158
  9.9 6.9 %fusion.22 = bf16[3072,128]{1,0:T(8,128)(2,1)S(1)} fusion(bf16[2352,128]{1,0:T(8,128)(2,1)S(1)} %copy-done, bf16[2352]{0:T(1024)(128)(2,1)S(1)} %get-tuple-element.78, bf16[2352]{0:T(1024)(128)(2,1)S(1)} %get-tuple-element.77, bf16[3072]{0:T(1024)(128)(2,1)S(1)} %get-tuple-element.52, bf16[3072]{0:T(1024)(128)(2,1)S(1)} %get-tuple-element.51), kind=kOutput, calls=%fused_computation.27 | convolution fusion | flops 1900658688 | bytes 1410240 | tf_op jit(solution)/shard_map/dot_general | solution.py:158
  16.9 0.4 maximum_bitcast_fusion
  17.3 1.3 %pad_maximum_fusion.3 = bf16[16,2,208,128]{3,2,1,0:T(8,128)(2,1)} fusion(bf16[16,1,208,128]{3,2,1,0:T(8,128)(2,1)S(1)} %get-tuple-element.66, bf16[16,1,208,128]{3,2,1,0:T(8,128)(2,1)S(1)} %get-tuple-element.65), kind=kLoop, calls=%fused_computation.43 | loop fusion | flops 851968 | bytes 3407872 | tf_op jit(solution)/shard_map/stack | solution.py:216
  18.6 7.9 %all-to-all-start = ((bf16[16,2,208,128]{3,2,1,0:T(8,128)(2,1)}), bf16[16,2,208,128]{3,2,1,0:T(8,128)(2,1)S(1)}, u32[]{:S(2)}, u32[]{:S(2)}) async-start(bf16[16,2,208,128]{3,2,1,0:T(8,128)(2,1)} %pad_maximum_fusion.3), calls=%async_computation | async-start | bytes 3407872 | tf_op jit(solution)/shard_map/all_to_all | solution.py:216
  26.7 24.0 %all-to-all-done = bf16[16,2,208,128]{3,2,1,0:T(8,128)(2,1)S(1)} async-done(((bf16[16,2,208,128]{3,2,1,0:T(8,128)(2,1)}), bf16[16,2,208,128]{3,2,1,0:T(8,128)(2,1)S(1)}, u32[]{:S(2)}, u32[]{:S(2)}) %all-to-all-start) | async-done | bytes 1703968 | tf_op jit(solution)/shard_map/all_to_all | solution.py:216
  51.4 0.3 reduce-window.9
  51.8 0.1 slice_reduce_fusion
  52.0 0.8 fusion.16
  52.8 1.0 fusion.39
  53.9 0.1 maximum_maximum_fusion
  54.0 1.9 %collective-permute-start = (bf16[1,528,128]{2,1,0:T(8,128)(2,1)S(1)}, bf16[1,528,128]{2,1,0:T(8,128)(2,1)S(1)}, u32[]{:S(2)}, u32[]{:S(2)}) collective-permute-start(bf16[1,528,128]{2,1,0:T(8,128)(2,1)S(1)} %maximum_maximum_fusion), channel_id=1, source_target_pairs={{16,0},{32,16},{48,32},{64,48},{80,64},{96,80},{112,96},{17,1},{33... | collective-permute-start | bytes 405512 | tf_op jit(solution)/shard_map/ppermute | solution.py:17
  55.9 3.7 %fusion.2 = f32[2048,128]{1,0:T(8,128)S(1)} fusion(bf16[3072,128]{1,0:T(8,128)(2,1)S(1)} %bitcast.112, s32[3072]{0:T(1024)S(1)} %eq.123, s32[2048]{0:T(1024)S(1)} %iota_add_fusion), kind=kOutput, calls=%fused_computation.4 | convolution fusion | flops 1616904192 | bytes 1855488 | tf_op jit(solution)/shard_map/dot_general | solution.py:149
  59.7 1.3 %fusion.29 = bf16[2048,128]{1,0:T(8,128)(2,1)S(1)} fusion(f32[2048,128]{1,0:T(8,128)S(1)} %fusion.2, s32[512]{0:T(512)S(1)} %bitcast.121, s32[2048]{0:T(1024)S(1)} %iota_add_fusion, bf16[1,528,128]{2,1,0:T(8,128)(2,1)S(1)} %collective-permute-done), kind=kOutput, calls=%fused_computation.33 | convolution fusion | flops 270008320 | bytes 1714176 | tf_op jit(solution)/shard_map/dot_general | solution.py:149
  61.0 0.3 reshape.441
  61.3 0.5 convolution_convert_fusion
  61.8 0.5 convolution_convert_fusion.1
  62.3 0.7 fusion.51
  63.1 0.7 fusion.50
  63.8 0.3 multiply_convert_fusion.3
  64.1 1.0 multiply_convert_fusion.2
  65.1 1.3 %fusion.60 = f32[512,2048]{1,0:T(8,128)S(1)} fusion(bf16[512,512]{1,0:T(8,128)(2,1)S(1)} %copy-done.3, bf16[512,512]{1,0:T(8,128)(2,1)S(1)} %get-tuple-element.21, bf16[512,512]{1,0:T(8,128)(2,1)S(1)} %get-tuple-element.22, bf16[512,512]{1,0:T(8,128)(2,1)S(1)} %get-tuple-element.20, bf16[512,512]{1,0:T(8,128)(2,1)S(1)} %get-tuple-element.5), kind=kOutput, calls=%fused_computation.89 | convolution fusion | flops 1082130432 | bytes 6815744 | tf_op jit(solution)/shard_map/dot_general | solution.py:51
  66.4 1.3 %fusion.61 = f32[512,2048]{1,0:T(8,128)S(1)} fusion(bf16[512,512]{1,0:T(8,128)(2,1)S(1)} %copy-done.2, bf16[512,512]{1,0:T(8,128)(2,1)S(1)} %get-tuple-element.21, bf16[512,512]{1,0:T(8,128)(2,1)S(1)} %get-tuple-element.22, bf16[512,512]{1,0:T(8,128)(2,1)S(1)} %get-tuple-element.20, bf16[512,512]{1,0:T(8,128)(2,1)S(1)} %get-tuple-element.5), kind=kOutput, calls=%fused_computation.90 | convolution fusion | flops 1082130432 | bytes 6815744 | tf_op jit(solution)/shard_map/dot_general | solution.py:51
  67.6 1.2 %fusion.33 = (bf16[512,1024]{1,0:T(8,128)(2,1)S(1)}, bf16[512,1024]{1,0:T(8,128)(2,1)S(1)}) fusion(f32[512,2048]{1,0:T(8,128)S(1)} %fusion.60, f32[512,2048]{1,0:T(8,128)S(1)} %fusion.61), kind=kLoop, calls=%fused_computation.37 | loop fusion | flops 2097152 | bytes 10485760 | tf_op jit(solution)/shard_map/convert.20
  69.0 1.3 %fusion.111 = f32[2048,512]{1,0:T(8,128)S(1)} fusion(bf16[512,512]{1,0:T(8,128)(2,1)S(1)} %copy-done.3, bf16[512,512]{1,0:T(8,128)(2,1)S(1)} %get-tuple-element.32, bf16[512,512]{1,0:T(8,128)(2,1)S(1)} %get-tuple-element.31, bf16[512,512]{1,0:T(8,128)(2,1)S(1)} %get-tuple-element.30, bf16[512,512]{1,0:T(8,128)(2,1)S(1)} %get-tuple-element.29), kind=kOutput, calls=%fused_computation.227 | convolution fusion | flops 1082130432 | bytes 6815744 | tf_op jit(solution)/shard_map/dot_general | solution.py:51
  70.3 1.3 %fusion.112 = f32[2048,512]{1,0:T(8,128)S(1)} fusion(bf16[512,512]{1,0:T(8,128)(2,1)S(1)} %copy-done.2, bf16[512,512]{1,0:T(8,128)(2,1)S(1)} %get-tuple-element.32, bf16[512,512]{1,0:T(8,128)(2,1)S(1)} %get-tuple-element.31, bf16[512,512]{1,0:T(8,128)(2,1)S(1)} %get-tuple-element.30, bf16[512,512]{1,0:T(8,128)(2,1)S(1)} %get-tuple-element.29), kind=kOutput, calls=%fused_computation.228 | convolution fusion | flops 1082130432 | bytes 6815744 | tf_op jit(solution)/shard_map/dot_general | solution.py:51
  71.6 1.2 %fusion.110 = f32[2048,512]{1,0:T(8,128)S(1)} fusion(bf16[512,512]{1,0:T(8,128)(2,1)S(1)} %copy-done.4, bf16[512,512]{1,0:T(8,128)(2,1)S(1)} %get-tuple-element.32, bf16[512,512]{1,0:T(8,128)(2,1)S(1)} %get-tuple-element.31, bf16[512,512]{1,0:T(8,128)(2,1)S(1)} %get-tuple-element.30, bf16[512,512]{1,0:T(8,128)(2,1)S(1)} %get-tuple-element.29), kind=kOutput, calls=%fused_computation.226 | convolution fusion | flops 1082130432 | bytes 6815744 | tf_op jit(solution)/shard_map/dot_general | solution.py:51
  72.8 0.3 fusion.62
  73.1 0.1 pad_maximum_fusion.5
  73.2 0.2 fusion.115
  73.4 2.0 %collective-permute-start.4 = (bf16[4,512,128]{2,1,0:T(8,128)(2,1)S(1)}, bf16[4,512,128]{2,1,0:T(8,128)(2,1)S(1)}, u32[]{:S(2)}, u32[]{:S(2)}) collective-permute-start(bf16[4,512,128]{2,1,0:T(8,128)(2,1)S(1)} %get-tuple-element.28), channel_id=1, source_target_pairs={{1,0},{2,1},{3,2},{4,3},{5,4},{6,5},{7,6},{8,7},{9,8},{10,9},{11,1... | collective-permute-start | bytes 1572872 | tf_op jit(solution)/shard_map/ppermute | solution.py:17
  75.4 3.9 %collective-permute-start.3 = (bf16[4,512,128]{2,1,0:T(8,128)(2,1)S(1)}, bf16[4,512,128]{2,1,0:T(8,128)(2,1)S(1)}, u32[]{:S(2)}, u32[]{:S(2)}) collective-permute-start(bf16[4,512,128]{2,1,0:T(8,128)(2,1)S(1)} %get-tuple-element.27), channel_id=1, source_target_pairs={{0,1},{1,2},{2,3},{3,4},{4,5},{5,6},{6,7},{7,8},{8,9},{9,10},{10,1... | collective-permute-start | bytes 1572872 | tf_op jit(solution)/shard_map/ppermute | solution.py:17
  79.3 1.2 %fusion.52 = (bf16[1,512,512]{2,1,0:T(8,128)(2,1)S(1)}, bf16[1,512,512]{2,1,0:T(8,128)(2,1)S(1)}, bf16[1,512,512]{2,1,0:T(8,128)(2,1)S(1)}, bf16[1,512,512]{2,1,0:T(8,128)(2,1)S(1)}) fusion(f32[2048,512]{1,0:T(8,128)S(1)} %fusion.111, f32[2048,512]{1,0:T(8,128)S(1)} %fusion.112), kind=kLoop, calls=%fused_computation.77 | loop fusion | flops 2097152 | bytes 10485760 | tf_op jit(solution)/shard_map/stack | solution.py:112
  80.5 0.3 pad_maximum_fusion.2
  80.9 2.0 %collective-permute-start.2 = (bf16[4,128,512]{2,1,0:T(8,128)(2,1)S(1)}, bf16[4,128,512]{2,1,0:T(8,128)(2,1)S(1)}, u32[]{:S(2)}, u32[]{:S(2)}) collective-permute-start(bf16[4,128,512]{2,1,0:T(8,128)(2,1)S(1)} %get-tuple-element.24), channel_id=1, source_target_pairs={{16,0},{32,16},{48,32},{64,48},{80,64},{96,80},{112,96},{17,1},{33... | collective-permute-start | bytes 1572872 | tf_op jit(solution)/shard_map/ppermute | solution.py:17
  82.9 2.3 %collective-permute-start.1 = (bf16[4,128,512]{2,1,0:T(8,128)(2,1)S(1)}, bf16[4,128,512]{2,1,0:T(8,128)(2,1)S(1)}, u32[]{:S(2)}, u32[]{:S(2)}) collective-permute-start(bf16[4,128,512]{2,1,0:T(8,128)(2,1)S(1)} %get-tuple-element.23), channel_id=1, source_target_pairs={{0,16},{16,32},{32,48},{48,64},{64,80},{80,96},{96,112},{1,17},{17... | collective-permute-start | bytes 1572872 | tf_op jit(solution)/shard_map/ppermute | solution.py:17
  85.2 4.5 %collective-permute-done.4 = bf16[4,512,128]{2,1,0:T(8,128)(2,1)S(1)} collective-permute-done((bf16[4,512,128]{2,1,0:T(8,128)(2,1)S(1)}, bf16[4,512,128]{2,1,0:T(8,128)(2,1)S(1)}, u32[]{:S(2)}, u32[]{:S(2)}) %collective-permute-start.4) | collective-permute-done | bytes 524320 | tf_op jit(solution)/shard_map/ppermute | solution.py:17
  89.8 4.0 %collective-permute-done.3 = bf16[4,512,128]{2,1,0:T(8,128)(2,1)S(1)} collective-permute-done((bf16[4,512,128]{2,1,0:T(8,128)(2,1)S(1)}, bf16[4,512,128]{2,1,0:T(8,128)(2,1)S(1)}, u32[]{:S(2)}, u32[]{:S(2)}) %collective-permute-start.3) | collective-permute-done | bytes 524320 | tf_op jit(solution)/shard_map/ppermute | solution.py:17
  93.9 1.9 %collective-permute-start.6 = (bf16[4,128,256]{2,1,0:T(8,128)(2,1)S(1)}, bf16[4,128,256]{2,1,0:T(8,128)(2,1)S(1)}, u32[]{:S(2)}, u32[]{:S(2)}) collective-permute-start(bf16[4,128,256]{2,1,0:T(8,128)(2,1)S(1)} %pad_maximum_fusion.11), channel_id=1, source_target_pairs={{16,0},{32,16},{48,32},{64,48},{80,64},{96,80},{112,96},{17,1},{33... | collective-permute-start | bytes 786440 | tf_op jit(solution)/shard_map/ppermute | solution.py:17
  95.8 2.4 %collective-permute-start.5 = (bf16[4,128,256]{2,1,0:T(8,128)(2,1)S(1)}, bf16[4,128,256]{2,1,0:T(8,128)(2,1)S(1)}, u32[]{:S(2)}, u32[]{:S(2)}) collective-permute-start(bf16[4,128,256]{2,1,0:T(8,128)(2,1)S(1)} %pad_maximum_fusion.10), channel_id=1, source_target_pairs={{0,16},{16,32},{32,48},{48,64},{64,80},{80,96},{96,112},{1,17},{17... | collective-permute-start | bytes 786440 | tf_op jit(solution)/shard_map/ppermute | solution.py:17
  98.3 0.1 convert_element_type.219
  98.5 0.1 convert_element_type.218
  98.6 1.1 collective-permute-done.6
  99.7 3.8 %collective-permute-done.5 = bf16[4,128,256]{2,1,0:T(8,128)(2,1)S(1)} collective-permute-done((bf16[4,128,256]{2,1,0:T(8,128)(2,1)S(1)}, bf16[4,128,256]{2,1,0:T(8,128)(2,1)S(1)}, u32[]{:S(2)}, u32[]{:S(2)}) %collective-permute-start.5) | collective-permute-done | bytes 262176 | tf_op jit(solution)/shard_map/ppermute | solution.py:17
  103.6 0.4 fusion.47
  104.0 3.5 %fusion.19 = f32[4,512,512]{2,1,0:T(8,128)} fusion(f32[4,128,512]{2,1,0:T(8,128)S(1)} %convert_element_type.219, f32[4,128,512]{2,1,0:T(8,128)S(1)} %convert_element_type.218, f32[4,512,128]{2,1,0:T(8,128)S(1)} %get-tuple-element.54, f32[4,512,128]{2,1,0:T(8,128)S(1)} %get-tuple-element.53, f32[512]{0:T(512)S(1)} %pad.18.clone, ...), kind=kLoop, calls=%fused_computation.23 | loop fusion | flops 14680064 | bytes 10496000 | tf_op jit(solution)/shard_map/add | solution.py:273
  (72 shorter events, 2.5 us)
Async XLA Ops:
  0.0 3.1 %copy-start = (bf16[2352,128]{1,0:T(8,128)(2,1)S(1)}, bf16[2352,128]{1,0:T(8,128)(2,1)}, u32[]{:S(2)}) copy-start(bf16[2352,128]{1,0:T(8,128)(2,1)} %param.6) | copy-start | bytes 1806340
  18.6 32.1 %all-to-all-start = ((bf16[16,2,208,128]{3,2,1,0:T(8,128)(2,1)}), bf16[16,2,208,128]{3,2,1,0:T(8,128)(2,1)S(1)}, u32[]{:S(2)}, u32[]{:S(2)}) async-start(bf16[16,2,208,128]{3,2,1,0:T(8,128)(2,1)} %pad_maximum_fusion.3), calls=%async_computation | async-start | bytes 3407872 | tf_op jit(solution)/shard_map/all_to_all | solution.py:216
  54.0 5.7 %collective-permute-start = (bf16[1,528,128]{2,1,0:T(8,128)(2,1)S(1)}, bf16[1,528,128]{2,1,0:T(8,128)(2,1)S(1)}, u32[]{:S(2)}, u32[]{:S(2)}) collective-permute-start(bf16[1,528,128]{2,1,0:T(8,128)(2,1)S(1)} %maximum_maximum_fusion), channel_id=1, source_target_pairs={{16,0},{32,16},{48,32},{64,48},{80,64},{96,80},{112,96},{17,1},{33... | collective-permute-start | bytes 405512 | tf_op jit(solution)/shard_map/ppermute | solution.py:17
  55.9 5.4 %copy-start.3 = (bf16[512,512]{1,0:T(8,128)(2,1)S(1)}, bf16[512,512]{1,0:T(8,128)(2,1)}, u32[]{:S(2)}) copy-start(bf16[512,512]{1,0:T(8,128)(2,1)} %constant.182.clone) | copy-start | bytes 1572868
  59.7 2.1 %copy-start.2 = (bf16[512,512]{1,0:T(8,128)(2,1)S(1)}, bf16[512,512]{1,0:T(8,128)(2,1)}, u32[]{:S(2)}) copy-start(bf16[512,512]{1,0:T(8,128)(2,1)} %constant.181.clone) | copy-start | bytes 1572868
  70.3 1.3 %copy-start.4 = (bf16[512,512]{1,0:T(8,128)(2,1)S(1)}, bf16[512,512]{1,0:T(8,128)(2,1)}, u32[]{:S(2)}) copy-start(bf16[512,512]{1,0:T(8,128)(2,1)} %constant.191) | copy-start | bytes 1572868
  73.4 16.3 %collective-permute-start.4 = (bf16[4,512,128]{2,1,0:T(8,128)(2,1)S(1)}, bf16[4,512,128]{2,1,0:T(8,128)(2,1)S(1)}, u32[]{:S(2)}, u32[]{:S(2)}) collective-permute-start(bf16[4,512,128]{2,1,0:T(8,128)(2,1)S(1)} %get-tuple-element.28), channel_id=1, source_target_pairs={{1,0},{2,1},{3,2},{4,3},{5,4},{6,5},{7,6},{8,7},{9,8},{10,9},{11,1... | collective-permute-start | bytes 1572872 | tf_op jit(solution)/shard_map/ppermute | solution.py:17
  75.4 18.4 %collective-permute-start.3 = (bf16[4,512,128]{2,1,0:T(8,128)(2,1)S(1)}, bf16[4,512,128]{2,1,0:T(8,128)(2,1)S(1)}, u32[]{:S(2)}, u32[]{:S(2)}) collective-permute-start(bf16[4,512,128]{2,1,0:T(8,128)(2,1)S(1)} %get-tuple-element.27), channel_id=1, source_target_pairs={{0,1},{1,2},{2,3},{3,4},{4,5},{5,6},{6,7},{7,8},{8,9},{9,10},{10,1... | collective-permute-start | bytes 1572872 | tf_op jit(solution)/shard_map/ppermute | solution.py:17
  80.9 17.4 %collective-permute-start.2 = (bf16[4,128,512]{2,1,0:T(8,128)(2,1)S(1)}, bf16[4,128,512]{2,1,0:T(8,128)(2,1)S(1)}, u32[]{:S(2)}, u32[]{:S(2)}) collective-permute-start(bf16[4,128,512]{2,1,0:T(8,128)(2,1)S(1)} %get-tuple-element.24), channel_id=1, source_target_pairs={{16,0},{32,16},{48,32},{64,48},{80,64},{96,80},{112,96},{17,1},{33... | collective-permute-start | bytes 1572872 | tf_op jit(solution)/shard_map/ppermute | solution.py:17
  82.9 15.5 %collective-permute-start.1 = (bf16[4,128,512]{2,1,0:T(8,128)(2,1)S(1)}, bf16[4,128,512]{2,1,0:T(8,128)(2,1)S(1)}, u32[]{:S(2)}, u32[]{:S(2)}) collective-permute-start(bf16[4,128,512]{2,1,0:T(8,128)(2,1)S(1)} %get-tuple-element.23), channel_id=1, source_target_pairs={{0,16},{16,32},{32,48},{48,64},{64,80},{80,96},{96,112},{1,17},{17... | collective-permute-start | bytes 1572872 | tf_op jit(solution)/shard_map/ppermute | solution.py:17
  93.9 5.8 %collective-permute-start.6 = (bf16[4,128,256]{2,1,0:T(8,128)(2,1)S(1)}, bf16[4,128,256]{2,1,0:T(8,128)(2,1)S(1)}, u32[]{:S(2)}, u32[]{:S(2)}) collective-permute-start(bf16[4,128,256]{2,1,0:T(8,128)(2,1)S(1)} %pad_maximum_fusion.11), channel_id=1, source_target_pairs={{16,0},{32,16},{48,32},{64,48},{80,64},{96,80},{112,96},{17,1},{33... | collective-permute-start | bytes 786440 | tf_op jit(solution)/shard_map/ppermute | solution.py:17
  95.8 7.7 %collective-permute-start.5 = (bf16[4,128,256]{2,1,0:T(8,128)(2,1)S(1)}, bf16[4,128,256]{2,1,0:T(8,128)(2,1)S(1)}, u32[]{:S(2)}, u32[]{:S(2)}) collective-permute-start(bf16[4,128,256]{2,1,0:T(8,128)(2,1)S(1)} %pad_maximum_fusion.10), channel_id=1, source_target_pairs={{0,16},{16,32},{32,48},{48,64},{64,80},{80,96},{96,112},{1,17},{17... | collective-permute-start | bytes 786440 | tf_op jit(solution)/shard_map/ppermute | solution.py:17
  104.0 3.6 %copy-start.1 = (bf16[2352,128]{1,0:T(8,128)(2,1)S(1)}, bf16[2352,128]{1,0:T(8,128)(2,1)}, u32[]{:S(2)}) copy-start(bf16[2352,128]{1,0:T(8,128)(2,1)} %param.6) | copy-start | bytes 1806340

commit v17 on v11

--- a/solution.py
+++ b/solution.py
@@ -209,9 +209,14 @@
     rise_sent = sent_block(
         kappa, band_rows(send_list, upper_band), band_rows(dest_slot, upper_band), upper_counts
     )
-    arrived = lax.all_to_all(jnp.stack([same_sent, rise_sent], axis=1), "py", 0, 0, tiled=True)
-    same_values, same_codes = split_codes(arrived[:, 0], slot_depth)
-    rise_values, rise_codes = split_codes(arrived[:, 1], slot_depth)
+    same_arrived = lax.all_to_all(same_sent, "py", 0, 0, tiled=True)
+    rise_blocks = [rise_sent[column_index]]
+    for shift in range(1, cols_axis):
+        target = lax.rem(column_index + shift, cols_axis)
+        pairs = [(i, (i + shift) % cols_axis) for i in range(cols_axis)]
+        rise_blocks.append(lax.ppermute(rise_sent[target], "py", pairs))
+    same_values, same_codes = split_codes(same_arrived, slot_depth)
+    rise_values, rise_codes = split_codes(jnp.stack(rise_blocks), slot_depth)
     rise_total = PATCH_ROWS * PATCH_COLS // tile_width // 4
     rise_live = rise_codes > 0
     rise_place = jnp.where(rise_live, jnp.cumsum(rise_live.astype(jnp.int32)), 0)

time: 105 us -> 126 us (1.20)
  starting transfers between devices: 24.5 us -> 56.1 us
  waiting for transfers between devices: 37.3 us -> 25.9 us
    ppermute x0 -> x15, starting transfers between devices: none -> 29.4 us  [on_device(): rise_blocks.append(lax.ppermute(rise_sent[target], 'py', pairs))]
    all_to_all x1, waiting for transfers between devices: 24 us -> 0.01 us  [on_device(): same_arrived = lax.all_to_all(same_sent, 'py', 0, 0, tiled=True)]
    ppermute x0 -> x15, waiting for transfers between devices: none -> 9.22 us  [on_device(): rise_blocks.append(lax.ppermute(rise_sent[target], 'py', pairs))]
    ppermute x7, waiting for transfers between devices: 13.4 us -> 16.7 us  [shifted(): return lax.ppermute(shard, axis, pairs)]
    ppermute x7, starting transfers between devices: 16.6 us -> 18.9 us  [shifted(): return lax.ppermute(shard, axis, pairs)]
    another operation x9 -> x7, other arithmetic: 4.73 us -> 3 us
    concatenate x1 -> x2, other arithmetic: 0.14 us -> 1.43 us  [with_codes(): return jnp.concatenate([values, code_rows, pad], axis=1)]
  transfers between devices with their start and end apart: 8 -> 23, of which waited for: 5 -> 8; matrix products, arithmetic and copies ran while one was open for 6% -> 4% of each run, Pallas kernels for 0% -> 0%
where the time goes in v17:
time: 126 us; the launch traced here: 125 us
  starting transfers between devices  56.1 us (45%)
  matrix products  26 us (21%)
  waiting for transfers between devices  25.9 us (21%)
  other arithmetic  12.8 us (10%)
  local copies, waits for them, and re-layouts  3.66 us (3%)
    ppermute x15, starting transfers between devices, on_device(): rise_blocks.append(lax.ppermute(rise_sent[target], 'py', pairs))  29.4 us
    ppermute x7, starting transfers between devices, shifted(): return lax.ppermute(shard, axis, pairs)  18.9 us
    ppermute x7, waiting for transfers between devices, shifted(): return lax.ppermute(shard, axis, pairs)  16.7 us
    dot_general x2, matrix products, gathered_rows(): jnp.dot(chosen.astype(table_rows.dtype), table_rows, preferred_element_ty...  11.2 us
    ppermute x15, waiting for transfers between devices, on_device(): rise_blocks.append(lax.ppermute(rise_sent[target], 'py', pairs))  9.22 us
    dot_general x9, matrix products, dot32(): return jnp.dot(a, b, preferred_element_type=jnp.float32)  8.77 us
    all_to_all x1, starting transfers between devices, on_device(): same_arrived = lax.all_to_all(same_sent, 'py', 0, 0, tiled=True)  7.9 us
    dot_general x3, matrix products, one_hot_rows(): jnp.dot(picks.astype(values.dtype), values, preferred_element_type=jnp.fl...  6.05 us
  transfers between devices with their start and end apart: 23, of which 8 were waited for; matrix products, arithmetic and copies ran while one was open for 4% of the time, Pallas kernels for 0%

profile of v17, /device:TPU:40, one launch (start us, length us, event | category | flops | bytes accessed | tf_op | source)
XLA Modules:
  0.0 125.2 jit_solution(12058226433348575722)
XLA Ops:
  0.0 1.3 %constant_dynamic-slice_fusion = (s32[1,16,192]{1,2,0:T(8,128)S(1)}, s32[1,16,192]{1,2,0:T(8,128)S(1)}, s32[1,16,192]{1,2,0:T(8,128)S(1)}, s32[1,16,192]{1,2,0:T(8,128)S(1)}) fusion(s32[1,128,192]{1,2,0:T(8,128)} %param.8, s32[]{:T(128)S(6)} %select_n.194, s32[]{:T(128)S(6)} %select_n.190, s32[1,128,192]{1,2,0:T(8,128)} %param.7), kind=kLoop, calls=%fused_computation.163 | loop fusion | bytes 98312 | tf_op jit(solution)/shard_map/dynamic_slice | solution.py:201
  1.3 0.8 fusion.81
  2.9 5.6 %fusion.16 = bf16[3072,128]{1,0:T(8,128)(2,1)S(1)} fusion(bf16[2352,128]{1,0:T(8,128)(2,1)S(1)} %copy-done, s32[3072]{0:T(1024)S(1)} %eq.93), kind=kOutput, calls=%fused_computation.21 | convolution fusion | flops 1857306624 | bytes 1400832 | tf_op jit(solution)/shard_map/dot_general | solution.py:154
  8.5 5.6 %fusion.17 = bf16[3072,128]{1,0:T(8,128)(2,1)S(1)} fusion(bf16[2352,128]{1,0:T(8,128)(2,1)S(1)} %copy-done, s32[3072]{0:T(1024)S(1)} %eq.43), kind=kOutput, calls=%fused_computation.22 | convolution fusion | flops 1857306624 | bytes 1400832 | tf_op jit(solution)/shard_map/dot_general | solution.py:154
  14.2 1.3 %maximum_maximum_fusion.1 = (bf16[16,208,128]{2,1,0:T(8,128)(2,1)S(1)}, bf16[16,208,128]{2,1,0:T(8,128)(2,1)}) fusion(bf16[16,3,128]{2,1,0:T(4,128)(2,1)S(1)} %convert_element_type.154, bf16[16,192,128]{2,1,0:T(8,128)(2,1)S(1)} %bitcast.166, bf16[208]{0:T(256)(128)(2,1)S(1)} %pad.45.clone, bf16[16,3,128]{2,1,0:T(4,128)(2,1)S(1)} %convert_element_type.150, ...), kind=kLoop, calls=%fused_computation.65 | loop fusion | flops 4685824 | bytes 3301792 | tf_op jit(solution)/shard_map/concatenate | solution.py:167
  15.5 7.9 %all-to-all-start = ((bf16[16,208,128]{2,1,0:T(8,128)(2,1)}), bf16[16,208,128]{2,1,0:T(8,128)(2,1)S(1)}, u32[]{:S(2)}, u32[]{:S(2)}) async-start(bf16[16,208,128]{2,1,0:T(8,128)(2,1)} %get-tuple-element.76), calls=%async_computation | async-start | bytes 1703936 | tf_op jit(solution)/shard_map/all_to_all | solution.py:212
  23.5 1.5 %collective-permute-start = (bf16[208,128]{1,0:T(8,128)(2,1)S(1)}, bf16[208,128]{1,0:T(8,128)(2,1)S(1)}, u32[]{:S(2)}, u32[]{:S(2)}) collective-permute-start(bf16[208,128]{1,0:T(8,128)(2,1)S(1)} %get-tuple-element.45), channel_id=1, source_target_pairs={{0,1},{1,2},{2,3},{3,4},{4,5},{5,6},{6,7},{7,8},{8,9},{9,10},{10,1... | collective-permute-start | bytes 159752 | tf_op jit(solution)/shard_map/ppermute | solution.py:217
  25.1 2.7 %collective-permute-start.1 = (bf16[208,128]{1,0:T(8,128)(2,1)S(1)}, bf16[208,128]{1,0:T(8,128)(2,1)S(1)}, u32[]{:S(2)}, u32[]{:S(2)}) collective-permute-start(bf16[208,128]{1,0:T(8,128)(2,1)S(1)} %get-tuple-element.44), channel_id=1, source_target_pairs={{0,2},{1,3},{2,4},{3,5},{4,6},{5,7},{6,8},{7,9},{8,10},{9,11},{10,... | collective-permute-start | bytes 159752 | tf_op jit(solution)/shard_map/ppermute | solution.py:217
  27.8 2.4 %collective-permute-start.2 = (bf16[208,128]{1,0:T(8,128)(2,1)S(1)}, bf16[208,128]{1,0:T(8,128)(2,1)S(1)}, u32[]{:S(2)}, u32[]{:S(2)}) collective-permute-start(bf16[208,128]{1,0:T(8,128)(2,1)S(1)} %get-tuple-element.43), channel_id=1, source_target_pairs={{0,3},{1,4},{2,5},{3,6},{4,7},{5,8},{6,9},{7,10},{8,11},{9,12},{10... | collective-permute-start | bytes 159752 | tf_op jit(solution)/shard_map/ppermute | solution.py:217
  30.1 1.2 collective-permute-start.3
  31.3 0.6 collective-permute-start.4
  32.1 6.2 %collective-permute-done = bf16[208,128]{1,0:T(8,128)(2,1)S(1)} collective-permute-done((bf16[208,128]{1,0:T(8,128)(2,1)S(1)}, bf16[208,128]{1,0:T(8,128)(2,1)S(1)}, u32[]{:S(2)}, u32[]{:S(2)}) %collective-permute-start) | collective-permute-done | bytes 53280 | tf_op jit(solution)/shard_map/ppermute | solution.py:217
  38.3 0.8 collective-permute-start.5
  39.3 1.3 %collective-permute-start.6 = (bf16[208,128]{1,0:T(8,128)(2,1)S(1)}, bf16[208,128]{1,0:T(8,128)(2,1)S(1)}, u32[]{:S(2)}, u32[]{:S(2)}) collective-permute-start(bf16[208,128]{1,0:T(8,128)(2,1)S(1)} %get-tuple-element.39), channel_id=1, source_target_pairs={{0,7},{1,8},{2,9},{3,10},{4,11},{5,12},{6,13},{7,14},{8,15},{9,0},... | collective-permute-start | bytes 159752 | tf_op jit(solution)/shard_map/ppermute | solution.py:217
  40.6 3.9 %collective-permute-start.7 = (bf16[208,128]{1,0:T(8,128)(2,1)S(1)}, bf16[208,128]{1,0:T(8,128)(2,1)S(1)}, u32[]{:S(2)}, u32[]{:S(2)}) collective-permute-start(bf16[208,128]{1,0:T(8,128)(2,1)S(1)} %get-tuple-element.38), channel_id=1, source_target_pairs={{0,8},{1,9},{2,10},{3,11},{4,12},{5,13},{6,14},{7,15},{8,0},{9,1},... | collective-permute-start | bytes 159752 | tf_op jit(solution)/shard_map/ppermute | solution.py:217
  44.5 1.7 %collective-permute-start.8 = (bf16[208,128]{1,0:T(8,128)(2,1)S(1)}, bf16[208,128]{1,0:T(8,128)(2,1)S(1)}, u32[]{:S(2)}, u32[]{:S(2)}) collective-permute-start(bf16[208,128]{1,0:T(8,128)(2,1)S(1)} %get-tuple-element.37), channel_id=1, source_target_pairs={{0,9},{1,10},{2,11},{3,12},{4,13},{5,14},{6,15},{7,0},{8,1},{9,2},... | collective-permute-start | bytes 159752 | tf_op jit(solution)/shard_map/ppermute | solution.py:217
  46.3 5.1 %collective-permute-start.9 = (bf16[208,128]{1,0:T(8,128)(2,1)S(1)}, bf16[208,128]{1,0:T(8,128)(2,1)S(1)}, u32[]{:S(2)}, u32[]{:S(2)}) collective-permute-start(bf16[208,128]{1,0:T(8,128)(2,1)S(1)} %get-tuple-element.36), channel_id=1, source_target_pairs={{0,10},{1,11},{2,12},{3,13},{4,14},{5,15},{6,0},{7,1},{8,2},{9,3},... | collective-permute-start | bytes 159752 | tf_op jit(solution)/shard_map/ppermute | solution.py:217
  51.6 1.1 collective-permute-start.11
  52.7 4.2 %collective-permute-start.12 = (bf16[208,128]{1,0:T(8,128)(2,1)S(1)}, bf16[208,128]{1,0:T(8,128)(2,1)S(1)}, u32[]{:S(2)}, u32[]{:S(2)}) collective-permute-start(bf16[208,128]{1,0:T(8,128)(2,1)S(1)} %get-tuple-element.33), channel_id=1, source_target_pairs={{0,13},{1,14},{2,15},{3,0},{4,1},{5,2},{6,3},{7,4},{8,5},{9,6},{10... | collective-permute-start | bytes 159752 | tf_op jit(solution)/shard_map/ppermute | solution.py:217
  57.1 2.7 %collective-permute-start.14 = (bf16[208,128]{1,0:T(8,128)(2,1)S(1)}, bf16[208,128]{1,0:T(8,128)(2,1)S(1)}, u32[]{:S(2)}, u32[]{:S(2)}) collective-permute-start(bf16[208,128]{1,0:T(8,128)(2,1)S(1)} %get-tuple-element.31), channel_id=1, source_target_pairs={{0,15},{1,0},{2,1},{3,2},{4,3},{5,4},{6,5},{7,6},{8,7},{9,8},{10,9... | collective-permute-start | bytes 159752 | tf_op jit(solution)/shard_map/ppermute | solution.py:217
  59.9 2.8 %collective-permute-done.13 = bf16[208,128]{1,0:T(8,128)(2,1)S(1)} collective-permute-done((bf16[208,128]{1,0:T(8,128)(2,1)S(1)}, bf16[208,128]{1,0:T(8,128)(2,1)S(1)}, u32[]{:S(2)}, u32[]{:S(2)}) %collective-permute-start.13) | collective-permute-done | bytes 53280 | tf_op jit(solution)/shard_map/ppermute | solution.py:217
  63.6 0.8 fusion.10
  64.4 1.0 fusion.33
  65.6 1.9 %collective-permute-start.15 = (bf16[1,528,128]{2,1,0:T(8,128)(2,1)S(1)}, bf16[1,528,128]{2,1,0:T(8,128)(2,1)S(1)}, u32[]{:S(2)}, u32[]{:S(2)}) collective-permute-start(bf16[1,528,128]{2,1,0:T(8,128)(2,1)S(1)} %maximum_maximum_fusion.2), channel_id=1, source_target_pairs={{16,0},{32,16},{48,32},{64,48},{80,64},{96,80},{112,96},{17,1},{33... | collective-permute-start | bytes 405512 | tf_op jit(solution)/shard_map/ppermute | solution.py:17
  67.6 2.5 %collective-permute-done.15 = bf16[1,528,128]{2,1,0:T(8,128)(2,1)S(1)} collective-permute-done((bf16[1,528,128]{2,1,0:T(8,128)(2,1)S(1)}, bf16[1,528,128]{2,1,0:T(8,128)(2,1)S(1)}, u32[]{:S(2)}, u32[]{:S(2)}) %collective-permute-start.15) | collective-permute-done | bytes 135200 | tf_op jit(solution)/shard_map/ppermute | solution.py:17
  70.4 3.7 %fusion.2 = f32[2048,128]{1,0:T(8,128)S(1)} fusion(bf16[3072,128]{1,0:T(8,128)(2,1)S(1)} %bitcast.165, s32[3072]{0:T(1024)S(1)} %eq.89, s32[2048]{0:T(1024)S(1)} %iota_add_fusion), kind=kOutput, calls=%fused_computation.4 | convolution fusion | flops 1616904192 | bytes 1855488 | tf_op jit(solution)/shard_map/dot_general | solution.py:149
  74.1 1.3 %fusion.23 = bf16[2048,128]{1,0:T(8,128)(2,1)S(1)} fusion(f32[2048,128]{1,0:T(8,128)S(1)} %fusion.2, s32[512]{0:T(512)S(1)} %bitcast.173, s32[2048]{0:T(1024)S(1)} %iota_add_fusion, bf16[1,528,128]{2,1,0:T(8,128)(2,1)S(1)} %collective-permute-done.15), kind=kOutput, calls=%fused_computation.27 | convolution fusion | flops 270008320 | bytes 1714176 | tf_op jit(solution)/shard_map/dot_general | solution.py:149
  76.7 0.7 fusion.45
  77.5 0.7 fusion.44
  78.6 1.0 multiply_convert_fusion.2
  79.5 1.3 %fusion.54 = f32[512,2048]{1,0:T(8,128)S(1)} fusion(bf16[512,512]{1,0:T(8,128)(2,1)S(1)} %copy-done.3, bf16[512,512]{1,0:T(8,128)(2,1)S(1)} %get-tuple-element.21, bf16[512,512]{1,0:T(8,128)(2,1)S(1)} %get-tuple-element.22, bf16[512,512]{1,0:T(8,128)(2,1)S(1)} %get-tuple-element.20, bf16[512,512]{1,0:T(8,128)(2,1)S(1)} %get-tuple-element.5), kind=kOutput, calls=%fused_computation.80 | convolution fusion | flops 1082130432 | bytes 6815744 | tf_op jit(solution)/shard_map/dot_general | solution.py:51
  80.8 1.3 %fusion.55 = f32[512,2048]{1,0:T(8,128)S(1)} fusion(bf16[512,512]{1,0:T(8,128)(2,1)S(1)} %copy-done.2, bf16[512,512]{1,0:T(8,128)(2,1)S(1)} %get-tuple-element.21, bf16[512,512]{1,0:T(8,128)(2,1)S(1)} %get-tuple-element.22, bf16[512,512]{1,0:T(8,128)(2,1)S(1)} %get-tuple-element.20, bf16[512,512]{1,0:T(8,128)(2,1)S(1)} %get-tuple-element.5), kind=kOutput, calls=%fused_computation.81 | convolution fusion | flops 1082130432 | bytes 6815744 | tf_op jit(solution)/shard_map/dot_general | solution.py:51
  82.1 1.2 fusion.27
  83.4 1.3 %fusion.88 = f32[2048,512]{1,0:T(8,128)S(1)} fusion(bf16[512,512]{1,0:T(8,128)(2,1)S(1)} %copy-done.3, bf16[512,512]{1,0:T(8,128)(2,1)S(1)} %get-tuple-element.30, bf16[512,512]{1,0:T(8,128)(2,1)S(1)} %get-tuple-element.29, bf16[512,512]{1,0:T(8,128)(2,1)S(1)} %get-tuple-element.28, bf16[512,512]{1,0:T(8,128)(2,1)S(1)} %get-tuple-element.27), kind=kOutput, calls=%fused_computation.216 | convolution fusion | flops 1082130432 | bytes 6815744 | tf_op jit(solution)/shard_map/dot_general | solution.py:51
  84.7 1.3 %fusion.89 = f32[2048,512]{1,0:T(8,128)S(1)} fusion(bf16[512,512]{1,0:T(8,128)(2,1)S(1)} %copy-done.2, bf16[512,512]{1,0:T(8,128)(2,1)S(1)} %get-tuple-element.30, bf16[512,512]{1,0:T(8,128)(2,1)S(1)} %get-tuple-element.29, bf16[512,512]{1,0:T(8,128)(2,1)S(1)} %get-tuple-element.28, bf16[512,512]{1,0:T(8,128)(2,1)S(1)} %get-tuple-element.27), kind=kOutput, calls=%fused_computation.217 | convolution fusion | flops 1082130432 | bytes 6815744 | tf_op jit(solution)/shard_map/dot_general | solution.py:51
  86.0 1.2 fusion.87
  87.9 5.3 %collective-permute-start.19 = (bf16[4,512,128]{2,1,0:T(8,128)(2,1)S(1)}, bf16[4,512,128]{2,1,0:T(8,128)(2,1)S(1)}, u32[]{:S(2)}, u32[]{:S(2)}) collective-permute-start(bf16[4,512,128]{2,1,0:T(8,128)(2,1)S(1)} %get-tuple-element.26), channel_id=1, source_target_pairs={{1,0},{2,1},{3,2},{4,3},{5,4},{6,5},{7,6},{8,7},{9,8},{10,9},{11,1... | collective-permute-start | bytes 1572872 | tf_op jit(solution)/shard_map/ppermute | solution.py:17
  93.2 1.9 %collective-permute-start.18 = (bf16[4,512,128]{2,1,0:T(8,128)(2,1)S(1)}, bf16[4,512,128]{2,1,0:T(8,128)(2,1)S(1)}, u32[]{:S(2)}, u32[]{:S(2)}) collective-permute-start(bf16[4,512,128]{2,1,0:T(8,128)(2,1)S(1)} %get-tuple-element.25), channel_id=1, source_target_pairs={{0,1},{1,2},{2,3},{3,4},{4,5},{5,6},{6,7},{7,8},{8,9},{9,10},{10,1... | collective-permute-start | bytes 1572872 | tf_op jit(solution)/shard_map/ppermute | solution.py:17
  95.1 1.2 fusion.46
  96.7 3.5 %collective-permute-start.17 = (bf16[4,128,512]{2,1,0:T(8,128)(2,1)S(1)}, bf16[4,128,512]{2,1,0:T(8,128)(2,1)S(1)}, u32[]{:S(2)}, u32[]{:S(2)}) collective-permute-start(bf16[4,128,512]{2,1,0:T(8,128)(2,1)S(1)} %get-tuple-element.24), channel_id=1, source_target_pairs={{16,0},{32,16},{48,32},{64,48},{80,64},{96,80},{112,96},{17,1},{33... | collective-permute-start | bytes 1572872 | tf_op jit(solution)/shard_map/ppermute | solution.py:17
  100.2 1.9 %collective-permute-start.16 = (bf16[4,128,512]{2,1,0:T(8,128)(2,1)S(1)}, bf16[4,128,512]{2,1,0:T(8,128)(2,1)S(1)}, u32[]{:S(2)}, u32[]{:S(2)}) collective-permute-start(bf16[4,128,512]{2,1,0:T(8,128)(2,1)S(1)} %get-tuple-element.23), channel_id=1, source_target_pairs={{0,16},{16,32},{32,48},{48,64},{64,80},{80,96},{96,112},{1,17},{17... | collective-permute-start | bytes 1572872 | tf_op jit(solution)/shard_map/ppermute | solution.py:17
  102.1 2.5 %collective-permute-done.19 = bf16[4,512,128]{2,1,0:T(8,128)(2,1)S(1)} collective-permute-done((bf16[4,512,128]{2,1,0:T(8,128)(2,1)S(1)}, bf16[4,512,128]{2,1,0:T(8,128)(2,1)S(1)}, u32[]{:S(2)}, u32[]{:S(2)}) %collective-permute-start.19) | collective-permute-done | bytes 524320 | tf_op jit(solution)/shard_map/ppermute | solution.py:17
  104.6 6.8 %collective-permute-done.18 = bf16[4,512,128]{2,1,0:T(8,128)(2,1)S(1)} collective-permute-done((bf16[4,512,128]{2,1,0:T(8,128)(2,1)S(1)}, bf16[4,512,128]{2,1,0:T(8,128)(2,1)S(1)}, u32[]{:S(2)}, u32[]{:S(2)}) %collective-permute-start.18) | collective-permute-done | bytes 524320 | tf_op jit(solution)/shard_map/ppermute | solution.py:17
  111.5 1.9 %collective-permute-start.21 = (bf16[4,128,256]{2,1,0:T(8,128)(2,1)S(1)}, bf16[4,128,256]{2,1,0:T(8,128)(2,1)S(1)}, u32[]{:S(2)}, u32[]{:S(2)}) collective-permute-start(bf16[4,128,256]{2,1,0:T(8,128)(2,1)S(1)} %pad_maximum_fusion.10), channel_id=1, source_target_pairs={{16,0},{32,16},{48,32},{64,48},{80,64},{96,80},{112,96},{17,1},{33... | collective-permute-start | bytes 786440 | tf_op jit(solution)/shard_map/ppermute | solution.py:17
  113.5 2.4 %collective-permute-start.20 = (bf16[4,128,256]{2,1,0:T(8,128)(2,1)S(1)}, bf16[4,128,256]{2,1,0:T(8,128)(2,1)S(1)}, u32[]{:S(2)}, u32[]{:S(2)}) collective-permute-start(bf16[4,128,256]{2,1,0:T(8,128)(2,1)S(1)} %pad_maximum_fusion.9), channel_id=1, source_target_pairs={{0,16},{16,32},{32,48},{48,64},{64,80},{80,96},{96,112},{1,17},{17... | collective-permute-start | bytes 786440 | tf_op jit(solution)/shard_map/ppermute | solution.py:17
  116.2 1.1 collective-permute-done.21
  117.3 3.8 %collective-permute-done.20 = bf16[4,128,256]{2,1,0:T(8,128)(2,1)S(1)} collective-permute-done((bf16[4,128,256]{2,1,0:T(8,128)(2,1)S(1)}, bf16[4,128,256]{2,1,0:T(8,128)(2,1)S(1)}, u32[]{:S(2)}, u32[]{:S(2)}) %collective-permute-start.20) | collective-permute-done | bytes 262176 | tf_op jit(solution)/shard_map/ppermute | solution.py:17
  121.6 3.5 %fusion.13 = f32[4,512,512]{2,1,0:T(8,128)} fusion(f32[4,128,512]{2,1,0:T(8,128)S(1)} %convert_element_type.165, f32[4,128,512]{2,1,0:T(8,128)S(1)} %convert_element_type.164, f32[4,512,128]{2,1,0:T(8,128)S(1)} %get-tuple-element.64, f32[4,512,128]{2,1,0:T(8,128)S(1)} %get-tuple-element.63, f32[512]{0:T(512)S(1)} %pad.18.clone, ...), kind=kLoop, calls=%fused_computation.17 | loop fusion | flops 14680064 | bytes 10496000 | tf_op jit(solution)/shard_map/add | solution.py:274
  (114 shorter events, 6.9 us)
Async XLA Ops:
  0.0 2.9 %copy-start = (bf16[2352,128]{1,0:T(8,128)(2,1)S(1)}, bf16[2352,128]{1,0:T(8,128)(2,1)}, u32[]{:S(2)}) copy-start(bf16[2352,128]{1,0:T(8,128)(2,1)} %param.6) | copy-start | bytes 1806340
  15.5 54.6 %all-to-all-start = ((bf16[16,208,128]{2,1,0:T(8,128)(2,1)}), bf16[16,208,128]{2,1,0:T(8,128)(2,1)S(1)}, u32[]{:S(2)}, u32[]{:S(2)}) async-start(bf16[16,208,128]{2,1,0:T(8,128)(2,1)} %get-tuple-element.76), calls=%async_computation | async-start | bytes 1703936 | tf_op jit(solution)/shard_map/all_to_all | solution.py:212
  23.5 14.7 %collective-permute-start = (bf16[208,128]{1,0:T(8,128)(2,1)S(1)}, bf16[208,128]{1,0:T(8,128)(2,1)S(1)}, u32[]{:S(2)}, u32[]{:S(2)}) collective-permute-start(bf16[208,128]{1,0:T(8,128)(2,1)S(1)} %get-tuple-element.45), channel_id=1, source_target_pairs={{0,1},{1,2},{2,3},{3,4},{4,5},{5,6},{6,7},{7,8},{8,9},{9,10},{10,1... | collective-permute-start | bytes 159752 | tf_op jit(solution)/shard_map/ppermute | solution.py:217
  25.1 14.2 %collective-permute-start.1 = (bf16[208,128]{1,0:T(8,128)(2,1)S(1)}, bf16[208,128]{1,0:T(8,128)(2,1)S(1)}, u32[]{:S(2)}, u32[]{:S(2)}) collective-permute-start(bf16[208,128]{1,0:T(8,128)(2,1)S(1)} %get-tuple-element.44), channel_id=1, source_target_pairs={{0,2},{1,3},{2,4},{3,5},{4,6},{5,7},{6,8},{7,9},{8,10},{9,11},{10,... | collective-permute-start | bytes 159752 | tf_op jit(solution)/shard_map/ppermute | solution.py:217
  27.8 12.9 %collective-permute-start.2 = (bf16[208,128]{1,0:T(8,128)(2,1)S(1)}, bf16[208,128]{1,0:T(8,128)(2,1)S(1)}, u32[]{:S(2)}, u32[]{:S(2)}) collective-permute-start(bf16[208,128]{1,0:T(8,128)(2,1)S(1)} %get-tuple-element.43), channel_id=1, source_target_pairs={{0,3},{1,4},{2,5},{3,6},{4,7},{5,8},{6,9},{7,10},{8,11},{9,12},{10... | collective-permute-start | bytes 159752 | tf_op jit(solution)/shard_map/ppermute | solution.py:217
  30.1 14.4 %collective-permute-start.3 = (bf16[208,128]{1,0:T(8,128)(2,1)S(1)}, bf16[208,128]{1,0:T(8,128)(2,1)S(1)}, u32[]{:S(2)}, u32[]{:S(2)}) collective-permute-start(bf16[208,128]{1,0:T(8,128)(2,1)S(1)} %get-tuple-element.42), channel_id=1, source_target_pairs={{0,4},{1,5},{2,6},{3,7},{4,8},{5,9},{6,10},{7,11},{8,12},{9,13},{1... | collective-permute-start | bytes 159752 | tf_op jit(solution)/shard_map/ppermute | solution.py:217
  31.3 15.0 %collective-permute-start.4 = (bf16[208,128]{1,0:T(8,128)(2,1)S(1)}, bf16[208,128]{1,0:T(8,128)(2,1)S(1)}, u32[]{:S(2)}, u32[]{:S(2)}) collective-permute-start(bf16[208,128]{1,0:T(8,128)(2,1)S(1)} %get-tuple-element.41), channel_id=1, source_target_pairs={{0,5},{1,6},{2,7},{3,8},{4,9},{5,10},{6,11},{7,12},{8,13},{9,14},{... | collective-permute-start | bytes 159752 | tf_op jit(solution)/shard_map/ppermute | solution.py:217
  38.3 13.1 %collective-permute-start.5 = (bf16[208,128]{1,0:T(8,128)(2,1)S(1)}, bf16[208,128]{1,0:T(8,128)(2,1)S(1)}, u32[]{:S(2)}, u32[]{:S(2)}) collective-permute-start(bf16[208,128]{1,0:T(8,128)(2,1)S(1)} %get-tuple-element.40), channel_id=1, source_target_pairs={{0,6},{1,7},{2,8},{3,9},{4,10},{5,11},{6,12},{7,13},{8,14},{9,15},... | collective-permute-start | bytes 159752 | tf_op jit(solution)/shard_map/ppermute | solution.py:217
  39.3 12.3 %collective-permute-start.6 = (bf16[208,128]{1,0:T(8,128)(2,1)S(1)}, bf16[208,128]{1,0:T(8,128)(2,1)S(1)}, u32[]{:S(2)}, u32[]{:S(2)}) collective-permute-start(bf16[208,128]{1,0:T(8,128)(2,1)S(1)} %get-tuple-element.39), channel_id=1, source_target_pairs={{0,7},{1,8},{2,9},{3,10},{4,11},{5,12},{6,13},{7,14},{8,15},{9,0},... | collective-permute-start | bytes 159752 | tf_op jit(solution)/shard_map/ppermute | solution.py:217
  40.6 12.1 %collective-permute-start.7 = (bf16[208,128]{1,0:T(8,128)(2,1)S(1)}, bf16[208,128]{1,0:T(8,128)(2,1)S(1)}, u32[]{:S(2)}, u32[]{:S(2)}) collective-permute-start(bf16[208,128]{1,0:T(8,128)(2,1)S(1)} %get-tuple-element.38), channel_id=1, source_target_pairs={{0,8},{1,9},{2,10},{3,11},{4,12},{5,13},{6,14},{7,15},{8,0},{9,1},... | collective-permute-start | bytes 159752 | tf_op jit(solution)/shard_map/ppermute | solution.py:217
  44.5 12.4 %collective-permute-start.8 = (bf16[208,128]{1,0:T(8,128)(2,1)S(1)}, bf16[208,128]{1,0:T(8,128)(2,1)S(1)}, u32[]{:S(2)}, u32[]{:S(2)}) collective-permute-start(bf16[208,128]{1,0:T(8,128)(2,1)S(1)} %get-tuple-element.37), channel_id=1, source_target_pairs={{0,9},{1,10},{2,11},{3,12},{4,13},{5,14},{6,15},{7,0},{8,1},{9,2},... | collective-permute-start | bytes 159752 | tf_op jit(solution)/shard_map/ppermute | solution.py:217
  46.3 10.8 %collective-permute-start.9 = (bf16[208,128]{1,0:T(8,128)(2,1)S(1)}, bf16[208,128]{1,0:T(8,128)(2,1)S(1)}, u32[]{:S(2)}, u32[]{:S(2)}) collective-permute-start(bf16[208,128]{1,0:T(8,128)(2,1)S(1)} %get-tuple-element.36), channel_id=1, source_target_pairs={{0,10},{1,11},{2,12},{3,13},{4,14},{5,15},{6,0},{7,1},{8,2},{9,3},... | collective-permute-start | bytes 159752 | tf_op jit(solution)/shard_map/ppermute | solution.py:217
  51.4 8.5 %collective-permute-start.10 = (bf16[208,128]{1,0:T(8,128)(2,1)S(1)}, bf16[208,128]{1,0:T(8,128)(2,1)S(1)}, u32[]{:S(2)}, u32[]{:S(2)}) collective-permute-start(bf16[208,128]{1,0:T(8,128)(2,1)S(1)} %get-tuple-element.35), channel_id=1, source_target_pairs={{0,11},{1,12},{2,13},{3,14},{4,15},{5,0},{6,1},{7,2},{8,3},{9,4},{... | collective-permute-start | bytes 159752 | tf_op jit(solution)/shard_map/ppermute | solution.py:217
  51.6 8.2 %collective-permute-start.11 = (bf16[208,128]{1,0:T(8,128)(2,1)S(1)}, bf16[208,128]{1,0:T(8,128)(2,1)S(1)}, u32[]{:S(2)}, u32[]{:S(2)}) collective-permute-start(bf16[208,128]{1,0:T(8,128)(2,1)S(1)} %get-tuple-element.34), channel_id=1, source_target_pairs={{0,12},{1,13},{2,14},{3,15},{4,0},{5,1},{6,2},{7,3},{8,4},{9,5},{1... | collective-permute-start | bytes 159752 | tf_op jit(solution)/shard_map/ppermute | solution.py:217
  52.7 7.2 %collective-permute-start.12 = (bf16[208,128]{1,0:T(8,128)(2,1)S(1)}, bf16[208,128]{1,0:T(8,128)(2,1)S(1)}, u32[]{:S(2)}, u32[]{:S(2)}) collective-permute-start(bf16[208,128]{1,0:T(8,128)(2,1)S(1)} %get-tuple-element.33), channel_id=1, source_target_pairs={{0,13},{1,14},{2,15},{3,0},{4,1},{5,2},{6,3},{7,4},{8,5},{9,6},{10... | collective-permute-start | bytes 159752 | tf_op jit(solution)/shard_map/ppermute | solution.py:217
  57.0 5.7 %collective-permute-start.13 = (bf16[208,128]{1,0:T(8,128)(2,1)S(1)}, bf16[208,128]{1,0:T(8,128)(2,1)S(1)}, u32[]{:S(2)}, u32[]{:S(2)}) collective-permute-start(bf16[208,128]{1,0:T(8,128)(2,1)S(1)} %get-tuple-element.32), channel_id=1, source_target_pairs={{0,14},{1,15},{2,0},{3,1},{4,2},{5,3},{6,4},{7,5},{8,6},{9,7},{10,... | collective-permute-start | bytes 159752 | tf_op jit(solution)/shard_map/ppermute | solution.py:217
  57.1 5.6 %collective-permute-start.14 = (bf16[208,128]{1,0:T(8,128)(2,1)S(1)}, bf16[208,128]{1,0:T(8,128)(2,1)S(1)}, u32[]{:S(2)}, u32[]{:S(2)}) collective-permute-start(bf16[208,128]{1,0:T(8,128)(2,1)S(1)} %get-tuple-element.31), channel_id=1, source_target_pairs={{0,15},{1,0},{2,1},{3,2},{4,3},{5,4},{6,5},{7,6},{8,7},{9,8},{10,9... | collective-permute-start | bytes 159752 | tf_op jit(solution)/shard_map/ppermute | solution.py:217
  65.6 4.5 %collective-permute-start.15 = (bf16[1,528,128]{2,1,0:T(8,128)(2,1)S(1)}, bf16[1,528,128]{2,1,0:T(8,128)(2,1)S(1)}, u32[]{:S(2)}, u32[]{:S(2)}) collective-permute-start(bf16[1,528,128]{2,1,0:T(8,128)(2,1)S(1)} %maximum_maximum_fusion.2), channel_id=1, source_target_pairs={{16,0},{32,16},{48,32},{64,48},{80,64},{96,80},{112,96},{17,1},{33... | collective-permute-start | bytes 405512 | tf_op jit(solution)/shard_map/ppermute | solution.py:17
  70.4 5.4 %copy-start.3 = (bf16[512,512]{1,0:T(8,128)(2,1)S(1)}, bf16[512,512]{1,0:T(8,128)(2,1)}, u32[]{:S(2)}) copy-start(bf16[512,512]{1,0:T(8,128)(2,1)} %constant.181.clone) | copy-start | bytes 1572868
  74.1 2.1 %copy-start.2 = (bf16[512,512]{1,0:T(8,128)(2,1)S(1)}, bf16[512,512]{1,0:T(8,128)(2,1)}, u32[]{:S(2)}) copy-start(bf16[512,512]{1,0:T(8,128)(2,1)} %constant.180.clone) | copy-start | bytes 1572868
  84.7 1.3 %copy-start.4 = (bf16[512,512]{1,0:T(8,128)(2,1)S(1)}, bf16[512,512]{1,0:T(8,128)(2,1)}, u32[]{:S(2)}) copy-start(bf16[512,512]{1,0:T(8,128)(2,1)} %constant.190) | copy-start | bytes 1572868
  87.9 16.7 %collective-permute-start.19 = (bf16[4,512,128]{2,1,0:T(8,128)(2,1)S(1)}, bf16[4,512,128]{2,1,0:T(8,128)(2,1)S(1)}, u32[]{:S(2)}, u32[]{:S(2)}) collective-permute-start(bf16[4,512,128]{2,1,0:T(8,128)(2,1)S(1)} %get-tuple-element.26), channel_id=1, source_target_pairs={{1,0},{2,1},{3,2},{4,3},{5,4},{6,5},{7,6},{8,7},{9,8},{10,9},{11,1... | collective-permute-start | bytes 1572872 | tf_op jit(solution)/shard_map/ppermute | solution.py:17
  93.2 18.3 %collective-permute-start.18 = (bf16[4,512,128]{2,1,0:T(8,128)(2,1)S(1)}, bf16[4,512,128]{2,1,0:T(8,128)(2,1)S(1)}, u32[]{:S(2)}, u32[]{:S(2)}) collective-permute-start(bf16[4,512,128]{2,1,0:T(8,128)(2,1)S(1)} %get-tuple-element.25), channel_id=1, source_target_pairs={{0,1},{1,2},{2,3},{3,4},{4,5},{5,6},{6,7},{7,8},{8,9},{9,10},{10,1... | collective-permute-start | bytes 1572872 | tf_op jit(solution)/shard_map/ppermute | solution.py:17
  96.7 19.3 %collective-permute-start.17 = (bf16[4,128,512]{2,1,0:T(8,128)(2,1)S(1)}, bf16[4,128,512]{2,1,0:T(8,128)(2,1)S(1)}, u32[]{:S(2)}, u32[]{:S(2)}) collective-permute-start(bf16[4,128,512]{2,1,0:T(8,128)(2,1)S(1)} %get-tuple-element.24), channel_id=1, source_target_pairs={{16,0},{32,16},{48,32},{64,48},{80,64},{96,80},{112,96},{17,1},{33... | collective-permute-start | bytes 1572872 | tf_op jit(solution)/shard_map/ppermute | solution.py:17
  100.2 15.9 %collective-permute-start.16 = (bf16[4,128,512]{2,1,0:T(8,128)(2,1)S(1)}, bf16[4,128,512]{2,1,0:T(8,128)(2,1)S(1)}, u32[]{:S(2)}, u32[]{:S(2)}) collective-permute-start(bf16[4,128,512]{2,1,0:T(8,128)(2,1)S(1)} %get-tuple-element.23), channel_id=1, source_target_pairs={{0,16},{16,32},{32,48},{48,64},{64,80},{80,96},{96,112},{1,17},{17... | collective-permute-start | bytes 1572872 | tf_op jit(solution)/shard_map/ppermute | solution.py:17
  111.5 5.8 %collective-permute-start.21 = (bf16[4,128,256]{2,1,0:T(8,128)(2,1)S(1)}, bf16[4,128,256]{2,1,0:T(8,128)(2,1)S(1)}, u32[]{:S(2)}, u32[]{:S(2)}) collective-permute-start(bf16[4,128,256]{2,1,0:T(8,128)(2,1)S(1)} %pad_maximum_fusion.10), channel_id=1, source_target_pairs={{16,0},{32,16},{48,32},{64,48},{80,64},{96,80},{112,96},{17,1},{33... | collective-permute-start | bytes 786440 | tf_op jit(solution)/shard_map/ppermute | solution.py:17
  113.5 7.7 %collective-permute-start.20 = (bf16[4,128,256]{2,1,0:T(8,128)(2,1)S(1)}, bf16[4,128,256]{2,1,0:T(8,128)(2,1)S(1)}, u32[]{:S(2)}, u32[]{:S(2)}) collective-permute-start(bf16[4,128,256]{2,1,0:T(8,128)(2,1)S(1)} %pad_maximum_fusion.9), channel_id=1, source_target_pairs={{0,16},{16,32},{32,48},{48,64},{64,80},{80,96},{96,112},{1,17},{17... | collective-permute-start | bytes 786440 | tf_op jit(solution)/shard_map/ppermute | solution.py:17
  121.6 3.6 %copy-start.1 = (bf16[2352,128]{1,0:T(8,128)(2,1)S(1)}, bf16[2352,128]{1,0:T(8,128)(2,1)}, u32[]{:S(2)}) copy-start(bf16[2352,128]{1,0:T(8,128)(2,1)} %param.6) | copy-start | bytes 1806340

commit v18 on v11

--- a/solution.py
+++ b/solution.py
@@ -51,6 +51,17 @@
     return jnp.dot(a, b, preferred_element_type=jnp.float32)
 
 
+def row_products(cosine, sine, values):
+    n = cosine.shape[0]
+    half = n // 2
+    top = half + 8
+    by_cos = dot32(cosine[:top], values)
+    by_sin = dot32(sine[:top], values)
+    by_cos = jnp.concatenate([by_cos[: half + 1], jnp.flip(by_cos[1:half], axis=0)], axis=0)
+    by_sin = jnp.concatenate([by_sin[: half + 1], -jnp.flip(by_sin[1:half], axis=0)], axis=0)
+    return by_cos, by_sin
+
+
 def flexion_fields(pixels):
     row_count = pixels.shape[0]
     col_count = pixels.shape[1]
@@ -61,8 +72,7 @@
     halves = jnp.concatenate([dot32(pixels, cosine), dot32(pixels, sine)], axis=1).astype(
         jnp.bfloat16
     )
-    by_cos = dot32(cosine, halves)
-    by_sin = dot32(sine, halves)
+    by_cos, by_sin = row_products(cosine, sine, halves)
     real_part = by_cos[:, :n] - by_sin[:, n:]
     imag_part = -(by_sin[:, :n] + by_cos[:, n:])
     across = wavenumbers(col_count)[None, :]
@@ -81,8 +91,7 @@
     spectra = jnp.concatenate([one_real, three_real, one_imag, three_imag], axis=1).astype(
         jnp.bfloat16
     )
-    by_cos = dot32(cosine, spectra)
-    by_sin = dot32(sine, spectra)
+    by_cos, by_sin = row_products(cosine, sine, spectra)
     columns_done = jnp.concatenate(
         [
             by_cos[:, : 2 * n] - by_sin[:, 2 * n :],

time: 105 us -> 172 us (1.64); the launches traced: 105 us -> 168 us
  local copies, waits for them, and re-layouts: 3.45 us -> 58.9 us
  other arithmetic: 13.2 us -> 20.2 us
    rev x0 -> x4, local copies, waits for them, and re-layouts: none -> 48.7 us  [the longest x2 26.1 us: row_products(): jnp.flip(by_sin[1:half], axis=0)]
    neg x0 -> x2, other arithmetic: none -> 4.72 us  [row_products(): -jnp.flip(by_sin[1:half], axis=0)]
    slice x1 -> x5, local copies, waits for them, and re-layouts: 0.08 us -> 4.44 us  [the longest x2 2.64 us: row_products(): by_sin[1:half]]
    another operation x7, other arithmetic: 3 us -> 5.36 us
    unnamed x14 -> x32, local copies, waits for them, and re-layouts: 0.17 us -> 2.48 us
  transfers between devices with their start and end apart: 8 -> 8, of which waited for: 5 -> 5; matrix products, arithmetic and copies ran while one was open for 6% -> 4% of each run, Pallas kernels for 0% -> 0%
where the time goes in v18:
time: 172 us; the launch traced here: 168 us
  local copies, waits for them, and re-layouts  58.9 us (34%)
  waiting for transfers between devices  37.4 us (22%)
  matrix products  26.7 us (16%)
  starting transfers between devices  24.5 us (14%)
  other arithmetic  20.2 us (12%)
    rev x2, local copies, waits for them, and re-layouts, row_products(): jnp.flip(by_sin[1:half], axis=0)  26.1 us
    all_to_all x1, waiting for transfers between devices, on_device(): lax.all_to_all(jnp.stack([same_sent, rise_sent], axis=1), 'py', 0, 0, til...  24 us
    rev x2, local copies, waits for them, and re-layouts, row_products(): jnp.flip(by_cos[1:half], axis=0)  22.7 us
    ppermute x7, starting transfers between devices, shifted(): return lax.ppermute(shard, axis, pairs)  16.6 us
    ppermute x7, waiting for transfers between devices, shifted(): return lax.ppermute(shard, axis, pairs)  13.4 us
    dot_general x2, matrix products, gathered_rows(): jnp.dot(chosen.astype(table_rows.dtype), table_rows, preferred_element_ty...  11.2 us
    dot_general x9, matrix products, dot32(): return jnp.dot(a, b, preferred_element_type=jnp.float32)  9.66 us
    all_to_all x1, starting transfers between devices, on_device(): lax.all_to_all(jnp.stack([same_sent, rise_sent], axis=1), 'py', 0, 0, til...  7.9 us
  transfers between devices with their start and end apart: 8, of which 5 were waited for; matrix products, arithmetic and copies ran while one was open for 4% of the time, Pallas kernels for 0%

profile of v18, /device:TPU:40, one launch (start us, length us, event | category | flops | bytes accessed | tf_op | source)
XLA Modules:
  0.0 168.2 jit_solution(6368798769323847577)
XLA Ops:
  0.0 1.3 constant_dynamic-slice_fusion.3
  1.3 0.8 fusion.90
  2.9 5.6 %fusion.17 = bf16[3072,128]{1,0:T(8,128)(2,1)S(1)} fusion(bf16[2352,128]{1,0:T(8,128)(2,1)S(1)} %copy-done, s32[3072]{0:T(1024)S(1)} %eq.43), kind=kOutput, calls=%fused_computation.26 | convolution fusion | flops 1857306624 | bytes 1400832 | tf_op jit(solution)/shard_map/dot_general | solution.py:163
  8.5 5.6 %fusion.16 = bf16[3072,128]{1,0:T(8,128)(2,1)S(1)} fusion(bf16[2352,128]{1,0:T(8,128)(2,1)S(1)} %copy-done, s32[3072]{0:T(1024)S(1)} %eq.89), kind=kOutput, calls=%fused_computation.25 | convolution fusion | flops 1857306624 | bytes 1400832 | tf_op jit(solution)/shard_map/dot_general | solution.py:163
  14.2 0.4 maximum_bitcast_fusion
  14.6 1.3 pad_maximum_fusion.5
  15.9 7.9 %all-to-all-start = ((bf16[16,2,208,128]{3,2,1,0:T(8,128)(2,1)}), bf16[16,2,208,128]{3,2,1,0:T(8,128)(2,1)S(1)}, u32[]{:S(2)}, u32[]{:S(2)}) async-start(bf16[16,2,208,128]{3,2,1,0:T(8,128)(2,1)} %pad_maximum_fusion.5), calls=%async_computation | async-start | bytes 3407872 | tf_op jit(solution)/shard_map/all_to_all | solution.py:221
  24.1 24.0 %all-to-all-done = bf16[16,2,208,128]{3,2,1,0:T(8,128)(2,1)S(1)} async-done(((bf16[16,2,208,128]{3,2,1,0:T(8,128)(2,1)}), bf16[16,2,208,128]{3,2,1,0:T(8,128)(2,1)S(1)}, u32[]{:S(2)}, u32[]{:S(2)}) %all-to-all-start) | async-done | bytes 1703968 | tf_op jit(solution)/shard_map/all_to_all | solution.py:221
  49.4 0.8 fusion.10
  50.1 1.0 fusion.37
  51.3 2.1 %collective-permute-start = (bf16[1,528,128]{2,1,0:T(8,128)(2,1)S(1)}, bf16[1,528,128]{2,1,0:T(8,128)(2,1)S(1)}, u32[]{:S(2)}, u32[]{:S(2)}) collective-permute-start(bf16[1,528,128]{2,1,0:T(8,128)(2,1)S(1)} %maximum_maximum_fusion), channel_id=1, source_target_pairs={{16,0},{32,16},{48,32},{64,48},{80,64},{96,80},{112,96},{17,1},{33... | collective-permute-start | bytes 405512 | tf_op jit(solution)/shard_map/ppermute | solution.py:17
  53.4 3.7 %fusion.2 = f32[2048,128]{1,0:T(8,128)S(1)} fusion(bf16[3072,128]{1,0:T(8,128)(2,1)S(1)} %bitcast.120, s32[3072]{0:T(1024)S(1)} %eq.93, s32[2048]{0:T(1024)S(1)} %iota_add_fusion), kind=kOutput, calls=%fused_computation.4 | convolution fusion | flops 1616904192 | bytes 1855488 | tf_op jit(solution)/shard_map/dot_general | solution.py:158
  57.2 1.1 fusion.23
  58.7 0.5 convolution_convert_fusion
  59.2 0.5 convolution_convert_fusion.1
  59.9 0.8 copy-done.9
  60.8 0.5 fusion.53
  61.4 5.6 %rev.19 = f32[255,1024]{1,0:T(8,128)} reverse(f32[255,1024]{1,0:T(8,128)S(1)} %slice.314), dimensions={0} | reverse | bytes 2088960 | tf_op jit(solution)/shard_map/jit(_flip)/rev | solution.py:60
  67.0 1.6 fusion.52
  68.6 1.1 slice.318
  69.6 9.1 %rev.20 = f32[255,1024]{1,0:T(8,128)} reverse(f32[255,1024]{1,0:T(8,128)} %slice.318), dimensions={0} | reverse | bytes 2088960 | tf_op jit(solution)/shard_map/jit(_flip)/rev | solution.py:61
  78.7 1.4 neg.23
  80.3 0.5 multiply_convert_fusion.3
  80.7 1.0 multiply_convert_fusion.2
  81.7 0.7 fusion.62
  82.7 2.1 %fusion.63 = f32[264,2048]{1,0:T(8,128)} fusion(bf16[264,512]{1,0:T(8,128)(2,1)S(1)} %copy-done.12, bf16[512,512]{1,0:T(8,128)(2,1)S(1)} %get-tuple-element.21, bf16[512,512]{1,0:T(8,128)(2,1)S(1)} %get-tuple-element.22, bf16[512,512]{1,0:T(8,128)(2,1)S(1)} %get-tuple-element.20, bf16[512,512]{1,0:T(8,128)(2,1)S(1)} %get-tuple-element.5), kind=kOutput, calls=%fused_computation.100 | convolution fusion | flops 562036736 | bytes 4530176 | tf_op jit(solution)/shard_map/dot_general | solution.py:51
  84.8 1.6 slice.326
  86.3 17.0 %rev.22 = f32[255,2048]{1,0:T(8,128)} reverse(f32[255,2048]{1,0:T(8,128)} %slice.326), dimensions={0} | reverse | bytes 4177920 | tf_op jit(solution)/shard_map/jit(_flip)/rev | solution.py:61
  103.3 3.3 %neg.26 = f32[255,2048]{1,0:T(8,128)} negate(f32[255,2048]{1,0:T(8,128)} %rev.22) | non-fusion elementwise | flops 522240 | bytes 4177920 | tf_op jit(solution)/shard_map/neg | solution.py:61
  106.6 1.6 slice.322
  108.2 17.1 %rev.21 = f32[255,2048]{1,0:T(8,128)} reverse(f32[255,2048]{1,0:T(8,128)} %slice.322), dimensions={0} | reverse | bytes 4177920 | tf_op jit(solution)/shard_map/jit(_flip)/rev | solution.py:60
  125.3 3.4 %fusion.28 = (bf16[512,1024]{1,0:T(8,128)(2,1)S(1)}, bf16[512,1024]{1,0:T(8,128)(2,1)S(1)}) fusion(f32[257,2048]{1,0:T(8,128)S(1)} %bitcast.116, f32[255,2048]{1,0:T(8,128)} %neg.26, f32[257,2048]{1,0:T(8,128)} %bitcast.117, f32[255,2048]{1,0:T(8,128)} %rev.21), kind=kLoop, calls=%fused_computation.34 | loop fusion | flops 4194304 | bytes 10485760 | tf_op jit(solution)/shard_map/convert.20
  128.9 0.9 copy-done.6
  129.8 1.3 fusion.96
  131.1 1.3 fusion.97
  132.4 1.2 fusion.95
  134.2 2.0 %collective-permute-start.4 = (bf16[4,512,128]{2,1,0:T(8,128)(2,1)S(1)}, bf16[4,512,128]{2,1,0:T(8,128)(2,1)S(1)}, u32[]{:S(2)}, u32[]{:S(2)}) collective-permute-start(bf16[4,512,128]{2,1,0:T(8,128)(2,1)S(1)} %get-tuple-element.28), channel_id=1, source_target_pairs={{1,0},{2,1},{3,2},{4,3},{5,4},{6,5},{7,6},{8,7},{9,8},{10,9},{11,1... | collective-permute-start | bytes 1572872 | tf_op jit(solution)/shard_map/ppermute | solution.py:17
  136.2 3.8 %collective-permute-start.3 = (bf16[4,512,128]{2,1,0:T(8,128)(2,1)S(1)}, bf16[4,512,128]{2,1,0:T(8,128)(2,1)S(1)}, u32[]{:S(2)}, u32[]{:S(2)}) collective-permute-start(bf16[4,512,128]{2,1,0:T(8,128)(2,1)S(1)} %get-tuple-element.27), channel_id=1, source_target_pairs={{0,1},{1,2},{2,3},{3,4},{4,5},{5,6},{6,7},{7,8},{8,9},{9,10},{10,1... | collective-permute-start | bytes 1572872 | tf_op jit(solution)/shard_map/ppermute | solution.py:17
  140.1 1.2 fusion.54
  141.7 1.9 %collective-permute-start.2 = (bf16[4,128,512]{2,1,0:T(8,128)(2,1)S(1)}, bf16[4,128,512]{2,1,0:T(8,128)(2,1)S(1)}, u32[]{:S(2)}, u32[]{:S(2)}) collective-permute-start(bf16[4,128,512]{2,1,0:T(8,128)(2,1)S(1)} %get-tuple-element.24), channel_id=1, source_target_pairs={{16,0},{32,16},{48,32},{64,48},{80,64},{96,80},{112,96},{17,1},{33... | collective-permute-start | bytes 1572872 | tf_op jit(solution)/shard_map/ppermute | solution.py:17
  143.6 2.4 %collective-permute-start.1 = (bf16[4,128,512]{2,1,0:T(8,128)(2,1)S(1)}, bf16[4,128,512]{2,1,0:T(8,128)(2,1)S(1)}, u32[]{:S(2)}, u32[]{:S(2)}) collective-permute-start(bf16[4,128,512]{2,1,0:T(8,128)(2,1)S(1)} %get-tuple-element.23), channel_id=1, source_target_pairs={{0,16},{16,32},{32,48},{48,64},{64,80},{80,96},{96,112},{1,17},{17... | collective-permute-start | bytes 1572872 | tf_op jit(solution)/shard_map/ppermute | solution.py:17
  146.0 4.4 %collective-permute-done.4 = bf16[4,512,128]{2,1,0:T(8,128)(2,1)S(1)} collective-permute-done((bf16[4,512,128]{2,1,0:T(8,128)(2,1)S(1)}, bf16[4,512,128]{2,1,0:T(8,128)(2,1)S(1)}, u32[]{:S(2)}, u32[]{:S(2)}) %collective-permute-start.4) | collective-permute-done | bytes 524320 | tf_op jit(solution)/shard_map/ppermute | solution.py:17
  150.5 4.0 %collective-permute-done.3 = bf16[4,512,128]{2,1,0:T(8,128)(2,1)S(1)} collective-permute-done((bf16[4,512,128]{2,1,0:T(8,128)(2,1)S(1)}, bf16[4,512,128]{2,1,0:T(8,128)(2,1)S(1)}, u32[]{:S(2)}, u32[]{:S(2)}) %collective-permute-start.3) | collective-permute-done | bytes 524320 | tf_op jit(solution)/shard_map/ppermute | solution.py:17
  154.6 1.9 %collective-permute-start.6 = (bf16[4,128,256]{2,1,0:T(8,128)(2,1)S(1)}, bf16[4,128,256]{2,1,0:T(8,128)(2,1)S(1)}, u32[]{:S(2)}, u32[]{:S(2)}) collective-permute-start(bf16[4,128,256]{2,1,0:T(8,128)(2,1)S(1)} %pad_maximum_fusion.15), channel_id=1, source_target_pairs={{16,0},{32,16},{48,32},{64,48},{80,64},{96,80},{112,96},{17,1},{33... | collective-permute-start | bytes 786440 | tf_op jit(solution)/shard_map/ppermute | solution.py:17
  156.6 2.4 %collective-permute-start.5 = (bf16[4,128,256]{2,1,0:T(8,128)(2,1)S(1)}, bf16[4,128,256]{2,1,0:T(8,128)(2,1)S(1)}, u32[]{:S(2)}, u32[]{:S(2)}) collective-permute-start(bf16[4,128,256]{2,1,0:T(8,128)(2,1)S(1)} %pad_maximum_fusion.14), channel_id=1, source_target_pairs={{0,16},{16,32},{32,48},{48,64},{64,80},{80,96},{96,112},{1,17},{17... | collective-permute-start | bytes 786440 | tf_op jit(solution)/shard_map/ppermute | solution.py:17
  159.3 1.1 collective-permute-done.6
  160.4 3.8 %collective-permute-done.5 = bf16[4,128,256]{2,1,0:T(8,128)(2,1)S(1)} collective-permute-done((bf16[4,128,256]{2,1,0:T(8,128)(2,1)S(1)}, bf16[4,128,256]{2,1,0:T(8,128)(2,1)S(1)}, u32[]{:S(2)}, u32[]{:S(2)}) %collective-permute-start.5) | collective-permute-done | bytes 262176 | tf_op jit(solution)/shard_map/ppermute | solution.py:17
  164.7 3.5 %fusion.13 = f32[4,512,512]{2,1,0:T(8,128)} fusion(f32[4,128,512]{2,1,0:T(8,128)S(1)} %convert_element_type.165, f32[4,128,512]{2,1,0:T(8,128)S(1)} %convert_element_type.164, f32[4,512,128]{2,1,0:T(8,128)S(1)} %get-tuple-element.50, f32[4,512,128]{2,1,0:T(8,128)S(1)} %get-tuple-element.49, f32[512]{0:T(512)S(1)} %pad.18.clone, ...), kind=kLoop, calls=%fused_computation.21 | loop fusion | flops 14680064 | bytes 10496000 | tf_op jit(solution)/shard_map/add | solution.py:278
  (97 shorter events, 5.6 us)
Async XLA Ops:
  0.0 2.9 %copy-start = (bf16[2352,128]{1,0:T(8,128)(2,1)S(1)}, bf16[2352,128]{1,0:T(8,128)(2,1)}, u32[]{:S(2)}) copy-start(bf16[2352,128]{1,0:T(8,128)(2,1)} %param.6) | copy-start | bytes 1806340
  15.9 32.1 %all-to-all-start = ((bf16[16,2,208,128]{3,2,1,0:T(8,128)(2,1)}), bf16[16,2,208,128]{3,2,1,0:T(8,128)(2,1)S(1)}, u32[]{:S(2)}, u32[]{:S(2)}) async-start(bf16[16,2,208,128]{3,2,1,0:T(8,128)(2,1)} %pad_maximum_fusion.5), calls=%async_computation | async-start | bytes 3407872 | tf_op jit(solution)/shard_map/all_to_all | solution.py:221
  51.3 5.9 %collective-permute-start = (bf16[1,528,128]{2,1,0:T(8,128)(2,1)S(1)}, bf16[1,528,128]{2,1,0:T(8,128)(2,1)S(1)}, u32[]{:S(2)}, u32[]{:S(2)}) collective-permute-start(bf16[1,528,128]{2,1,0:T(8,128)(2,1)S(1)} %maximum_maximum_fusion), channel_id=1, source_target_pairs={{16,0},{32,16},{48,32},{64,48},{80,64},{96,80},{112,96},{17,1},{33... | collective-permute-start | bytes 405512 | tf_op jit(solution)/shard_map/ppermute | solution.py:17
  57.2 1.5 copy-start.5
  57.2 1.9 %copy-start.4 = (bf16[512,512]{1,0:T(8,128)(2,1)S(1)}, bf16[512,512]{1,0:T(8,128)(2,1)}, u32[]{:S(2)}) copy-start(bf16[512,512]{1,0:T(8,128)(2,1)} %constant.127.clone) | copy-start | bytes 1572868
  58.6 2.1 %copy-start.11 = (bf16[264,512]{1,0:T(8,128)(2,1)S(1)}, bf16[264,512]{1,0:T(8,128)(2,1)}, u32[]{:S(2)}) copy-start(bf16[264,512]{1,0:T(8,128)(2,1)} %constant.133) | copy-start | bytes 811012
  59.2 0.8 copy-start.7
  59.9 0.8 copy-start.9
  61.2 5.7 %copy-start.8 = (bf16[512,512]{0,1:T(8,128)(2,1)S(1)}, bf16[512,512]{0,1:T(8,128)(2,1)}, u32[]{:S(2)}) copy-start(bf16[512,512]{0,1:T(8,128)(2,1)} %copy-done.7) | copy-start | bytes 1572868
  78.7 1.5 copy-start.3
  80.7 1.0 copy-start.13
  81.7 1.0 copy-start.12
  103.3 3.3 %copy-start.2 = (f32[264,2048]{1,0:T(8,128)S(1)}, f32[264,2048]{1,0:T(8,128)}, u32[]{:S(2)}) copy-start(f32[264,2048]{1,0:T(8,128)} %fusion.63) | copy-start | bytes 6488068
  128.7 1.0 copy-start.6
  131.1 1.3 copy-start.10
  134.2 16.2 %collective-permute-start.4 = (bf16[4,512,128]{2,1,0:T(8,128)(2,1)S(1)}, bf16[4,512,128]{2,1,0:T(8,128)(2,1)S(1)}, u32[]{:S(2)}, u32[]{:S(2)}) collective-permute-start(bf16[4,512,128]{2,1,0:T(8,128)(2,1)S(1)} %get-tuple-element.28), channel_id=1, source_target_pairs={{1,0},{2,1},{3,2},{4,3},{5,4},{6,5},{7,6},{8,7},{9,8},{10,9},{11,1... | collective-permute-start | bytes 1572872 | tf_op jit(solution)/shard_map/ppermute | solution.py:17
  136.2 18.3 %collective-permute-start.3 = (bf16[4,512,128]{2,1,0:T(8,128)(2,1)S(1)}, bf16[4,512,128]{2,1,0:T(8,128)(2,1)S(1)}, u32[]{:S(2)}, u32[]{:S(2)}) collective-permute-start(bf16[4,512,128]{2,1,0:T(8,128)(2,1)S(1)} %get-tuple-element.27), channel_id=1, source_target_pairs={{0,1},{1,2},{2,3},{3,4},{4,5},{5,6},{6,7},{7,8},{8,9},{9,10},{10,1... | collective-permute-start | bytes 1572872 | tf_op jit(solution)/shard_map/ppermute | solution.py:17
  141.7 17.4 %collective-permute-start.2 = (bf16[4,128,512]{2,1,0:T(8,128)(2,1)S(1)}, bf16[4,128,512]{2,1,0:T(8,128)(2,1)S(1)}, u32[]{:S(2)}, u32[]{:S(2)}) collective-permute-start(bf16[4,128,512]{2,1,0:T(8,128)(2,1)S(1)} %get-tuple-element.24), channel_id=1, source_target_pairs={{16,0},{32,16},{48,32},{64,48},{80,64},{96,80},{112,96},{17,1},{33... | collective-permute-start | bytes 1572872 | tf_op jit(solution)/shard_map/ppermute | solution.py:17
  143.6 15.6 %collective-permute-start.1 = (bf16[4,128,512]{2,1,0:T(8,128)(2,1)S(1)}, bf16[4,128,512]{2,1,0:T(8,128)(2,1)S(1)}, u32[]{:S(2)}, u32[]{:S(2)}) collective-permute-start(bf16[4,128,512]{2,1,0:T(8,128)(2,1)S(1)} %get-tuple-element.23), channel_id=1, source_target_pairs={{0,16},{16,32},{32,48},{48,64},{64,80},{80,96},{96,112},{1,17},{17... | collective-permute-start | bytes 1572872 | tf_op jit(solution)/shard_map/ppermute | solution.py:17
  154.6 5.8 %collective-permute-start.6 = (bf16[4,128,256]{2,1,0:T(8,128)(2,1)S(1)}, bf16[4,128,256]{2,1,0:T(8,128)(2,1)S(1)}, u32[]{:S(2)}, u32[]{:S(2)}) collective-permute-start(bf16[4,128,256]{2,1,0:T(8,128)(2,1)S(1)} %pad_maximum_fusion.15), channel_id=1, source_target_pairs={{16,0},{32,16},{48,32},{64,48},{80,64},{96,80},{112,96},{17,1},{33... | collective-permute-start | bytes 786440 | tf_op jit(solution)/shard_map/ppermute | solution.py:17
  156.6 7.7 %collective-permute-start.5 = (bf16[4,128,256]{2,1,0:T(8,128)(2,1)S(1)}, bf16[4,128,256]{2,1,0:T(8,128)(2,1)S(1)}, u32[]{:S(2)}, u32[]{:S(2)}) collective-permute-start(bf16[4,128,256]{2,1,0:T(8,128)(2,1)S(1)} %pad_maximum_fusion.14), channel_id=1, source_target_pairs={{0,16},{16,32},{32,48},{48,64},{64,80},{80,96},{96,112},{1,17},{17... | collective-permute-start | bytes 786440 | tf_op jit(solution)/shard_map/ppermute | solution.py:17
  164.7 3.5 %copy-start.1 = (bf16[2352,128]{1,0:T(8,128)(2,1)S(1)}, bf16[2352,128]{1,0:T(8,128)(2,1)}, u32[]{:S(2)}) copy-start(bf16[2352,128]{1,0:T(8,128)(2,1)} %param.6) | copy-start | bytes 1806340

commit v19 on v11

--- a/solution.py
+++ b/solution.py
@@ -146,7 +146,7 @@
 
 def one_hot_rows(codes, count, values):
     picks = codes[None, :] == jnp.arange(1, count + 1, dtype=jnp.int32)[:, None]
-    return jnp.dot(picks.astype(values.dtype), values, preferred_element_type=jnp.float32)
+    return jnp.dot(picks.astype(values.dtype), values, preferred_element_type=values.dtype)
 
 
 def gathered_rows(table_rows, picks):

time: 105 us -> 105 us (level)
  no operation moved by 1% of the time
where the time goes in v19:
time: 105 us
  waiting for transfers between devices  37.3 us (36%)
  matrix products  25.8 us (25%)
  starting transfers between devices  24.5 us (23%)
  other arithmetic  13.2 us (13%)
  local copies, waits for them, and re-layouts  3.45 us (3%)
    all_to_all x1, waiting for transfers between devices, on_device(): lax.all_to_all(jnp.stack([same_sent, rise_sent], axis=1), 'py', 0, 0, til...  24 us
    ppermute x7, starting transfers between devices, shifted(): return lax.ppermute(shard, axis, pairs)  16.6 us
    ppermute x7, waiting for transfers between devices, shifted(): return lax.ppermute(shard, axis, pairs)  13.4 us
    dot_general x2, matrix products, gathered_rows(): jnp.dot(chosen.astype(table_rows.dtype), table_rows, preferred_element_ty...  11.2 us
    dot_general x9, matrix products, dot32(): return jnp.dot(a, b, preferred_element_type=jnp.float32)  8.77 us
    all_to_all x1, starting transfers between devices, on_device(): lax.all_to_all(jnp.stack([same_sent, rise_sent], axis=1), 'py', 0, 0, til...  7.89 us
    dot_general x3, matrix products, one_hot_rows(): jnp.dot(picks.astype(values.dtype), values, preferred_element_type=values...  5.8 us
    add x1, other arithmetic, on_device(): return col_weight * rows_done + (1.0 - col_weight) * horizontal  3.54 us
  transfers between devices with their start and end apart: 8, of which 5 were waited for; matrix products, arithmetic and copies ran while one was open for 6% of the time, Pallas kernels for 0%

profile of v19, /device:TPU:40, one launch (start us, length us, event | category | flops | bytes accessed | tf_op | source)
XLA Modules:
  0.0 104.7 jit_solution(9259014898427396414)
XLA Ops:
  0.0 1.3 %constant_dynamic-slice_fusion.3 = (s32[1,16,192]{1,2,0:T(8,128)S(1)}, s32[1,16,192]{1,2,0:T(8,128)S(1)}, s32[1,16,192]{1,2,0:T(8,128)S(1)}, s32[1,16,192]{1,2,0:T(8,128)S(1)}) fusion(s32[1,128,192]{1,2,0:T(8,128)} %param.8, s32[]{:T(128)S(6)} %select_n.142, s32[]{:T(128)S(6)} %select_n.146, s32[1,128,192]{1,2,0:T(8,128)} %param.7), kind=kLoop, calls=%fused_computation.160 | loop fusion | bytes 98312 | tf_op jit(solution)/shard_map/dynamic_slice | solution.py:201
  1.3 0.8 fusion.76
  2.9 5.6 %fusion.17 = bf16[3072,128]{1,0:T(8,128)(2,1)S(1)} fusion(bf16[2352,128]{1,0:T(8,128)(2,1)S(1)} %copy-done, s32[3072]{0:T(1024)S(1)} %eq.43), kind=kOutput, calls=%fused_computation.22 | convolution fusion | flops 1857306624 | bytes 1400832 | tf_op jit(solution)/shard_map/dot_general | solution.py:154
  8.5 5.6 %fusion.16 = bf16[3072,128]{1,0:T(8,128)(2,1)S(1)} fusion(bf16[2352,128]{1,0:T(8,128)(2,1)S(1)} %copy-done, s32[3072]{0:T(1024)S(1)} %eq.89), kind=kOutput, calls=%fused_computation.21 | convolution fusion | flops 1857306624 | bytes 1400832 | tf_op jit(solution)/shard_map/dot_general | solution.py:154
  14.2 0.4 maximum_bitcast_fusion
  14.6 1.3 %pad_maximum_fusion.3 = bf16[16,2,208,128]{3,2,1,0:T(8,128)(2,1)} fusion(bf16[16,1,208,128]{3,2,1,0:T(8,128)(2,1)S(1)} %get-tuple-element.62, bf16[16,1,208,128]{3,2,1,0:T(8,128)(2,1)S(1)} %get-tuple-element.61), kind=kLoop, calls=%fused_computation.36 | loop fusion | flops 851968 | bytes 3407872 | tf_op jit(solution)/shard_map/stack | solution.py:212
  15.9 7.9 %all-to-all-start = ((bf16[16,2,208,128]{3,2,1,0:T(8,128)(2,1)}), bf16[16,2,208,128]{3,2,1,0:T(8,128)(2,1)S(1)}, u32[]{:S(2)}, u32[]{:S(2)}) async-start(bf16[16,2,208,128]{3,2,1,0:T(8,128)(2,1)} %pad_maximum_fusion.3), calls=%async_computation | async-start | bytes 3407872 | tf_op jit(solution)/shard_map/all_to_all | solution.py:212
  24.1 24.0 %all-to-all-done = bf16[16,2,208,128]{3,2,1,0:T(8,128)(2,1)S(1)} async-done(((bf16[16,2,208,128]{3,2,1,0:T(8,128)(2,1)}), bf16[16,2,208,128]{3,2,1,0:T(8,128)(2,1)S(1)}, u32[]{:S(2)}, u32[]{:S(2)}) %all-to-all-start) | async-done | bytes 1703968 | tf_op jit(solution)/shard_map/all_to_all | solution.py:212
  48.8 0.3 reduce-window.9
  49.2 0.1 slice_reduce_fusion
  49.4 0.8 fusion.10
  50.1 1.0 fusion.27
  51.2 0.1 maximum_maximum_fusion
  51.3 2.1 %collective-permute-start = (bf16[1,528,128]{2,1,0:T(8,128)(2,1)S(1)}, bf16[1,528,128]{2,1,0:T(8,128)(2,1)S(1)}, u32[]{:S(2)}, u32[]{:S(2)}) collective-permute-start(bf16[1,528,128]{2,1,0:T(8,128)(2,1)S(1)} %maximum_maximum_fusion), channel_id=1, source_target_pairs={{16,0},{32,16},{48,32},{64,48},{80,64},{96,80},{112,96},{17,1},{33... | collective-permute-start | bytes 405512 | tf_op jit(solution)/shard_map/ppermute | solution.py:17
  53.4 3.7 %fusion.2 = bf16[2048,128]{1,0:T(8,128)(2,1)S(1)} fusion(bf16[3072,128]{1,0:T(8,128)(2,1)S(1)} %bitcast.112, s32[3072]{0:T(1024)S(1)} %eq.93, s32[2048]{0:T(1024)S(1)} %iota_add_fusion), kind=kOutput, calls=%fused_computation.4 | convolution fusion | flops 1616904192 | bytes 1331200 | tf_op jit(solution)/shard_map/dot_general | solution.py:149
  57.2 1.1 %fusion.20 = bf16[2048,128]{1,0:T(8,128)(2,1)S(1)} fusion(bf16[2048,128]{1,0:T(8,128)(2,1)S(1)} %fusion.2, s32[512]{0:T(512)S(1)} %bitcast.121, s32[2048]{0:T(1024)S(1)} %iota_add_fusion, bf16[1,528,128]{2,1,0:T(8,128)(2,1)S(1)} %collective-permute-done), kind=kOutput, calls=%fused_computation.26 | convolution fusion | flops 269746176 | bytes 1189888 | tf_op jit(solution)/shard_map/dot_general | solution.py:149
  58.3 0.3 reshape.309
  58.6 0.5 convolution_convert_fusion
  59.1 0.5 convolution_convert_fusion.1
  59.6 0.7 fusion.39
  60.4 0.7 fusion.38
  61.1 0.3 multiply_convert_fusion.3
  61.4 1.0 multiply_convert_fusion.2
  62.4 1.3 %fusion.48 = f32[512,2048]{1,0:T(8,128)S(1)} fusion(bf16[512,512]{1,0:T(8,128)(2,1)S(1)} %copy-done.3, bf16[512,512]{1,0:T(8,128)(2,1)S(1)} %get-tuple-element.21, bf16[512,512]{1,0:T(8,128)(2,1)S(1)} %get-tuple-element.22, bf16[512,512]{1,0:T(8,128)(2,1)S(1)} %get-tuple-element.20, bf16[512,512]{1,0:T(8,128)(2,1)S(1)} %get-tuple-element.5), kind=kOutput, calls=%fused_computation.81 | convolution fusion | flops 1082130432 | bytes 6815744 | tf_op jit(solution)/shard_map/dot_general | solution.py:51
  63.6 1.3 %fusion.49 = f32[512,2048]{1,0:T(8,128)S(1)} fusion(bf16[512,512]{1,0:T(8,128)(2,1)S(1)} %copy-done.2, bf16[512,512]{1,0:T(8,128)(2,1)S(1)} %get-tuple-element.21, bf16[512,512]{1,0:T(8,128)(2,1)S(1)} %get-tuple-element.22, bf16[512,512]{1,0:T(8,128)(2,1)S(1)} %get-tuple-element.20, bf16[512,512]{1,0:T(8,128)(2,1)S(1)} %get-tuple-element.5), kind=kOutput, calls=%fused_computation.82 | convolution fusion | flops 1082130432 | bytes 6815744 | tf_op jit(solution)/shard_map/dot_general | solution.py:51
  64.9 1.2 %fusion.24 = (bf16[512,1024]{1,0:T(8,128)(2,1)S(1)}, bf16[512,1024]{1,0:T(8,128)(2,1)S(1)}) fusion(f32[512,2048]{1,0:T(8,128)S(1)} %fusion.48, f32[512,2048]{1,0:T(8,128)S(1)} %fusion.49), kind=kLoop, calls=%fused_computation.30 | loop fusion | flops 2097152 | bytes 10485760 | tf_op jit(solution)/shard_map/convert.20
  66.3 1.3 %fusion.82 = f32[2048,512]{1,0:T(8,128)S(1)} fusion(bf16[512,512]{1,0:T(8,128)(2,1)S(1)} %copy-done.3, bf16[512,512]{1,0:T(8,128)(2,1)S(1)} %get-tuple-element.32, bf16[512,512]{1,0:T(8,128)(2,1)S(1)} %get-tuple-element.31, bf16[512,512]{1,0:T(8,128)(2,1)S(1)} %get-tuple-element.30, bf16[512,512]{1,0:T(8,128)(2,1)S(1)} %get-tuple-element.29), kind=kOutput, calls=%fused_computation.186 | convolution fusion | flops 1082130432 | bytes 6815744 | tf_op jit(solution)/shard_map/dot_general | solution.py:51
  67.6 1.3 %fusion.83 = f32[2048,512]{1,0:T(8,128)S(1)} fusion(bf16[512,512]{1,0:T(8,128)(2,1)S(1)} %copy-done.2, bf16[512,512]{1,0:T(8,128)(2,1)S(1)} %get-tuple-element.32, bf16[512,512]{1,0:T(8,128)(2,1)S(1)} %get-tuple-element.31, bf16[512,512]{1,0:T(8,128)(2,1)S(1)} %get-tuple-element.30, bf16[512,512]{1,0:T(8,128)(2,1)S(1)} %get-tuple-element.29), kind=kOutput, calls=%fused_computation.187 | convolution fusion | flops 1082130432 | bytes 6815744 | tf_op jit(solution)/shard_map/dot_general | solution.py:51
  68.9 1.2 %fusion.81 = f32[2048,512]{1,0:T(8,128)S(1)} fusion(bf16[512,512]{1,0:T(8,128)(2,1)S(1)} %copy-done.4, bf16[512,512]{1,0:T(8,128)(2,1)S(1)} %get-tuple-element.32, bf16[512,512]{1,0:T(8,128)(2,1)S(1)} %get-tuple-element.31, bf16[512,512]{1,0:T(8,128)(2,1)S(1)} %get-tuple-element.30, bf16[512,512]{1,0:T(8,128)(2,1)S(1)} %get-tuple-element.29), kind=kOutput, calls=%fused_computation.185 | convolution fusion | flops 1082130432 | bytes 6815744 | tf_op jit(solution)/shard_map/dot_general | solution.py:51
  70.1 0.3 fusion.50
  70.4 0.1 pad_maximum_fusion.5
  70.5 0.2 fusion.86
  70.7 2.0 %collective-permute-start.4 = (bf16[4,512,128]{2,1,0:T(8,128)(2,1)S(1)}, bf16[4,512,128]{2,1,0:T(8,128)(2,1)S(1)}, u32[]{:S(2)}, u32[]{:S(2)}) collective-permute-start(bf16[4,512,128]{2,1,0:T(8,128)(2,1)S(1)} %get-tuple-element.28), channel_id=1, source_target_pairs={{1,0},{2,1},{3,2},{4,3},{5,4},{6,5},{7,6},{8,7},{9,8},{10,9},{11,1... | collective-permute-start | bytes 1572872 | tf_op jit(solution)/shard_map/ppermute | solution.py:17
  72.7 3.8 %collective-permute-start.3 = (bf16[4,512,128]{2,1,0:T(8,128)(2,1)S(1)}, bf16[4,512,128]{2,1,0:T(8,128)(2,1)S(1)}, u32[]{:S(2)}, u32[]{:S(2)}) collective-permute-start(bf16[4,512,128]{2,1,0:T(8,128)(2,1)S(1)} %get-tuple-element.27), channel_id=1, source_target_pairs={{0,1},{1,2},{2,3},{3,4},{4,5},{5,6},{6,7},{7,8},{8,9},{9,10},{10,1... | collective-permute-start | bytes 1572872 | tf_op jit(solution)/shard_map/ppermute | solution.py:17
  76.6 1.2 %fusion.40 = (bf16[1,512,512]{2,1,0:T(8,128)(2,1)S(1)}, bf16[1,512,512]{2,1,0:T(8,128)(2,1)S(1)}, bf16[1,512,512]{2,1,0:T(8,128)(2,1)S(1)}, bf16[1,512,512]{2,1,0:T(8,128)(2,1)S(1)}) fusion(f32[2048,512]{1,0:T(8,128)S(1)} %fusion.82, f32[2048,512]{1,0:T(8,128)S(1)} %fusion.83), kind=kLoop, calls=%fused_computation.69 | loop fusion | flops 2097152 | bytes 10485760 | tf_op jit(solution)/shard_map/stack | solution.py:112
  77.8 0.3 pad_maximum_fusion.2
  78.2 1.9 %collective-permute-start.2 = (bf16[4,128,512]{2,1,0:T(8,128)(2,1)S(1)}, bf16[4,128,512]{2,1,0:T(8,128)(2,1)S(1)}, u32[]{:S(2)}, u32[]{:S(2)}) collective-permute-start(bf16[4,128,512]{2,1,0:T(8,128)(2,1)S(1)} %get-tuple-element.24), channel_id=1, source_target_pairs={{16,0},{32,16},{48,32},{64,48},{80,64},{96,80},{112,96},{17,1},{33... | collective-permute-start | bytes 1572872 | tf_op jit(solution)/shard_map/ppermute | solution.py:17
  80.1 2.4 %collective-permute-start.1 = (bf16[4,128,512]{2,1,0:T(8,128)(2,1)S(1)}, bf16[4,128,512]{2,1,0:T(8,128)(2,1)S(1)}, u32[]{:S(2)}, u32[]{:S(2)}) collective-permute-start(bf16[4,128,512]{2,1,0:T(8,128)(2,1)S(1)} %get-tuple-element.23), channel_id=1, source_target_pairs={{0,16},{16,32},{32,48},{48,64},{64,80},{80,96},{96,112},{1,17},{17... | collective-permute-start | bytes 1572872 | tf_op jit(solution)/shard_map/ppermute | solution.py:17
  82.5 4.4 %collective-permute-done.4 = bf16[4,512,128]{2,1,0:T(8,128)(2,1)S(1)} collective-permute-done((bf16[4,512,128]{2,1,0:T(8,128)(2,1)S(1)}, bf16[4,512,128]{2,1,0:T(8,128)(2,1)S(1)}, u32[]{:S(2)}, u32[]{:S(2)}) %collective-permute-start.4) | collective-permute-done | bytes 524320 | tf_op jit(solution)/shard_map/ppermute | solution.py:17
  87.0 4.0 %collective-permute-done.3 = bf16[4,512,128]{2,1,0:T(8,128)(2,1)S(1)} collective-permute-done((bf16[4,512,128]{2,1,0:T(8,128)(2,1)S(1)}, bf16[4,512,128]{2,1,0:T(8,128)(2,1)S(1)}, u32[]{:S(2)}, u32[]{:S(2)}) %collective-permute-start.3) | collective-permute-done | bytes 524320 | tf_op jit(solution)/shard_map/ppermute | solution.py:17
  91.1 1.9 %collective-permute-start.6 = (bf16[4,128,256]{2,1,0:T(8,128)(2,1)S(1)}, bf16[4,128,256]{2,1,0:T(8,128)(2,1)S(1)}, u32[]{:S(2)}, u32[]{:S(2)}) collective-permute-start(bf16[4,128,256]{2,1,0:T(8,128)(2,1)S(1)} %pad_maximum_fusion.11), channel_id=1, source_target_pairs={{16,0},{32,16},{48,32},{64,48},{80,64},{96,80},{112,96},{17,1},{33... | collective-permute-start | bytes 786440 | tf_op jit(solution)/shard_map/ppermute | solution.py:17
  93.1 2.4 %collective-permute-start.5 = (bf16[4,128,256]{2,1,0:T(8,128)(2,1)S(1)}, bf16[4,128,256]{2,1,0:T(8,128)(2,1)S(1)}, u32[]{:S(2)}, u32[]{:S(2)}) collective-permute-start(bf16[4,128,256]{2,1,0:T(8,128)(2,1)S(1)} %pad_maximum_fusion.10), channel_id=1, source_target_pairs={{0,16},{16,32},{32,48},{48,64},{64,80},{80,96},{96,112},{1,17},{17... | collective-permute-start | bytes 786440 | tf_op jit(solution)/shard_map/ppermute | solution.py:17
  95.5 0.1 convert_element_type.157
  95.7 0.1 convert_element_type.156
  95.8 1.1 %collective-permute-done.6 = bf16[4,128,256]{2,1,0:T(8,128)(2,1)S(1)} collective-permute-done((bf16[4,128,256]{2,1,0:T(8,128)(2,1)S(1)}, bf16[4,128,256]{2,1,0:T(8,128)(2,1)S(1)}, u32[]{:S(2)}, u32[]{:S(2)}) %collective-permute-start.6) | collective-permute-done | bytes 262176 | tf_op jit(solution)/shard_map/ppermute | solution.py:17
  96.9 3.8 %collective-permute-done.5 = bf16[4,128,256]{2,1,0:T(8,128)(2,1)S(1)} collective-permute-done((bf16[4,128,256]{2,1,0:T(8,128)(2,1)S(1)}, bf16[4,128,256]{2,1,0:T(8,128)(2,1)S(1)}, u32[]{:S(2)}, u32[]{:S(2)}) %collective-permute-start.5) | collective-permute-done | bytes 262176 | tf_op jit(solution)/shard_map/ppermute | solution.py:17
  100.8 0.4 fusion.35
  101.2 3.5 %fusion.13 = f32[4,512,512]{2,1,0:T(8,128)} fusion(f32[4,128,512]{2,1,0:T(8,128)S(1)} %convert_element_type.157, f32[4,128,512]{2,1,0:T(8,128)S(1)} %convert_element_type.156, f32[4,512,128]{2,1,0:T(8,128)S(1)} %get-tuple-element.50, f32[4,512,128]{2,1,0:T(8,128)S(1)} %get-tuple-element.49, f32[512]{0:T(512)S(1)} %pad.18.clone, ...), kind=kLoop, calls=%fused_computation.17 | loop fusion | flops 14680064 | bytes 10496000 | tf_op jit(solution)/shard_map/add | solution.py:269
  (69 shorter events, 2.4 us)
Async XLA Ops:
  0.0 2.9 %copy-start = (bf16[2352,128]{1,0:T(8,128)(2,1)S(1)}, bf16[2352,128]{1,0:T(8,128)(2,1)}, u32[]{:S(2)}) copy-start(bf16[2352,128]{1,0:T(8,128)(2,1)} %param.6) | copy-start | bytes 1806340
  15.9 32.1 %all-to-all-start = ((bf16[16,2,208,128]{3,2,1,0:T(8,128)(2,1)}), bf16[16,2,208,128]{3,2,1,0:T(8,128)(2,1)S(1)}, u32[]{:S(2)}, u32[]{:S(2)}) async-start(bf16[16,2,208,128]{3,2,1,0:T(8,128)(2,1)} %pad_maximum_fusion.3), calls=%async_computation | async-start | bytes 3407872 | tf_op jit(solution)/shard_map/all_to_all | solution.py:212
  51.3 5.8 %collective-permute-start = (bf16[1,528,128]{2,1,0:T(8,128)(2,1)S(1)}, bf16[1,528,128]{2,1,0:T(8,128)(2,1)S(1)}, u32[]{:S(2)}, u32[]{:S(2)}) collective-permute-start(bf16[1,528,128]{2,1,0:T(8,128)(2,1)S(1)} %maximum_maximum_fusion), channel_id=1, source_target_pairs={{16,0},{32,16},{48,32},{64,48},{80,64},{96,80},{112,96},{17,1},{33... | collective-permute-start | bytes 405512 | tf_op jit(solution)/shard_map/ppermute | solution.py:17
  53.4 5.2 %copy-start.3 = (bf16[512,512]{1,0:T(8,128)(2,1)S(1)}, bf16[512,512]{1,0:T(8,128)(2,1)}, u32[]{:S(2)}) copy-start(bf16[512,512]{1,0:T(8,128)(2,1)} %constant.128.clone) | copy-start | bytes 1572868
  57.2 1.9 %copy-start.2 = (bf16[512,512]{1,0:T(8,128)(2,1)S(1)}, bf16[512,512]{1,0:T(8,128)(2,1)}, u32[]{:S(2)}) copy-start(bf16[512,512]{1,0:T(8,128)(2,1)} %constant.127.clone) | copy-start | bytes 1572868
  67.6 1.3 %copy-start.4 = (bf16[512,512]{1,0:T(8,128)(2,1)S(1)}, bf16[512,512]{1,0:T(8,128)(2,1)}, u32[]{:S(2)}) copy-start(bf16[512,512]{1,0:T(8,128)(2,1)} %constant.137) | copy-start | bytes 1572868
  70.7 16.2 %collective-permute-start.4 = (bf16[4,512,128]{2,1,0:T(8,128)(2,1)S(1)}, bf16[4,512,128]{2,1,0:T(8,128)(2,1)S(1)}, u32[]{:S(2)}, u32[]{:S(2)}) collective-permute-start(bf16[4,512,128]{2,1,0:T(8,128)(2,1)S(1)} %get-tuple-element.28), channel_id=1, source_target_pairs={{1,0},{2,1},{3,2},{4,3},{5,4},{6,5},{7,6},{8,7},{9,8},{10,9},{11,1... | collective-permute-start | bytes 1572872 | tf_op jit(solution)/shard_map/ppermute | solution.py:17
  72.7 18.3 %collective-permute-start.3 = (bf16[4,512,128]{2,1,0:T(8,128)(2,1)S(1)}, bf16[4,512,128]{2,1,0:T(8,128)(2,1)S(1)}, u32[]{:S(2)}, u32[]{:S(2)}) collective-permute-start(bf16[4,512,128]{2,1,0:T(8,128)(2,1)S(1)} %get-tuple-element.27), channel_id=1, source_target_pairs={{0,1},{1,2},{2,3},{3,4},{4,5},{5,6},{6,7},{7,8},{8,9},{9,10},{10,1... | collective-permute-start | bytes 1572872 | tf_op jit(solution)/shard_map/ppermute | solution.py:17
  78.2 17.3 %collective-permute-start.2 = (bf16[4,128,512]{2,1,0:T(8,128)(2,1)S(1)}, bf16[4,128,512]{2,1,0:T(8,128)(2,1)S(1)}, u32[]{:S(2)}, u32[]{:S(2)}) collective-permute-start(bf16[4,128,512]{2,1,0:T(8,128)(2,1)S(1)} %get-tuple-element.24), channel_id=1, source_target_pairs={{16,0},{32,16},{48,32},{64,48},{80,64},{96,80},{112,96},{17,1},{33... | collective-permute-start | bytes 1572872 | tf_op jit(solution)/shard_map/ppermute | solution.py:17
  80.1 15.5 %collective-permute-start.1 = (bf16[4,128,512]{2,1,0:T(8,128)(2,1)S(1)}, bf16[4,128,512]{2,1,0:T(8,128)(2,1)S(1)}, u32[]{:S(2)}, u32[]{:S(2)}) collective-permute-start(bf16[4,128,512]{2,1,0:T(8,128)(2,1)S(1)} %get-tuple-element.23), channel_id=1, source_target_pairs={{0,16},{16,32},{32,48},{48,64},{64,80},{80,96},{96,112},{1,17},{17... | collective-permute-start | bytes 1572872 | tf_op jit(solution)/shard_map/ppermute | solution.py:17
  91.1 5.8 %collective-permute-start.6 = (bf16[4,128,256]{2,1,0:T(8,128)(2,1)S(1)}, bf16[4,128,256]{2,1,0:T(8,128)(2,1)S(1)}, u32[]{:S(2)}, u32[]{:S(2)}) collective-permute-start(bf16[4,128,256]{2,1,0:T(8,128)(2,1)S(1)} %pad_maximum_fusion.11), channel_id=1, source_target_pairs={{16,0},{32,16},{48,32},{64,48},{80,64},{96,80},{112,96},{17,1},{33... | collective-permute-start | bytes 786440 | tf_op jit(solution)/shard_map/ppermute | solution.py:17
  93.1 7.7 %collective-permute-start.5 = (bf16[4,128,256]{2,1,0:T(8,128)(2,1)S(1)}, bf16[4,128,256]{2,1,0:T(8,128)(2,1)S(1)}, u32[]{:S(2)}, u32[]{:S(2)}) collective-permute-start(bf16[4,128,256]{2,1,0:T(8,128)(2,1)S(1)} %pad_maximum_fusion.10), channel_id=1, source_target_pairs={{0,16},{16,32},{32,48},{48,64},{64,80},{80,96},{96,112},{1,17},{17... | collective-permute-start | bytes 786440 | tf_op jit(solution)/shard_map/ppermute | solution.py:17
  101.2 3.6 %copy-start.1 = (bf16[2352,128]{1,0:T(8,128)(2,1)S(1)}, bf16[2352,128]{1,0:T(8,128)(2,1)}, u32[]{:S(2)}) copy-start(bf16[2352,128]{1,0:T(8,128)(2,1)} %param.6) | copy-start | bytes 1806340

commit v20 on v19

--- a/solution.py
+++ b/solution.py
@@ -216,8 +216,10 @@
     rise_live = rise_codes > 0
     rise_place = jnp.where(rise_live, jnp.cumsum(rise_live.astype(jnp.int32)), 0)
     packed_values = one_hot_rows(rise_place, rise_total, rise_values).astype(kappa.dtype)
-    packed_picks = rise_place[None, :] == jnp.arange(1, rise_total + 1, dtype=jnp.int32)[:, None]
-    packed_codes = jnp.sum(jnp.where(packed_picks, rise_codes[None, :], 0), axis=1)
+    code_parts = jnp.stack([rise_codes // CODE_SPLIT, rise_codes % CODE_SPLIT], axis=1)
+    packed_parts = one_hot_rows(rise_place, rise_total, code_parts.astype(kappa.dtype))
+    packed_parts = packed_parts.astype(jnp.int32)
+    packed_codes = packed_parts[:, 0] * CODE_SPLIT + packed_parts[:, 1]
     packed = with_codes(packed_values.reshape(1, rise_total, tile_width), packed_codes[None])
     raised_values, raised_codes = split_codes(shifted(packed, "px", -1), rise_total)
     slot_total = PATCH_ROWS * PATCH_COLS // tile_width

time: 105 us -> 106 us (level)
  matrix products: 25.8 us -> 26.9 us
    dot_general x3 -> x4, matrix products: 5.8 us -> 6.91 us  [one_hot_rows(): jnp.dot(picks.astype(values.dtype), values, preferred_element_type=values...]
    another operation x7 -> x9, other arithmetic: 3 us -> 3.1 us
where the time goes in v20:
time: 106 us; the launch traced here: 105 us
  waiting for transfers between devices  37.3 us (35%)
  matrix products  26.9 us (25%)
  starting transfers between devices  24.5 us (23%)
  other arithmetic  12.5 us (12%)
  local copies, waits for them, and re-layouts  3.55 us (3%)
    all_to_all x1, waiting for transfers between devices, on_device(): lax.all_to_all(jnp.stack([same_sent, rise_sent], axis=1), 'py', 0, 0, til...  24 us
    ppermute x7, starting transfers between devices, shifted(): return lax.ppermute(shard, axis, pairs)  16.6 us
    ppermute x7, waiting for transfers between devices, shifted(): return lax.ppermute(shard, axis, pairs)  13.3 us
    dot_general x2, matrix products, gathered_rows(): jnp.dot(chosen.astype(table_rows.dtype), table_rows, preferred_element_ty...  11.2 us
    dot_general x9, matrix products, dot32(): return jnp.dot(a, b, preferred_element_type=jnp.float32)  8.78 us
    all_to_all x1, starting transfers between devices, on_device(): lax.all_to_all(jnp.stack([same_sent, rise_sent], axis=1), 'py', 0, 0, til...  7.89 us
    dot_general x4, matrix products, one_hot_rows(): jnp.dot(picks.astype(values.dtype), values, preferred_element_type=values...  6.91 us
    add x1, other arithmetic, on_device(): return col_weight * rows_done + (1.0 - col_weight) * horizontal  3.54 us
  transfers between devices with their start and end apart: 8, of which 5 were waited for; matrix products, arithmetic and copies ran while one was open for 6% of the time, Pallas kernels for 0%

profile of v20, /device:TPU:40, one launch (start us, length us, event | category | flops | bytes accessed | tf_op | source)
XLA Modules:
  0.0 105.3 jit_solution(2529202553445841576)
XLA Ops:
  0.0 1.3 %constant_dynamic-slice_fusion.3 = (s32[1,16,192]{1,2,0:T(8,128)S(1)}, s32[1,16,192]{1,2,0:T(8,128)S(1)}, s32[1,16,192]{1,2,0:T(8,128)S(1)}, s32[1,16,192]{1,2,0:T(8,128)S(1)}) fusion(s32[1,128,192]{1,2,0:T(8,128)} %param.8, s32[]{:T(128)S(6)} %select_n.163, s32[]{:T(128)S(6)} %select_n.167, s32[1,128,192]{1,2,0:T(8,128)} %param.7), kind=kLoop, calls=%fused_computation.173 | loop fusion | bytes 98312 | tf_op jit(solution)/shard_map/dynamic_slice | solution.py:201
  1.3 0.8 fusion.86
  2.9 5.6 %fusion.18 = bf16[3072,128]{1,0:T(8,128)(2,1)S(1)} fusion(bf16[2352,128]{1,0:T(8,128)(2,1)S(1)} %copy-done, s32[3072]{0:T(1024)S(1)} %eq.45), kind=kOutput, calls=%fused_computation.22 | convolution fusion | flops 1857306624 | bytes 1400832 | tf_op jit(solution)/shard_map/dot_general | solution.py:154
  8.5 5.6 %fusion.17 = bf16[3072,128]{1,0:T(8,128)(2,1)S(1)} fusion(bf16[2352,128]{1,0:T(8,128)(2,1)S(1)} %copy-done, s32[3072]{0:T(1024)S(1)} %eq.91), kind=kOutput, calls=%fused_computation.21 | convolution fusion | flops 1857306624 | bytes 1400832 | tf_op jit(solution)/shard_map/dot_general | solution.py:154
  14.2 0.4 maximum_bitcast_fusion
  14.6 1.3 %pad_maximum_fusion.3 = bf16[16,2,208,128]{3,2,1,0:T(8,128)(2,1)} fusion(bf16[16,1,208,128]{3,2,1,0:T(8,128)(2,1)S(1)} %get-tuple-element.65, bf16[16,1,208,128]{3,2,1,0:T(8,128)(2,1)S(1)} %get-tuple-element.64), kind=kLoop, calls=%fused_computation.38 | loop fusion | flops 851968 | bytes 3407872 | tf_op jit(solution)/shard_map/stack | solution.py:212
  15.9 7.9 %all-to-all-start = ((bf16[16,2,208,128]{3,2,1,0:T(8,128)(2,1)}), bf16[16,2,208,128]{3,2,1,0:T(8,128)(2,1)S(1)}, u32[]{:S(2)}, u32[]{:S(2)}) async-start(bf16[16,2,208,128]{3,2,1,0:T(8,128)(2,1)} %pad_maximum_fusion.3), calls=%async_computation | async-start | bytes 3407872 | tf_op jit(solution)/shard_map/all_to_all | solution.py:212
  24.1 24.0 %all-to-all-done = bf16[16,2,208,128]{3,2,1,0:T(8,128)(2,1)S(1)} async-done(((bf16[16,2,208,128]{3,2,1,0:T(8,128)(2,1)}), bf16[16,2,208,128]{3,2,1,0:T(8,128)(2,1)S(1)}, u32[]{:S(2)}, u32[]{:S(2)}) %all-to-all-start) | async-done | bytes 1703968 | tf_op jit(solution)/shard_map/all_to_all | solution.py:212
  48.8 0.3 reduce-window.9
  49.2 0.1 slice_reduce_fusion
  49.6 1.1 %fusion.33 = s32[512,2]{0,1:T(2,128)S(1)} fusion(s32[3072]{0:T(1024)S(1)} %bitcast_select_fusion.2, s32[512]{0:T(512)S(1)} %iota_add_fusion.1, bf16[3072,1]{0,1:T(2,128)(2,1)S(1)} %fusion.66, bf16[3072,1]{0,1:T(2,128)(2,1)S(1)} %get-tuple-element.8), kind=kOutput, calls=%fused_computation.42 | convolution fusion | flops 7889920 | bytes 30720 | tf_op jit(solution)/shard_map/dot_general | solution.py:149
  50.7 1.0 fusion.30
  51.8 0.1 maximum_maximum_fusion
  51.9 2.1 %collective-permute-start = (bf16[1,528,128]{2,1,0:T(8,128)(2,1)S(1)}, bf16[1,528,128]{2,1,0:T(8,128)(2,1)S(1)}, u32[]{:S(2)}, u32[]{:S(2)}) collective-permute-start(bf16[1,528,128]{2,1,0:T(8,128)(2,1)S(1)} %maximum_maximum_fusion), channel_id=1, source_target_pairs={{16,0},{32,16},{48,32},{64,48},{80,64},{96,80},{112,96},{17,1},{33... | collective-permute-start | bytes 405512 | tf_op jit(solution)/shard_map/ppermute | solution.py:17
  54.0 3.7 %fusion.2 = bf16[2048,128]{1,0:T(8,128)(2,1)S(1)} fusion(bf16[3072,128]{1,0:T(8,128)(2,1)S(1)} %bitcast.89, s32[3072]{0:T(1024)S(1)} %eq.95, s32[2048]{0:T(1024)S(1)} %iota_add_fusion), kind=kOutput, calls=%fused_computation.4 | convolution fusion | flops 1616904192 | bytes 1331200 | tf_op jit(solution)/shard_map/dot_general | solution.py:149
  57.8 1.1 %fusion.23 = bf16[2048,128]{1,0:T(8,128)(2,1)S(1)} fusion(bf16[2048,128]{1,0:T(8,128)(2,1)S(1)} %fusion.2, s32[512]{0:T(512)S(1)} %bitcast.99, s32[2048]{0:T(1024)S(1)} %iota_add_fusion, bf16[1,528,128]{2,1,0:T(8,128)(2,1)S(1)} %collective-permute-done), kind=kOutput, calls=%fused_computation.28 | convolution fusion | flops 269746176 | bytes 1189888 | tf_op jit(solution)/shard_map/dot_general | solution.py:149
  58.8 0.3 reshape.435
  59.2 0.5 convolution_convert_fusion
  59.7 0.5 convolution_convert_fusion.1
  60.2 0.7 fusion.45
  60.9 0.7 fusion.44
  61.7 0.3 multiply_convert_fusion.3
  62.0 1.0 multiply_convert_fusion.2
  63.0 1.3 %fusion.54 = f32[512,2048]{1,0:T(8,128)S(1)} fusion(bf16[512,512]{1,0:T(8,128)(2,1)S(1)} %copy-done.3, bf16[512,512]{1,0:T(8,128)(2,1)S(1)} %get-tuple-element.24, bf16[512,512]{1,0:T(8,128)(2,1)S(1)} %get-tuple-element.25, bf16[512,512]{1,0:T(8,128)(2,1)S(1)} %get-tuple-element.23, bf16[512,512]{1,0:T(8,128)(2,1)S(1)} %get-tuple-element.5), kind=kOutput, calls=%fused_computation.84 | convolution fusion | flops 1082130432 | bytes 6815744 | tf_op jit(solution)/shard_map/dot_general | solution.py:51
  64.2 1.3 %fusion.55 = f32[512,2048]{1,0:T(8,128)S(1)} fusion(bf16[512,512]{1,0:T(8,128)(2,1)S(1)} %copy-done.2, bf16[512,512]{1,0:T(8,128)(2,1)S(1)} %get-tuple-element.24, bf16[512,512]{1,0:T(8,128)(2,1)S(1)} %get-tuple-element.25, bf16[512,512]{1,0:T(8,128)(2,1)S(1)} %get-tuple-element.23, bf16[512,512]{1,0:T(8,128)(2,1)S(1)} %get-tuple-element.5), kind=kOutput, calls=%fused_computation.85 | convolution fusion | flops 1082130432 | bytes 6815744 | tf_op jit(solution)/shard_map/dot_general | solution.py:51
  65.5 1.2 %fusion.27 = (bf16[512,1024]{1,0:T(8,128)(2,1)S(1)}, bf16[512,1024]{1,0:T(8,128)(2,1)S(1)}) fusion(f32[512,2048]{1,0:T(8,128)S(1)} %fusion.54, f32[512,2048]{1,0:T(8,128)S(1)} %fusion.55), kind=kLoop, calls=%fused_computation.32 | loop fusion | flops 2097152 | bytes 10485760 | tf_op jit(solution)/shard_map/convert.20
  66.9 1.3 %fusion.93 = f32[2048,512]{1,0:T(8,128)S(1)} fusion(bf16[512,512]{1,0:T(8,128)(2,1)S(1)} %copy-done.3, bf16[512,512]{1,0:T(8,128)(2,1)S(1)} %get-tuple-element.35, bf16[512,512]{1,0:T(8,128)(2,1)S(1)} %get-tuple-element.34, bf16[512,512]{1,0:T(8,128)(2,1)S(1)} %get-tuple-element.33, bf16[512,512]{1,0:T(8,128)(2,1)S(1)} %get-tuple-element.32), kind=kOutput, calls=%fused_computation.200 | convolution fusion | flops 1082130432 | bytes 6815744 | tf_op jit(solution)/shard_map/dot_general | solution.py:51
  68.2 1.3 %fusion.94 = f32[2048,512]{1,0:T(8,128)S(1)} fusion(bf16[512,512]{1,0:T(8,128)(2,1)S(1)} %copy-done.2, bf16[512,512]{1,0:T(8,128)(2,1)S(1)} %get-tuple-element.35, bf16[512,512]{1,0:T(8,128)(2,1)S(1)} %get-tuple-element.34, bf16[512,512]{1,0:T(8,128)(2,1)S(1)} %get-tuple-element.33, bf16[512,512]{1,0:T(8,128)(2,1)S(1)} %get-tuple-element.32), kind=kOutput, calls=%fused_computation.201 | convolution fusion | flops 1082130432 | bytes 6815744 | tf_op jit(solution)/shard_map/dot_general | solution.py:51
  69.5 1.2 %fusion.92 = f32[2048,512]{1,0:T(8,128)S(1)} fusion(bf16[512,512]{1,0:T(8,128)(2,1)S(1)} %copy-done.4, bf16[512,512]{1,0:T(8,128)(2,1)S(1)} %get-tuple-element.35, bf16[512,512]{1,0:T(8,128)(2,1)S(1)} %get-tuple-element.34, bf16[512,512]{1,0:T(8,128)(2,1)S(1)} %get-tuple-element.33, bf16[512,512]{1,0:T(8,128)(2,1)S(1)} %get-tuple-element.32), kind=kOutput, calls=%fused_computation.199 | convolution fusion | flops 1082130432 | bytes 6815744 | tf_op jit(solution)/shard_map/dot_general | solution.py:51
  70.7 0.3 fusion.56
  71.0 0.1 pad_maximum_fusion.5
  71.1 0.2 fusion.98
  71.3 2.0 %collective-permute-start.4 = (bf16[4,512,128]{2,1,0:T(8,128)(2,1)S(1)}, bf16[4,512,128]{2,1,0:T(8,128)(2,1)S(1)}, u32[]{:S(2)}, u32[]{:S(2)}) collective-permute-start(bf16[4,512,128]{2,1,0:T(8,128)(2,1)S(1)} %get-tuple-element.31), channel_id=1, source_target_pairs={{1,0},{2,1},{3,2},{4,3},{5,4},{6,5},{7,6},{8,7},{9,8},{10,9},{11,1... | collective-permute-start | bytes 1572872 | tf_op jit(solution)/shard_map/ppermute | solution.py:17
  73.3 3.8 %collective-permute-start.3 = (bf16[4,512,128]{2,1,0:T(8,128)(2,1)S(1)}, bf16[4,512,128]{2,1,0:T(8,128)(2,1)S(1)}, u32[]{:S(2)}, u32[]{:S(2)}) collective-permute-start(bf16[4,512,128]{2,1,0:T(8,128)(2,1)S(1)} %get-tuple-element.30), channel_id=1, source_target_pairs={{0,1},{1,2},{2,3},{3,4},{4,5},{5,6},{6,7},{7,8},{8,9},{9,10},{10,1... | collective-permute-start | bytes 1572872 | tf_op jit(solution)/shard_map/ppermute | solution.py:17
  77.2 1.2 %fusion.46 = (bf16[1,512,512]{2,1,0:T(8,128)(2,1)S(1)}, bf16[1,512,512]{2,1,0:T(8,128)(2,1)S(1)}, bf16[1,512,512]{2,1,0:T(8,128)(2,1)S(1)}, bf16[1,512,512]{2,1,0:T(8,128)(2,1)S(1)}) fusion(f32[2048,512]{1,0:T(8,128)S(1)} %fusion.93, f32[2048,512]{1,0:T(8,128)S(1)} %fusion.94), kind=kLoop, calls=%fused_computation.72 | loop fusion | flops 2097152 | bytes 10485760 | tf_op jit(solution)/shard_map/stack | solution.py:112
  78.4 0.3 pad_maximum_fusion.2
  78.8 1.9 %collective-permute-start.2 = (bf16[4,128,512]{2,1,0:T(8,128)(2,1)S(1)}, bf16[4,128,512]{2,1,0:T(8,128)(2,1)S(1)}, u32[]{:S(2)}, u32[]{:S(2)}) collective-permute-start(bf16[4,128,512]{2,1,0:T(8,128)(2,1)S(1)} %get-tuple-element.27), channel_id=1, source_target_pairs={{16,0},{32,16},{48,32},{64,48},{80,64},{96,80},{112,96},{17,1},{33... | collective-permute-start | bytes 1572872 | tf_op jit(solution)/shard_map/ppermute | solution.py:17
  80.7 2.4 %collective-permute-start.1 = (bf16[4,128,512]{2,1,0:T(8,128)(2,1)S(1)}, bf16[4,128,512]{2,1,0:T(8,128)(2,1)S(1)}, u32[]{:S(2)}, u32[]{:S(2)}) collective-permute-start(bf16[4,128,512]{2,1,0:T(8,128)(2,1)S(1)} %get-tuple-element.26), channel_id=1, source_target_pairs={{0,16},{16,32},{32,48},{48,64},{64,80},{80,96},{96,112},{1,17},{17... | collective-permute-start | bytes 1572872 | tf_op jit(solution)/shard_map/ppermute | solution.py:17
  83.1 4.4 %collective-permute-done.4 = bf16[4,512,128]{2,1,0:T(8,128)(2,1)S(1)} collective-permute-done((bf16[4,512,128]{2,1,0:T(8,128)(2,1)S(1)}, bf16[4,512,128]{2,1,0:T(8,128)(2,1)S(1)}, u32[]{:S(2)}, u32[]{:S(2)}) %collective-permute-start.4) | collective-permute-done | bytes 524320 | tf_op jit(solution)/shard_map/ppermute | solution.py:17
  87.5 4.0 %collective-permute-done.3 = bf16[4,512,128]{2,1,0:T(8,128)(2,1)S(1)} collective-permute-done((bf16[4,512,128]{2,1,0:T(8,128)(2,1)S(1)}, bf16[4,512,128]{2,1,0:T(8,128)(2,1)S(1)}, u32[]{:S(2)}, u32[]{:S(2)}) %collective-permute-start.3) | collective-permute-done | bytes 524320 | tf_op jit(solution)/shard_map/ppermute | solution.py:17
  91.6 1.9 %collective-permute-start.6 = (bf16[4,128,256]{2,1,0:T(8,128)(2,1)S(1)}, bf16[4,128,256]{2,1,0:T(8,128)(2,1)S(1)}, u32[]{:S(2)}, u32[]{:S(2)}) collective-permute-start(bf16[4,128,256]{2,1,0:T(8,128)(2,1)S(1)} %pad_maximum_fusion.11), channel_id=1, source_target_pairs={{16,0},{32,16},{48,32},{64,48},{80,64},{96,80},{112,96},{17,1},{33... | collective-permute-start | bytes 786440 | tf_op jit(solution)/shard_map/ppermute | solution.py:17
  93.6 2.4 %collective-permute-start.5 = (bf16[4,128,256]{2,1,0:T(8,128)(2,1)S(1)}, bf16[4,128,256]{2,1,0:T(8,128)(2,1)S(1)}, u32[]{:S(2)}, u32[]{:S(2)}) collective-permute-start(bf16[4,128,256]{2,1,0:T(8,128)(2,1)S(1)} %pad_maximum_fusion.10), channel_id=1, source_target_pairs={{0,16},{16,32},{32,48},{48,64},{64,80},{80,96},{96,112},{1,17},{17... | collective-permute-start | bytes 786440 | tf_op jit(solution)/shard_map/ppermute | solution.py:17
  96.1 0.1 convert_element_type.163
  96.2 0.1 convert_element_type.162
  96.4 1.1 %collective-permute-done.6 = bf16[4,128,256]{2,1,0:T(8,128)(2,1)S(1)} collective-permute-done((bf16[4,128,256]{2,1,0:T(8,128)(2,1)S(1)}, bf16[4,128,256]{2,1,0:T(8,128)(2,1)S(1)}, u32[]{:S(2)}, u32[]{:S(2)}) %collective-permute-start.6) | collective-permute-done | bytes 262176 | tf_op jit(solution)/shard_map/ppermute | solution.py:17
  97.5 3.8 %collective-permute-done.5 = bf16[4,128,256]{2,1,0:T(8,128)(2,1)S(1)} collective-permute-done((bf16[4,128,256]{2,1,0:T(8,128)(2,1)S(1)}, bf16[4,128,256]{2,1,0:T(8,128)(2,1)S(1)}, u32[]{:S(2)}, u32[]{:S(2)}) %collective-permute-start.5) | collective-permute-done | bytes 262176 | tf_op jit(solution)/shard_map/ppermute | solution.py:17
  101.4 0.4 fusion.41
  101.8 3.5 %fusion.14 = f32[4,512,512]{2,1,0:T(8,128)} fusion(f32[4,128,512]{2,1,0:T(8,128)S(1)} %convert_element_type.163, f32[4,128,512]{2,1,0:T(8,128)S(1)} %convert_element_type.162, f32[4,512,128]{2,1,0:T(8,128)S(1)} %get-tuple-element.53, f32[4,512,128]{2,1,0:T(8,128)S(1)} %get-tuple-element.52, f32[512]{0:T(512)S(1)} %pad.18.clone, ...), kind=kLoop, calls=%fused_computation.17 | loop fusion | flops 14680064 | bytes 10496000 | tf_op jit(solution)/shard_map/add | solution.py:271
  (73 shorter events, 2.7 us)
Async XLA Ops:
  0.0 2.9 %copy-start = (bf16[2352,128]{1,0:T(8,128)(2,1)S(1)}, bf16[2352,128]{1,0:T(8,128)(2,1)}, u32[]{:S(2)}) copy-start(bf16[2352,128]{1,0:T(8,128)(2,1)} %param.6) | copy-start | bytes 1806340
  15.9 32.1 %all-to-all-start = ((bf16[16,2,208,128]{3,2,1,0:T(8,128)(2,1)}), bf16[16,2,208,128]{3,2,1,0:T(8,128)(2,1)S(1)}, u32[]{:S(2)}, u32[]{:S(2)}) async-start(bf16[16,2,208,128]{3,2,1,0:T(8,128)(2,1)} %pad_maximum_fusion.3), calls=%async_computation | async-start | bytes 3407872 | tf_op jit(solution)/shard_map/all_to_all | solution.py:212
  51.9 5.8 %collective-permute-start = (bf16[1,528,128]{2,1,0:T(8,128)(2,1)S(1)}, bf16[1,528,128]{2,1,0:T(8,128)(2,1)S(1)}, u32[]{:S(2)}, u32[]{:S(2)}) collective-permute-start(bf16[1,528,128]{2,1,0:T(8,128)(2,1)S(1)} %maximum_maximum_fusion), channel_id=1, source_target_pairs={{16,0},{32,16},{48,32},{64,48},{80,64},{96,80},{112,96},{17,1},{33... | collective-permute-start | bytes 405512 | tf_op jit(solution)/shard_map/ppermute | solution.py:17
  54.0 5.2 %copy-start.3 = (bf16[512,512]{1,0:T(8,128)(2,1)S(1)}, bf16[512,512]{1,0:T(8,128)(2,1)}, u32[]{:S(2)}) copy-start(bf16[512,512]{1,0:T(8,128)(2,1)} %constant.146.clone) | copy-start | bytes 1572868
  57.7 1.9 %copy-start.2 = (bf16[512,512]{1,0:T(8,128)(2,1)S(1)}, bf16[512,512]{1,0:T(8,128)(2,1)}, u32[]{:S(2)}) copy-start(bf16[512,512]{1,0:T(8,128)(2,1)} %constant.145.clone) | copy-start | bytes 1572868
  68.1 1.3 %copy-start.4 = (bf16[512,512]{1,0:T(8,128)(2,1)S(1)}, bf16[512,512]{1,0:T(8,128)(2,1)}, u32[]{:S(2)}) copy-start(bf16[512,512]{1,0:T(8,128)(2,1)} %constant.155) | copy-start | bytes 1572868
  71.3 16.2 %collective-permute-start.4 = (bf16[4,512,128]{2,1,0:T(8,128)(2,1)S(1)}, bf16[4,512,128]{2,1,0:T(8,128)(2,1)S(1)}, u32[]{:S(2)}, u32[]{:S(2)}) collective-permute-start(bf16[4,512,128]{2,1,0:T(8,128)(2,1)S(1)} %get-tuple-element.31), channel_id=1, source_target_pairs={{1,0},{2,1},{3,2},{4,3},{5,4},{6,5},{7,6},{8,7},{9,8},{10,9},{11,1... | collective-permute-start | bytes 1572872 | tf_op jit(solution)/shard_map/ppermute | solution.py:17
  73.3 18.3 %collective-permute-start.3 = (bf16[4,512,128]{2,1,0:T(8,128)(2,1)S(1)}, bf16[4,512,128]{2,1,0:T(8,128)(2,1)S(1)}, u32[]{:S(2)}, u32[]{:S(2)}) collective-permute-start(bf16[4,512,128]{2,1,0:T(8,128)(2,1)S(1)} %get-tuple-element.30), channel_id=1, source_target_pairs={{0,1},{1,2},{2,3},{3,4},{4,5},{5,6},{6,7},{7,8},{8,9},{9,10},{10,1... | collective-permute-start | bytes 1572872 | tf_op jit(solution)/shard_map/ppermute | solution.py:17
  78.8 17.3 %collective-permute-start.2 = (bf16[4,128,512]{2,1,0:T(8,128)(2,1)S(1)}, bf16[4,128,512]{2,1,0:T(8,128)(2,1)S(1)}, u32[]{:S(2)}, u32[]{:S(2)}) collective-permute-start(bf16[4,128,512]{2,1,0:T(8,128)(2,1)S(1)} %get-tuple-element.27), channel_id=1, source_target_pairs={{16,0},{32,16},{48,32},{64,48},{80,64},{96,80},{112,96},{17,1},{33... | collective-permute-start | bytes 1572872 | tf_op jit(solution)/shard_map/ppermute | solution.py:17
  80.7 15.5 %collective-permute-start.1 = (bf16[4,128,512]{2,1,0:T(8,128)(2,1)S(1)}, bf16[4,128,512]{2,1,0:T(8,128)(2,1)S(1)}, u32[]{:S(2)}, u32[]{:S(2)}) collective-permute-start(bf16[4,128,512]{2,1,0:T(8,128)(2,1)S(1)} %get-tuple-element.26), channel_id=1, source_target_pairs={{0,16},{16,32},{32,48},{48,64},{64,80},{80,96},{96,112},{1,17},{17... | collective-permute-start | bytes 1572872 | tf_op jit(solution)/shard_map/ppermute | solution.py:17
  91.6 5.8 %collective-permute-start.6 = (bf16[4,128,256]{2,1,0:T(8,128)(2,1)S(1)}, bf16[4,128,256]{2,1,0:T(8,128)(2,1)S(1)}, u32[]{:S(2)}, u32[]{:S(2)}) collective-permute-start(bf16[4,128,256]{2,1,0:T(8,128)(2,1)S(1)} %pad_maximum_fusion.11), channel_id=1, source_target_pairs={{16,0},{32,16},{48,32},{64,48},{80,64},{96,80},{112,96},{17,1},{33... | collective-permute-start | bytes 786440 | tf_op jit(solution)/shard_map/ppermute | solution.py:17
  93.6 7.7 %collective-permute-start.5 = (bf16[4,128,256]{2,1,0:T(8,128)(2,1)S(1)}, bf16[4,128,256]{2,1,0:T(8,128)(2,1)S(1)}, u32[]{:S(2)}, u32[]{:S(2)}) collective-permute-start(bf16[4,128,256]{2,1,0:T(8,128)(2,1)S(1)} %pad_maximum_fusion.10), channel_id=1, source_target_pairs={{0,16},{16,32},{32,48},{48,64},{64,80},{80,96},{96,112},{1,17},{17... | collective-permute-start | bytes 786440 | tf_op jit(solution)/shard_map/ppermute | solution.py:17
  101.8 3.6 %copy-start.1 = (bf16[2352,128]{1,0:T(8,128)(2,1)S(1)}, bf16[2352,128]{1,0:T(8,128)(2,1)}, u32[]{:S(2)}) copy-start(bf16[2352,128]{1,0:T(8,128)(2,1)} %param.6) | copy-start | bytes 1806340

commit v21 on v19

--- a/solution.py
+++ b/solution.py
@@ -58,9 +58,8 @@
     cos_np, sin_np = dft_tables(row_count)
     cosine, sine = table(cos_np), table(sin_np)
     n = row_count
-    halves = jnp.concatenate([dot32(pixels, cosine), dot32(pixels, sine)], axis=1).astype(
-        jnp.bfloat16
-    )
+    halves = jnp.dot(pixels, jnp.concatenate([cosine, sine], axis=1), preferred_element_type=jnp.float32)
+    halves = halves.astype(jnp.bfloat16)
     by_cos = dot32(cosine, halves)
     by_sin = dot32(sine, halves)
     real_part = by_cos[:, :n] - by_sin[:, n:]

time: 105 us -> 105 us (level)
    dot_general x9 -> x7, matrix products: 8.77 us -> 7.74 us  [dot32(): return jnp.dot(a, b, preferred_element_type=jnp.float32)]
where the time goes in v21:
time: 105 us; the launch traced here: 104 us
  waiting for transfers between devices  37.3 us (36%)
  matrix products  25.4 us (24%)
  starting transfers between devices  24.5 us (23%)
  other arithmetic  13.2 us (13%)
  local copies, waits for them, and re-layouts  3.45 us (3%)
    all_to_all x1, waiting for transfers between devices, on_device(): lax.all_to_all(jnp.stack([same_sent, rise_sent], axis=1), 'py', 0, 0, til...  24 us
    ppermute x7, starting transfers between devices, shifted(): return lax.ppermute(shard, axis, pairs)  16.6 us
    ppermute x7, waiting for transfers between devices, shifted(): return lax.ppermute(shard, axis, pairs)  13.4 us
    dot_general x2, matrix products, gathered_rows(): jnp.dot(chosen.astype(table_rows.dtype), table_rows, preferred_element_ty...  11.2 us
    all_to_all x1, starting transfers between devices, on_device(): lax.all_to_all(jnp.stack([same_sent, rise_sent], axis=1), 'py', 0, 0, til...  7.89 us
    dot_general x7, matrix products, dot32(): return jnp.dot(a, b, preferred_element_type=jnp.float32)  7.74 us
    dot_general x3, matrix products, one_hot_rows(): jnp.dot(picks.astype(values.dtype), values, preferred_element_type=values...  5.8 us
    add x1, other arithmetic, on_device(): return col_weight * rows_done + (1.0 - col_weight) * horizontal  3.54 us
  transfers between devices with their start and end apart: 8, of which 5 were waited for; matrix products, arithmetic and copies ran while one was open for 6% of the time, Pallas kernels for 0%

profile of v21, /device:TPU:40, one launch (start us, length us, event | category | flops | bytes accessed | tf_op | source)
XLA Modules:
  0.0 104.4 jit_solution(3024380695209489862)
XLA Ops:
  0.0 1.3 %constant_dynamic-slice_fusion.3 = (s32[1,16,192]{1,2,0:T(8,128)S(1)}, s32[1,16,192]{1,2,0:T(8,128)S(1)}, s32[1,16,192]{1,2,0:T(8,128)S(1)}, s32[1,16,192]{1,2,0:T(8,128)S(1)}) fusion(s32[1,128,192]{1,2,0:T(8,128)} %param.8, s32[]{:T(128)S(6)} %select_n.142, s32[]{:T(128)S(6)} %select_n.146, s32[1,128,192]{1,2,0:T(8,128)} %param.7), kind=kLoop, calls=%fused_computation.156 | loop fusion | bytes 98312 | tf_op jit(solution)/shard_map/dynamic_slice | solution.py:200
  1.3 0.8 fusion.74
  2.9 5.6 %fusion.17 = bf16[3072,128]{1,0:T(8,128)(2,1)S(1)} fusion(bf16[2352,128]{1,0:T(8,128)(2,1)S(1)} %copy-done, s32[3072]{0:T(1024)S(1)} %eq.43), kind=kOutput, calls=%fused_computation.22 | convolution fusion | flops 1857306624 | bytes 1400832 | tf_op jit(solution)/shard_map/dot_general | solution.py:153
  8.5 5.6 %fusion.16 = bf16[3072,128]{1,0:T(8,128)(2,1)S(1)} fusion(bf16[2352,128]{1,0:T(8,128)(2,1)S(1)} %copy-done, s32[3072]{0:T(1024)S(1)} %eq.89), kind=kOutput, calls=%fused_computation.21 | convolution fusion | flops 1857306624 | bytes 1400832 | tf_op jit(solution)/shard_map/dot_general | solution.py:153
  14.2 0.4 maximum_bitcast_fusion
  14.6 1.3 %pad_maximum_fusion.3 = bf16[16,2,208,128]{3,2,1,0:T(8,128)(2,1)} fusion(bf16[16,1,208,128]{3,2,1,0:T(8,128)(2,1)S(1)} %get-tuple-element.62, bf16[16,1,208,128]{3,2,1,0:T(8,128)(2,1)S(1)} %get-tuple-element.61), kind=kLoop, calls=%fused_computation.36 | loop fusion | flops 851968 | bytes 3407872 | tf_op jit(solution)/shard_map/stack | solution.py:211
  15.9 7.9 %all-to-all-start = ((bf16[16,2,208,128]{3,2,1,0:T(8,128)(2,1)}), bf16[16,2,208,128]{3,2,1,0:T(8,128)(2,1)S(1)}, u32[]{:S(2)}, u32[]{:S(2)}) async-start(bf16[16,2,208,128]{3,2,1,0:T(8,128)(2,1)} %pad_maximum_fusion.3), calls=%async_computation | async-start | bytes 3407872 | tf_op jit(solution)/shard_map/all_to_all | solution.py:211
  24.1 24.0 %all-to-all-done = bf16[16,2,208,128]{3,2,1,0:T(8,128)(2,1)S(1)} async-done(((bf16[16,2,208,128]{3,2,1,0:T(8,128)(2,1)}), bf16[16,2,208,128]{3,2,1,0:T(8,128)(2,1)S(1)}, u32[]{:S(2)}, u32[]{:S(2)}) %all-to-all-start) | async-done | bytes 1703968 | tf_op jit(solution)/shard_map/all_to_all | solution.py:211
  48.0 0.1 slice_bitcast_fusion
  48.8 0.3 reduce-window.9
  49.2 0.1 slice_reduce_fusion
  49.4 0.8 fusion.10
  50.1 1.0 fusion.27
  51.2 0.1 maximum_maximum_fusion
  51.3 2.1 %collective-permute-start = (bf16[1,528,128]{2,1,0:T(8,128)(2,1)S(1)}, bf16[1,528,128]{2,1,0:T(8,128)(2,1)S(1)}, u32[]{:S(2)}, u32[]{:S(2)}) collective-permute-start(bf16[1,528,128]{2,1,0:T(8,128)(2,1)S(1)} %maximum_maximum_fusion), channel_id=1, source_target_pairs={{16,0},{32,16},{48,32},{64,48},{80,64},{96,80},{112,96},{17,1},{33... | collective-permute-start | bytes 405512 | tf_op jit(solution)/shard_map/ppermute | solution.py:17
  53.4 3.7 %fusion.2 = bf16[2048,128]{1,0:T(8,128)(2,1)S(1)} fusion(bf16[3072,128]{1,0:T(8,128)(2,1)S(1)} %bitcast.112, s32[3072]{0:T(1024)S(1)} %eq.93, s32[2048]{0:T(1024)S(1)} %iota_add_fusion), kind=kOutput, calls=%fused_computation.4 | convolution fusion | flops 1616904192 | bytes 1331200 | tf_op jit(solution)/shard_map/dot_general | solution.py:148
  57.2 1.1 %fusion.20 = bf16[2048,128]{1,0:T(8,128)(2,1)S(1)} fusion(bf16[2048,128]{1,0:T(8,128)(2,1)S(1)} %fusion.2, s32[512]{0:T(512)S(1)} %bitcast.121, s32[2048]{0:T(1024)S(1)} %iota_add_fusion, bf16[1,528,128]{2,1,0:T(8,128)(2,1)S(1)} %collective-permute-done), kind=kOutput, calls=%fused_computation.26 | convolution fusion | flops 269746176 | bytes 1189888 | tf_op jit(solution)/shard_map/dot_general | solution.py:148
  58.3 0.3 reshape.309
  58.6 0.7 convolution_convert_fusion
  59.4 0.7 fusion.87
  60.1 0.7 fusion.88
  60.8 0.3 multiply_convert_fusion.3
  61.1 1.0 multiply_convert_fusion.2
  62.1 1.3 %fusion.46 = f32[512,2048]{1,0:T(8,128)S(1)} fusion(bf16[512,512]{1,0:T(8,128)(2,1)S(1)} %copy-done.3, bf16[512,512]{1,0:T(8,128)(2,1)S(1)} %get-tuple-element.21, bf16[512,512]{1,0:T(8,128)(2,1)S(1)} %get-tuple-element.22, bf16[512,512]{1,0:T(8,128)(2,1)S(1)} %get-tuple-element.20, bf16[512,512]{1,0:T(8,128)(2,1)S(1)} %get-tuple-element.5), kind=kOutput, calls=%fused_computation.77 | convolution fusion | flops 1082130432 | bytes 6815744 | tf_op jit(solution)/shard_map/dot_general | solution.py:51
  63.3 1.3 %fusion.47 = f32[512,2048]{1,0:T(8,128)S(1)} fusion(bf16[512,512]{1,0:T(8,128)(2,1)S(1)} %copy-done.2, bf16[512,512]{1,0:T(8,128)(2,1)S(1)} %get-tuple-element.21, bf16[512,512]{1,0:T(8,128)(2,1)S(1)} %get-tuple-element.22, bf16[512,512]{1,0:T(8,128)(2,1)S(1)} %get-tuple-element.20, bf16[512,512]{1,0:T(8,128)(2,1)S(1)} %get-tuple-element.5), kind=kOutput, calls=%fused_computation.78 | convolution fusion | flops 1082130432 | bytes 6815744 | tf_op jit(solution)/shard_map/dot_general | solution.py:51
  64.6 1.2 %fusion.24 = (bf16[512,1024]{1,0:T(8,128)(2,1)S(1)}, bf16[512,1024]{1,0:T(8,128)(2,1)S(1)}) fusion(f32[512,2048]{1,0:T(8,128)S(1)} %fusion.46, f32[512,2048]{1,0:T(8,128)S(1)} %fusion.47), kind=kLoop, calls=%fused_computation.30 | loop fusion | flops 2097152 | bytes 10485760 | tf_op jit(solution)/shard_map/convert.20
  66.0 1.3 %fusion.78 = f32[2048,512]{1,0:T(8,128)S(1)} fusion(bf16[512,512]{1,0:T(8,128)(2,1)S(1)} %copy-done.3, bf16[512,512]{1,0:T(8,128)(2,1)S(1)} %get-tuple-element.32, bf16[512,512]{1,0:T(8,128)(2,1)S(1)} %get-tuple-element.31, bf16[512,512]{1,0:T(8,128)(2,1)S(1)} %get-tuple-element.30, bf16[512,512]{1,0:T(8,128)(2,1)S(1)} %get-tuple-element.29), kind=kOutput, calls=%fused_computation.180 | convolution fusion | flops 1082130432 | bytes 6815744 | tf_op jit(solution)/shard_map/dot_general | solution.py:51
  67.3 1.3 %fusion.79 = f32[2048,512]{1,0:T(8,128)S(1)} fusion(bf16[512,512]{1,0:T(8,128)(2,1)S(1)} %copy-done.2, bf16[512,512]{1,0:T(8,128)(2,1)S(1)} %get-tuple-element.32, bf16[512,512]{1,0:T(8,128)(2,1)S(1)} %get-tuple-element.31, bf16[512,512]{1,0:T(8,128)(2,1)S(1)} %get-tuple-element.30, bf16[512,512]{1,0:T(8,128)(2,1)S(1)} %get-tuple-element.29), kind=kOutput, calls=%fused_computation.181 | convolution fusion | flops 1082130432 | bytes 6815744 | tf_op jit(solution)/shard_map/dot_general | solution.py:51
  68.6 1.2 %fusion.77 = f32[2048,512]{1,0:T(8,128)S(1)} fusion(bf16[512,512]{1,0:T(8,128)(2,1)S(1)} %copy-done.5, bf16[512,512]{1,0:T(8,128)(2,1)S(1)} %get-tuple-element.32, bf16[512,512]{1,0:T(8,128)(2,1)S(1)} %get-tuple-element.31, bf16[512,512]{1,0:T(8,128)(2,1)S(1)} %get-tuple-element.30, bf16[512,512]{1,0:T(8,128)(2,1)S(1)} %get-tuple-element.29), kind=kOutput, calls=%fused_computation.179 | convolution fusion | flops 1082130432 | bytes 6815744 | tf_op jit(solution)/shard_map/dot_general | solution.py:51
  69.8 0.3 fusion.48
  70.1 0.1 pad_maximum_fusion.4
  70.2 0.2 fusion.82
  70.4 2.0 %collective-permute-start.4 = (bf16[4,512,128]{2,1,0:T(8,128)(2,1)S(1)}, bf16[4,512,128]{2,1,0:T(8,128)(2,1)S(1)}, u32[]{:S(2)}, u32[]{:S(2)}) collective-permute-start(bf16[4,512,128]{2,1,0:T(8,128)(2,1)S(1)} %get-tuple-element.28), channel_id=1, source_target_pairs={{1,0},{2,1},{3,2},{4,3},{5,4},{6,5},{7,6},{8,7},{9,8},{10,9},{11,1... | collective-permute-start | bytes 1572872 | tf_op jit(solution)/shard_map/ppermute | solution.py:17
  72.4 3.8 %collective-permute-start.3 = (bf16[4,512,128]{2,1,0:T(8,128)(2,1)S(1)}, bf16[4,512,128]{2,1,0:T(8,128)(2,1)S(1)}, u32[]{:S(2)}, u32[]{:S(2)}) collective-permute-start(bf16[4,512,128]{2,1,0:T(8,128)(2,1)S(1)} %get-tuple-element.27), channel_id=1, source_target_pairs={{0,1},{1,2},{2,3},{3,4},{4,5},{5,6},{6,7},{7,8},{8,9},{9,10},{10,1... | collective-permute-start | bytes 1572872 | tf_op jit(solution)/shard_map/ppermute | solution.py:17
  76.3 1.2 %fusion.38 = (bf16[1,512,512]{2,1,0:T(8,128)(2,1)S(1)}, bf16[1,512,512]{2,1,0:T(8,128)(2,1)S(1)}, bf16[1,512,512]{2,1,0:T(8,128)(2,1)S(1)}, bf16[1,512,512]{2,1,0:T(8,128)(2,1)S(1)}) fusion(f32[2048,512]{1,0:T(8,128)S(1)} %fusion.78, f32[2048,512]{1,0:T(8,128)S(1)} %fusion.79), kind=kLoop, calls=%fused_computation.65 | loop fusion | flops 2097152 | bytes 10485760 | tf_op jit(solution)/shard_map/stack | solution.py:111
  77.5 0.3 pad_maximum_fusion.2
  77.9 1.9 %collective-permute-start.2 = (bf16[4,128,512]{2,1,0:T(8,128)(2,1)S(1)}, bf16[4,128,512]{2,1,0:T(8,128)(2,1)S(1)}, u32[]{:S(2)}, u32[]{:S(2)}) collective-permute-start(bf16[4,128,512]{2,1,0:T(8,128)(2,1)S(1)} %get-tuple-element.24), channel_id=1, source_target_pairs={{16,0},{32,16},{48,32},{64,48},{80,64},{96,80},{112,96},{17,1},{33... | collective-permute-start | bytes 1572872 | tf_op jit(solution)/shard_map/ppermute | solution.py:17
  79.8 2.4 %collective-permute-start.1 = (bf16[4,128,512]{2,1,0:T(8,128)(2,1)S(1)}, bf16[4,128,512]{2,1,0:T(8,128)(2,1)S(1)}, u32[]{:S(2)}, u32[]{:S(2)}) collective-permute-start(bf16[4,128,512]{2,1,0:T(8,128)(2,1)S(1)} %get-tuple-element.23), channel_id=1, source_target_pairs={{0,16},{16,32},{32,48},{48,64},{64,80},{80,96},{96,112},{1,17},{17... | collective-permute-start | bytes 1572872 | tf_op jit(solution)/shard_map/ppermute | solution.py:17
  82.2 4.4 %collective-permute-done.4 = bf16[4,512,128]{2,1,0:T(8,128)(2,1)S(1)} collective-permute-done((bf16[4,512,128]{2,1,0:T(8,128)(2,1)S(1)}, bf16[4,512,128]{2,1,0:T(8,128)(2,1)S(1)}, u32[]{:S(2)}, u32[]{:S(2)}) %collective-permute-start.4) | collective-permute-done | bytes 524320 | tf_op jit(solution)/shard_map/ppermute | solution.py:17
  86.7 4.0 %collective-permute-done.3 = bf16[4,512,128]{2,1,0:T(8,128)(2,1)S(1)} collective-permute-done((bf16[4,512,128]{2,1,0:T(8,128)(2,1)S(1)}, bf16[4,512,128]{2,1,0:T(8,128)(2,1)S(1)}, u32[]{:S(2)}, u32[]{:S(2)}) %collective-permute-start.3) | collective-permute-done | bytes 524320 | tf_op jit(solution)/shard_map/ppermute | solution.py:17
  90.8 1.9 %collective-permute-start.6 = (bf16[4,128,256]{2,1,0:T(8,128)(2,1)S(1)}, bf16[4,128,256]{2,1,0:T(8,128)(2,1)S(1)}, u32[]{:S(2)}, u32[]{:S(2)}) collective-permute-start(bf16[4,128,256]{2,1,0:T(8,128)(2,1)S(1)} %pad_maximum_fusion.8), channel_id=1, source_target_pairs={{16,0},{32,16},{48,32},{64,48},{80,64},{96,80},{112,96},{17,1},{33... | collective-permute-start | bytes 786440 | tf_op jit(solution)/shard_map/ppermute | solution.py:17
  92.8 2.4 %collective-permute-start.5 = (bf16[4,128,256]{2,1,0:T(8,128)(2,1)S(1)}, bf16[4,128,256]{2,1,0:T(8,128)(2,1)S(1)}, u32[]{:S(2)}, u32[]{:S(2)}) collective-permute-start(bf16[4,128,256]{2,1,0:T(8,128)(2,1)S(1)} %pad_maximum_fusion.7), channel_id=1, source_target_pairs={{0,16},{16,32},{32,48},{48,64},{64,80},{80,96},{96,112},{1,17},{17... | collective-permute-start | bytes 786440 | tf_op jit(solution)/shard_map/ppermute | solution.py:17
  95.2 0.1 convert_element_type.160
  95.4 0.1 convert_element_type.159
  95.5 1.1 %collective-permute-done.6 = bf16[4,128,256]{2,1,0:T(8,128)(2,1)S(1)} collective-permute-done((bf16[4,128,256]{2,1,0:T(8,128)(2,1)S(1)}, bf16[4,128,256]{2,1,0:T(8,128)(2,1)S(1)}, u32[]{:S(2)}, u32[]{:S(2)}) %collective-permute-start.6) | collective-permute-done | bytes 262176 | tf_op jit(solution)/shard_map/ppermute | solution.py:17
  96.6 3.8 %collective-permute-done.5 = bf16[4,128,256]{2,1,0:T(8,128)(2,1)S(1)} collective-permute-done((bf16[4,128,256]{2,1,0:T(8,128)(2,1)S(1)}, bf16[4,128,256]{2,1,0:T(8,128)(2,1)S(1)}, u32[]{:S(2)}, u32[]{:S(2)}) %collective-permute-start.5) | collective-permute-done | bytes 262176 | tf_op jit(solution)/shard_map/ppermute | solution.py:17
  100.5 0.4 fusion.35
  100.9 3.5 %fusion.13 = f32[4,512,512]{2,1,0:T(8,128)} fusion(f32[4,128,512]{2,1,0:T(8,128)S(1)} %convert_element_type.160, f32[4,128,512]{2,1,0:T(8,128)S(1)} %convert_element_type.159, f32[4,512,128]{2,1,0:T(8,128)S(1)} %get-tuple-element.50, f32[4,512,128]{2,1,0:T(8,128)S(1)} %get-tuple-element.49, f32[512]{0:T(512)S(1)} %pad.18.clone, ...), kind=kLoop, calls=%fused_computation.17 | loop fusion | flops 14680064 | bytes 10496000 | tf_op jit(solution)/shard_map/add | solution.py:268
  (70 shorter events, 2.3 us)
Async XLA Ops:
  0.0 2.9 %copy-start = (bf16[2352,128]{1,0:T(8,128)(2,1)S(1)}, bf16[2352,128]{1,0:T(8,128)(2,1)}, u32[]{:S(2)}) copy-start(bf16[2352,128]{1,0:T(8,128)(2,1)} %param.6) | copy-start | bytes 1806340
  15.9 32.1 %all-to-all-start = ((bf16[16,2,208,128]{3,2,1,0:T(8,128)(2,1)}), bf16[16,2,208,128]{3,2,1,0:T(8,128)(2,1)S(1)}, u32[]{:S(2)}, u32[]{:S(2)}) async-start(bf16[16,2,208,128]{3,2,1,0:T(8,128)(2,1)} %pad_maximum_fusion.3), calls=%async_computation | async-start | bytes 3407872 | tf_op jit(solution)/shard_map/all_to_all | solution.py:211
  51.3 5.8 %collective-permute-start = (bf16[1,528,128]{2,1,0:T(8,128)(2,1)S(1)}, bf16[1,528,128]{2,1,0:T(8,128)(2,1)S(1)}, u32[]{:S(2)}, u32[]{:S(2)}) collective-permute-start(bf16[1,528,128]{2,1,0:T(8,128)(2,1)S(1)} %maximum_maximum_fusion), channel_id=1, source_target_pairs={{16,0},{32,16},{48,32},{64,48},{80,64},{96,80},{112,96},{17,1},{33... | collective-permute-start | bytes 405512 | tf_op jit(solution)/shard_map/ppermute | solution.py:17
  53.4 5.2 %copy-start.4 = (bf16[512,1024]{1,0:T(8,128)(2,1)S(1)}, bf16[512,1024]{1,0:T(8,128)(2,1)}, u32[]{:S(2)}) copy-start(bf16[512,1024]{1,0:T(8,128)(2,1)} %constant.133) | copy-start | bytes 3145732
  57.2 2.2 %copy-start.2 = (bf16[512,512]{1,0:T(8,128)(2,1)S(1)}, bf16[512,512]{1,0:T(8,128)(2,1)}, u32[]{:S(2)}) copy-start(bf16[512,512]{1,0:T(8,128)(2,1)} %constant.127.clone) | copy-start | bytes 1572868
  58.3 1.8 %copy-start.3 = (bf16[512,512]{1,0:T(8,128)(2,1)S(1)}, bf16[512,512]{1,0:T(8,128)(2,1)}, u32[]{:S(2)}) copy-start(bf16[512,512]{1,0:T(8,128)(2,1)} %constant.128.clone) | copy-start | bytes 1572868
  67.3 1.3 %copy-start.5 = (bf16[512,512]{1,0:T(8,128)(2,1)S(1)}, bf16[512,512]{1,0:T(8,128)(2,1)}, u32[]{:S(2)}) copy-start(bf16[512,512]{1,0:T(8,128)(2,1)} %constant.138) | copy-start | bytes 1572868
  70.4 16.2 %collective-permute-start.4 = (bf16[4,512,128]{2,1,0:T(8,128)(2,1)S(1)}, bf16[4,512,128]{2,1,0:T(8,128)(2,1)S(1)}, u32[]{:S(2)}, u32[]{:S(2)}) collective-permute-start(bf16[4,512,128]{2,1,0:T(8,128)(2,1)S(1)} %get-tuple-element.28), channel_id=1, source_target_pairs={{1,0},{2,1},{3,2},{4,3},{5,4},{6,5},{7,6},{8,7},{9,8},{10,9},{11,1... | collective-permute-start | bytes 1572872 | tf_op jit(solution)/shard_map/ppermute | solution.py:17
  72.4 18.3 %collective-permute-start.3 = (bf16[4,512,128]{2,1,0:T(8,128)(2,1)S(1)}, bf16[4,512,128]{2,1,0:T(8,128)(2,1)S(1)}, u32[]{:S(2)}, u32[]{:S(2)}) collective-permute-start(bf16[4,512,128]{2,1,0:T(8,128)(2,1)S(1)} %get-tuple-element.27), channel_id=1, source_target_pairs={{0,1},{1,2},{2,3},{3,4},{4,5},{5,6},{6,7},{7,8},{8,9},{9,10},{10,1... | collective-permute-start | bytes 1572872 | tf_op jit(solution)/shard_map/ppermute | solution.py:17
  77.9 17.3 %collective-permute-start.2 = (bf16[4,128,512]{2,1,0:T(8,128)(2,1)S(1)}, bf16[4,128,512]{2,1,0:T(8,128)(2,1)S(1)}, u32[]{:S(2)}, u32[]{:S(2)}) collective-permute-start(bf16[4,128,512]{2,1,0:T(8,128)(2,1)S(1)} %get-tuple-element.24), channel_id=1, source_target_pairs={{16,0},{32,16},{48,32},{64,48},{80,64},{96,80},{112,96},{17,1},{33... | collective-permute-start | bytes 1572872 | tf_op jit(solution)/shard_map/ppermute | solution.py:17
  79.8 15.5 %collective-permute-start.1 = (bf16[4,128,512]{2,1,0:T(8,128)(2,1)S(1)}, bf16[4,128,512]{2,1,0:T(8,128)(2,1)S(1)}, u32[]{:S(2)}, u32[]{:S(2)}) collective-permute-start(bf16[4,128,512]{2,1,0:T(8,128)(2,1)S(1)} %get-tuple-element.23), channel_id=1, source_target_pairs={{0,16},{16,32},{32,48},{48,64},{64,80},{80,96},{96,112},{1,17},{17... | collective-permute-start | bytes 1572872 | tf_op jit(solution)/shard_map/ppermute | solution.py:17
  90.8 5.8 %collective-permute-start.6 = (bf16[4,128,256]{2,1,0:T(8,128)(2,1)S(1)}, bf16[4,128,256]{2,1,0:T(8,128)(2,1)S(1)}, u32[]{:S(2)}, u32[]{:S(2)}) collective-permute-start(bf16[4,128,256]{2,1,0:T(8,128)(2,1)S(1)} %pad_maximum_fusion.8), channel_id=1, source_target_pairs={{16,0},{32,16},{48,32},{64,48},{80,64},{96,80},{112,96},{17,1},{33... | collective-permute-start | bytes 786440 | tf_op jit(solution)/shard_map/ppermute | solution.py:17
  92.8 7.7 %collective-permute-start.5 = (bf16[4,128,256]{2,1,0:T(8,128)(2,1)S(1)}, bf16[4,128,256]{2,1,0:T(8,128)(2,1)S(1)}, u32[]{:S(2)}, u32[]{:S(2)}) collective-permute-start(bf16[4,128,256]{2,1,0:T(8,128)(2,1)S(1)} %pad_maximum_fusion.7), channel_id=1, source_target_pairs={{0,16},{16,32},{32,48},{48,64},{64,80},{80,96},{96,112},{1,17},{17... | collective-permute-start | bytes 786440 | tf_op jit(solution)/shard_map/ppermute | solution.py:17
  100.9 3.6 %copy-start.1 = (bf16[2352,128]{1,0:T(8,128)(2,1)S(1)}, bf16[2352,128]{1,0:T(8,128)(2,1)}, u32[]{:S(2)}) copy-start(bf16[2352,128]{1,0:T(8,128)(2,1)} %param.6) | copy-start | bytes 1806340

commit v22 on v21

--- a/solution.py
+++ b/solution.py
@@ -106,8 +106,8 @@
             edge_sin[n : 2 * n] + edge_cos[3 * n :],
         ]
     ).astype(jnp.bfloat16)
-    by_cos = dot32(arranged, cosine)
-    by_sin = dot32(arranged, sine)
+    both = dot32(arranged, jnp.concatenate([cosine, sine], axis=1))
+    by_cos, by_sin = both[:, :n], both[:, n:]
     return edge_fields, jnp.stack(
         [
             by_cos[:n] - by_sin[2 * n : 3 * n],

time: 105 us -> 106 us (level)
  waiting for transfers between devices: 37.3 us -> 38.6 us
    ppermute x7, waiting for transfers between devices: 13.4 us -> 14.6 us  [shifted(): return lax.ppermute(shard, axis, pairs)]
    dot_general x7 -> x6, matrix products: 7.74 us -> 7.64 us  [dot32(): return jnp.dot(a, b, preferred_element_type=jnp.float32)]
  transfers between devices with their start and end apart: 8 -> 8, of which waited for: 5 -> 5; matrix products, arithmetic and copies ran while one was open for 6% -> 5% of each run, Pallas kernels for 0% -> 0%
where the time goes in v22:
time: 106 us; the launch traced here: 105 us
  waiting for transfers between devices  38.6 us (36%)
  matrix products  25.3 us (24%)
  starting transfers between devices  24.5 us (23%)
  other arithmetic  12.7 us (12%)
  local copies, waits for them, and re-layouts  3.47 us (3%)
    all_to_all x1, waiting for transfers between devices, on_device(): lax.all_to_all(jnp.stack([same_sent, rise_sent], axis=1), 'py', 0, 0, til...  24 us
    ppermute x7, starting transfers between devices, shifted(): return lax.ppermute(shard, axis, pairs)  16.6 us
    ppermute x7, waiting for transfers between devices, shifted(): return lax.ppermute(shard, axis, pairs)  14.6 us
    dot_general x2, matrix products, gathered_rows(): jnp.dot(chosen.astype(table_rows.dtype), table_rows, preferred_element_ty...  11.2 us
    all_to_all x1, starting transfers between devices, on_device(): lax.all_to_all(jnp.stack([same_sent, rise_sent], axis=1), 'py', 0, 0, til...  7.89 us
    dot_general x6, matrix products, dot32(): return jnp.dot(a, b, preferred_element_type=jnp.float32)  7.64 us
    dot_general x3, matrix products, one_hot_rows(): jnp.dot(picks.astype(values.dtype), values, preferred_element_type=values...  5.8 us
    add x1, other arithmetic, on_device(): return col_weight * rows_done + (1.0 - col_weight) * horizontal  3.54 us
  transfers between devices with their start and end apart: 8, of which 5 were waited for; matrix products, arithmetic and copies ran while one was open for 5% of the time, Pallas kernels for 0%

profile of v22, /device:TPU:40, one launch (start us, length us, event | category | flops | bytes accessed | tf_op | source)
XLA Modules:
  0.0 105.1 jit_solution(17854748183500776610)
XLA Ops:
  0.0 1.3 %constant_dynamic-slice_fusion.3 = (s32[1,16,192]{1,2,0:T(8,128)S(1)}, s32[1,16,192]{1,2,0:T(8,128)S(1)}, s32[1,16,192]{1,2,0:T(8,128)S(1)}, s32[1,16,192]{1,2,0:T(8,128)S(1)}) fusion(s32[1,128,192]{1,2,0:T(8,128)} %param.8, s32[]{:T(128)S(6)} %select_n.142, s32[]{:T(128)S(6)} %select_n.146, s32[1,128,192]{1,2,0:T(8,128)} %param.7), kind=kLoop, calls=%fused_computation.158 | loop fusion | bytes 98312 | tf_op jit(solution)/shard_map/dynamic_slice | solution.py:200
  1.3 0.8 fusion.76
  2.5 0.1 fusion.56
  2.9 5.6 %fusion.17 = bf16[3072,128]{1,0:T(8,128)(2,1)S(1)} fusion(bf16[2352,128]{1,0:T(8,128)(2,1)S(1)} %copy-done, s32[3072]{0:T(1024)S(1)} %eq.43), kind=kOutput, calls=%fused_computation.22 | convolution fusion | flops 1857306624 | bytes 1400832 | tf_op jit(solution)/shard_map/dot_general | solution.py:153
  8.5 5.6 %fusion.16 = bf16[3072,128]{1,0:T(8,128)(2,1)S(1)} fusion(bf16[2352,128]{1,0:T(8,128)(2,1)S(1)} %copy-done, s32[3072]{0:T(1024)S(1)} %eq.89), kind=kOutput, calls=%fused_computation.21 | convolution fusion | flops 1857306624 | bytes 1400832 | tf_op jit(solution)/shard_map/dot_general | solution.py:153
  14.2 0.4 maximum_bitcast_fusion
  14.6 1.3 %pad_maximum_fusion.3 = bf16[16,2,208,128]{3,2,1,0:T(8,128)(2,1)} fusion(bf16[16,1,208,128]{3,2,1,0:T(8,128)(2,1)S(1)} %get-tuple-element.62, bf16[16,1,208,128]{3,2,1,0:T(8,128)(2,1)S(1)} %get-tuple-element.61), kind=kLoop, calls=%fused_computation.36 | loop fusion | flops 851968 | bytes 3407872 | tf_op jit(solution)/shard_map/stack | solution.py:211
  15.9 7.9 %all-to-all-start = ((bf16[16,2,208,128]{3,2,1,0:T(8,128)(2,1)}), bf16[16,2,208,128]{3,2,1,0:T(8,128)(2,1)S(1)}, u32[]{:S(2)}, u32[]{:S(2)}) async-start(bf16[16,2,208,128]{3,2,1,0:T(8,128)(2,1)} %pad_maximum_fusion.3), calls=%async_computation | async-start | bytes 3407872 | tf_op jit(solution)/shard_map/all_to_all | solution.py:211
  24.1 24.0 %all-to-all-done = bf16[16,2,208,128]{3,2,1,0:T(8,128)(2,1)S(1)} async-done(((bf16[16,2,208,128]{3,2,1,0:T(8,128)(2,1)}), bf16[16,2,208,128]{3,2,1,0:T(8,128)(2,1)S(1)}, u32[]{:S(2)}, u32[]{:S(2)}) %all-to-all-start) | async-done | bytes 1703968 | tf_op jit(solution)/shard_map/all_to_all | solution.py:211
  48.0 0.1 slice_bitcast_fusion
  48.8 0.3 reduce-window.9
  49.2 0.1 slice_reduce_fusion
  49.4 0.8 fusion.10
  50.1 1.0 fusion.27
  51.2 0.1 maximum_maximum_fusion
  51.3 2.1 %collective-permute-start = (bf16[1,528,128]{2,1,0:T(8,128)(2,1)S(1)}, bf16[1,528,128]{2,1,0:T(8,128)(2,1)S(1)}, u32[]{:S(2)}, u32[]{:S(2)}) collective-permute-start(bf16[1,528,128]{2,1,0:T(8,128)(2,1)S(1)} %maximum_maximum_fusion), channel_id=1, source_target_pairs={{16,0},{32,16},{48,32},{64,48},{80,64},{96,80},{112,96},{17,1},{33... | collective-permute-start | bytes 405512 | tf_op jit(solution)/shard_map/ppermute | solution.py:17
  53.4 3.7 %fusion.2 = bf16[2048,128]{1,0:T(8,128)(2,1)S(1)} fusion(bf16[3072,128]{1,0:T(8,128)(2,1)S(1)} %bitcast.111, s32[3072]{0:T(1024)S(1)} %eq.93, s32[2048]{0:T(1024)S(1)} %iota_add_fusion), kind=kOutput, calls=%fused_computation.4 | convolution fusion | flops 1616904192 | bytes 1331200 | tf_op jit(solution)/shard_map/dot_general | solution.py:148
  57.2 1.1 %fusion.20 = bf16[2048,128]{1,0:T(8,128)(2,1)S(1)} fusion(bf16[2048,128]{1,0:T(8,128)(2,1)S(1)} %fusion.2, s32[512]{0:T(512)S(1)} %bitcast.120, s32[2048]{0:T(1024)S(1)} %iota_add_fusion, bf16[1,528,128]{2,1,0:T(8,128)(2,1)S(1)} %collective-permute-done), kind=kOutput, calls=%fused_computation.26 | convolution fusion | flops 269746176 | bytes 1189888 | tf_op jit(solution)/shard_map/dot_general | solution.py:148
  58.3 0.3 reshape.309
  58.6 0.7 convolution_convert_fusion
  59.4 0.7 fusion.88
  60.1 0.7 fusion.89
  60.8 0.3 multiply_convert_fusion.3
  61.1 1.0 multiply_convert_fusion.2
  62.1 1.3 %fusion.48 = f32[512,2048]{1,0:T(8,128)S(1)} fusion(bf16[512,512]{1,0:T(8,128)(2,1)S(1)} %copy-done.3, bf16[512,512]{1,0:T(8,128)(2,1)S(1)} %get-tuple-element.21, bf16[512,512]{1,0:T(8,128)(2,1)S(1)} %get-tuple-element.22, bf16[512,512]{1,0:T(8,128)(2,1)S(1)} %get-tuple-element.20, bf16[512,512]{1,0:T(8,128)(2,1)S(1)} %get-tuple-element.5), kind=kOutput, calls=%fused_computation.79 | convolution fusion | flops 1082130432 | bytes 6815744 | tf_op jit(solution)/shard_map/dot_general | solution.py:51
  63.3 1.3 %fusion.49 = f32[512,2048]{1,0:T(8,128)S(1)} fusion(bf16[512,512]{1,0:T(8,128)(2,1)S(1)} %copy-done.2, bf16[512,512]{1,0:T(8,128)(2,1)S(1)} %get-tuple-element.21, bf16[512,512]{1,0:T(8,128)(2,1)S(1)} %get-tuple-element.22, bf16[512,512]{1,0:T(8,128)(2,1)S(1)} %get-tuple-element.20, bf16[512,512]{1,0:T(8,128)(2,1)S(1)} %get-tuple-element.5), kind=kOutput, calls=%fused_computation.80 | convolution fusion | flops 1082130432 | bytes 6815744 | tf_op jit(solution)/shard_map/dot_general | solution.py:51
  64.6 1.2 %fusion.24 = (bf16[512,1024]{1,0:T(8,128)(2,1)S(1)}, bf16[512,1024]{1,0:T(8,128)(2,1)S(1)}) fusion(f32[512,2048]{1,0:T(8,128)S(1)} %fusion.48, f32[512,2048]{1,0:T(8,128)S(1)} %fusion.49), kind=kLoop, calls=%fused_computation.30 | loop fusion | flops 2097152 | bytes 10485760 | tf_op jit(solution)/shard_map/convert.20
  66.0 2.5 %fusion.47 = f32[2048,1024]{1,0:T(8,128)S(1)} fusion(bf16[512,1024]{1,0:T(8,128)(2,1)S(1)} %copy-done.4, bf16[512,512]{1,0:T(8,128)(2,1)S(1)} %get-tuple-element.32, bf16[512,512]{1,0:T(8,128)(2,1)S(1)} %get-tuple-element.31, bf16[512,512]{1,0:T(8,128)(2,1)S(1)} %get-tuple-element.30, bf16[512,512]{1,0:T(8,128)(2,1)S(1)} %get-tuple-element.29), kind=kOutput, calls=%fused_computation.78 | convolution fusion | flops 2155872256 | bytes 11534336 | tf_op jit(solution)/shard_map/dot_general | solution.py:51
  68.5 1.2 %fusion.46 = f32[2048,512]{1,0:T(8,128)S(1)} fusion(bf16[512,512]{1,0:T(8,128)(2,1)S(1)} %copy-done.5, bf16[512,512]{1,0:T(8,128)(2,1)S(1)} %get-tuple-element.32, bf16[512,512]{1,0:T(8,128)(2,1)S(1)} %get-tuple-element.31, bf16[512,512]{1,0:T(8,128)(2,1)S(1)} %get-tuple-element.30, bf16[512,512]{1,0:T(8,128)(2,1)S(1)} %get-tuple-element.29), kind=kOutput, calls=%fused_computation.77 | convolution fusion | flops 1082130432 | bytes 6815744 | tf_op jit(solution)/shard_map/dot_general | solution.py:51
  69.7 0.3 fusion.50
  70.0 0.1 pad_maximum_fusion.4
  70.1 0.2 fusion.83
  70.3 2.0 %collective-permute-start.4 = (bf16[4,512,128]{2,1,0:T(8,128)(2,1)S(1)}, bf16[4,512,128]{2,1,0:T(8,128)(2,1)S(1)}, u32[]{:S(2)}, u32[]{:S(2)}) collective-permute-start(bf16[4,512,128]{2,1,0:T(8,128)(2,1)S(1)} %get-tuple-element.28), channel_id=1, source_target_pairs={{1,0},{2,1},{3,2},{4,3},{5,4},{6,5},{7,6},{8,7},{9,8},{10,9},{11,1... | collective-permute-start | bytes 1572872 | tf_op jit(solution)/shard_map/ppermute | solution.py:17
  72.3 0.8 fusion.38
  73.1 3.8 %collective-permute-start.3 = (bf16[4,512,128]{2,1,0:T(8,128)(2,1)S(1)}, bf16[4,512,128]{2,1,0:T(8,128)(2,1)S(1)}, u32[]{:S(2)}, u32[]{:S(2)}) collective-permute-start(bf16[4,512,128]{2,1,0:T(8,128)(2,1)S(1)} %get-tuple-element.27), channel_id=1, source_target_pairs={{0,1},{1,2},{2,3},{3,4},{4,5},{5,6},{6,7},{7,8},{8,9},{9,10},{10,1... | collective-permute-start | bytes 1572872 | tf_op jit(solution)/shard_map/ppermute | solution.py:17
  77.0 0.3 pad_maximum_fusion.2
  77.4 1.9 %collective-permute-start.2 = (bf16[4,128,512]{2,1,0:T(8,128)(2,1)S(1)}, bf16[4,128,512]{2,1,0:T(8,128)(2,1)S(1)}, u32[]{:S(2)}, u32[]{:S(2)}) collective-permute-start(bf16[4,128,512]{2,1,0:T(8,128)(2,1)S(1)} %get-tuple-element.24), channel_id=1, source_target_pairs={{16,0},{32,16},{48,32},{64,48},{80,64},{96,80},{112,96},{17,1},{33... | collective-permute-start | bytes 1572872 | tf_op jit(solution)/shard_map/ppermute | solution.py:17
  79.3 2.4 %collective-permute-start.1 = (bf16[4,128,512]{2,1,0:T(8,128)(2,1)S(1)}, bf16[4,128,512]{2,1,0:T(8,128)(2,1)S(1)}, u32[]{:S(2)}, u32[]{:S(2)}) collective-permute-start(bf16[4,128,512]{2,1,0:T(8,128)(2,1)S(1)} %get-tuple-element.23), channel_id=1, source_target_pairs={{0,16},{16,32},{32,48},{48,64},{64,80},{80,96},{96,112},{1,17},{17... | collective-permute-start | bytes 1572872 | tf_op jit(solution)/shard_map/ppermute | solution.py:17
  81.7 4.8 %collective-permute-done.4 = bf16[4,512,128]{2,1,0:T(8,128)(2,1)S(1)} collective-permute-done((bf16[4,512,128]{2,1,0:T(8,128)(2,1)S(1)}, bf16[4,512,128]{2,1,0:T(8,128)(2,1)S(1)}, u32[]{:S(2)}, u32[]{:S(2)}) %collective-permute-start.4) | collective-permute-done | bytes 524320 | tf_op jit(solution)/shard_map/ppermute | solution.py:17
  86.6 4.8 %collective-permute-done.3 = bf16[4,512,128]{2,1,0:T(8,128)(2,1)S(1)} collective-permute-done((bf16[4,512,128]{2,1,0:T(8,128)(2,1)S(1)}, bf16[4,512,128]{2,1,0:T(8,128)(2,1)S(1)}, u32[]{:S(2)}, u32[]{:S(2)}) %collective-permute-start.3) | collective-permute-done | bytes 524320 | tf_op jit(solution)/shard_map/ppermute | solution.py:17
  91.5 1.9 %collective-permute-start.6 = (bf16[4,128,256]{2,1,0:T(8,128)(2,1)S(1)}, bf16[4,128,256]{2,1,0:T(8,128)(2,1)S(1)}, u32[]{:S(2)}, u32[]{:S(2)}) collective-permute-start(bf16[4,128,256]{2,1,0:T(8,128)(2,1)S(1)} %pad_maximum_fusion.10), channel_id=1, source_target_pairs={{16,0},{32,16},{48,32},{64,48},{80,64},{96,80},{112,96},{17,1},{33... | collective-permute-start | bytes 786440 | tf_op jit(solution)/shard_map/ppermute | solution.py:17
  93.5 2.4 %collective-permute-start.5 = (bf16[4,128,256]{2,1,0:T(8,128)(2,1)S(1)}, bf16[4,128,256]{2,1,0:T(8,128)(2,1)S(1)}, u32[]{:S(2)}, u32[]{:S(2)}) collective-permute-start(bf16[4,128,256]{2,1,0:T(8,128)(2,1)S(1)} %pad_maximum_fusion.9), channel_id=1, source_target_pairs={{0,16},{16,32},{32,48},{48,64},{64,80},{80,96},{96,112},{1,17},{17... | collective-permute-start | bytes 786440 | tf_op jit(solution)/shard_map/ppermute | solution.py:17
  95.9 0.1 convert_element_type.160
  96.1 0.1 convert_element_type.159
  96.2 1.1 %collective-permute-done.6 = bf16[4,128,256]{2,1,0:T(8,128)(2,1)S(1)} collective-permute-done((bf16[4,128,256]{2,1,0:T(8,128)(2,1)S(1)}, bf16[4,128,256]{2,1,0:T(8,128)(2,1)S(1)}, u32[]{:S(2)}, u32[]{:S(2)}) %collective-permute-start.6) | collective-permute-done | bytes 262176 | tf_op jit(solution)/shard_map/ppermute | solution.py:17
  97.3 3.8 %collective-permute-done.5 = bf16[4,128,256]{2,1,0:T(8,128)(2,1)S(1)} collective-permute-done((bf16[4,128,256]{2,1,0:T(8,128)(2,1)S(1)}, bf16[4,128,256]{2,1,0:T(8,128)(2,1)S(1)}, u32[]{:S(2)}, u32[]{:S(2)}) %collective-permute-start.5) | collective-permute-done | bytes 262176 | tf_op jit(solution)/shard_map/ppermute | solution.py:17
  101.2 0.4 fusion.35
  101.6 3.5 %fusion.13 = f32[4,512,512]{2,1,0:T(8,128)} fusion(f32[4,128,512]{2,1,0:T(8,128)S(1)} %convert_element_type.160, f32[4,128,512]{2,1,0:T(8,128)S(1)} %convert_element_type.159, f32[4,512,128]{2,1,0:T(8,128)S(1)} %get-tuple-element.50, f32[4,512,128]{2,1,0:T(8,128)S(1)} %get-tuple-element.49, f32[512]{0:T(512)S(1)} %pad.18.clone, ...), kind=kLoop, calls=%fused_computation.17 | loop fusion | flops 14680064 | bytes 10496000 | tf_op jit(solution)/shard_map/add | solution.py:268
  (69 shorter events, 2.3 us)
Async XLA Ops:
  0.0 2.9 %copy-start = (bf16[2352,128]{1,0:T(8,128)(2,1)S(1)}, bf16[2352,128]{1,0:T(8,128)(2,1)}, u32[]{:S(2)}) copy-start(bf16[2352,128]{1,0:T(8,128)(2,1)} %param.6) | copy-start | bytes 1806340
  15.9 32.1 %all-to-all-start = ((bf16[16,2,208,128]{3,2,1,0:T(8,128)(2,1)}), bf16[16,2,208,128]{3,2,1,0:T(8,128)(2,1)S(1)}, u32[]{:S(2)}, u32[]{:S(2)}) async-start(bf16[16,2,208,128]{3,2,1,0:T(8,128)(2,1)} %pad_maximum_fusion.3), calls=%async_computation | async-start | bytes 3407872 | tf_op jit(solution)/shard_map/all_to_all | solution.py:211
  51.3 5.8 %collective-permute-start = (bf16[1,528,128]{2,1,0:T(8,128)(2,1)S(1)}, bf16[1,528,128]{2,1,0:T(8,128)(2,1)S(1)}, u32[]{:S(2)}, u32[]{:S(2)}) collective-permute-start(bf16[1,528,128]{2,1,0:T(8,128)(2,1)S(1)} %maximum_maximum_fusion), channel_id=1, source_target_pairs={{16,0},{32,16},{48,32},{64,48},{80,64},{96,80},{112,96},{17,1},{33... | collective-permute-start | bytes 405512 | tf_op jit(solution)/shard_map/ppermute | solution.py:17
  53.4 5.2 %copy-start.4 = (bf16[512,1024]{1,0:T(8,128)(2,1)S(1)}, bf16[512,1024]{1,0:T(8,128)(2,1)}, u32[]{:S(2)}) copy-start(bf16[512,1024]{1,0:T(8,128)(2,1)} %constant.133) | copy-start | bytes 3145732
  57.2 2.2 %copy-start.2 = (bf16[512,512]{1,0:T(8,128)(2,1)S(1)}, bf16[512,512]{1,0:T(8,128)(2,1)}, u32[]{:S(2)}) copy-start(bf16[512,512]{1,0:T(8,128)(2,1)} %constant.127.clone) | copy-start | bytes 1572868
  58.3 1.8 %copy-start.3 = (bf16[512,512]{1,0:T(8,128)(2,1)S(1)}, bf16[512,512]{1,0:T(8,128)(2,1)}, u32[]{:S(2)}) copy-start(bf16[512,512]{1,0:T(8,128)(2,1)} %constant.128.clone) | copy-start | bytes 1572868
  66.0 2.5 %copy-start.5 = (bf16[512,512]{1,0:T(8,128)(2,1)S(1)}, bf16[512,512]{1,0:T(8,128)(2,1)}, u32[]{:S(2)}) copy-start(bf16[512,512]{1,0:T(8,128)(2,1)} %constant.138) | copy-start | bytes 1572868
  70.3 16.2 %collective-permute-start.4 = (bf16[4,512,128]{2,1,0:T(8,128)(2,1)S(1)}, bf16[4,512,128]{2,1,0:T(8,128)(2,1)S(1)}, u32[]{:S(2)}, u32[]{:S(2)}) collective-permute-start(bf16[4,512,128]{2,1,0:T(8,128)(2,1)S(1)} %get-tuple-element.28), channel_id=1, source_target_pairs={{1,0},{2,1},{3,2},{4,3},{5,4},{6,5},{7,6},{8,7},{9,8},{10,9},{11,1... | collective-permute-start | bytes 1572872 | tf_op jit(solution)/shard_map/ppermute | solution.py:17
  73.1 18.3 %collective-permute-start.3 = (bf16[4,512,128]{2,1,0:T(8,128)(2,1)S(1)}, bf16[4,512,128]{2,1,0:T(8,128)(2,1)S(1)}, u32[]{:S(2)}, u32[]{:S(2)}) collective-permute-start(bf16[4,512,128]{2,1,0:T(8,128)(2,1)S(1)} %get-tuple-element.27), channel_id=1, source_target_pairs={{0,1},{1,2},{2,3},{3,4},{4,5},{5,6},{6,7},{7,8},{8,9},{9,10},{10,1... | collective-permute-start | bytes 1572872 | tf_op jit(solution)/shard_map/ppermute | solution.py:17
  77.4 18.6 %collective-permute-start.2 = (bf16[4,128,512]{2,1,0:T(8,128)(2,1)S(1)}, bf16[4,128,512]{2,1,0:T(8,128)(2,1)S(1)}, u32[]{:S(2)}, u32[]{:S(2)}) collective-permute-start(bf16[4,128,512]{2,1,0:T(8,128)(2,1)S(1)} %get-tuple-element.24), channel_id=1, source_target_pairs={{16,0},{32,16},{48,32},{64,48},{80,64},{96,80},{112,96},{17,1},{33... | collective-permute-start | bytes 1572872 | tf_op jit(solution)/shard_map/ppermute | solution.py:17
  79.3 16.8 %collective-permute-start.1 = (bf16[4,128,512]{2,1,0:T(8,128)(2,1)S(1)}, bf16[4,128,512]{2,1,0:T(8,128)(2,1)S(1)}, u32[]{:S(2)}, u32[]{:S(2)}) collective-permute-start(bf16[4,128,512]{2,1,0:T(8,128)(2,1)S(1)} %get-tuple-element.23), channel_id=1, source_target_pairs={{0,16},{16,32},{32,48},{48,64},{64,80},{80,96},{96,112},{1,17},{17... | collective-permute-start | bytes 1572872 | tf_op jit(solution)/shard_map/ppermute | solution.py:17
  91.5 5.8 %collective-permute-start.6 = (bf16[4,128,256]{2,1,0:T(8,128)(2,1)S(1)}, bf16[4,128,256]{2,1,0:T(8,128)(2,1)S(1)}, u32[]{:S(2)}, u32[]{:S(2)}) collective-permute-start(bf16[4,128,256]{2,1,0:T(8,128)(2,1)S(1)} %pad_maximum_fusion.10), channel_id=1, source_target_pairs={{16,0},{32,16},{48,32},{64,48},{80,64},{96,80},{112,96},{17,1},{33... | collective-permute-start | bytes 786440 | tf_op jit(solution)/shard_map/ppermute | solution.py:17
  93.5 7.7 %collective-permute-start.5 = (bf16[4,128,256]{2,1,0:T(8,128)(2,1)S(1)}, bf16[4,128,256]{2,1,0:T(8,128)(2,1)S(1)}, u32[]{:S(2)}, u32[]{:S(2)}) collective-permute-start(bf16[4,128,256]{2,1,0:T(8,128)(2,1)S(1)} %pad_maximum_fusion.9), channel_id=1, source_target_pairs={{0,16},{16,32},{32,48},{48,64},{64,80},{80,96},{96,112},{1,17},{17... | collective-permute-start | bytes 786440 | tf_op jit(solution)/shard_map/ppermute | solution.py:17
  101.6 3.6 %copy-start.1 = (bf16[2352,128]{1,0:T(8,128)(2,1)S(1)}, bf16[2352,128]{1,0:T(8,128)(2,1)}, u32[]{:S(2)}) copy-start(bf16[2352,128]{1,0:T(8,128)(2,1)} %param.6) | copy-start | bytes 1806340
